TPU v7x, 256 devices: a whole 4x4x8 slice. The times are simulated.
256 devices in a mesh: seq: 32 (over z, x_hi, core), mp: 8 (over x_lo, y).
Axes of the slice: x: 4 (x_hi: 2, x_lo: 2; x = x_hi * 2 + x_lo), y: 4, z: 8, core: 2. Of those that a mesh axis runs over, the one named last changes fastest.
Arguments:
- queries: bfloat16 [4096, 8192], P('seq', 'mp'), may hold values from -200 to 200
- keys: bfloat16 [4096, 1024], P('seq', 'mp'), may hold values from -7 to 7
- values: float32 [4096, 1024], P('seq', 'mp'), may hold values from -24 to 24
- inputs_x: bfloat16 [4096, 8192], P('seq', 'mp'), may hold values from -6 to 6
- in_b: bfloat16 [4096, 128], P('seq'), may hold values from -6 to 6
- in_c: bfloat16 [4096, 128], P('seq'), may hold values from -6 to 6
- log_decay: float32 [4096, 64], P('seq', 'mp'), may hold values from -2 to 0
Outputs:
- grad_x: float32 [4096, 8192], P('seq', 'mp')
- grad_b: float32 [4096, 128], P(('seq', 'mp'))
- grad_c: float32 [4096, 128], P(('seq', 'mp'))
All inputs are finite; a program needn't handle non-finite values.
Results may differ from a plain program's by a relative error of at most 0.00035.
Values may be sent and summed in bfloat16 or wider, within the bound.
No kernel may reach another device: no remote copies, remote signals or barrier semaphores. Data moves between devices by JAX's collectives and lax.ppermute only.
A program may use at most 128 MiB of HBM per device.

v0:
```python
import math

import jax
import jax.numpy as jnp
from jax import lax
from jax.sharding import PartitionSpec as P

HEAD_WIDTH = 128
N = 128
HQ_DEV = 8
KV_DEV = 1


very_negative = -1e30
highest = lax.Precision.HIGHEST


def prefix(value, axis, join, neutral):
    count, mine = (lax.axis_size(axis), lax.axis_index(axis))
    pieces = jax.tree.map(lambda part: lax.all_gather(part, axis), value)
    subtotal = jax.tree.map(
        lambda part, zero: jnp.full_like(part, 0) + jnp.asarray(zero, part.dtype), value, neutral
    )

    def hop(position, subtotal):
        longer = join(subtotal, jax.tree.map(lambda part: part[position], pieces))
        return jax.tree.map(lambda new, old: jnp.where(position < mine, new, old), longer, subtotal)

    return lax.fori_loop(0, count - 1, hop, subtotal)


def chain_step(earlier, later):
    return (earlier[0] + later[0], jnp.exp(later[0])[:, None, None] * earlier[1] + later[1])


def attend_rows(current, query_head_rows, query_pos, key_piece, value_piece):
    row_top, denominator, mixture = current
    piece_rows = key_piece.shape[0]
    kv_heads = query_head_rows.shape[1]
    key_head_rows = key_piece.reshape(piece_rows, kv_heads, HEAD_WIDTH)
    value_head_rows = value_piece.reshape(piece_rows, kv_heads, HEAD_WIDTH)
    scores = jnp.einsum(
        "qkgd,nkd->qkgn", query_head_rows, key_head_rows, precision=highest
    ) / math.sqrt(HEAD_WIDTH)
    key_pos = jnp.arange(piece_rows, dtype=jnp.int32)
    allowed = (key_pos[None, :] <= query_pos[:, None])[:, None, None, :]
    scores = jnp.where(allowed, scores, very_negative)
    new_top = jnp.maximum(row_top, jnp.max(scores, axis=-1))
    weights = jnp.where(allowed, jnp.exp(scores - new_top[..., None]), 0.0)
    denominator = jnp.sum(weights, axis=-1)
    mixture = jnp.einsum("qkgn,nkd->qkgd", weights, value_head_rows, precision=highest)
    return (new_top, denominator, mixture)


def local(queries, keys, values, inputs_x, in_b, in_c, log_decay):
    row_count = queries.shape[0]
    group_width = HQ_DEV // KV_DEV
    seq_count = lax.axis_size("seq")
    own_index = lax.axis_index("seq")
    first_query = own_index * row_count
    query_sets = ((queries, first_query + jnp.arange(row_count, dtype=jnp.int32)),)
    head_sets = tuple(
        (
            rows.astype(jnp.float32).reshape(rows.shape[0], KV_DEV, group_width, HEAD_WIDTH)
            for rows, positions in query_sets
        )
    )
    pos_sets = tuple((positions for rows, positions in query_sets))
    start_state = tuple(
        (
            (
                jnp.full((positions.shape[0], KV_DEV, group_width), very_negative, jnp.float32),
                jnp.zeros((positions.shape[0], KV_DEV, group_width), jnp.float32),
                jnp.zeros((positions.shape[0], KV_DEV, group_width, HEAD_WIDTH), jnp.float32),
            )
            for positions in pos_sets
        )
    )
    key_piece = lax.all_gather(keys.astype(jnp.float32), "seq", axis=0, tiled=True)
    value_piece = lax.all_gather(values, "seq", axis=0, tiled=True)
    updated = []
    for current, query_head_rows, query_pos in zip(start_state, head_sets, pos_sets):

        def compute(state_now, query_head_rows=query_head_rows, query_pos=query_pos):
            return attend_rows(state_now, query_head_rows, query_pos, key_piece, value_piece)

        updated.append(compute(current))
    finished = tuple(updated)
    outputs = [
        (mixture / denominator[..., None]).reshape(mixture.shape[0], HQ_DEV, HEAD_WIDTH)
        for row_top, denominator, mixture in finished
    ]
    teacher_out = outputs[0]
    c_scale = 0.5 / math.sqrt(N * row_count * seq_count)
    student_x = inputs_x.astype(jnp.float32).reshape(row_count, HQ_DEV, HEAD_WIDTH)
    b_rows = in_b.astype(jnp.float32)
    c_rows = in_c.astype(jnp.float32) * c_scale
    cumulative = jnp.cumsum(log_decay, axis=0)
    totals = cumulative[-1]
    heads_first = cumulative.T
    causal = jnp.arange(row_count)[:, None] >= jnp.arange(row_count)[None, :]
    decays = jnp.exp(
        jnp.where(causal[None], heads_first[:, :, None] - heads_first[:, None, :], -jnp.inf)
    )
    inner_products = jnp.dot(in_c, in_b.T, preferred_element_type=jnp.float32) * c_scale
    mixing = decays * inner_products[None]
    rising = jnp.exp(cumulative)
    ending = jnp.exp(totals[None, :] - cumulative)
    local_state = jnp.einsum(
        "shp,sn->hpn", student_x * ending[:, :, None], b_rows, precision=highest
    )
    identity = (jnp.zeros_like(totals), jnp.zeros_like(local_state))
    prefix_log, state_in = prefix((totals, local_state), "seq", chain_step, identity)
    y_intra = jnp.einsum("hts,shp->thp", mixing, student_x, precision=highest)
    y_inter = jnp.einsum("tn,hpn->thp", c_rows, state_in, precision=highest) * rising[:, :, None]
    mismatch = y_intra + y_inter - teacher_out
    scaled_mismatch = mismatch * rising[:, :, None]
    local_grad = jnp.einsum("thp,tn->hpn", scaled_mismatch, c_rows, precision=highest)
    grad_pieces = lax.all_gather(local_grad[None], "seq", axis=0, tiled=True)
    log_pieces = lax.all_gather(prefix_log[None], "seq", axis=0, tiled=True)
    shard_ids = jnp.arange(grad_pieces.shape[0], dtype=jnp.int32)
    log_gaps = jnp.where(
        (shard_ids > own_index)[:, None], log_pieces - (prefix_log + totals)[None, :], -jnp.inf
    )
    later_grad = jnp.zeros_like(local_grad) + jnp.einsum(
        "ch,chpn->hpn", jnp.exp(log_gaps), grad_pieces, precision=highest
    )
    grad_x = jnp.einsum("hts,thp->shp", mixing, mismatch, precision=highest)
    grad_x = (
        grad_x
        + jnp.einsum("hpn,sn->shp", later_grad, b_rows, precision=highest) * ending[:, :, None]
    )
    products = jnp.einsum("thp,shp->hts", mismatch, student_x, precision=highest)
    weighted = decays * products
    grad_b = jnp.einsum("hts,tn->sn", weighted, c_rows, precision=highest)
    grad_b = grad_b + jnp.einsum(
        "shp,hpn->sn", student_x * ending[:, :, None], later_grad, precision=highest
    )
    grad_c = jnp.einsum("hts,sn->tn", weighted, b_rows, precision=highest)
    grad_c = grad_c + jnp.einsum("thp,hpn->tn", scaled_mismatch, state_in, precision=highest)
    summed_b, summed_c = (
        lax.psum_scatter(grad_b, "mp", scatter_dimension=0, tiled=True),
        lax.psum_scatter(grad_c, "mp", scatter_dimension=0, tiled=True),
    )
    return (grad_x.reshape(row_count, HQ_DEV * HEAD_WIDTH), summed_b, summed_c * c_scale)


def solution(mesh):
    in_specs = (
        P("seq", "mp"),
        P("seq", "mp"),
        P("seq", "mp"),
        P("seq", "mp"),
        P("seq", None),
        P("seq", None),
        P("seq", "mp"),
    )
    out_specs = (P("seq", "mp"), P(("seq", "mp"), None), P(("seq", "mp"), None))
    return jax.shard_map(local, mesh=mesh, in_specs=in_specs, out_specs=out_specs, check_vma=False)
```

profile of v0, /device:TPU:68, one launch (start us, length us, event | category | flops | bytes accessed | tf_op | source)
XLA Modules:
  0.0 594.0 jit_solution(6456232489600451371)
XLA Ops:
  7.2 1.4 convert_element_type.10
  11.7 1.9 fusion.35
  13.8 36.4 %all-gather.3 = f32[32,1,8]{2,1,0:T(1,128)S(1)} all-gather(f32[1,1,8]{2,1,0:T(1,128)S(1)} %get-tuple-element.162), channel_id=1, replica_groups=mesh['seq'=32,'mp'=8] {'seq'}, dimensions={0}, use_global_device_ids=true | all-gather | bytes 1056 | tf_op jit(solution)/shard_map/all_gather | solution.py:20
  52.2 37.3 %all-gather.9.cloned.1.call-done = f32[4096,128]{1,0:T(8,128)} async-done(((f32[128,128]{1,0:T(8,128)}), f32[4096,128]{1,0:T(8,128)}) %all-gather.9.cloned.1.call-update) | async-done | bytes 2097168 | tf_op jit(solution)/shard_map/all_gather | solution.py:79
  89.5 10.0 %fusion.5 = (f32[128,8]{0,1:T(8,128)S(1)}, f32[4096,128,8]{1,0,2:T(8,128)S(1)}) fusion(pred[128,4096]{0,1:T(8,128)(4,1)S(1)} %iota_compare_fusion, f32[4096,128]{1,0:T(8,128)} %all-gather.9.cloned.1.call-done, bf16[128,1024]{1,0:T(8,128)(2,1)S(1)} %copy-done), kind=kOutput, calls=%fused_computation.12 | convolution fusion | flops 6455032832 | bytes 19664896 | tf_op jit(solution)/shard_map/qkgd,nkd->qkgn/dot_general | solution.py:42
  99.6 5.7 copy-done.1
  105.3 4.0 fusion.6
  109.3 59.6 %all-gather.11.cloned.1.call-done = f32[4096,128]{1,0:T(8,128)} async-done(((f32[128,128]{1,0:T(8,128)}), f32[4096,128]{1,0:T(8,128)}) %all-gather.11.cloned.1.call-update) | async-done | bytes 2097168 | tf_op jit(solution)/shard_map/all_gather | solution.py:80
  168.9 32.2 %fusion.30 = f32[128,8,128]{2,0,1:T(8,128)S(1)} fusion(f32[4096,128]{1,0:T(8,128)} %all-gather.11.cloned.1.call-done, f32[4096,128,8]{1,0,2:T(8,128)} %copy-done.1, f32[128,8]{0,1:T(8,128)S(1)} %broadcast_maximum_fusion, pred[128,4096]{0,1:T(8,128)(4,1)S(1)} %iota_compare_fusion, f32[128,8]{0,1:T(8,128)S(1)} %fusion.6), kind=kOutput, calls=%fused_computation.40 | convolution fusion | flops 6459359232 | bytes 19931136 | tf_op jit(solution)/shard_map/qkgn,nkd->qkgd/dot_general | solution.py:51
  201.2 104.9 %all-gather.13.cloned.1.call-done = f32[256,128,128]{2,1,0:T(8,128)} async-done(((f32[8,128,128]{2,1,0:T(8,128)}), f32[256,128,128]{2,1,0:T(8,128)}) %all-gather.13.cloned.1.call-update) | async-done | bytes 16777232 | tf_op jit(solution)/shard_map/all_gather | solution.py:20
  306.1 37.8 %while.16 = (s32[]{:T(128)}, f32[8]{0:T(128)S(1)}, f32[8,128,128]{2,1,0:T(8,128)S(1)}, s32[]{:T(128)}, f32[32,8]{1,0:T(8,128)S(1)}, /*index=5*/f32[32,8,128,128]{3,2,1,0:T(8,128)}, s32[]{:T(128)}, s32[]{:T(128)}) while((s32[]{:T(128)}, f32[8]{0:T(128)S(1)}, f32[8,128,128]{2,1,0:T(8,128)S(1)}, s32[]{:T(128)}, ...), condition=%wide.region_2.3_spmd.clone, body=%wide.region_1.2_spmd.clone.sunk | while | flops 524316 | bytes 1573139 | solution.py:29
  307.4 1.2 fusion.91
  308.6 1.2 fusion.91
  309.8 1.2 fusion.91
  311.0 1.2 fusion.91
  312.2 1.2 fusion.91
  313.5 1.2 fusion.91
  314.7 1.2 fusion.91
  315.9 1.2 fusion.91
  317.1 1.2 fusion.91
  318.4 1.2 fusion.91
  319.6 1.2 fusion.91
  320.8 1.2 fusion.91
  322.0 1.2 fusion.91
  323.2 1.2 fusion.91
  324.5 1.2 fusion.91
  325.7 1.2 fusion.91
  326.9 1.2 fusion.91
  328.1 1.2 fusion.91
  329.3 1.2 fusion.91
  330.6 1.2 fusion.91
  331.8 1.2 fusion.91
  333.0 1.2 fusion.91
  334.2 1.2 fusion.91
  335.5 1.2 fusion.91
  336.7 1.2 fusion.91
  337.9 1.2 fusion.91
  339.1 1.2 fusion.91
  340.3 1.2 fusion.91
  341.6 1.2 fusion.91
  342.8 1.2 fusion.91
  346.6 1.9 fusion.40
  350.2 56.6 %all-reduce = f32[256]{0:T(256)S(1)} all-reduce(f32[256]{0:T(256)S(1)} %dynamic-update-slice), channel_id=3, replica_groups=mesh['seq'=32,'mp'=8] {'seq'}, use_global_device_ids=true, to_apply=%add | all-reduce | flops 256 | bytes 2048
  407.0 1.2 convolution_bitcast_fusion.2
  408.2 1.3 broadcast_multiply_fusion
  409.5 113.7 %all-gather.15.cloned.1.call-done = f32[256,128,128]{2,1,0:T(8,128)} async-done(((f32[8,128,128]{2,1,0:T(8,128)}), f32[256,128,128]{2,1,0:T(8,128)}) %all-gather.15.cloned.1.call-update) | async-done | bytes 16777232 | tf_op jit(solution)/shard_map/all_gather | solution.py:119
  523.2 21.8 %fusion.3 = f32[8,1,128,128]{3,1,2,0:T(1,128)S(1)} fusion(f32[32,8,1,1]{0,2,3,1:T(1,128)S(1)} %copy.56, f32[32,8,128,128]{3,2,1,0:T(8,128)} %bitcast.129), kind=kOutput, calls=%fused_computation.9 | convolution fusion | flops 50331648 | bytes 17302528 | tf_op jit(solution)/shard_map/ch,chpn->hpn/dot_general | solution.py:125
  548.4 38.8 %reduce-scatter.3.cloned.1.call-done = f32[16,128]{1,0:T(8,128)} async-done(((f32[128,128]{1,0:T(8,128)}), f32[16,128]{1,0:T(8,128)}) %reduce-scatter.3.cloned.1.call-update) | async-done | bytes 8208 | tf_op jit(solution)/shard_map/reduce_scatter | solution.py:142
  (86 shorter events, 14.0 us)
Async XLA Ops:
  7.2 82.4 %copy-start = (bf16[128,1024]{1,0:T(8,128)(2,1)S(1)}, bf16[128,1024]{1,0:T(8,128)(2,1)}, u32[]{:S(2)}) copy-start(bf16[128,1024]{1,0:T(8,128)(2,1)} %param.9) | copy-start | bytes 786436
  7.2 82.4 %all-gather.9.cloned.1.call-start = ((), (), s32[]{:S(2)}) async-start(), calls=%async_computation.2 | async-start | bytes 2162688 | tf_op jit(solution)/shard_map/all_gather | solution.py:79
  8.7 160.3 %all-gather.11.cloned.1.call-start = ((), (), s32[]{:S(2)}) async-start(), calls=%async_computation.3 | async-start | bytes 2162688 | tf_op jit(solution)/shard_map/all_gather | solution.py:80
  9.4 296.7 %all-gather.13.cloned.1.call-start = ((), (), s32[]{:S(2)}) async-start(), calls=%async_computation.6 | async-start | bytes 17301504 | tf_op jit(solution)/shard_map/all_gather | solution.py:20
  13.6 394.6 %reduce-scatter.5.cloned.1.call-start = ((), (), s32[]{:S(2)}) async-start(), calls=%async_computation.5 | async-start | bytes 73728 | tf_op jit(solution)/shard_map/reduce_scatter | solution.py:143
  99.5 5.7 copy-start.1
  109.3 234.7 %copy-start.2 = (bf16[128,128]{1,0:T(8,128)(2,1)S(1)}, bf16[128,128]{1,0:T(8,128)(2,1)}, u32[]{:S(2)}) copy-start(bf16[128,128]{1,0:T(8,128)(2,1)} %param.14) | copy-start | bytes 98308
  109.3 236.4 %copy-start.3 = (bf16[128,128]{1,0:T(8,128)(2,1)S(1)}, bf16[128,128]{1,0:T(8,128)(2,1)}, u32[]{:S(2)}) copy-start(bf16[128,128]{1,0:T(8,128)(2,1)} %param.13) | copy-start | bytes 98308
  109.3 239.3 %copy-start.4 = (u32[256]{0:T(256)S(1)}, u32[256]{0:T(256)}, u32[]{:S(2)}) copy-start(u32[256]{0:T(256)} %constant.52) | copy-start | bytes 3076
  346.6 176.7 %all-gather.15.cloned.1.call-start = ((), (), s32[]{:S(2)}) async-start(), calls=%async_computation.7 | async-start | bytes 17301504 | tf_op jit(solution)/shard_map/all_gather | solution.py:119
  348.6 238.6 %reduce-scatter.3.cloned.1.call-start = ((), (), s32[]{:S(2)}) async-start(), calls=%async_computation.4 | async-start | bytes 73728 | tf_op jit(solution)/shard_map/reduce_scatter | solution.py:142
Sparse Core Ops, SparseCore 0:
  10.8 78.6 all-gather.8
  92.3 76.5 all-gather.10
  172.3 133.7 all-gather.12
  346.7 39.9 reduce-scatter.4
  390.3 132.8 all-gather.14
  547.1 39.9 reduce-scatter.2
where the time goes:
time: 597 us; the launch traced here: 594 us
  waiting for transfers between devices  355 us (59%)
  blocking collectives  93 us (16%)
  matrix products  75.6 us (13%)
  other arithmetic  44.4 us (7%)
  between operations  15 us (3%)
  local copies, waits for them, and re-layouts  9.81 us (2%)
    all_gather x1, waiting for transfers between devices, local(): grad_pieces = lax.all_gather(local_grad[None], 'seq', axis=0, tiled=True)  114 us
    all_gather x1, waiting for transfers between devices, prefix(): pieces = jax.tree.map(lambda part: lax.all_gather(part, axis), value)  105 us
    all_gather x1, waiting for transfers between devices, local(): value_piece = lax.all_gather(values, 'seq', axis=0, tiled=True)  59.6 us
    unnamed x1, blocking collectives  56.6 us
    reduce_scatter x1, waiting for transfers between devices, local(): lax.psum_scatter(grad_b, 'mp', scatter_dimension=0, tiled=True)  38.8 us
    all_gather x1, waiting for transfers between devices, local(): lax.all_gather(keys.astype(jnp.float32), 'seq', axis=0, tiled=True)  37.3 us
    select_n x31, other arithmetic, hop(): jnp.where(position < mine, new, old)  36.4 us
    all_gather x1, blocking collectives, prefix(): pieces = jax.tree.map(lambda part: lax.all_gather(part, axis), value)  36.4 us
  transfers between devices with their start and end apart: 6, of which 5 were waited for; matrix products, arithmetic and copies ran while one was open for 10% of the time, Pallas kernels for 0%

commit v1 on v0

v1 whole, which is shorter than its diff:
```python
import math

import jax
import jax.numpy as jnp
from jax import lax
from jax.sharding import PartitionSpec as P

HEAD_WIDTH = 128
N = 128

very_negative = -1e30
highest = lax.Precision.HIGHEST


def shift(value, axis, distance, forward):
    count = lax.axis_size(axis)
    if forward:
        perm = [(j, j + distance) for j in range(count - distance)]
    else:
        perm = [(j + distance, j) for j in range(count - distance)]
    return lax.ppermute(value, axis, perm)


def exclusive_scan(state, logs, axis, forward):
    count = lax.axis_size(axis)
    window_state, window_log = shift((state, logs), axis, 1, forward)
    width = 1
    while width < count:
        if width * 2 < count:
            got_state, got_log = shift((window_state, window_log), axis, width, forward)
            window_log_next = window_log + got_log
        else:
            got_state = shift(window_state, axis, width, forward)
            window_log_next = window_log
        window_state = window_state + jnp.exp(window_log)[:, None, None] * got_state
        window_log = window_log_next
        width *= 2
    return window_state


def split_bf16(value):
    upper = lax.reduce_precision(value, exponent_bits=8, mantissa_bits=7)
    return upper.astype(jnp.bfloat16), (value - upper).astype(jnp.bfloat16)


def mp_reduce_scatter(value, axis):
    count = lax.axis_size(axis)
    mine = lax.axis_index(axis)
    current = value
    step = count // 2
    while step >= 1:
        half = current.shape[0] // 2
        upper = (mine // step) % 2 == 1
        low_part, high_part = current[:half], current[half:]
        keep = jnp.where(upper, high_part, low_part)
        send = jnp.where(upper, low_part, high_part)
        got = lax.ppermute(send, axis, [(j, j ^ step) for j in range(count)])
        current = keep + got
        step //= 2
    return current


def local(queries, keys, values, inputs_x, in_b, in_c, log_decay):
    row_count = queries.shape[0]
    heads = queries.shape[1] // HEAD_WIDTH
    seq_count = lax.axis_size("seq")
    own_index = lax.axis_index("seq")
    first_query = own_index * row_count

    values_hi, values_lo = split_bf16(values)
    packed = jnp.concatenate([keys, values_hi, values_lo], axis=1)
    every = lax.all_gather(packed, "seq", axis=0, tiled=True)
    every_key = every[:, :HEAD_WIDTH]
    every_hi = every[:, HEAD_WIDTH:2 * HEAD_WIDTH]
    every_lo = every[:, 2 * HEAD_WIDTH:]

    c_scale = 0.5 / math.sqrt(N * row_count * seq_count)
    student_x = inputs_x.astype(jnp.float32).reshape(row_count, heads, HEAD_WIDTH)
    b_rows = in_b.astype(jnp.float32)
    c_rows = in_c.astype(jnp.float32) * c_scale
    cumulative = jnp.cumsum(log_decay, axis=0)
    totals = cumulative[-1]
    heads_first = cumulative.T
    causal = jnp.arange(row_count)[:, None] >= jnp.arange(row_count)[None, :]
    decays = jnp.exp(
        jnp.where(causal[None], heads_first[:, :, None] - heads_first[:, None, :], -jnp.inf)
    )
    inner_products = jnp.dot(in_c, in_b.T, preferred_element_type=jnp.float32) * c_scale
    mixing = decays * inner_products[None]
    rising = jnp.exp(cumulative)
    ending = jnp.exp(totals[None, :] - cumulative)
    local_state = jnp.einsum(
        "shp,sn->hpn", student_x * ending[:, :, None], b_rows, precision=highest
    )
    state_in = exclusive_scan(local_state, totals, "seq", True)

    query_rows = queries.reshape(row_count, heads, HEAD_WIDTH)
    scores = jnp.einsum(
        "qgd,nd->qgn", query_rows, every_key, preferred_element_type=jnp.float32
    ) / math.sqrt(HEAD_WIDTH)
    query_pos = first_query + jnp.arange(row_count, dtype=jnp.int32)
    key_pos = jnp.arange(every.shape[0], dtype=jnp.int32)
    allowed = (key_pos[None, :] <= query_pos[:, None])[:, None, :]
    scores = jnp.where(allowed, scores, very_negative)
    row_top = jnp.max(scores, axis=-1, keepdims=True)
    weights = jnp.where(allowed, jnp.exp(scores - row_top), 0.0)
    denominator = jnp.sum(weights, axis=-1)
    weights_hi, weights_lo = split_bf16(weights)
    mixture = (
        jnp.einsum("qgn,nd->qgd", weights_hi, every_hi, preferred_element_type=jnp.float32)
        + jnp.einsum("qgn,nd->qgd", weights_hi, every_lo, preferred_element_type=jnp.float32)
        + jnp.einsum("qgn,nd->qgd", weights_lo, every_hi, preferred_element_type=jnp.float32)
    )
    teacher_out = mixture / denominator[..., None]

    y_intra = jnp.einsum("hts,shp->thp", mixing, student_x, precision=highest)
    y_inter = jnp.einsum("tn,hpn->thp", c_rows, state_in, precision=highest) * rising[:, :, None]
    mismatch = y_intra + y_inter - teacher_out
    scaled_mismatch = mismatch * rising[:, :, None]
    local_grad = jnp.einsum("thp,tn->hpn", scaled_mismatch, c_rows, precision=highest)
    later_grad = exclusive_scan(local_grad, totals, "seq", False)
    grad_x = jnp.einsum("hts,thp->shp", mixing, mismatch, precision=highest)
    grad_x = (
        grad_x
        + jnp.einsum("hpn,sn->shp", later_grad, b_rows, precision=highest) * ending[:, :, None]
    )
    products = jnp.einsum("thp,shp->hts", mismatch, student_x, precision=highest)
    weighted = decays * products
    grad_b = jnp.einsum("hts,tn->sn", weighted, c_rows, precision=highest)
    grad_b = grad_b + jnp.einsum(
        "shp,hpn->sn", student_x * ending[:, :, None], later_grad, precision=highest
    )
    grad_c = jnp.einsum("hts,sn->tn", weighted, b_rows, precision=highest)
    grad_c = grad_c + jnp.einsum("thp,hpn->tn", scaled_mismatch, state_in, precision=highest)
    summed = mp_reduce_scatter(jnp.concatenate([grad_b, grad_c], axis=1), "mp")
    summed_b, summed_c = summed[:, :N], summed[:, N:]
    return (grad_x.reshape(row_count, heads * HEAD_WIDTH), summed_b, summed_c * c_scale)


def solution(mesh):
    in_specs = (
        P("seq", "mp"),
        P("seq", "mp"),
        P("seq", "mp"),
        P("seq", "mp"),
        P("seq", None),
        P("seq", None),
        P("seq", "mp"),
    )
    out_specs = (P("seq", "mp"), P(("seq", "mp"), None), P(("seq", "mp"), None))
    return jax.shard_map(local, mesh=mesh, in_specs=in_specs, out_specs=out_specs, check_vma=False)
```

time: 597 us -> 313 us (0.52)
  waiting for transfers between devices: 355 us -> 146 us
  starting transfers between devices: 0.24 us -> 101 us
  blocking collectives: 93 us -> 0 us
  other arithmetic: 44.4 us -> 4.44 us
  matrix products: 75.6 us -> 37.6 us
    all_gather x4 -> x1, waiting for transfers between devices: 316 us -> 0.02 us  [local(): every = lax.all_gather(packed, 'seq', axis=0, tiled=True)]
    ppermute x0 -> x25, waiting for transfers between devices: none -> 146 us  [the longest x22 139 us: shift(): return lax.ppermute(value, axis, perm)]
    ppermute x0 -> x25, starting transfers between devices: none -> 101 us  [the longest x22 88.5 us: shift(): return lax.ppermute(value, axis, perm)]
    unnamed x1 -> x0, blocking collectives: 56.6 us -> none
    dot_general x3, matrix products: 64.1 us -> 15.8 us  [the longest x1 8.51 us: local(): jnp.einsum('qgn,nd->qgd', weights_lo, every_hi, preferred_element_type=jn...]
    reduce_scatter x2 -> x0, waiting for transfers between devices: 38.8 us -> none  [the longest x1 38.8 us: local(): lax.psum_scatter(grad_b, 'mp', scatter_dimension=0, tiled=True)]
    all_gather x1 -> x0, blocking collectives: 36.4 us -> none  [prefix(): pieces = jax.tree.map(lambda part: lax.all_gather(part, axis), value)]
    select_n x31 -> x3, other arithmetic: 36.4 us -> 0.29 us  [mp_reduce_scatter(): send = jnp.where(upper, low_part, high_part)]
  transfers between devices with their start and end apart: 6 -> 26, of which waited for: 5 -> 17; matrix products, arithmetic and copies ran while one was open for 10% -> 13% of each run, Pallas kernels for 0% -> 0%
where the time goes in v1:
time: 313 us; the launch traced here: 311 us
  waiting for transfers between devices  146 us (47%)
  starting transfers between devices  101 us (32%)
  matrix products  37.6 us (12%)
  between operations  14.6 us (5%)
  local copies, waits for them, and re-layouts  6.74 us (2%)
  other arithmetic  4.44 us (1%)
    ppermute x22, waiting for transfers between devices, shift(): return lax.ppermute(value, axis, perm)  139 us
    ppermute x22, starting transfers between devices, shift(): return lax.ppermute(value, axis, perm)  88.5 us
    ppermute x3, starting transfers between devices, mp_reduce_scatter(): got = lax.ppermute(send, axis, [(j, j ^ step) for j in range(count)])  12.9 us
    sub x1, matrix products, local(): weights = jnp.where(allowed, jnp.exp(scores - row_top), 0.0)  11.6 us
    dot_general x1, matrix products, local(): jnp.einsum('qgn,nd->qgd', weights_lo, every_hi, preferred_element_type=jn...  8.51 us
    ppermute x3, waiting for transfers between devices, mp_reduce_scatter(): got = lax.ppermute(send, axis, [(j, j ^ step) for j in range(count)])  6.96 us
    unnamed x15, local copies, waits for them, and re-layouts  6.59 us
  transfers between devices with their start and end apart: 26, of which 17 were waited for; matrix products, arithmetic and copies ran while one was open for 13% of the time, Pallas kernels for 0%

profile of v1, /device:TPU:68, one launch (start us, length us, event | category | flops | bytes accessed | tf_op | source)
XLA Modules:
  0.0 310.7 jit_solution(15556653566416447946)
XLA Ops:
  8.1 1.4 pad_maximum_fusion.1
  12.9 1.9 collective-permute-start
  14.8 10.1 %collective-permute-done = f32[8,128,128]{2,1,0:T(8,128)S(1)} collective-permute-done((f32[8,128,128]{2,1,0:T(8,128)S(1)}, f32[8,128,128]{2,1,0:T(8,128)S(1)}, u32[]{:S(2)}, u32[]{:S(2)}) %collective-permute-start) | collective-permute-done | bytes 524320 | tf_op jit(solution)/shard_map/ppermute | solution.py:21
  24.9 1.9 collective-permute-start.2
  26.8 4.8 %collective-permute-start.1 = (f32[8]{0:T(128)S(1)}, f32[8]{0:T(128)S(1)}, u32[]{:S(2)}, u32[]{:S(2)}) collective-permute-start(f32[8]{0:T(128)S(1)} %slice_bitcast_fusion.12), channel_id=1, source_target_pairs={{0,8},{8,16},{16,24},{24,32},{32,40},{40,48},{48,56},{56,64},{64,7... | collective-permute-start | bytes 104 | tf_op jit(solution)/shard_map/ppermute | solution.py:21
  31.7 5.3 %collective-permute-done.1 = f32[8]{0:T(128)S(1)} collective-permute-done((f32[8]{0:T(128)S(1)}, f32[8]{0:T(128)S(1)}, u32[]{:S(2)}, u32[]{:S(2)}) %collective-permute-start.1) | collective-permute-done | bytes 64 | tf_op jit(solution)/shard_map/ppermute | solution.py:21
  37.0 1.9 collective-permute-start.3
  38.9 4.4 %collective-permute-done.3 = f32[8]{0:T(128)S(1)} collective-permute-done((f32[8]{0:T(128)S(1)}, f32[8]{0:T(128)S(1)}, u32[]{:S(2)}, u32[]{:S(2)}) %collective-permute-start.3) | collective-permute-done | bytes 64 | tf_op jit(solution)/shard_map/ppermute | solution.py:21
  43.4 7.4 %collective-permute-start.4 = (f32[8,128,128]{2,1,0:T(8,128)S(1)}, f32[8,128,128]{2,1,0:T(8,128)S(1)}, u32[]{:S(2)}, u32[]{:S(2)}) collective-permute-start(f32[8,128,128]{2,1,0:T(8,128)S(1)} %multiply_add_fusion.9), channel_id=1, source_target_pairs={{0,16},{8,24},{16,32},{24,40},{32,48},{40,56},{48,64},{56,72},{64,... | collective-permute-start | bytes 1572872 | tf_op jit(solution)/shard_map/ppermute | solution.py:21
  51.2 10.4 %collective-permute-done.4 = f32[8,128,128]{2,1,0:T(8,128)S(1)} collective-permute-done((f32[8,128,128]{2,1,0:T(8,128)S(1)}, f32[8,128,128]{2,1,0:T(8,128)S(1)}, u32[]{:S(2)}, u32[]{:S(2)}) %collective-permute-start.4) | collective-permute-done | bytes 524320 | tf_op jit(solution)/shard_map/ppermute | solution.py:21
  61.7 5.7 %collective-permute-start.6 = (f32[8,128,128]{2,1,0:T(8,128)S(1)}, f32[8,128,128]{2,1,0:T(8,128)S(1)}, u32[]{:S(2)}, u32[]{:S(2)}) collective-permute-start(f32[8,128,128]{2,1,0:T(8,128)S(1)} %multiply_add_fusion.8), channel_id=1, source_target_pairs={{0,32},{8,40},{16,48},{24,56},{32,64},{40,72},{48,80},{56,88},{64,... | collective-permute-start | bytes 1572872 | tf_op jit(solution)/shard_map/ppermute | solution.py:21
  68.4 8.0 %collective-permute-start.5 = (f32[8]{0:T(128)S(1)}, f32[8]{0:T(128)S(1)}, u32[]{:S(2)}, u32[]{:S(2)}) collective-permute-start(f32[8]{0:T(128)S(1)} %get-tuple-element.17), channel_id=1, source_target_pairs={{0,16},{8,24},{16,32},{24,40},{32,48},{40,56},{48,64},{56,72},{64,... | collective-permute-start | bytes 104 | tf_op jit(solution)/shard_map/ppermute | solution.py:21
  76.4 4.7 %collective-permute-done.5 = f32[8]{0:T(128)S(1)} collective-permute-done((f32[8]{0:T(128)S(1)}, f32[8]{0:T(128)S(1)}, u32[]{:S(2)}, u32[]{:S(2)}) %collective-permute-start.5) | collective-permute-done | bytes 64 | tf_op jit(solution)/shard_map/ppermute | solution.py:21
  81.2 5.0 %collective-permute-start.8 = (f32[8,128,128]{2,1,0:T(8,128)S(1)}, f32[8,128,128]{2,1,0:T(8,128)S(1)}, u32[]{:S(2)}, u32[]{:S(2)}) collective-permute-start(f32[8,128,128]{2,1,0:T(8,128)S(1)} %multiply_add_fusion.7), channel_id=1, source_target_pairs={{0,64},{8,72},{16,80},{24,88},{32,96},{40,104},{48,112},{56,120},{... | collective-permute-start | bytes 1572872 | tf_op jit(solution)/shard_map/ppermute | solution.py:21
  86.2 1.5 convolution_bitcast_fusion.1
  87.8 2.0 collective-permute-start.7
  89.7 18.7 %collective-permute-done.7 = f32[8]{0:T(128)S(1)} collective-permute-done((f32[8]{0:T(128)S(1)}, f32[8]{0:T(128)S(1)}, u32[]{:S(2)}, u32[]{:S(2)}) %collective-permute-start.7) | collective-permute-done | bytes 64 | tf_op jit(solution)/shard_map/ppermute | solution.py:21
  108.5 4.5 %collective-permute-start.9 = (f32[8]{0:T(128)S(1)}, f32[8]{0:T(128)S(1)}, u32[]{:S(2)}, u32[]{:S(2)}) collective-permute-start(f32[8]{0:T(128)S(1)} %get-tuple-element.13), channel_id=1, source_target_pairs={{0,64},{8,72},{16,80},{24,88},{32,96},{40,104},{48,112},{56,120},{... | collective-permute-start | bytes 104 | tf_op jit(solution)/shard_map/ppermute | solution.py:21
  113.0 1.9 collective-permute-done.9
  114.9 3.9 %collective-permute-start.10 = (f32[8,128,128]{2,1,0:T(8,128)S(1)}, f32[8,128,128]{2,1,0:T(8,128)S(1)}, u32[]{:S(2)}, u32[]{:S(2)}) collective-permute-start(f32[8,128,128]{2,1,0:T(8,128)S(1)} %multiply_add_fusion.6), channel_id=1, source_target_pairs={{0,128},{8,136},{16,144},{24,152},{32,160},{40,168},{48,176},{56,1... | collective-permute-start | bytes 1572872 | tf_op jit(solution)/shard_map/ppermute | solution.py:21
  118.9 11.6 %fusion.75 = (f32[128,8]{0,1:T(8,128)S(1)}, f32[128,8,4096]{0,2,1:T(8,128)}) fusion(pred[128,4096]{0,1:T(8,128)(4,1)S(1)} %iota_compare_fusion, bf16[4096,384]{1,0:T(8,128)(2,1)} %all-gather.2.cloned.1.call-done, bf16[128,1024]{1,0:T(8,128)(2,1)S(1)} %copy-done), kind=kOutput, calls=%fused_computation.113 | convolution fusion | flops 1094717440 | bytes 19140608 | tf_op jit(solution)/shard_map/sub | solution.py:106
  130.5 8.5 %fusion.3 = f32[128,8,128]{2,0,1:T(8,128)S(1)} fusion(f32[128,8,4096]{0,2,1:T(8,128)} %get-tuple-element.27, bf16[4096,384]{1,0:T(8,128)(2,1)} %all-gather.2.cloned.1.call-done), kind=kOutput, calls=%fused_computation.7 | convolution fusion | flops 1086324736 | bytes 18350080 | tf_op jit(solution)/shard_map/qgn,nd->qgd/dot_general | solution.py:112
  139.0 2.3 copy-done.1
  141.4 3.6 %fusion.8 = f32[128,8,128]{2,0,1:T(8,128)S(1)} fusion(f32[128,8,4096]{0,2,1:T(8,128)S(1)} %copy-done.1, bf16[4096,384]{1,0:T(8,128)(2,1)} %all-gather.2.cloned.1.call-done), kind=kOutput, calls=%fused_computation.11 | convolution fusion | flops 1082130432 | bytes 18350080 | tf_op jit(solution)/shard_map/qgn,nd->qgd/dot_general | solution.py:111
  145.0 3.6 %fusion.21 = f32[128,8,128]{2,0,1:T(8,128)S(1)} fusion(f32[128,8,128]{2,0,1:T(8,128)S(1)} %fusion.3, f32[128,8,128]{2,0,1:T(8,128)S(1)} %fusion.8, f32[128,8,4096]{0,2,1:T(8,128)S(1)} %copy-done.1, bf16[4096,384]{1,0:T(8,128)(2,1)} %all-gather.2.cloned.1.call-done, f32[128,8]{0,1:T(8,128)S(1)} %get-tuple-element.26), kind=kOutput, calls=%fused_computation.32 | convolution fusion | flops 1082523648 | bytes 19402752 | tf_op jit(solution)/shard_map/qgn,nd->qgd/dot_general | solution.py:110
  150.6 1.9 collective-permute-start.11
  152.5 6.7 %collective-permute-done.11 = f32[8,128,128]{2,1,0:T(8,128)S(1)} collective-permute-done((f32[8,128,128]{2,1,0:T(8,128)S(1)}, f32[8,128,128]{2,1,0:T(8,128)S(1)}, u32[]{:S(2)}, u32[]{:S(2)}) %collective-permute-start.11) | collective-permute-done | bytes 524320 | tf_op jit(solution)/shard_map/ppermute | solution.py:21
  159.2 5.3 %collective-permute-start.13 = (f32[8,128,128]{2,1,0:T(8,128)S(1)}, f32[8,128,128]{2,1,0:T(8,128)S(1)}, u32[]{:S(2)}, u32[]{:S(2)}) collective-permute-start(f32[8,128,128]{2,1,0:T(8,128)S(1)} %collective-permute-done.11), channel_id=1, source_target_pairs={{8,0},{16,8},{24,16},{32,24},{40,32},{48,40},{56,48},{64,56},{72,6... | collective-permute-start | bytes 1572872 | tf_op jit(solution)/shard_map/ppermute | solution.py:21
  164.5 1.9 collective-permute-start.12
  166.4 4.8 %collective-permute-done.12 = f32[8]{0:T(128)S(1)} collective-permute-done((f32[8]{0:T(128)S(1)}, f32[8]{0:T(128)S(1)}, u32[]{:S(2)}, u32[]{:S(2)}) %collective-permute-start.12) | collective-permute-done | bytes 64 | tf_op jit(solution)/shard_map/ppermute | solution.py:21
  171.2 5.3 %collective-permute-start.14 = (f32[8]{0:T(128)S(1)}, f32[8]{0:T(128)S(1)}, u32[]{:S(2)}, u32[]{:S(2)}) collective-permute-start(f32[8]{0:T(128)S(1)} %collective-permute-done.12), channel_id=1, source_target_pairs={{8,0},{16,8},{24,16},{32,24},{40,32},{48,40},{56,48},{64,56},{72,6... | collective-permute-start | bytes 104 | tf_op jit(solution)/shard_map/ppermute | solution.py:21
  178.0 6.3 %collective-permute-start.15 = (f32[8,128,128]{2,1,0:T(8,128)S(1)}, f32[8,128,128]{2,1,0:T(8,128)S(1)}, u32[]{:S(2)}, u32[]{:S(2)}) collective-permute-start(f32[8,128,128]{2,1,0:T(8,128)S(1)} %multiply_add_fusion.4), channel_id=1, source_target_pairs={{16,0},{24,8},{32,16},{40,24},{48,32},{56,40},{64,48},{72,56},{80,... | collective-permute-start | bytes 1572872 | tf_op jit(solution)/shard_map/ppermute | solution.py:21
  184.2 10.7 %collective-permute-done.15 = f32[8,128,128]{2,1,0:T(8,128)S(1)} collective-permute-done((f32[8,128,128]{2,1,0:T(8,128)S(1)}, f32[8,128,128]{2,1,0:T(8,128)S(1)}, u32[]{:S(2)}, u32[]{:S(2)}) %collective-permute-start.15) | collective-permute-done | bytes 524320 | tf_op jit(solution)/shard_map/ppermute | solution.py:21
  195.1 4.3 %collective-permute-start.17 = (f32[8,128,128]{2,1,0:T(8,128)S(1)}, f32[8,128,128]{2,1,0:T(8,128)S(1)}, u32[]{:S(2)}, u32[]{:S(2)}) collective-permute-start(f32[8,128,128]{2,1,0:T(8,128)S(1)} %multiply_add_fusion.3), channel_id=1, source_target_pairs={{32,0},{40,8},{48,16},{56,24},{64,32},{72,40},{80,48},{88,56},{96,... | collective-permute-start | bytes 1572872 | tf_op jit(solution)/shard_map/ppermute | solution.py:21
  199.4 5.9 %collective-permute-start.16 = (f32[8]{0:T(128)S(1)}, f32[8]{0:T(128)S(1)}, u32[]{:S(2)}, u32[]{:S(2)}) collective-permute-start(f32[8]{0:T(128)S(1)} %get-tuple-element.11), channel_id=1, source_target_pairs={{16,0},{24,8},{32,16},{40,24},{48,32},{56,40},{64,48},{72,56},{80,... | collective-permute-start | bytes 104 | tf_op jit(solution)/shard_map/ppermute | solution.py:21
  205.3 8.2 %collective-permute-done.16 = f32[8]{0:T(128)S(1)} collective-permute-done((f32[8]{0:T(128)S(1)}, f32[8]{0:T(128)S(1)}, u32[]{:S(2)}, u32[]{:S(2)}) %collective-permute-start.16) | collective-permute-done | bytes 64 | tf_op jit(solution)/shard_map/ppermute | solution.py:21
  213.5 3.9 %collective-permute-start.18 = (f32[8]{0:T(128)S(1)}, f32[8]{0:T(128)S(1)}, u32[]{:S(2)}, u32[]{:S(2)}) collective-permute-start(f32[8]{0:T(128)S(1)} %get-tuple-element.9), channel_id=1, source_target_pairs={{32,0},{40,8},{48,16},{56,24},{64,32},{72,40},{80,48},{88,56},{96,... | collective-permute-start | bytes 104 | tf_op jit(solution)/shard_map/ppermute | solution.py:21
  217.5 1.9 collective-permute-start.19
  219.5 3.2 %collective-permute-start.20 = (f32[8]{0:T(128)S(1)}, f32[8]{0:T(128)S(1)}, u32[]{:S(2)}, u32[]{:S(2)}) collective-permute-start(f32[8]{0:T(128)S(1)} %get-tuple-element.7), channel_id=1, source_target_pairs={{64,0},{72,8},{80,16},{88,24},{96,32},{104,40},{112,48},{120,56},{... | collective-permute-start | bytes 104 | tf_op jit(solution)/shard_map/ppermute | solution.py:21
  222.7 27.1 %collective-permute-done.20 = f32[8]{0:T(128)S(1)} collective-permute-done((f32[8]{0:T(128)S(1)}, f32[8]{0:T(128)S(1)}, u32[]{:S(2)}, u32[]{:S(2)}) %collective-permute-start.20) | collective-permute-done | bytes 64 | tf_op jit(solution)/shard_map/ppermute | solution.py:21
  250.4 1.5 collective-permute-start.21
  253.7 24.6 %collective-permute-done.21 = f32[8,128,128]{2,1,0:T(8,128)S(1)} collective-permute-done((f32[8,128,128]{2,1,0:T(8,128)S(1)}, f32[8,128,128]{2,1,0:T(8,128)S(1)}, u32[]{:S(2)}, u32[]{:S(2)}) %collective-permute-start.21) | collective-permute-done | bytes 524320 | tf_op jit(solution)/shard_map/ppermute | solution.py:21
  279.5 2.1 collective-permute-start.22
  281.5 3.7 %collective-permute-done.22 = f32[64,256]{0,1:T(8,128)S(1)} collective-permute-done((f32[64,256]{0,1:T(8,128)S(1)}, f32[64,256]{0,1:T(8,128)S(1)}, u32[]{:S(2)}, u32[]{:S(2)}) %collective-permute-start.22) | collective-permute-done | bytes 65568 | tf_op jit(solution)/shard_map/ppermute | solution.py:57
  285.4 8.8 %collective-permute-start.23 = (f32[32,256]{0,1:T(8,128)S(1)}, f32[32,256]{0,1:T(8,128)S(1)}, u32[]{:S(2)}, u32[]{:S(2)}) collective-permute-start(f32[32,256]{0,1:T(8,128)S(1)} %slice_select_fusion.1), channel_id=1, source_target_pairs={{0,2},{1,3},{2,0},{3,1},{4,6},{5,7},{6,4},{7,5},{8,10},{9,11},{10,... | collective-permute-start | bytes 98312 | tf_op jit(solution)/shard_map/ppermute | solution.py:57
  295.4 1.8 collective-permute-done.23
  297.4 2.1 collective-permute-start.24
  300.9 1.5 collective-permute-done.24
  (70 shorter events, 17.5 us)
Async XLA Ops:
  7.2 111.8 %copy-start = (bf16[128,1024]{1,0:T(8,128)(2,1)S(1)}, bf16[128,1024]{1,0:T(8,128)(2,1)}, u32[]{:S(2)}) copy-start(bf16[128,1024]{1,0:T(8,128)(2,1)} %param.7) | copy-start | bytes 786436
  7.2 111.7 %all-gather.2.cloned.1.call-start = ((), (), s32[]{:S(2)}) async-start(), calls=%async_computation | async-start | bytes 3244032 | tf_op jit(solution)/shard_map/all_gather | solution.py:72
  12.9 12.0 %collective-permute-start = (f32[8,128,128]{2,1,0:T(8,128)S(1)}, f32[8,128,128]{2,1,0:T(8,128)S(1)}, u32[]{:S(2)}, u32[]{:S(2)}) collective-permute-start(f32[8,128,128]{2,1,0:T(8,128)S(1)} %fusion.23), channel_id=1, source_target_pairs={{0,8},{8,16},{16,24},{24,32},{32,40},{40,48},{48,56},{56,64},{64,7... | collective-permute-start | bytes 1572872 | tf_op jit(solution)/shard_map/ppermute | solution.py:21
  24.9 18.4 %collective-permute-start.2 = (f32[8,128,128]{2,1,0:T(8,128)S(1)}, f32[8,128,128]{2,1,0:T(8,128)S(1)}, u32[]{:S(2)}, u32[]{:S(2)}) collective-permute-start(f32[8,128,128]{2,1,0:T(8,128)S(1)} %collective-permute-done), channel_id=1, source_target_pairs={{0,8},{8,16},{16,24},{24,32},{32,40},{40,48},{48,56},{56,64},{64,7... | collective-permute-start | bytes 1572872 | tf_op jit(solution)/shard_map/ppermute | solution.py:21
  26.8 10.1 %collective-permute-start.1 = (f32[8]{0:T(128)S(1)}, f32[8]{0:T(128)S(1)}, u32[]{:S(2)}, u32[]{:S(2)}) collective-permute-start(f32[8]{0:T(128)S(1)} %slice_bitcast_fusion.12), channel_id=1, source_target_pairs={{0,8},{8,16},{16,24},{24,32},{32,40},{40,48},{48,56},{56,64},{64,7... | collective-permute-start | bytes 104 | tf_op jit(solution)/shard_map/ppermute | solution.py:21
  37.0 6.4 %collective-permute-start.3 = (f32[8]{0:T(128)S(1)}, f32[8]{0:T(128)S(1)}, u32[]{:S(2)}, u32[]{:S(2)}) collective-permute-start(f32[8]{0:T(128)S(1)} %collective-permute-done.1), channel_id=1, source_target_pairs={{0,8},{8,16},{16,24},{24,32},{32,40},{40,48},{48,56},{56,64},{64,7... | collective-permute-start | bytes 104 | tf_op jit(solution)/shard_map/ppermute | solution.py:21
  43.4 18.2 %collective-permute-start.4 = (f32[8,128,128]{2,1,0:T(8,128)S(1)}, f32[8,128,128]{2,1,0:T(8,128)S(1)}, u32[]{:S(2)}, u32[]{:S(2)}) collective-permute-start(f32[8,128,128]{2,1,0:T(8,128)S(1)} %multiply_add_fusion.9), channel_id=1, source_target_pairs={{0,16},{8,24},{16,32},{24,40},{32,48},{40,56},{48,64},{56,72},{64,... | collective-permute-start | bytes 1572872 | tf_op jit(solution)/shard_map/ppermute | solution.py:21
  61.7 19.3 %collective-permute-start.6 = (f32[8,128,128]{2,1,0:T(8,128)S(1)}, f32[8,128,128]{2,1,0:T(8,128)S(1)}, u32[]{:S(2)}, u32[]{:S(2)}) collective-permute-start(f32[8,128,128]{2,1,0:T(8,128)S(1)} %multiply_add_fusion.8), channel_id=1, source_target_pairs={{0,32},{8,40},{16,48},{24,56},{32,64},{40,72},{48,80},{56,88},{64,... | collective-permute-start | bytes 1572872 | tf_op jit(solution)/shard_map/ppermute | solution.py:21
  68.4 12.7 %collective-permute-start.5 = (f32[8]{0:T(128)S(1)}, f32[8]{0:T(128)S(1)}, u32[]{:S(2)}, u32[]{:S(2)}) collective-permute-start(f32[8]{0:T(128)S(1)} %get-tuple-element.17), channel_id=1, source_target_pairs={{0,16},{8,24},{16,32},{24,40},{32,48},{40,56},{48,64},{56,72},{64,... | collective-permute-start | bytes 104 | tf_op jit(solution)/shard_map/ppermute | solution.py:21
  81.2 33.6 %collective-permute-start.8 = (f32[8,128,128]{2,1,0:T(8,128)S(1)}, f32[8,128,128]{2,1,0:T(8,128)S(1)}, u32[]{:S(2)}, u32[]{:S(2)}) collective-permute-start(f32[8,128,128]{2,1,0:T(8,128)S(1)} %multiply_add_fusion.7), channel_id=1, source_target_pairs={{0,64},{8,72},{16,80},{24,88},{32,96},{40,104},{48,112},{56,120},{... | collective-permute-start | bytes 1572872 | tf_op jit(solution)/shard_map/ppermute | solution.py:21
  87.8 20.7 %collective-permute-start.7 = (f32[8]{0:T(128)S(1)}, f32[8]{0:T(128)S(1)}, u32[]{:S(2)}, u32[]{:S(2)}) collective-permute-start(f32[8]{0:T(128)S(1)} %get-tuple-element.15), channel_id=1, source_target_pairs={{0,32},{8,40},{16,48},{24,56},{32,64},{40,72},{48,80},{56,88},{64,... | collective-permute-start | bytes 104 | tf_op jit(solution)/shard_map/ppermute | solution.py:21
  108.5 6.3 %collective-permute-start.9 = (f32[8]{0:T(128)S(1)}, f32[8]{0:T(128)S(1)}, u32[]{:S(2)}, u32[]{:S(2)}) collective-permute-start(f32[8]{0:T(128)S(1)} %get-tuple-element.13), channel_id=1, source_target_pairs={{0,64},{8,72},{16,80},{24,88},{32,96},{40,104},{48,112},{56,120},{... | collective-permute-start | bytes 104 | tf_op jit(solution)/shard_map/ppermute | solution.py:21
  114.9 33.7 %collective-permute-start.10 = (f32[8,128,128]{2,1,0:T(8,128)S(1)}, f32[8,128,128]{2,1,0:T(8,128)S(1)}, u32[]{:S(2)}, u32[]{:S(2)}) collective-permute-start(f32[8,128,128]{2,1,0:T(8,128)S(1)} %multiply_add_fusion.6), channel_id=1, source_target_pairs={{0,128},{8,136},{16,144},{24,152},{32,160},{40,168},{48,176},{56,1... | collective-permute-start | bytes 1572872 | tf_op jit(solution)/shard_map/ppermute | solution.py:21
  130.5 10.8 %copy-start.1 = (f32[128,8,4096]{0,2,1:T(8,128)S(1)}, f32[128,8,4096]{0,2,1:T(8,128)}, u32[]{:S(2)}) copy-start(f32[128,8,4096]{0,2,1:T(8,128)} %get-tuple-element.27) | copy-start | bytes 50331652
  141.4 7.3 %copy-start.2 = (bf16[128,128]{1,0:T(8,128)(2,1)S(1)}, bf16[128,128]{1,0:T(8,128)(2,1)}, u32[]{:S(2)}) copy-start(bf16[128,128]{1,0:T(8,128)(2,1)} %param.12) | copy-start | bytes 98308
  141.4 7.3 %copy-start.4 = (f32[128,8,128]{2,0,1:T(8,128)S(1)}, f32[128,8,128]{2,0,1:T(8,128)}, u32[]{:S(2)}) copy-start(f32[128,8,128]{2,0,1:T(8,128)} %convolution_bitcast_fusion.1) | copy-start | bytes 1572868
  145.0 106.9 %copy-start.3 = (bf16[128,128]{1,0:T(8,128)(2,1)S(1)}, bf16[128,128]{1,0:T(8,128)(2,1)}, u32[]{:S(2)}) copy-start(bf16[128,128]{1,0:T(8,128)(2,1)} %param.11) | copy-start | bytes 98308
  150.6 8.6 %collective-permute-start.11 = (f32[8,128,128]{2,1,0:T(8,128)S(1)}, f32[8,128,128]{2,1,0:T(8,128)S(1)}, u32[]{:S(2)}, u32[]{:S(2)}) collective-permute-start(f32[8,128,128]{2,1,0:T(8,128)S(1)} %fusion.28), channel_id=1, source_target_pairs={{8,0},{16,8},{24,16},{32,24},{40,32},{48,40},{56,48},{64,56},{72,6... | collective-permute-start | bytes 1572872 | tf_op jit(solution)/shard_map/ppermute | solution.py:21
  159.2 18.7 %collective-permute-start.13 = (f32[8,128,128]{2,1,0:T(8,128)S(1)}, f32[8,128,128]{2,1,0:T(8,128)S(1)}, u32[]{:S(2)}, u32[]{:S(2)}) collective-permute-start(f32[8,128,128]{2,1,0:T(8,128)S(1)} %collective-permute-done.11), channel_id=1, source_target_pairs={{8,0},{16,8},{24,16},{32,24},{40,32},{48,40},{56,48},{64,56},{72,6... | collective-permute-start | bytes 1572872 | tf_op jit(solution)/shard_map/ppermute | solution.py:21
  164.5 6.7 %collective-permute-start.12 = (f32[8]{0:T(128)S(1)}, f32[8]{0:T(128)S(1)}, u32[]{:S(2)}, u32[]{:S(2)}) collective-permute-start(f32[8]{0:T(128)S(1)} %slice_bitcast_fusion.12), channel_id=1, source_target_pairs={{8,0},{16,8},{24,16},{32,24},{40,32},{48,40},{56,48},{64,56},{72,6... | collective-permute-start | bytes 104 | tf_op jit(solution)/shard_map/ppermute | solution.py:21
  171.2 6.6 %collective-permute-start.14 = (f32[8]{0:T(128)S(1)}, f32[8]{0:T(128)S(1)}, u32[]{:S(2)}, u32[]{:S(2)}) collective-permute-start(f32[8]{0:T(128)S(1)} %collective-permute-done.12), channel_id=1, source_target_pairs={{8,0},{16,8},{24,16},{32,24},{40,32},{48,40},{56,48},{64,56},{72,6... | collective-permute-start | bytes 104 | tf_op jit(solution)/shard_map/ppermute | solution.py:21
  178.0 17.0 %collective-permute-start.15 = (f32[8,128,128]{2,1,0:T(8,128)S(1)}, f32[8,128,128]{2,1,0:T(8,128)S(1)}, u32[]{:S(2)}, u32[]{:S(2)}) collective-permute-start(f32[8,128,128]{2,1,0:T(8,128)S(1)} %multiply_add_fusion.4), channel_id=1, source_target_pairs={{16,0},{24,8},{32,16},{40,24},{48,32},{56,40},{64,48},{72,56},{80,... | collective-permute-start | bytes 1572872 | tf_op jit(solution)/shard_map/ppermute | solution.py:21
  195.1 22.4 %collective-permute-start.17 = (f32[8,128,128]{2,1,0:T(8,128)S(1)}, f32[8,128,128]{2,1,0:T(8,128)S(1)}, u32[]{:S(2)}, u32[]{:S(2)}) collective-permute-start(f32[8,128,128]{2,1,0:T(8,128)S(1)} %multiply_add_fusion.3), channel_id=1, source_target_pairs={{32,0},{40,8},{48,16},{56,24},{64,32},{72,40},{80,48},{88,56},{96,... | collective-permute-start | bytes 1572872 | tf_op jit(solution)/shard_map/ppermute | solution.py:21
  199.4 14.1 %collective-permute-start.16 = (f32[8]{0:T(128)S(1)}, f32[8]{0:T(128)S(1)}, u32[]{:S(2)}, u32[]{:S(2)}) collective-permute-start(f32[8]{0:T(128)S(1)} %get-tuple-element.11), channel_id=1, source_target_pairs={{16,0},{24,8},{32,16},{40,24},{48,32},{56,40},{64,48},{72,56},{80,... | collective-permute-start | bytes 104 | tf_op jit(solution)/shard_map/ppermute | solution.py:21
  213.5 6.0 %collective-permute-start.18 = (f32[8]{0:T(128)S(1)}, f32[8]{0:T(128)S(1)}, u32[]{:S(2)}, u32[]{:S(2)}) collective-permute-start(f32[8]{0:T(128)S(1)} %get-tuple-element.9), channel_id=1, source_target_pairs={{32,0},{40,8},{48,16},{56,24},{64,32},{72,40},{80,48},{88,56},{96,... | collective-permute-start | bytes 104 | tf_op jit(solution)/shard_map/ppermute | solution.py:21
  217.5 32.8 %collective-permute-start.19 = (f32[8,128,128]{2,1,0:T(8,128)S(1)}, f32[8,128,128]{2,1,0:T(8,128)S(1)}, u32[]{:S(2)}, u32[]{:S(2)}) collective-permute-start(f32[8,128,128]{2,1,0:T(8,128)S(1)} %multiply_add_fusion.2), channel_id=1, source_target_pairs={{64,0},{72,8},{80,16},{88,24},{96,32},{104,40},{112,48},{120,56},{... | collective-permute-start | bytes 1572872 | tf_op jit(solution)/shard_map/ppermute | solution.py:21
  219.5 30.4 %collective-permute-start.20 = (f32[8]{0:T(128)S(1)}, f32[8]{0:T(128)S(1)}, u32[]{:S(2)}, u32[]{:S(2)}) collective-permute-start(f32[8]{0:T(128)S(1)} %get-tuple-element.7), channel_id=1, source_target_pairs={{64,0},{72,8},{80,16},{88,24},{96,32},{104,40},{112,48},{120,56},{... | collective-permute-start | bytes 104 | tf_op jit(solution)/shard_map/ppermute | solution.py:21
  250.4 27.9 %collective-permute-start.21 = (f32[8,128,128]{2,1,0:T(8,128)S(1)}, f32[8,128,128]{2,1,0:T(8,128)S(1)}, u32[]{:S(2)}, u32[]{:S(2)}) collective-permute-start(f32[8,128,128]{2,1,0:T(8,128)S(1)} %multiply_add_fusion.1), channel_id=1, source_target_pairs={{128,0},{136,8},{144,16},{152,24},{160,32},{168,40},{176,48},{184,... | collective-permute-start | bytes 1572872 | tf_op jit(solution)/shard_map/ppermute | solution.py:21
  279.5 5.7 %collective-permute-start.22 = (f32[64,256]{0,1:T(8,128)S(1)}, f32[64,256]{0,1:T(8,128)S(1)}, u32[]{:S(2)}, u32[]{:S(2)}) collective-permute-start(f32[64,256]{0,1:T(8,128)S(1)} %fusion.52), channel_id=1, source_target_pairs={{0,4},{1,5},{2,6},{3,7},{4,0},{5,1},{6,2},{7,3},{8,12},{9,13},{10,... | collective-permute-start | bytes 196616 | tf_op jit(solution)/shard_map/ppermute | solution.py:57
  285.4 11.7 %collective-permute-start.23 = (f32[32,256]{0,1:T(8,128)S(1)}, f32[32,256]{0,1:T(8,128)S(1)}, u32[]{:S(2)}, u32[]{:S(2)}) collective-permute-start(f32[32,256]{0,1:T(8,128)S(1)} %slice_select_fusion.1), channel_id=1, source_target_pairs={{0,2},{1,3},{2,0},{3,1},{4,6},{5,7},{6,4},{7,5},{8,10},{9,11},{10,... | collective-permute-start | bytes 98312 | tf_op jit(solution)/shard_map/ppermute | solution.py:57
  297.4 5.1 %collective-permute-start.24 = (f32[16,256]{0,1:T(8,128)S(1)}, f32[16,256]{0,1:T(8,128)S(1)}, u32[]{:S(2)}, u32[]{:S(2)}) collective-permute-start(f32[16,256]{0,1:T(8,128)S(1)} %slice_select_fusion), channel_id=1, source_target_pairs={{0,1},{1,0},{2,3},{3,2},{4,5},{5,4},{6,7},{7,6},{8,9},{9,8},{10,11... | collective-permute-start | bytes 49160 | tf_op jit(solution)/shard_map/ppermute | solution.py:57
Sparse Core Ops, SparseCore 0:
  10.8 89.9 all-gather.1

commit v2 on v1

--- a/solution.py
+++ b/solution.py
@@ -23,19 +23,48 @@
 
 def exclusive_scan(state, logs, axis, forward):
     count = lax.axis_size(axis)
-    window_state, window_log = shift((state, logs), axis, 1, forward)
+    chips = count // 2
+    core = lax.axis_index(axis) % 2
+    first = core == 0 if forward else core == 1
+    heads = state.shape[0]
+    half = heads // 2
+    mine = core * half
+    partner = (1 - core) * half
+    swap = [(j, j ^ 1) for j in range(count)]
+
+    own_half = lax.dynamic_slice_in_dim(state, mine, half, axis=0)
+    got_half, got_logs = lax.ppermute(
+        (lax.dynamic_slice_in_dim(state, partner, half, axis=0), logs), axis, swap
+    )
+    first_half = jnp.where(first, own_half, got_half)
+    second_half = jnp.where(first, got_half, own_half)
+    first_logs = jnp.where(first, logs, got_logs)
+    second_logs = jnp.where(first, got_logs, logs)
+    first_logs_half = lax.dynamic_slice_in_dim(first_logs, mine, half)
+    second_logs_half = lax.dynamic_slice_in_dim(second_logs, mine, half)
+    chip_state = jnp.exp(second_logs_half)[:, None, None] * first_half + second_half
+    chip_logs = first_logs_half + second_logs_half
+
+    window_state, window_log = shift((chip_state, chip_logs), axis, 2, forward)
     width = 1
-    while width < count:
-        if width * 2 < count:
-            got_state, got_log = shift((window_state, window_log), axis, width, forward)
+    while width < chips:
+        if width * 2 < chips:
+            got_state, got_log = shift((window_state, window_log), axis, 2 * width, forward)
             window_log_next = window_log + got_log
         else:
-            got_state = shift(window_state, axis, width, forward)
+            got_state = shift(window_state, axis, 2 * width, forward)
             window_log_next = window_log
         window_state = window_state + jnp.exp(window_log)[:, None, None] * got_state
         window_log = window_log_next
         width *= 2
-    return window_state
+
+    second_state = jnp.exp(first_logs_half)[:, None, None] * window_state + first_half
+    keep = jnp.where(first, window_state, second_state)
+    send = jnp.where(first, second_state, window_state)
+    got = lax.ppermute(send, axis, swap)
+    return jnp.where(
+        core == 0, jnp.concatenate([keep, got], axis=0), jnp.concatenate([got, keep], axis=0)
+    )
 
 
 def split_bf16(value):

time: 313 us -> 236 us (0.75)
  waiting for transfers between devices: 146 us -> 87.3 us
  starting transfers between devices: 101 us -> 75.6 us
  matrix products: 37.6 us -> 41.3 us
    ppermute x22 -> x18, waiting for transfers between devices: 139 us -> 73.5 us  [shift(): return lax.ppermute(value, axis, perm)]
    ppermute x22 -> x18, starting transfers between devices: 88.5 us -> 68.8 us  [shift(): return lax.ppermute(value, axis, perm)]
    ppermute x3, starting transfers between devices: 12.9 us -> 5.45 us  [mp_reduce_scatter(): got = lax.ppermute(send, axis, [(j, j ^ step) for j in range(count)])]
    all_gather x1, waiting for transfers between devices: 0.02 us -> 3.75 us  [local(): every = lax.all_gather(packed, 'seq', axis=0, tiled=True)]
    unnamed x15 -> x33, local copies, waits for them, and re-layouts: 6.59 us -> 6.55 us
  transfers between devices with their start and end apart: 26 -> 27, of which waited for: 17 -> 18; matrix products, arithmetic and copies ran while one was open for 13% -> 19% of each run, Pallas kernels for 0% -> 0%
where the time goes in v2:
time: 236 us; the launch traced here: 233 us
  waiting for transfers between devices  87.3 us (37%)
  starting transfers between devices  75.6 us (32%)
  matrix products  41.3 us (18%)
  between operations  14.6 us (6%)
  local copies, waits for them, and re-layouts  7.37 us (3%)
  other arithmetic  6.81 us (3%)
    ppermute x18, waiting for transfers between devices, shift(): return lax.ppermute(value, axis, perm)  73.5 us
    ppermute x18, starting transfers between devices, shift(): return lax.ppermute(value, axis, perm)  68.8 us
    sub x1, matrix products, local(): weights = jnp.where(allowed, jnp.exp(scores - row_top), 0.0)  12.6 us
    ppermute x3, waiting for transfers between devices, mp_reduce_scatter(): got = lax.ppermute(send, axis, [(j, j ^ step) for j in range(count)])  8.31 us
    dot_general x1, matrix products, local(): jnp.einsum('qgn,nd->qgd', weights_lo, every_hi, preferred_element_type=jn...  8.28 us
    unnamed x33, local copies, waits for them, and re-layouts  6.55 us
    ppermute x3, starting transfers between devices, mp_reduce_scatter(): got = lax.ppermute(send, axis, [(j, j ^ step) for j in range(count)])  5.45 us
  transfers between devices with their start and end apart: 27, of which 18 were waited for; matrix products, arithmetic and copies ran while one was open for 19% of the time, Pallas kernels for 0%

profile of v2, /device:TPU:68, one launch (start us, length us, event | category | flops | bytes accessed | tf_op | source)
XLA Modules:
  0.0 233.0 jit_solution(2930432445650439539)
XLA Ops:
  8.1 1.4 pad_maximum_fusion.1
  14.9 3.8 %collective-permute-start.2 = (f32[4,128,128]{2,1,0:T(8,128)S(1)}, f32[4,128,128]{2,1,0:T(8,128)S(1)}, u32[]{:S(2)}, u32[]{:S(2)}) collective-permute-start(f32[4,128,128]{2,1,0:T(8,128)S(1)} %select_add_fusion.1), channel_id=1, source_target_pairs={{0,16},{8,24},{16,32},{24,40},{32,48},{40,56},{48,64},{56,72},{64,... | collective-permute-start | bytes 786440 | tf_op jit(solution)/shard_map/ppermute | solution.py:21
  18.7 8.2 %collective-permute-done.2 = f32[4,128,128]{2,1,0:T(8,128)S(1)} collective-permute-done((f32[4,128,128]{2,1,0:T(8,128)S(1)}, f32[4,128,128]{2,1,0:T(8,128)S(1)}, u32[]{:S(2)}, u32[]{:S(2)}) %collective-permute-start.2) | collective-permute-done | bytes 262176 | tf_op jit(solution)/shard_map/ppermute | solution.py:21
  26.9 4.7 %collective-permute-start.4 = (f32[4,128,128]{2,1,0:T(8,128)S(1)}, f32[4,128,128]{2,1,0:T(8,128)S(1)}, u32[]{:S(2)}, u32[]{:S(2)}) collective-permute-start(f32[4,128,128]{2,1,0:T(8,128)S(1)} %collective-permute-done.2), channel_id=1, source_target_pairs={{0,16},{8,24},{16,32},{24,40},{32,48},{40,56},{48,64},{56,72},{64,... | collective-permute-start | bytes 786440 | tf_op jit(solution)/shard_map/ppermute | solution.py:21
  31.5 4.0 %collective-permute-start.3 = (f32[4]{0:T(128)S(1)}, f32[4]{0:T(128)S(1)}, u32[]{:S(2)}, u32[]{:S(2)}) collective-permute-start(f32[4]{0:T(128)S(1)} %get-tuple-element.33), channel_id=1, source_target_pairs={{0,16},{8,24},{16,32},{24,40},{32,48},{40,56},{48,64},{56,72},{64,... | collective-permute-start | bytes 56 | tf_op jit(solution)/shard_map/ppermute | solution.py:21
  35.6 2.9 %collective-permute-done.3 = f32[4]{0:T(128)S(1)} collective-permute-done((f32[4]{0:T(128)S(1)}, f32[4]{0:T(128)S(1)}, u32[]{:S(2)}, u32[]{:S(2)}) %collective-permute-start.3) | collective-permute-done | bytes 48 | tf_op jit(solution)/shard_map/ppermute | solution.py:21
  38.5 6.1 %collective-permute-start.5 = (f32[4]{0:T(128)S(1)}, f32[4]{0:T(128)S(1)}, u32[]{:S(2)}, u32[]{:S(2)}) collective-permute-start(f32[4]{0:T(128)S(1)} %collective-permute-done.3), channel_id=1, source_target_pairs={{0,16},{8,24},{16,32},{24,40},{32,48},{40,56},{48,64},{56,72},{64,... | collective-permute-start | bytes 56 | tf_op jit(solution)/shard_map/ppermute | solution.py:21
  44.6 1.3 collective-permute-done.5
  46.0 7.7 %collective-permute-start.6 = (f32[4,128,128]{2,1,0:T(8,128)S(1)}, f32[4,128,128]{2,1,0:T(8,128)S(1)}, u32[]{:S(2)}, u32[]{:S(2)}) collective-permute-start(f32[4,128,128]{2,1,0:T(8,128)S(1)} %multiply_add_fusion.9), channel_id=1, source_target_pairs={{0,32},{8,40},{16,48},{24,56},{32,64},{40,72},{48,80},{56,88},{64,... | collective-permute-start | bytes 786440 | tf_op jit(solution)/shard_map/ppermute | solution.py:21
  55.7 1.8 collective-permute-done.6
  57.6 5.8 %collective-permute-start.8 = (f32[4,128,128]{2,1,0:T(8,128)S(1)}, f32[4,128,128]{2,1,0:T(8,128)S(1)}, u32[]{:S(2)}, u32[]{:S(2)}) collective-permute-start(f32[4,128,128]{2,1,0:T(8,128)S(1)} %multiply_add_fusion.8), channel_id=1, source_target_pairs={{0,64},{8,72},{16,80},{24,88},{32,96},{40,104},{48,112},{56,120},{... | collective-permute-start | bytes 786440 | tf_op jit(solution)/shard_map/ppermute | solution.py:21
  63.6 1.9 collective-permute-start.7
  65.5 10.4 %collective-permute-done.7 = f32[4]{0:T(128)S(1)} collective-permute-done((f32[4]{0:T(128)S(1)}, f32[4]{0:T(128)S(1)}, u32[]{:S(2)}, u32[]{:S(2)}) %collective-permute-start.7) | collective-permute-done | bytes 48 | tf_op jit(solution)/shard_map/ppermute | solution.py:21
  76.0 2.9 %collective-permute-start.10 = (f32[4,128,128]{2,1,0:T(8,128)S(1)}, f32[4,128,128]{2,1,0:T(8,128)S(1)}, u32[]{:S(2)}, u32[]{:S(2)}) collective-permute-start(f32[4,128,128]{2,1,0:T(8,128)S(1)} %multiply_add_fusion.7), channel_id=1, source_target_pairs={{0,128},{8,136},{16,144},{24,152},{32,160},{40,168},{48,176},{56,1... | collective-permute-start | bytes 786440 | tf_op jit(solution)/shard_map/ppermute | solution.py:21
  78.9 1.5 convolution_bitcast_fusion.1
  81.0 4.8 %collective-permute-start.9 = (f32[4]{0:T(128)S(1)}, f32[4]{0:T(128)S(1)}, u32[]{:S(2)}, u32[]{:S(2)}) collective-permute-start(f32[4]{0:T(128)S(1)} %get-tuple-element.11), channel_id=1, source_target_pairs={{0,64},{8,72},{16,80},{24,88},{32,96},{40,104},{48,112},{56,120},{... | collective-permute-start | bytes 56 | tf_op jit(solution)/shard_map/ppermute | solution.py:21
  85.8 4.4 %collective-permute-done.9 = f32[4]{0:T(128)S(1)} collective-permute-done((f32[4]{0:T(128)S(1)}, f32[4]{0:T(128)S(1)}, u32[]{:S(2)}, u32[]{:S(2)}) %collective-permute-start.9) | collective-permute-done | bytes 48 | tf_op jit(solution)/shard_map/ppermute | solution.py:21
  91.1 3.7 %all-gather.2.cloned.1.call-done = bf16[4096,384]{1,0:T(8,128)(2,1)} async-done(((bf16[128,384]{1,0:T(8,128)(2,1)}), bf16[4096,384]{1,0:T(8,128)(2,1)}) %all-gather.2.cloned.1.call-update) | async-done | bytes 3145744 | tf_op jit(solution)/shard_map/all_gather | solution.py:101
  94.9 12.6 %fusion.86 = (f32[128,8]{0,1:T(8,128)}, f32[128,8,4096]{0,2,1:T(8,128)}) fusion(pred[128,4096]{0,1:T(8,128)(4,1)} %iota_compare_fusion, bf16[4096,384]{1,0:T(8,128)(2,1)} %all-gather.2.cloned.1.call-done, bf16[128,1024]{1,0:T(8,128)(2,1)S(1)} %copy-done), kind=kOutput, calls=%fused_computation.142 | convolution fusion | flops 1094717440 | bytes 19140608 | tf_op jit(solution)/shard_map/sub | solution.py:135
  107.5 8.3 %fusion.3 = f32[128,8,128]{2,0,1:T(8,128)S(1)} fusion(f32[128,8,4096]{0,2,1:T(8,128)} %get-tuple-element.37, bf16[4096,384]{1,0:T(8,128)(2,1)S(1)} %copy-done.2), kind=kOutput, calls=%fused_computation.7 | convolution fusion | flops 1086324736 | bytes 18350080 | tf_op jit(solution)/shard_map/qgn,nd->qgd/dot_general | solution.py:141
  115.8 2.3 copy-done.1
  118.1 2.4 %fusion.8 = f32[128,8,128]{2,0,1:T(8,128)S(1)} fusion(f32[128,8,4096]{0,2,1:T(8,128)S(1)} %copy-done.1, bf16[4096,384]{1,0:T(8,128)(2,1)S(1)} %copy-done.2), kind=kOutput, calls=%fused_computation.11 | convolution fusion | flops 1082130432 | bytes 18350080 | tf_op jit(solution)/shard_map/qgn,nd->qgd/dot_general | solution.py:140
  120.5 2.4 %fusion.21 = f32[128,8,128]{2,0,1:T(8,128)S(1)} fusion(f32[128,8,128]{2,0,1:T(8,128)S(1)} %fusion.3, f32[128,8,128]{2,0,1:T(8,128)S(1)} %fusion.8, f32[128,8,4096]{0,2,1:T(8,128)S(1)} %copy-done.1, bf16[4096,384]{1,0:T(8,128)(2,1)S(1)} %copy-done.2, f32[128,8]{0,1:T(8,128)S(1)} %copy-done.11), kind=kOutput, calls=%fused_computation.32 | convolution fusion | flops 1082523648 | bytes 19402752 | tf_op jit(solution)/shard_map/qgn,nd->qgd/dot_general | solution.py:139
  123.0 1.7 fusion.13
  127.5 8.0 %collective-permute-start.13 = (f32[4,128,128]{2,1,0:T(8,128)S(1)}, f32[4,128,128]{2,1,0:T(8,128)S(1)}, u32[]{:S(2)}, u32[]{:S(2)}) collective-permute-start(f32[4,128,128]{2,1,0:T(8,128)S(1)} %select_add_fusion), channel_id=1, source_target_pairs={{16,0},{24,8},{32,16},{40,24},{48,32},{56,40},{64,48},{72,56},{80,... | collective-permute-start | bytes 786440 | tf_op jit(solution)/shard_map/ppermute | solution.py:21
  135.5 7.9 %collective-permute-done.13 = f32[4,128,128]{2,1,0:T(8,128)S(1)} collective-permute-done((f32[4,128,128]{2,1,0:T(8,128)S(1)}, f32[4,128,128]{2,1,0:T(8,128)S(1)}, u32[]{:S(2)}, u32[]{:S(2)}) %collective-permute-start.13) | collective-permute-done | bytes 262176 | tf_op jit(solution)/shard_map/ppermute | solution.py:21
  143.4 4.0 %collective-permute-start.15 = (f32[4,128,128]{2,1,0:T(8,128)S(1)}, f32[4,128,128]{2,1,0:T(8,128)S(1)}, u32[]{:S(2)}, u32[]{:S(2)}) collective-permute-start(f32[4,128,128]{2,1,0:T(8,128)S(1)} %collective-permute-done.13), channel_id=1, source_target_pairs={{16,0},{24,8},{32,16},{40,24},{48,32},{56,40},{64,48},{72,56},{80,... | collective-permute-start | bytes 786440 | tf_op jit(solution)/shard_map/ppermute | solution.py:21
  147.4 3.1 %collective-permute-start.14 = (f32[4]{0:T(128)S(1)}, f32[4]{0:T(128)S(1)}, u32[]{:S(2)}, u32[]{:S(2)}) collective-permute-start(f32[4]{0:T(128)S(1)} %get-tuple-element.29), channel_id=1, source_target_pairs={{16,0},{24,8},{32,16},{40,24},{48,32},{56,40},{64,48},{72,56},{80,... | collective-permute-start | bytes 56 | tf_op jit(solution)/shard_map/ppermute | solution.py:21
  150.5 5.2 %collective-permute-done.14 = f32[4]{0:T(128)S(1)} collective-permute-done((f32[4]{0:T(128)S(1)}, f32[4]{0:T(128)S(1)}, u32[]{:S(2)}, u32[]{:S(2)}) %collective-permute-start.14) | collective-permute-done | bytes 48 | tf_op jit(solution)/shard_map/ppermute | solution.py:21
  155.7 2.8 %collective-permute-start.16 = (f32[4]{0:T(128)S(1)}, f32[4]{0:T(128)S(1)}, u32[]{:S(2)}, u32[]{:S(2)}) collective-permute-start(f32[4]{0:T(128)S(1)} %collective-permute-done.14), channel_id=1, source_target_pairs={{16,0},{24,8},{32,16},{40,24},{48,32},{56,40},{64,48},{72,56},{80,... | collective-permute-start | bytes 56 | tf_op jit(solution)/shard_map/ppermute | solution.py:21
  158.5 5.0 %collective-permute-done.16 = f32[4]{0:T(128)S(1)} collective-permute-done((f32[4]{0:T(128)S(1)}, f32[4]{0:T(128)S(1)}, u32[]{:S(2)}, u32[]{:S(2)}) %collective-permute-start.16) | collective-permute-done | bytes 48 | tf_op jit(solution)/shard_map/ppermute | solution.py:21
  163.7 2.2 collective-permute-start.17
  165.9 1.9 collective-permute-start.18
  167.9 5.7 %collective-permute-done.17 = f32[4,128,128]{2,1,0:T(8,128)S(1)} collective-permute-done((f32[4,128,128]{2,1,0:T(8,128)S(1)}, f32[4,128,128]{2,1,0:T(8,128)S(1)}, u32[]{:S(2)}, u32[]{:S(2)}) %collective-permute-start.17) | collective-permute-done | bytes 262176 | tf_op jit(solution)/shard_map/ppermute | solution.py:21
  173.7 1.9 collective-permute-start.19
  175.6 1.9 collective-permute-start.20
  177.5 8.8 %collective-permute-done.20 = f32[4]{0:T(128)S(1)} collective-permute-done((f32[4]{0:T(128)S(1)}, f32[4]{0:T(128)S(1)}, u32[]{:S(2)}, u32[]{:S(2)}) %collective-permute-start.20) | collective-permute-done | bytes 48 | tf_op jit(solution)/shard_map/ppermute | solution.py:21
  186.4 1.3 collective-permute-start.21
  187.7 1.4 fusion.16
  189.4 12.0 %collective-permute-done.21 = f32[4,128,128]{2,1,0:T(8,128)S(1)} collective-permute-done((f32[4,128,128]{2,1,0:T(8,128)S(1)}, f32[4,128,128]{2,1,0:T(8,128)S(1)}, u32[]{:S(2)}, u32[]{:S(2)}) %collective-permute-start.21) | collective-permute-done | bytes 262176 | tf_op jit(solution)/shard_map/ppermute | solution.py:21
  202.1 2.4 %fusion.18 = f32[128,128]{0,1:T(8,128)S(1)} fusion(f32[128,128]{0,1:T(8,128)S(1)} %fusion.91, f32[128,8,128]{2,0,1:T(8,128)S(1)} %fusion.13, f32[4,128,128]{2,1,0:T(8,128)} %collective-permute-done.11, f32[4,128,128]{2,1,0:T(8,128)} %get-tuple-element.16, f32[128,8]{0,1:T(8,128)} %copy.16, pred[]{:T(512)S(6)} %eq.23), kind=kOutput, calls=%fused_computation.30 | convolution fusion | flops 201867264 | bytes 1183745 | tf_op jit(solution)/shard_map/thp,hpn->tn/dot_general | solution.py:163
  204.5 2.0 fusion.17
  207.6 4.9 %collective-permute-done.23 = f32[64,256]{0,1:T(8,128)S(1)} collective-permute-done((f32[64,256]{0,1:T(8,128)S(1)}, f32[64,256]{0,1:T(8,128)S(1)}, u32[]{:S(2)}, u32[]{:S(2)}) %collective-permute-start.23) | collective-permute-done | bytes 65568 | tf_op jit(solution)/shard_map/ppermute | solution.py:86
  212.7 2.9 %collective-permute-start.24 = (f32[32,256]{0,1:T(8,128)S(1)}, f32[32,256]{0,1:T(8,128)S(1)}, u32[]{:S(2)}, u32[]{:S(2)}) collective-permute-start(f32[32,256]{0,1:T(8,128)S(1)} %slice_select_fusion.1), channel_id=1, source_target_pairs={{0,2},{1,3},{2,0},{3,1},{4,6},{5,7},{6,4},{7,5},{8,10},{9,11},{10,... | collective-permute-start | bytes 98312 | tf_op jit(solution)/shard_map/ppermute | solution.py:86
  215.6 1.9 convolution_bitcast_fusion.2
  217.5 1.9 collective-permute-done.24
  219.7 1.5 collective-permute-start.25
  223.2 1.5 collective-permute-done.25
  (95 shorter events, 19.5 us)
Async XLA Ops:
  7.2 87.7 %copy-start = (bf16[128,1024]{1,0:T(8,128)(2,1)S(1)}, bf16[128,1024]{1,0:T(8,128)(2,1)}, u32[]{:S(2)}) copy-start(bf16[128,1024]{1,0:T(8,128)(2,1)} %param.7) | copy-start | bytes 786436
  7.2 87.7 %all-gather.2.cloned.1.call-start = ((), (), s32[]{:S(2)}) async-start(), calls=%async_computation | async-start | bytes 3244032 | tf_op jit(solution)/shard_map/all_gather | solution.py:101
  10.5 3.1 %collective-permute-start = (f32[8]{0:T(128)S(1)}, f32[8]{0:T(128)S(1)}, u32[]{:S(2)}, u32[]{:S(2)}) collective-permute-start(f32[8]{0:T(128)S(1)} %slice_bitcast_fusion.12), channel_id=1, source_target_pairs={{0,8},{8,0},{16,24},{24,16},{32,40},{40,32},{48,56},{56,48},{64,72... | collective-permute-start | bytes 104 | tf_op jit(solution)/shard_map/ppermute | solution.py:36
  11.7 79.4 %copy-start.3 = (bf16[128,1024]{0,1:T(8,128)(2,1)}, bf16[128,1024]{0,1:T(8,128)(2,1)S(1)}, u32[]{:S(2)}) copy-start(bf16[128,1024]{0,1:T(8,128)(2,1)S(1)} %copy.13) | copy-start | bytes 786436
  11.8 1.2 copy-start.8
  13.1 1.7 collective-permute-start.1
  14.9 12.0 %collective-permute-start.2 = (f32[4,128,128]{2,1,0:T(8,128)S(1)}, f32[4,128,128]{2,1,0:T(8,128)S(1)}, u32[]{:S(2)}, u32[]{:S(2)}) collective-permute-start(f32[4,128,128]{2,1,0:T(8,128)S(1)} %select_add_fusion.1), channel_id=1, source_target_pairs={{0,16},{8,24},{16,32},{24,40},{32,48},{40,56},{48,64},{56,72},{64,... | collective-permute-start | bytes 786440 | tf_op jit(solution)/shard_map/ppermute | solution.py:21
  26.9 19.0 %collective-permute-start.4 = (f32[4,128,128]{2,1,0:T(8,128)S(1)}, f32[4,128,128]{2,1,0:T(8,128)S(1)}, u32[]{:S(2)}, u32[]{:S(2)}) collective-permute-start(f32[4,128,128]{2,1,0:T(8,128)S(1)} %collective-permute-done.2), channel_id=1, source_target_pairs={{0,16},{8,24},{16,32},{24,40},{32,48},{40,56},{48,64},{56,72},{64,... | collective-permute-start | bytes 786440 | tf_op jit(solution)/shard_map/ppermute | solution.py:21
  31.5 6.9 %collective-permute-start.3 = (f32[4]{0:T(128)S(1)}, f32[4]{0:T(128)S(1)}, u32[]{:S(2)}, u32[]{:S(2)}) collective-permute-start(f32[4]{0:T(128)S(1)} %get-tuple-element.33), channel_id=1, source_target_pairs={{0,16},{8,24},{16,32},{24,40},{32,48},{40,56},{48,64},{56,72},{64,... | collective-permute-start | bytes 56 | tf_op jit(solution)/shard_map/ppermute | solution.py:21
  38.5 7.4 %collective-permute-start.5 = (f32[4]{0:T(128)S(1)}, f32[4]{0:T(128)S(1)}, u32[]{:S(2)}, u32[]{:S(2)}) collective-permute-start(f32[4]{0:T(128)S(1)} %collective-permute-done.3), channel_id=1, source_target_pairs={{0,16},{8,24},{16,32},{24,40},{32,48},{40,56},{48,64},{56,72},{64,... | collective-permute-start | bytes 56 | tf_op jit(solution)/shard_map/ppermute | solution.py:21
  46.0 11.6 %collective-permute-start.6 = (f32[4,128,128]{2,1,0:T(8,128)S(1)}, f32[4,128,128]{2,1,0:T(8,128)S(1)}, u32[]{:S(2)}, u32[]{:S(2)}) collective-permute-start(f32[4,128,128]{2,1,0:T(8,128)S(1)} %multiply_add_fusion.9), channel_id=1, source_target_pairs={{0,32},{8,40},{16,48},{24,56},{32,64},{40,72},{48,80},{56,88},{64,... | collective-permute-start | bytes 786440 | tf_op jit(solution)/shard_map/ppermute | solution.py:21
  57.6 18.2 %collective-permute-start.8 = (f32[4,128,128]{2,1,0:T(8,128)S(1)}, f32[4,128,128]{2,1,0:T(8,128)S(1)}, u32[]{:S(2)}, u32[]{:S(2)}) collective-permute-start(f32[4,128,128]{2,1,0:T(8,128)S(1)} %multiply_add_fusion.8), channel_id=1, source_target_pairs={{0,64},{8,72},{16,80},{24,88},{32,96},{40,104},{48,112},{56,120},{... | collective-permute-start | bytes 786440 | tf_op jit(solution)/shard_map/ppermute | solution.py:21
  63.6 27.6 %copy-start.9 = (f32[8,128]{1,0:T(8,128)}, f32[8,128]{1,0:T(8,128)S(1)}, u32[]{:S(2)}) copy-start(f32[8,128]{1,0:T(8,128)S(1)} %copy.11) | copy-start | bytes 12292
  63.6 12.3 %collective-permute-start.7 = (f32[4]{0:T(128)S(1)}, f32[4]{0:T(128)S(1)}, u32[]{:S(2)}, u32[]{:S(2)}) collective-permute-start(f32[4]{0:T(128)S(1)} %get-tuple-element.13), channel_id=1, source_target_pairs={{0,32},{8,40},{16,48},{24,56},{32,64},{40,72},{48,80},{56,88},{64,... | collective-permute-start | bytes 56 | tf_op jit(solution)/shard_map/ppermute | solution.py:21
  76.0 14.2 %collective-permute-start.10 = (f32[4,128,128]{2,1,0:T(8,128)S(1)}, f32[4,128,128]{2,1,0:T(8,128)S(1)}, u32[]{:S(2)}, u32[]{:S(2)}) collective-permute-start(f32[4,128,128]{2,1,0:T(8,128)S(1)} %multiply_add_fusion.7), channel_id=1, source_target_pairs={{0,128},{8,136},{16,144},{24,152},{32,160},{40,168},{48,176},{56,1... | collective-permute-start | bytes 786440 | tf_op jit(solution)/shard_map/ppermute | solution.py:21
  81.0 9.1 %collective-permute-start.9 = (f32[4]{0:T(128)S(1)}, f32[4]{0:T(128)S(1)}, u32[]{:S(2)}, u32[]{:S(2)}) collective-permute-start(f32[4]{0:T(128)S(1)} %get-tuple-element.11), channel_id=1, source_target_pairs={{0,64},{8,72},{16,80},{24,88},{32,96},{40,104},{48,112},{56,120},{... | collective-permute-start | bytes 56 | tf_op jit(solution)/shard_map/ppermute | solution.py:21
  91.1 31.8 %collective-permute-start.11 = (f32[4,128,128]{2,1,0:T(8,128)}, f32[4,128,128]{2,1,0:T(8,128)}, u32[]{:S(2)}, u32[]{:S(2)}) collective-permute-start(f32[4,128,128]{2,1,0:T(8,128)} %get-tuple-element.17), channel_id=1, source_target_pairs={{0,8},{8,0},{16,24},{24,16},{32,40},{40,32},{48,56},{56,48},{64,72... | collective-permute-start | bytes 786440 | tf_op jit(solution)/shard_map/ppermute | solution.py:64
  94.9 12.7 %copy-start.2 = (bf16[4096,384]{1,0:T(8,128)(2,1)S(1)}, bf16[4096,384]{1,0:T(8,128)(2,1)}, u32[]{:S(2)}) copy-start(bf16[4096,384]{1,0:T(8,128)(2,1)} %all-gather.2.cloned.1.call-done) | copy-start | bytes 9437188
  107.5 10.5 %copy-start.1 = (f32[128,8,4096]{0,2,1:T(8,128)S(1)}, f32[128,8,4096]{0,2,1:T(8,128)}, u32[]{:S(2)}) copy-start(f32[128,8,4096]{0,2,1:T(8,128)} %get-tuple-element.37) | copy-start | bytes 50331652
  107.5 12.9 %copy-start.11 = (f32[128,8]{0,1:T(8,128)S(1)}, f32[128,8]{0,1:T(8,128)}, u32[]{:S(2)}) copy-start(f32[128,8]{0,1:T(8,128)} %get-tuple-element.36) | copy-start | bytes 12292
  118.1 4.9 %copy-start.4 = (f32[4,128,128]{2,1,0:T(8,128)S(1)}, f32[4,128,128]{2,1,0:T(8,128)}, u32[]{:S(2)}) copy-start(f32[4,128,128]{2,1,0:T(8,128)} %get-tuple-element.16) | copy-start | bytes 786436
  118.1 4.9 %copy-start.5 = (bf16[128,128]{1,0:T(8,128)(2,1)S(1)}, bf16[128,128]{1,0:T(8,128)(2,1)}, u32[]{:S(2)}) copy-start(bf16[128,128]{1,0:T(8,128)(2,1)} %param.12) | copy-start | bytes 98308
  118.1 4.9 %copy-start.6 = (f32[128,8,128]{2,0,1:T(8,128)S(1)}, f32[128,8,128]{2,0,1:T(8,128)}, u32[]{:S(2)}) copy-start(f32[128,8,128]{2,0,1:T(8,128)} %convolution_bitcast_fusion.1) | copy-start | bytes 1572868
  118.1 4.9 %copy-start.10 = (f32[128,8]{0,1:T(8,128)S(1)}, f32[128,8]{0,1:T(8,128)}, u32[]{:S(2)}) copy-start(f32[128,8]{0,1:T(8,128)} %copy.16) | copy-start | bytes 12292
  118.1 8.1 %copy-start.12 = (f32[8]{0:T(128)S(1)}, f32[8]{0:T(128)}, u32[]{:S(2)}) copy-start(f32[8]{0:T(128)} %get-tuple-element.20) | copy-start | bytes 100
  118.1 8.1 %copy-start.13 = (f32[8]{0:T(128)S(1)}, f32[8]{0:T(128)}, u32[]{:S(2)}) copy-start(f32[8]{0:T(128)} %get-tuple-element.21) | copy-start | bytes 100
  120.5 68.6 %copy-start.7 = (bf16[128,128]{1,0:T(8,128)(2,1)S(1)}, bf16[128,128]{1,0:T(8,128)(2,1)}, u32[]{:S(2)}) copy-start(bf16[128,128]{1,0:T(8,128)(2,1)} %param.11) | copy-start | bytes 98308
  125.8 1.6 collective-permute-start.12
  127.5 15.9 %collective-permute-start.13 = (f32[4,128,128]{2,1,0:T(8,128)S(1)}, f32[4,128,128]{2,1,0:T(8,128)S(1)}, u32[]{:S(2)}, u32[]{:S(2)}) collective-permute-start(f32[4,128,128]{2,1,0:T(8,128)S(1)} %select_add_fusion), channel_id=1, source_target_pairs={{16,0},{24,8},{32,16},{40,24},{48,32},{56,40},{64,48},{72,56},{80,... | collective-permute-start | bytes 786440 | tf_op jit(solution)/shard_map/ppermute | solution.py:21
  143.4 20.2 %collective-permute-start.15 = (f32[4,128,128]{2,1,0:T(8,128)S(1)}, f32[4,128,128]{2,1,0:T(8,128)S(1)}, u32[]{:S(2)}, u32[]{:S(2)}) collective-permute-start(f32[4,128,128]{2,1,0:T(8,128)S(1)} %collective-permute-done.13), channel_id=1, source_target_pairs={{16,0},{24,8},{32,16},{40,24},{48,32},{56,40},{64,48},{72,56},{80,... | collective-permute-start | bytes 786440 | tf_op jit(solution)/shard_map/ppermute | solution.py:21
  147.4 8.3 %collective-permute-start.14 = (f32[4]{0:T(128)S(1)}, f32[4]{0:T(128)S(1)}, u32[]{:S(2)}, u32[]{:S(2)}) collective-permute-start(f32[4]{0:T(128)S(1)} %get-tuple-element.29), channel_id=1, source_target_pairs={{16,0},{24,8},{32,16},{40,24},{48,32},{56,40},{64,48},{72,56},{80,... | collective-permute-start | bytes 56 | tf_op jit(solution)/shard_map/ppermute | solution.py:21
  155.7 7.8 %collective-permute-start.16 = (f32[4]{0:T(128)S(1)}, f32[4]{0:T(128)S(1)}, u32[]{:S(2)}, u32[]{:S(2)}) collective-permute-start(f32[4]{0:T(128)S(1)} %collective-permute-done.14), channel_id=1, source_target_pairs={{16,0},{24,8},{32,16},{40,24},{48,32},{56,40},{64,48},{72,56},{80,... | collective-permute-start | bytes 56 | tf_op jit(solution)/shard_map/ppermute | solution.py:21
  163.7 9.9 %collective-permute-start.17 = (f32[4,128,128]{2,1,0:T(8,128)S(1)}, f32[4,128,128]{2,1,0:T(8,128)S(1)}, u32[]{:S(2)}, u32[]{:S(2)}) collective-permute-start(f32[4,128,128]{2,1,0:T(8,128)S(1)} %multiply_add_fusion.4), channel_id=1, source_target_pairs={{32,0},{40,8},{48,16},{56,24},{64,32},{72,40},{80,48},{88,56},{96,... | collective-permute-start | bytes 786440 | tf_op jit(solution)/shard_map/ppermute | solution.py:21
  165.9 9.7 %collective-permute-start.18 = (f32[4]{0:T(128)S(1)}, f32[4]{0:T(128)S(1)}, u32[]{:S(2)}, u32[]{:S(2)}) collective-permute-start(f32[4]{0:T(128)S(1)} %get-tuple-element.9), channel_id=1, source_target_pairs={{32,0},{40,8},{48,16},{56,24},{64,32},{72,40},{80,48},{88,56},{96,... | collective-permute-start | bytes 56 | tf_op jit(solution)/shard_map/ppermute | solution.py:21
  173.7 12.7 %collective-permute-start.19 = (f32[4,128,128]{2,1,0:T(8,128)S(1)}, f32[4,128,128]{2,1,0:T(8,128)S(1)}, u32[]{:S(2)}, u32[]{:S(2)}) collective-permute-start(f32[4,128,128]{2,1,0:T(8,128)S(1)} %multiply_add_fusion.3), channel_id=1, source_target_pairs={{64,0},{72,8},{80,16},{88,24},{96,32},{104,40},{112,48},{120,56},{... | collective-permute-start | bytes 786440 | tf_op jit(solution)/shard_map/ppermute | solution.py:21
  175.6 10.7 %collective-permute-start.20 = (f32[4]{0:T(128)S(1)}, f32[4]{0:T(128)S(1)}, u32[]{:S(2)}, u32[]{:S(2)}) collective-permute-start(f32[4]{0:T(128)S(1)} %get-tuple-element.7), channel_id=1, source_target_pairs={{64,0},{72,8},{80,16},{88,24},{96,32},{104,40},{112,48},{120,56},{... | collective-permute-start | bytes 56 | tf_op jit(solution)/shard_map/ppermute | solution.py:21
  186.4 14.9 %collective-permute-start.21 = (f32[4,128,128]{2,1,0:T(8,128)S(1)}, f32[4,128,128]{2,1,0:T(8,128)S(1)}, u32[]{:S(2)}, u32[]{:S(2)}) collective-permute-start(f32[4,128,128]{2,1,0:T(8,128)S(1)} %multiply_add_fusion.2), channel_id=1, source_target_pairs={{128,0},{136,8},{144,16},{152,24},{160,32},{168,40},{176,48},{184,... | collective-permute-start | bytes 786440 | tf_op jit(solution)/shard_map/ppermute | solution.py:21
  201.4 3.0 %collective-permute-start.22 = (f32[4,128,128]{2,1,0:T(8,128)S(1)}, f32[4,128,128]{2,1,0:T(8,128)S(1)}, u32[]{:S(2)}, u32[]{:S(2)}) collective-permute-start(f32[4,128,128]{2,1,0:T(8,128)S(1)} %get-tuple-element.15), channel_id=1, source_target_pairs={{0,8},{8,0},{16,24},{24,16},{32,40},{40,32},{48,56},{56,48},{64,72... | collective-permute-start | bytes 786440 | tf_op jit(solution)/shard_map/ppermute | solution.py:64
  206.6 6.0 %collective-permute-start.23 = (f32[64,256]{0,1:T(8,128)S(1)}, f32[64,256]{0,1:T(8,128)S(1)}, u32[]{:S(2)}, u32[]{:S(2)}) collective-permute-start(f32[64,256]{0,1:T(8,128)S(1)} %fusion.60), channel_id=1, source_target_pairs={{0,4},{1,5},{2,6},{3,7},{4,0},{5,1},{6,2},{7,3},{8,12},{9,13},{10,... | collective-permute-start | bytes 196616 | tf_op jit(solution)/shard_map/ppermute | solution.py:86
  212.7 6.7 %collective-permute-start.24 = (f32[32,256]{0,1:T(8,128)S(1)}, f32[32,256]{0,1:T(8,128)S(1)}, u32[]{:S(2)}, u32[]{:S(2)}) collective-permute-start(f32[32,256]{0,1:T(8,128)S(1)} %slice_select_fusion.1), channel_id=1, source_target_pairs={{0,2},{1,3},{2,0},{3,1},{4,6},{5,7},{6,4},{7,5},{8,10},{9,11},{10,... | collective-permute-start | bytes 98312 | tf_op jit(solution)/shard_map/ppermute | solution.py:86
  219.7 5.1 %collective-permute-start.25 = (f32[16,256]{0,1:T(8,128)S(1)}, f32[16,256]{0,1:T(8,128)S(1)}, u32[]{:S(2)}, u32[]{:S(2)}) collective-permute-start(f32[16,256]{0,1:T(8,128)S(1)} %slice_select_fusion), channel_id=1, source_target_pairs={{0,1},{1,0},{2,3},{3,2},{4,5},{5,4},{6,7},{7,6},{8,9},{9,8},{10,11... | collective-permute-start | bytes 49160 | tf_op jit(solution)/shard_map/ppermute | solution.py:86
Sparse Core Ops, SparseCore 0:
  10.8 84.0 all-gather.1

commit v3 on v2

--- a/solution.py
+++ b/solution.py
@@ -72,21 +72,10 @@
     return upper.astype(jnp.bfloat16), (value - upper).astype(jnp.bfloat16)
 
 
-def mp_reduce_scatter(value, axis):
+def mp_sum_scatter(value, axis):
     count = lax.axis_size(axis)
-    mine = lax.axis_index(axis)
-    current = value
-    step = count // 2
-    while step >= 1:
-        half = current.shape[0] // 2
-        upper = (mine // step) % 2 == 1
-        low_part, high_part = current[:half], current[half:]
-        keep = jnp.where(upper, high_part, low_part)
-        send = jnp.where(upper, low_part, high_part)
-        got = lax.ppermute(send, axis, [(j, j ^ step) for j in range(count)])
-        current = keep + got
-        step //= 2
-    return current
+    blocks = value.reshape(count, value.shape[0] // count, value.shape[1])
+    return jnp.sum(lax.all_to_all(blocks, axis, 0, 0), axis=0)
 
 
 def local(queries, keys, values, inputs_x, in_b, in_c, log_decay):
@@ -156,13 +145,14 @@
     products = jnp.einsum("thp,shp->hts", mismatch, student_x, precision=highest)
     weighted = decays * products
     grad_b = jnp.einsum("hts,tn->sn", weighted, c_rows, precision=highest)
-    grad_b = grad_b + jnp.einsum(
+    grad_c = jnp.einsum("hts,sn->tn", weighted, b_rows, precision=highest)
+    grad_c = grad_c + jnp.einsum("thp,hpn->tn", scaled_mismatch, state_in, precision=highest)
+    early = mp_sum_scatter(jnp.concatenate([grad_b, grad_c], axis=1), "mp")
+    grad_b_later = jnp.einsum(
         "shp,hpn->sn", student_x * ending[:, :, None], later_grad, precision=highest
     )
-    grad_c = jnp.einsum("hts,sn->tn", weighted, b_rows, precision=highest)
-    grad_c = grad_c + jnp.einsum("thp,hpn->tn", scaled_mismatch, state_in, precision=highest)
-    summed = mp_reduce_scatter(jnp.concatenate([grad_b, grad_c], axis=1), "mp")
-    summed_b, summed_c = summed[:, :N], summed[:, N:]
+    summed_b = early[:, :N] + mp_sum_scatter(grad_b_later, "mp")
+    summed_c = early[:, N:]
     return (grad_x.reshape(row_count, heads * HEAD_WIDTH), summed_b, summed_c * c_scale)
 
 

time: 236 us -> 241 us (1.021)
  starting transfers between devices: 75.6 us -> 81.8 us
    all_to_all x0 -> x2, starting transfers between devices: none -> 11.6 us  [mp_sum_scatter(): return jnp.sum(lax.all_to_all(blocks, axis, 0, 0), axis=0)]
    all_to_all x0 -> x2, waiting for transfers between devices: none -> 9.44 us  [mp_sum_scatter(): return jnp.sum(lax.all_to_all(blocks, axis, 0, 0), axis=0)]
    ppermute x3 -> x0, waiting for transfers between devices: 8.31 us -> none  [mp_reduce_scatter(): got = lax.ppermute(send, axis, [(j, j ^ step) for j in range(count)])]
    ppermute x3 -> x0, starting transfers between devices: 5.45 us -> none  [mp_reduce_scatter(): got = lax.ppermute(send, axis, [(j, j ^ step) for j in range(count)])]
    unnamed x33 -> x39, local copies, waits for them, and re-layouts: 6.55 us -> 4.23 us
  transfers between devices with their start and end apart: 27 -> 26, of which waited for: 18 -> 18; matrix products, arithmetic and copies ran while one was open for 19% -> 19% of each run, Pallas kernels for 0% -> 0%
where the time goes in v3:
time: 241 us; the launch traced here: 238 us
  waiting for transfers between devices  87 us (36%)
  starting transfers between devices  81.8 us (34%)
  matrix products  41.1 us (17%)
  between operations  14.6 us (6%)
  local copies, waits for them, and re-layouts  6.96 us (3%)
  other arithmetic  6.91 us (3%)
    ppermute x18, waiting for transfers between devices, shift(): return lax.ppermute(value, axis, perm)  72 us
    ppermute x18, starting transfers between devices, shift(): return lax.ppermute(value, axis, perm)  69 us
    sub x1, matrix products, local(): weights = jnp.where(allowed, jnp.exp(scores - row_top), 0.0)  12.6 us
    all_to_all x2, starting transfers between devices, mp_sum_scatter(): return jnp.sum(lax.all_to_all(blocks, axis, 0, 0), axis=0)  11.6 us
    all_to_all x2, waiting for transfers between devices, mp_sum_scatter(): return jnp.sum(lax.all_to_all(blocks, axis, 0, 0), axis=0)  9.44 us
    dot_general x1, matrix products, local(): jnp.einsum('qgn,nd->qgd', weights_lo, every_hi, preferred_element_type=jn...  8.28 us
  transfers between devices with their start and end apart: 26, of which 18 were waited for; matrix products, arithmetic and copies ran while one was open for 19% of the time, Pallas kernels for 0%

profile of v3, /device:TPU:68, one launch (start us, length us, event | category | flops | bytes accessed | tf_op | source)
XLA Modules:
  0.0 238.4 jit_solution(9626070121024540400)
XLA Ops:
  8.1 1.4 pad_maximum_fusion.1
  14.8 3.8 %collective-permute-start.2 = (f32[4,128,128]{2,1,0:T(8,128)S(1)}, f32[4,128,128]{2,1,0:T(8,128)S(1)}, u32[]{:S(2)}, u32[]{:S(2)}) collective-permute-start(f32[4,128,128]{2,1,0:T(8,128)S(1)} %select_add_fusion.1), channel_id=1, source_target_pairs={{0,16},{8,24},{16,32},{24,40},{32,48},{40,56},{48,64},{56,72},{64,... | collective-permute-start | bytes 786440 | tf_op jit(solution)/shard_map/ppermute | solution.py:21
  18.6 8.2 %collective-permute-done.2 = f32[4,128,128]{2,1,0:T(8,128)S(1)} collective-permute-done((f32[4,128,128]{2,1,0:T(8,128)S(1)}, f32[4,128,128]{2,1,0:T(8,128)S(1)}, u32[]{:S(2)}, u32[]{:S(2)}) %collective-permute-start.2) | collective-permute-done | bytes 262176 | tf_op jit(solution)/shard_map/ppermute | solution.py:21
  26.8 4.7 %collective-permute-start.4 = (f32[4,128,128]{2,1,0:T(8,128)S(1)}, f32[4,128,128]{2,1,0:T(8,128)S(1)}, u32[]{:S(2)}, u32[]{:S(2)}) collective-permute-start(f32[4,128,128]{2,1,0:T(8,128)S(1)} %collective-permute-done.2), channel_id=1, source_target_pairs={{0,16},{8,24},{16,32},{24,40},{32,48},{40,56},{48,64},{56,72},{64,... | collective-permute-start | bytes 786440 | tf_op jit(solution)/shard_map/ppermute | solution.py:21
  31.5 4.0 %collective-permute-start.3 = (f32[4]{0:T(128)S(1)}, f32[4]{0:T(128)S(1)}, u32[]{:S(2)}, u32[]{:S(2)}) collective-permute-start(f32[4]{0:T(128)S(1)} %get-tuple-element.36), channel_id=1, source_target_pairs={{0,16},{8,24},{16,32},{24,40},{32,48},{40,56},{48,64},{56,72},{64,... | collective-permute-start | bytes 56 | tf_op jit(solution)/shard_map/ppermute | solution.py:21
  35.5 2.9 %collective-permute-done.3 = f32[4]{0:T(128)S(1)} collective-permute-done((f32[4]{0:T(128)S(1)}, f32[4]{0:T(128)S(1)}, u32[]{:S(2)}, u32[]{:S(2)}) %collective-permute-start.3) | collective-permute-done | bytes 48 | tf_op jit(solution)/shard_map/ppermute | solution.py:21
  38.4 6.1 %collective-permute-start.5 = (f32[4]{0:T(128)S(1)}, f32[4]{0:T(128)S(1)}, u32[]{:S(2)}, u32[]{:S(2)}) collective-permute-start(f32[4]{0:T(128)S(1)} %collective-permute-done.3), channel_id=1, source_target_pairs={{0,16},{8,24},{16,32},{24,40},{32,48},{40,56},{48,64},{56,72},{64,... | collective-permute-start | bytes 56 | tf_op jit(solution)/shard_map/ppermute | solution.py:21
  44.5 1.3 collective-permute-done.5
  45.9 7.7 %collective-permute-start.6 = (f32[4,128,128]{2,1,0:T(8,128)S(1)}, f32[4,128,128]{2,1,0:T(8,128)S(1)}, u32[]{:S(2)}, u32[]{:S(2)}) collective-permute-start(f32[4,128,128]{2,1,0:T(8,128)S(1)} %multiply_add_fusion.9), channel_id=1, source_target_pairs={{0,32},{8,40},{16,48},{24,56},{32,64},{40,72},{48,80},{56,88},{64,... | collective-permute-start | bytes 786440 | tf_op jit(solution)/shard_map/ppermute | solution.py:21
  55.7 1.8 collective-permute-done.6
  57.6 5.8 %collective-permute-start.8 = (f32[4,128,128]{2,1,0:T(8,128)S(1)}, f32[4,128,128]{2,1,0:T(8,128)S(1)}, u32[]{:S(2)}, u32[]{:S(2)}) collective-permute-start(f32[4,128,128]{2,1,0:T(8,128)S(1)} %multiply_add_fusion.8), channel_id=1, source_target_pairs={{0,64},{8,72},{16,80},{24,88},{32,96},{40,104},{48,112},{56,120},{... | collective-permute-start | bytes 786440 | tf_op jit(solution)/shard_map/ppermute | solution.py:21
  63.5 1.9 collective-permute-start.7
  65.5 10.3 %collective-permute-done.7 = f32[4]{0:T(128)S(1)} collective-permute-done((f32[4]{0:T(128)S(1)}, f32[4]{0:T(128)S(1)}, u32[]{:S(2)}, u32[]{:S(2)}) %collective-permute-start.7) | collective-permute-done | bytes 48 | tf_op jit(solution)/shard_map/ppermute | solution.py:21
  75.8 3.0 %collective-permute-start.10 = (f32[4,128,128]{2,1,0:T(8,128)S(1)}, f32[4,128,128]{2,1,0:T(8,128)S(1)}, u32[]{:S(2)}, u32[]{:S(2)}) collective-permute-start(f32[4,128,128]{2,1,0:T(8,128)S(1)} %multiply_add_fusion.7), channel_id=1, source_target_pairs={{0,128},{8,136},{16,144},{24,152},{32,160},{40,168},{48,176},{56,1... | collective-permute-start | bytes 786440 | tf_op jit(solution)/shard_map/ppermute | solution.py:21
  78.9 2.3 convolution_bitcast_fusion.1
  81.8 4.8 %collective-permute-start.9 = (f32[4]{0:T(128)S(1)}, f32[4]{0:T(128)S(1)}, u32[]{:S(2)}, u32[]{:S(2)}) collective-permute-start(f32[4]{0:T(128)S(1)} %get-tuple-element.14), channel_id=1, source_target_pairs={{0,64},{8,72},{16,80},{24,88},{32,96},{40,104},{48,112},{56,120},{... | collective-permute-start | bytes 56 | tf_op jit(solution)/shard_map/ppermute | solution.py:21
  86.5 3.9 %collective-permute-done.9 = f32[4]{0:T(128)S(1)} collective-permute-done((f32[4]{0:T(128)S(1)}, f32[4]{0:T(128)S(1)}, u32[]{:S(2)}, u32[]{:S(2)}) %collective-permute-start.9) | collective-permute-done | bytes 48 | tf_op jit(solution)/shard_map/ppermute | solution.py:21
  91.3 3.8 %all-gather.2.cloned.1.call-done = bf16[4096,384]{1,0:T(8,128)(2,1)} async-done(((bf16[128,384]{1,0:T(8,128)(2,1)}), bf16[4096,384]{1,0:T(8,128)(2,1)}) %all-gather.2.cloned.1.call-update) | async-done | bytes 3145744 | tf_op jit(solution)/shard_map/all_gather | solution.py:90
  95.1 12.6 %fusion.90 = (f32[128,8]{0,1:T(8,128)}, f32[128,8,4096]{0,2,1:T(8,128)}) fusion(pred[128,4096]{0,1:T(8,128)(4,1)} %iota_compare_fusion, bf16[4096,384]{1,0:T(8,128)(2,1)} %all-gather.2.cloned.1.call-done, bf16[128,1024]{1,0:T(8,128)(2,1)S(1)} %copy-done), kind=kOutput, calls=%fused_computation.143 | convolution fusion | flops 1094717440 | bytes 19140608 | tf_op jit(solution)/shard_map/sub | solution.py:124
  107.8 8.3 %fusion.3 = f32[128,8,128]{2,0,1:T(8,128)S(1)} fusion(f32[128,8,4096]{0,2,1:T(8,128)} %get-tuple-element.40, bf16[4096,384]{1,0:T(8,128)(2,1)S(1)} %copy-done.2), kind=kOutput, calls=%fused_computation.7 | convolution fusion | flops 1086324736 | bytes 18350080 | tf_op jit(solution)/shard_map/qgn,nd->qgd/dot_general | solution.py:130
  116.1 2.3 copy-done.1
  118.4 2.4 fusion.8
  120.8 2.4 %fusion.20 = f32[128,8,128]{2,0,1:T(8,128)S(1)} fusion(f32[128,8,128]{2,0,1:T(8,128)S(1)} %fusion.3, f32[128,8,128]{2,0,1:T(8,128)S(1)} %fusion.8, f32[128,8,4096]{0,2,1:T(8,128)S(1)} %copy-done.1, bf16[4096,384]{1,0:T(8,128)(2,1)S(1)} %copy-done.2, f32[128,8]{0,1:T(8,128)S(1)} %copy-done.13), kind=kOutput, calls=%fused_computation.31 | convolution fusion | flops 1082523648 | bytes 19402752 | tf_op jit(solution)/shard_map/qgn,nd->qgd/dot_general | solution.py:128
  123.2 1.7 fusion.13
  127.8 7.8 %collective-permute-start.13 = (f32[4,128,128]{2,1,0:T(8,128)S(1)}, f32[4,128,128]{2,1,0:T(8,128)S(1)}, u32[]{:S(2)}, u32[]{:S(2)}) collective-permute-start(f32[4,128,128]{2,1,0:T(8,128)S(1)} %select_add_fusion), channel_id=1, source_target_pairs={{16,0},{24,8},{32,16},{40,24},{48,32},{56,40},{64,48},{72,56},{80,... | collective-permute-start | bytes 786440 | tf_op jit(solution)/shard_map/ppermute | solution.py:21
  135.6 7.7 %collective-permute-done.13 = f32[4,128,128]{2,1,0:T(8,128)S(1)} collective-permute-done((f32[4,128,128]{2,1,0:T(8,128)S(1)}, f32[4,128,128]{2,1,0:T(8,128)S(1)}, u32[]{:S(2)}, u32[]{:S(2)}) %collective-permute-start.13) | collective-permute-done | bytes 262176 | tf_op jit(solution)/shard_map/ppermute | solution.py:21
  143.4 4.0 %collective-permute-start.15 = (f32[4,128,128]{2,1,0:T(8,128)S(1)}, f32[4,128,128]{2,1,0:T(8,128)S(1)}, u32[]{:S(2)}, u32[]{:S(2)}) collective-permute-start(f32[4,128,128]{2,1,0:T(8,128)S(1)} %collective-permute-done.13), channel_id=1, source_target_pairs={{16,0},{24,8},{32,16},{40,24},{48,32},{56,40},{64,48},{72,56},{80,... | collective-permute-start | bytes 786440 | tf_op jit(solution)/shard_map/ppermute | solution.py:21
  147.6 3.1 %collective-permute-start.14 = (f32[4]{0:T(128)S(1)}, f32[4]{0:T(128)S(1)}, u32[]{:S(2)}, u32[]{:S(2)}) collective-permute-start(f32[4]{0:T(128)S(1)} %get-tuple-element.32), channel_id=1, source_target_pairs={{16,0},{24,8},{32,16},{40,24},{48,32},{56,40},{64,48},{72,56},{80,... | collective-permute-start | bytes 56 | tf_op jit(solution)/shard_map/ppermute | solution.py:21
  150.7 5.0 %collective-permute-done.14 = f32[4]{0:T(128)S(1)} collective-permute-done((f32[4]{0:T(128)S(1)}, f32[4]{0:T(128)S(1)}, u32[]{:S(2)}, u32[]{:S(2)}) %collective-permute-start.14) | collective-permute-done | bytes 48 | tf_op jit(solution)/shard_map/ppermute | solution.py:21
  155.7 2.8 %collective-permute-start.16 = (f32[4]{0:T(128)S(1)}, f32[4]{0:T(128)S(1)}, u32[]{:S(2)}, u32[]{:S(2)}) collective-permute-start(f32[4]{0:T(128)S(1)} %collective-permute-done.14), channel_id=1, source_target_pairs={{16,0},{24,8},{32,16},{40,24},{48,32},{56,40},{64,48},{72,56},{80,... | collective-permute-start | bytes 56 | tf_op jit(solution)/shard_map/ppermute | solution.py:21
  158.5 5.0 %collective-permute-done.16 = f32[4]{0:T(128)S(1)} collective-permute-done((f32[4]{0:T(128)S(1)}, f32[4]{0:T(128)S(1)}, u32[]{:S(2)}, u32[]{:S(2)}) %collective-permute-start.16) | collective-permute-done | bytes 48 | tf_op jit(solution)/shard_map/ppermute | solution.py:21
  163.5 2.3 collective-permute-start.18
  165.9 1.9 collective-permute-start.17
  167.8 3.0 %collective-permute-done.18 = f32[4]{0:T(128)S(1)} collective-permute-done((f32[4]{0:T(128)S(1)}, f32[4]{0:T(128)S(1)}, u32[]{:S(2)}, u32[]{:S(2)}) %collective-permute-start.18) | collective-permute-done | bytes 48 | tf_op jit(solution)/shard_map/ppermute | solution.py:21
  170.9 1.9 collective-permute-start.20
  172.8 5.6 %collective-permute-done.20 = f32[4]{0:T(128)S(1)} collective-permute-done((f32[4]{0:T(128)S(1)}, f32[4]{0:T(128)S(1)}, u32[]{:S(2)}, u32[]{:S(2)}) %collective-permute-start.20) | collective-permute-done | bytes 48 | tf_op jit(solution)/shard_map/ppermute | solution.py:21
  178.5 1.9 collective-permute-start.19
  180.5 1.6 fusion.16
  182.4 9.2 %collective-permute-done.19 = f32[4,128,128]{2,1,0:T(8,128)S(1)} collective-permute-done((f32[4,128,128]{2,1,0:T(8,128)S(1)}, f32[4,128,128]{2,1,0:T(8,128)S(1)}, u32[]{:S(2)}, u32[]{:S(2)}) %collective-permute-start.19) | collective-permute-done | bytes 262176 | tf_op jit(solution)/shard_map/ppermute | solution.py:21
  191.6 1.5 collective-permute-start.21
  193.5 2.4 fusion.17
  195.8 8.2 %collective-permute-done.21 = f32[4,128,128]{2,1,0:T(8,128)S(1)} collective-permute-done((f32[4,128,128]{2,1,0:T(8,128)S(1)}, f32[4,128,128]{2,1,0:T(8,128)S(1)}, u32[]{:S(2)}, u32[]{:S(2)}) %collective-permute-start.21) | collective-permute-done | bytes 262176 | tf_op jit(solution)/shard_map/ppermute | solution.py:21
  205.0 8.3 %all-to-all-start = ((f32[8,16,256]{2,1,0:T(8,128)}), f32[8,16,256]{2,1,0:T(8,128)S(1)}, u32[]{:S(2)}, u32[]{:S(2)}) async-start(f32[8,16,256]{2,1,0:T(8,128)} %bitcast.14), calls=%async_computation | async-start | bytes 262144 | tf_op jit(solution)/shard_map/all_to_all | solution.py:78
  213.3 2.0 convolution_bitcast_fusion.2
  215.3 4.6 %all-to-all-done = f32[8,16,256]{2,1,0:T(8,128)S(1)} async-done(((f32[8,16,256]{2,1,0:T(8,128)}), f32[8,16,256]{2,1,0:T(8,128)S(1)}, u32[]{:S(2)}, u32[]{:S(2)}) %all-to-all-start) | async-done | bytes 131104 | tf_op jit(solution)/shard_map/all_to_all | solution.py:78
  219.9 1.4 convolution_bitcast_fusion.3
  221.3 3.3 %all-to-all-start.1 = ((f32[8,16,128]{2,1,0:T(8,128)}), f32[8,16,128]{2,1,0:T(8,128)S(1)}, u32[]{:S(2)}, u32[]{:S(2)}) async-start(f32[8,16,128]{2,1,0:T(8,128)} %convolution_bitcast_fusion.3), calls=%async_computation.1 | async-start | bytes 131072 | tf_op jit(solution)/shard_map/all_to_all | solution.py:78
  226.1 4.9 %all-to-all-done.1 = f32[8,16,128]{2,1,0:T(8,128)S(1)} async-done(((f32[8,16,128]{2,1,0:T(8,128)}), f32[8,16,128]{2,1,0:T(8,128)S(1)}, u32[]{:S(2)}, u32[]{:S(2)}) %all-to-all-start.1) | async-done | bytes 65568 | tf_op jit(solution)/shard_map/all_to_all | solution.py:78
  (101 shorter events, 17.2 us)
Async XLA Ops:
  7.2 88.0 %copy-start = (bf16[128,1024]{1,0:T(8,128)(2,1)S(1)}, bf16[128,1024]{1,0:T(8,128)(2,1)}, u32[]{:S(2)}) copy-start(bf16[128,1024]{1,0:T(8,128)(2,1)} %param.7) | copy-start | bytes 786436
  7.2 88.0 %all-gather.2.cloned.1.call-start = ((), (), s32[]{:S(2)}) async-start(), calls=%async_computation.2 | async-start | bytes 3244032 | tf_op jit(solution)/shard_map/all_gather | solution.py:90
  10.5 4.2 %copy-start.14 = (f32[8]{0:T(128)}, f32[8]{0:T(128)S(1)}, u32[]{:S(2)}) copy-start(f32[8]{0:T(128)S(1)} %slice_bitcast_fusion.12) | copy-start | bytes 100
  10.5 3.1 %collective-permute-start = (f32[8]{0:T(128)S(1)}, f32[8]{0:T(128)S(1)}, u32[]{:S(2)}, u32[]{:S(2)}) collective-permute-start(f32[8]{0:T(128)S(1)} %slice_bitcast_fusion.12), channel_id=1, source_target_pairs={{0,8},{8,0},{16,24},{24,16},{32,40},{40,32},{48,56},{56,48},{64,72... | collective-permute-start | bytes 104 | tf_op jit(solution)/shard_map/ppermute | solution.py:36
  11.8 2.9 %copy-start.9 = (f32[128,8]{0,1:T(8,128)}, f32[128,8]{0,1:T(8,128)S(1)}, u32[]{:S(2)}) copy-start(f32[128,8]{0,1:T(8,128)S(1)} %copy.33) | copy-start | bytes 12292
  13.0 1.7 collective-permute-start.1
  14.8 12.0 %collective-permute-start.2 = (f32[4,128,128]{2,1,0:T(8,128)S(1)}, f32[4,128,128]{2,1,0:T(8,128)S(1)}, u32[]{:S(2)}, u32[]{:S(2)}) collective-permute-start(f32[4,128,128]{2,1,0:T(8,128)S(1)} %select_add_fusion.1), channel_id=1, source_target_pairs={{0,16},{8,24},{16,32},{24,40},{32,48},{40,56},{48,64},{56,72},{64,... | collective-permute-start | bytes 786440 | tf_op jit(solution)/shard_map/ppermute | solution.py:21
  26.8 19.0 %collective-permute-start.4 = (f32[4,128,128]{2,1,0:T(8,128)S(1)}, f32[4,128,128]{2,1,0:T(8,128)S(1)}, u32[]{:S(2)}, u32[]{:S(2)}) collective-permute-start(f32[4,128,128]{2,1,0:T(8,128)S(1)} %collective-permute-done.2), channel_id=1, source_target_pairs={{0,16},{8,24},{16,32},{24,40},{32,48},{40,56},{48,64},{56,72},{64,... | collective-permute-start | bytes 786440 | tf_op jit(solution)/shard_map/ppermute | solution.py:21
  31.5 6.9 %collective-permute-start.3 = (f32[4]{0:T(128)S(1)}, f32[4]{0:T(128)S(1)}, u32[]{:S(2)}, u32[]{:S(2)}) collective-permute-start(f32[4]{0:T(128)S(1)} %get-tuple-element.36), channel_id=1, source_target_pairs={{0,16},{8,24},{16,32},{24,40},{32,48},{40,56},{48,64},{56,72},{64,... | collective-permute-start | bytes 56 | tf_op jit(solution)/shard_map/ppermute | solution.py:21
  38.4 7.4 %collective-permute-start.5 = (f32[4]{0:T(128)S(1)}, f32[4]{0:T(128)S(1)}, u32[]{:S(2)}, u32[]{:S(2)}) collective-permute-start(f32[4]{0:T(128)S(1)} %collective-permute-done.3), channel_id=1, source_target_pairs={{0,16},{8,24},{16,32},{24,40},{32,48},{40,56},{48,64},{56,72},{64,... | collective-permute-start | bytes 56 | tf_op jit(solution)/shard_map/ppermute | solution.py:21
  45.9 11.6 %collective-permute-start.6 = (f32[4,128,128]{2,1,0:T(8,128)S(1)}, f32[4,128,128]{2,1,0:T(8,128)S(1)}, u32[]{:S(2)}, u32[]{:S(2)}) collective-permute-start(f32[4,128,128]{2,1,0:T(8,128)S(1)} %multiply_add_fusion.9), channel_id=1, source_target_pairs={{0,32},{8,40},{16,48},{24,56},{32,64},{40,72},{48,80},{56,88},{64,... | collective-permute-start | bytes 786440 | tf_op jit(solution)/shard_map/ppermute | solution.py:21
  55.7 35.7 %copy-start.8 = (f32[128,128]{1,0:T(8,128)}, f32[128,128]{1,0:T(8,128)S(1)}, u32[]{:S(2)}) copy-start(f32[128,128]{1,0:T(8,128)S(1)} %convolution_multiply_fusion.2) | copy-start | bytes 196612
  57.6 18.1 %collective-permute-start.8 = (f32[4,128,128]{2,1,0:T(8,128)S(1)}, f32[4,128,128]{2,1,0:T(8,128)S(1)}, u32[]{:S(2)}, u32[]{:S(2)}) collective-permute-start(f32[4,128,128]{2,1,0:T(8,128)S(1)} %multiply_add_fusion.8), channel_id=1, source_target_pairs={{0,64},{8,72},{16,80},{24,88},{32,96},{40,104},{48,112},{56,120},{... | collective-permute-start | bytes 786440 | tf_op jit(solution)/shard_map/ppermute | solution.py:21
  63.5 27.8 %copy-start.11 = (f32[8,128]{1,0:T(8,128)}, f32[8,128]{1,0:T(8,128)S(1)}, u32[]{:S(2)}) copy-start(f32[8,128]{1,0:T(8,128)S(1)} %copy.29) | copy-start | bytes 12292
  63.5 12.2 %collective-permute-start.7 = (f32[4]{0:T(128)S(1)}, f32[4]{0:T(128)S(1)}, u32[]{:S(2)}, u32[]{:S(2)}) collective-permute-start(f32[4]{0:T(128)S(1)} %get-tuple-element.16), channel_id=1, source_target_pairs={{0,32},{8,40},{16,48},{24,56},{32,64},{40,72},{48,80},{56,88},{64,... | collective-permute-start | bytes 56 | tf_op jit(solution)/shard_map/ppermute | solution.py:21
  75.8 14.6 %collective-permute-start.10 = (f32[4,128,128]{2,1,0:T(8,128)S(1)}, f32[4,128,128]{2,1,0:T(8,128)S(1)}, u32[]{:S(2)}, u32[]{:S(2)}) collective-permute-start(f32[4,128,128]{2,1,0:T(8,128)S(1)} %multiply_add_fusion.7), channel_id=1, source_target_pairs={{0,128},{8,136},{16,144},{24,152},{32,160},{40,168},{48,176},{56,1... | collective-permute-start | bytes 786440 | tf_op jit(solution)/shard_map/ppermute | solution.py:21
  81.8 8.6 %collective-permute-start.9 = (f32[4]{0:T(128)S(1)}, f32[4]{0:T(128)S(1)}, u32[]{:S(2)}, u32[]{:S(2)}) collective-permute-start(f32[4]{0:T(128)S(1)} %get-tuple-element.14), channel_id=1, source_target_pairs={{0,64},{8,72},{16,80},{24,88},{32,96},{40,104},{48,112},{56,120},{... | collective-permute-start | bytes 56 | tf_op jit(solution)/shard_map/ppermute | solution.py:21
  91.3 31.9 %collective-permute-start.11 = (f32[4,128,128]{2,1,0:T(8,128)}, f32[4,128,128]{2,1,0:T(8,128)}, u32[]{:S(2)}, u32[]{:S(2)}) collective-permute-start(f32[4,128,128]{2,1,0:T(8,128)} %get-tuple-element.20), channel_id=1, source_target_pairs={{0,8},{8,0},{16,24},{24,16},{32,40},{40,32},{48,56},{56,48},{64,72... | collective-permute-start | bytes 786440 | tf_op jit(solution)/shard_map/ppermute | solution.py:64
  95.1 12.6 %copy-start.2 = (bf16[4096,384]{1,0:T(8,128)(2,1)S(1)}, bf16[4096,384]{1,0:T(8,128)(2,1)}, u32[]{:S(2)}) copy-start(bf16[4096,384]{1,0:T(8,128)(2,1)} %all-gather.2.cloned.1.call-done) | copy-start | bytes 9437188
  107.8 10.5 %copy-start.1 = (f32[128,8,4096]{0,2,1:T(8,128)S(1)}, f32[128,8,4096]{0,2,1:T(8,128)}, u32[]{:S(2)}) copy-start(f32[128,8,4096]{0,2,1:T(8,128)} %get-tuple-element.40) | copy-start | bytes 50331652
  107.8 13.0 %copy-start.13 = (f32[128,8]{0,1:T(8,128)S(1)}, f32[128,8]{0,1:T(8,128)}, u32[]{:S(2)}) copy-start(f32[128,8]{0,1:T(8,128)} %get-tuple-element.39) | copy-start | bytes 12292
  118.3 4.9 %copy-start.4 = (f32[4,128,128]{2,1,0:T(8,128)S(1)}, f32[4,128,128]{2,1,0:T(8,128)}, u32[]{:S(2)}) copy-start(f32[4,128,128]{2,1,0:T(8,128)} %get-tuple-element.19) | copy-start | bytes 786436
  118.3 4.9 %copy-start.5 = (bf16[128,128]{1,0:T(8,128)(2,1)S(1)}, bf16[128,128]{1,0:T(8,128)(2,1)}, u32[]{:S(2)}) copy-start(bf16[128,128]{1,0:T(8,128)(2,1)} %param.12) | copy-start | bytes 98308
  118.3 4.9 %copy-start.6 = (f32[128,8,128]{2,0,1:T(8,128)S(1)}, f32[128,8,128]{2,0,1:T(8,128)}, u32[]{:S(2)}) copy-start(f32[128,8,128]{2,0,1:T(8,128)} %convolution_bitcast_fusion.1) | copy-start | bytes 1572868
  118.3 4.9 %copy-start.12 = (f32[128,8]{0,1:T(8,128)S(1)}, f32[128,8]{0,1:T(8,128)}, u32[]{:S(2)}) copy-start(f32[128,8]{0,1:T(8,128)} %copy.34) | copy-start | bytes 12292
  118.3 8.1 %copy-start.16 = (f32[8]{0:T(128)S(1)}, f32[8]{0:T(128)}, u32[]{:S(2)}) copy-start(f32[8]{0:T(128)} %get-tuple-element.21) | copy-start | bytes 100
  118.3 8.1 %copy-start.17 = (f32[8]{0:T(128)S(1)}, f32[8]{0:T(128)}, u32[]{:S(2)}) copy-start(f32[8]{0:T(128)} %get-tuple-element.22) | copy-start | bytes 100
  118.3 17.2 %copy-start.3 = (bf16[128,1024]{1,0:T(8,128)(2,1)S(1)}, bf16[128,1024]{1,0:T(8,128)(2,1)}, u32[]{:S(2)}) copy-start(bf16[128,1024]{1,0:T(8,128)(2,1)} %param.10) | copy-start | bytes 786436
  120.7 26.7 %copy-start.15 = (f32[8]{0:T(128)S(1)}, f32[8]{0:T(128)}, u32[]{:S(2)}) copy-start(f32[8]{0:T(128)} %copy-done.14) | copy-start | bytes 100
  120.7 61.4 %copy-start.7 = (bf16[128,128]{1,0:T(8,128)(2,1)S(1)}, bf16[128,128]{1,0:T(8,128)(2,1)}, u32[]{:S(2)}) copy-start(bf16[128,128]{1,0:T(8,128)(2,1)} %param.11) | copy-start | bytes 98308
  123.2 101.5 %copy-start.10 = (f32[128,8]{0,1:T(8,128)S(1)}, f32[128,8]{0,1:T(8,128)}, u32[]{:S(2)}) copy-start(f32[128,8]{0,1:T(8,128)} %copy-done.9) | copy-start | bytes 12292
  126.1 1.6 collective-permute-start.12
  127.8 15.6 %collective-permute-start.13 = (f32[4,128,128]{2,1,0:T(8,128)S(1)}, f32[4,128,128]{2,1,0:T(8,128)S(1)}, u32[]{:S(2)}, u32[]{:S(2)}) collective-permute-start(f32[4,128,128]{2,1,0:T(8,128)S(1)} %select_add_fusion), channel_id=1, source_target_pairs={{16,0},{24,8},{32,16},{40,24},{48,32},{56,40},{64,48},{72,56},{80,... | collective-permute-start | bytes 786440 | tf_op jit(solution)/shard_map/ppermute | solution.py:21
  143.4 22.4 %collective-permute-start.15 = (f32[4,128,128]{2,1,0:T(8,128)S(1)}, f32[4,128,128]{2,1,0:T(8,128)S(1)}, u32[]{:S(2)}, u32[]{:S(2)}) collective-permute-start(f32[4,128,128]{2,1,0:T(8,128)S(1)} %collective-permute-done.13), channel_id=1, source_target_pairs={{16,0},{24,8},{32,16},{40,24},{48,32},{56,40},{64,48},{72,56},{80,... | collective-permute-start | bytes 786440 | tf_op jit(solution)/shard_map/ppermute | solution.py:21
  147.6 8.1 %collective-permute-start.14 = (f32[4]{0:T(128)S(1)}, f32[4]{0:T(128)S(1)}, u32[]{:S(2)}, u32[]{:S(2)}) collective-permute-start(f32[4]{0:T(128)S(1)} %get-tuple-element.32), channel_id=1, source_target_pairs={{16,0},{24,8},{32,16},{40,24},{48,32},{56,40},{64,48},{72,56},{80,... | collective-permute-start | bytes 56 | tf_op jit(solution)/shard_map/ppermute | solution.py:21
  155.7 7.8 %collective-permute-start.16 = (f32[4]{0:T(128)S(1)}, f32[4]{0:T(128)S(1)}, u32[]{:S(2)}, u32[]{:S(2)}) collective-permute-start(f32[4]{0:T(128)S(1)} %collective-permute-done.14), channel_id=1, source_target_pairs={{16,0},{24,8},{32,16},{40,24},{48,32},{56,40},{64,48},{72,56},{80,... | collective-permute-start | bytes 56 | tf_op jit(solution)/shard_map/ppermute | solution.py:21
  163.5 7.3 %collective-permute-start.18 = (f32[4]{0:T(128)S(1)}, f32[4]{0:T(128)S(1)}, u32[]{:S(2)}, u32[]{:S(2)}) collective-permute-start(f32[4]{0:T(128)S(1)} %get-tuple-element.12), channel_id=1, source_target_pairs={{32,0},{40,8},{48,16},{56,24},{64,32},{72,40},{80,48},{88,56},{96,... | collective-permute-start | bytes 56 | tf_op jit(solution)/shard_map/ppermute | solution.py:21
  165.9 12.5 %collective-permute-start.17 = (f32[4,128,128]{2,1,0:T(8,128)S(1)}, f32[4,128,128]{2,1,0:T(8,128)S(1)}, u32[]{:S(2)}, u32[]{:S(2)}) collective-permute-start(f32[4,128,128]{2,1,0:T(8,128)S(1)} %multiply_add_fusion.4), channel_id=1, source_target_pairs={{32,0},{40,8},{48,16},{56,24},{64,32},{72,40},{80,48},{88,56},{96,... | collective-permute-start | bytes 786440 | tf_op jit(solution)/shard_map/ppermute | solution.py:21
  170.9 7.5 %collective-permute-start.20 = (f32[4]{0:T(128)S(1)}, f32[4]{0:T(128)S(1)}, u32[]{:S(2)}, u32[]{:S(2)}) collective-permute-start(f32[4]{0:T(128)S(1)} %get-tuple-element.10), channel_id=1, source_target_pairs={{64,0},{72,8},{80,16},{88,24},{96,32},{104,40},{112,48},{120,56},{... | collective-permute-start | bytes 56 | tf_op jit(solution)/shard_map/ppermute | solution.py:21
  178.5 13.0 %collective-permute-start.19 = (f32[4,128,128]{2,1,0:T(8,128)S(1)}, f32[4,128,128]{2,1,0:T(8,128)S(1)}, u32[]{:S(2)}, u32[]{:S(2)}) collective-permute-start(f32[4,128,128]{2,1,0:T(8,128)S(1)} %multiply_add_fusion.3), channel_id=1, source_target_pairs={{64,0},{72,8},{80,16},{88,24},{96,32},{104,40},{112,48},{120,56},{... | collective-permute-start | bytes 786440 | tf_op jit(solution)/shard_map/ppermute | solution.py:21
  191.6 12.4 %collective-permute-start.21 = (f32[4,128,128]{2,1,0:T(8,128)S(1)}, f32[4,128,128]{2,1,0:T(8,128)S(1)}, u32[]{:S(2)}, u32[]{:S(2)}) collective-permute-start(f32[4,128,128]{2,1,0:T(8,128)S(1)} %multiply_add_fusion.2), channel_id=1, source_target_pairs={{128,0},{136,8},{144,16},{152,24},{160,32},{168,40},{176,48},{184,... | collective-permute-start | bytes 786440 | tf_op jit(solution)/shard_map/ppermute | solution.py:21
  204.1 15.8 %collective-permute-start.22 = (f32[4,128,128]{2,1,0:T(8,128)S(1)}, f32[4,128,128]{2,1,0:T(8,128)S(1)}, u32[]{:S(2)}, u32[]{:S(2)}) collective-permute-start(f32[4,128,128]{2,1,0:T(8,128)S(1)} %get-tuple-element.18), channel_id=1, source_target_pairs={{0,8},{8,0},{16,24},{24,16},{32,40},{40,32},{48,56},{56,48},{64,72... | collective-permute-start | bytes 786440 | tf_op jit(solution)/shard_map/ppermute | solution.py:64
  205.0 14.9 %all-to-all-start = ((f32[8,16,256]{2,1,0:T(8,128)}), f32[8,16,256]{2,1,0:T(8,128)S(1)}, u32[]{:S(2)}, u32[]{:S(2)}) async-start(f32[8,16,256]{2,1,0:T(8,128)} %bitcast.14), calls=%async_computation | async-start | bytes 262144 | tf_op jit(solution)/shard_map/all_to_all | solution.py:78
  221.3 9.6 %all-to-all-start.1 = ((f32[8,16,128]{2,1,0:T(8,128)}), f32[8,16,128]{2,1,0:T(8,128)S(1)}, u32[]{:S(2)}, u32[]{:S(2)}) async-start(f32[8,16,128]{2,1,0:T(8,128)} %convolution_bitcast_fusion.3), calls=%async_computation.1 | async-start | bytes 131072 | tf_op jit(solution)/shard_map/all_to_all | solution.py:78
Sparse Core Ops, SparseCore 0:
  10.8 84.2 all-gather.1

commit v4 on v3

--- a/solution.py
+++ b/solution.py
@@ -1,8 +1,11 @@
+import functools
 import math
 
 import jax
 import jax.numpy as jnp
 from jax import lax
+from jax.experimental import pallas as pl
+from jax.experimental.pallas import tpu as pltpu
 from jax.sharding import PartitionSpec as P
 
 HEAD_WIDTH = 128
@@ -78,6 +81,81 @@
     return jnp.sum(lax.all_to_all(blocks, axis, 0, 0), axis=0)
 
 
+def attend_kernel(first_ref, query_ref, key_ref, upper_ref, lower_ref, out_ref, top_ref, total_ref, mix_ref, *, heads):
+    block = pl.program_id(0)
+    rows = query_ref.shape[0]
+    width = query_ref.shape[1]
+    keys_per_block = key_ref.shape[0]
+    first = first_ref[0]
+
+    @pl.when(block == 0)
+    def _():
+        top_ref[...] = jnp.full(top_ref.shape, very_negative, jnp.float32)
+        total_ref[...] = jnp.zeros(total_ref.shape, jnp.float32)
+        mix_ref[...] = jnp.zeros(mix_ref.shape, jnp.float32)
+
+    @pl.when(block * keys_per_block <= first + rows // heads - 1)
+    def _():
+        scores = lax.dot_general(
+            query_ref[...], key_ref[...], (((1,), (1,)), ((), ())), preferred_element_type=jnp.float32
+        ) / math.sqrt(width)
+        row = lax.broadcasted_iota(jnp.int32, scores.shape, 0)
+        col = lax.broadcasted_iota(jnp.int32, scores.shape, 1)
+        allowed = block * keys_per_block + col <= first + row // heads
+        scores = jnp.where(allowed, scores, very_negative)
+        top_old = top_ref[...]
+        top_new = jnp.maximum(top_old, jnp.max(scores, axis=1, keepdims=True))
+        rescale = jnp.exp(top_old - top_new)
+        weights = jnp.where(allowed, jnp.exp(scores - top_new), 0.0)
+        total_ref[...] = rescale * total_ref[...] + jnp.sum(weights, axis=1, keepdims=True)
+        weights_hi = weights.astype(jnp.bfloat16)
+        weights_lo = (weights - weights_hi.astype(jnp.float32)).astype(jnp.bfloat16)
+        upper = upper_ref[...]
+        mixed = (
+            jnp.dot(weights_hi, upper, preferred_element_type=jnp.float32)
+            + jnp.dot(weights_hi, lower_ref[...], preferred_element_type=jnp.float32)
+            + jnp.dot(weights_lo, upper, preferred_element_type=jnp.float32)
+        )
+        mix_ref[...] = rescale * mix_ref[...] + mixed
+        top_ref[...] = top_new
+
+    @pl.when(block == pl.num_programs(0) - 1)
+    def _():
+        out_ref[...] = mix_ref[...] / total_ref[...]
+
+
+def attend(first_query, query_rows, every, heads, keys_per_block=512):
+    rows, width = query_rows.shape
+    blocks = every.shape[0] // keys_per_block
+    flops = 2 * rows * every.shape[0] * width * 4
+    return pl.pallas_call(
+        functools.partial(attend_kernel, heads=heads),
+        out_shape=jax.ShapeDtypeStruct((rows, width), jnp.float32),
+        grid_spec=pltpu.PrefetchScalarGridSpec(
+            num_scalar_prefetch=1,
+            grid=(blocks,),
+            in_specs=[
+                pl.BlockSpec((rows, width), lambda b, f: (0, 0)),
+                pl.BlockSpec((keys_per_block, width), lambda b, f: (b, 0)),
+                pl.BlockSpec((keys_per_block, width), lambda b, f: (b, 1)),
+                pl.BlockSpec((keys_per_block, width), lambda b, f: (b, 2)),
+            ],
+            out_specs=pl.BlockSpec((rows, width), lambda b, f: (0, 0)),
+            scratch_shapes=[
+                pltpu.VMEM((rows, 1), jnp.float32),
+                pltpu.VMEM((rows, 1), jnp.float32),
+                pltpu.VMEM((rows, width), jnp.float32),
+            ],
+        ),
+        compiler_params=pltpu.CompilerParams(dimension_semantics=("arbitrary",)),
+        cost_estimate=pl.CostEstimate(
+            flops=flops,
+            transcendentals=rows * every.shape[0],
+            bytes_accessed=every.size * 2 + query_rows.size * 2 + rows * width * 4,
+        ),
+    )(first_query, query_rows, every, every, every)
+
+
 def local(queries, keys, values, inputs_x, in_b, in_c, log_decay):
     row_count = queries.shape[0]
     heads = queries.shape[1] // HEAD_WIDTH
@@ -88,9 +166,6 @@
     values_hi, values_lo = split_bf16(values)
     packed = jnp.concatenate([keys, values_hi, values_lo], axis=1)
     every = lax.all_gather(packed, "seq", axis=0, tiled=True)
-    every_key = every[:, :HEAD_WIDTH]
-    every_hi = every[:, HEAD_WIDTH:2 * HEAD_WIDTH]
-    every_lo = every[:, 2 * HEAD_WIDTH:]
 
     c_scale = 0.5 / math.sqrt(N * row_count * seq_count)
     student_x = inputs_x.astype(jnp.float32).reshape(row_count, heads, HEAD_WIDTH)
@@ -112,24 +187,10 @@
     )
     state_in = exclusive_scan(local_state, totals, "seq", True)
 
-    query_rows = queries.reshape(row_count, heads, HEAD_WIDTH)
-    scores = jnp.einsum(
-        "qgd,nd->qgn", query_rows, every_key, preferred_element_type=jnp.float32
-    ) / math.sqrt(HEAD_WIDTH)
-    query_pos = first_query + jnp.arange(row_count, dtype=jnp.int32)
-    key_pos = jnp.arange(every.shape[0], dtype=jnp.int32)
-    allowed = (key_pos[None, :] <= query_pos[:, None])[:, None, :]
-    scores = jnp.where(allowed, scores, very_negative)
-    row_top = jnp.max(scores, axis=-1, keepdims=True)
-    weights = jnp.where(allowed, jnp.exp(scores - row_top), 0.0)
-    denominator = jnp.sum(weights, axis=-1)
-    weights_hi, weights_lo = split_bf16(weights)
-    mixture = (
-        jnp.einsum("qgn,nd->qgd", weights_hi, every_hi, preferred_element_type=jnp.float32)
-        + jnp.einsum("qgn,nd->qgd", weights_hi, every_lo, preferred_element_type=jnp.float32)
-        + jnp.einsum("qgn,nd->qgd", weights_lo, every_hi, preferred_element_type=jnp.float32)
-    )
-    teacher_out = mixture / denominator[..., None]
+    query_rows = queries.reshape(row_count * heads, HEAD_WIDTH)
+    teacher_out = attend(
+        jnp.reshape(first_query, (1,)).astype(jnp.int32), query_rows, every, heads
+    ).reshape(row_count, heads, HEAD_WIDTH)
 
     y_intra = jnp.einsum("hts,shp->thp", mixing, student_x, precision=highest)
     y_inter = jnp.einsum("tn,hpn->thp", c_rows, state_in, precision=highest) * rising[:, :, None]
@@ -145,14 +206,13 @@
     products = jnp.einsum("thp,shp->hts", mismatch, student_x, precision=highest)
     weighted = decays * products
     grad_b = jnp.einsum("hts,tn->sn", weighted, c_rows, precision=highest)
+    grad_b = grad_b + jnp.einsum(
+        "shp,hpn->sn", student_x * ending[:, :, None], later_grad, precision=highest
+    )
     grad_c = jnp.einsum("hts,sn->tn", weighted, b_rows, precision=highest)
     grad_c = grad_c + jnp.einsum("thp,hpn->tn", scaled_mismatch, state_in, precision=highest)
-    early = mp_sum_scatter(jnp.concatenate([grad_b, grad_c], axis=1), "mp")
-    grad_b_later = jnp.einsum(
-        "shp,hpn->sn", student_x * ending[:, :, None], later_grad, precision=highest
-    )
-    summed_b = early[:, :N] + mp_sum_scatter(grad_b_later, "mp")
-    summed_c = early[:, N:]
+    summed = mp_sum_scatter(jnp.concatenate([grad_b, grad_c], axis=1), "mp")
+    summed_b, summed_c = summed[:, :N], summed[:, N:]
     return (grad_x.reshape(row_count, heads * HEAD_WIDTH), summed_b, summed_c * c_scale)
 
 

time: 241 us -> 219 us (0.909)
  matrix products: 41.1 us -> 8.75 us
  waiting for transfers between devices: 87 us -> 98.7 us
  Pallas kernels: 0 us -> 10.9 us
  starting transfers between devices: 81.8 us -> 72.8 us
  other arithmetic: 6.91 us -> 4.31 us
    dot_general x3 -> x0, matrix products: 13.1 us -> none  [the longest x1 8.28 us: local(): jnp.einsum('qgn,nd->qgd', weights_lo, every_hi, preferred_element_type=jn...]
    sub x1 -> x0, matrix products: 12.6 us -> none  [local(): weights = jnp.where(allowed, jnp.exp(scores - row_top), 0.0)]
    ppermute x18, waiting for transfers between devices: 72 us -> 83.4 us  [shift(): return lax.ppermute(value, axis, perm)]
    pallas_call x0 -> x1, Pallas kernels: none -> 10.9 us  [attend(): pl.pallas_call(functools.partial(attend_kernel, heads=heads), out_shape=j...]
    all_to_all x2 -> x1, starting transfers between devices: 11.6 us -> 4.47 us  [mp_sum_scatter(): return jnp.sum(lax.all_to_all(blocks, axis, 0, 0), axis=0)]
    all_to_all x2 -> x1, waiting for transfers between devices: 9.44 us -> 5.19 us  [mp_sum_scatter(): return jnp.sum(lax.all_to_all(blocks, axis, 0, 0), axis=0)]
    all_gather x1, waiting for transfers between devices: 3.78 us -> 7.7 us  [local(): every = lax.all_gather(packed, 'seq', axis=0, tiled=True)]
  transfers between devices with their start and end apart: 26 -> 25, of which waited for: 18 -> 17; matrix products, arithmetic and copies ran while one was open for 19% -> 5% of each run, Pallas kernels for 0% -> 5%
where the time goes in v4:
time: 219 us; the launch traced here: 215 us
  waiting for transfers between devices  98.7 us (45%)
  starting transfers between devices  72.8 us (33%)
  between operations  14.4 us (7%)
  Pallas kernels  10.9 us (5%)
  matrix products  8.75 us (4%)
  local copies, waits for them, and re-layouts  4.77 us (2%)
  other arithmetic  4.31 us (2%)
    ppermute x18, waiting for transfers between devices, shift(): return lax.ppermute(value, axis, perm)  83.4 us
    ppermute x18, starting transfers between devices, shift(): return lax.ppermute(value, axis, perm)  67 us
    pallas_call x1, Pallas kernels, attend(): pl.pallas_call(functools.partial(attend_kernel, heads=heads), out_shape=j...  10.9 us
    all_gather x1, waiting for transfers between devices, local(): every = lax.all_gather(packed, 'seq', axis=0, tiled=True)  7.7 us
    all_to_all x1, waiting for transfers between devices, mp_sum_scatter(): return jnp.sum(lax.all_to_all(blocks, axis, 0, 0), axis=0)  5.19 us
    all_to_all x1, starting transfers between devices, mp_sum_scatter(): return jnp.sum(lax.all_to_all(blocks, axis, 0, 0), axis=0)  4.47 us
  transfers between devices with their start and end apart: 25, of which 17 were waited for; matrix products, arithmetic and copies ran while one was open for 5% of the time, Pallas kernels for 5%

profile of v4, /device:TPU:68, one launch (start us, length us, event | category | flops | bytes accessed | tf_op | source)
XLA Modules:
  0.0 214.7 jit_solution(7955606966258459818)
XLA Ops:
  7.2 0.9 reduce-precision_convert_fusion
  8.1 1.4 pad_maximum_fusion.1
  9.5 0.8 copy.25
  10.7 1.2 copy.28
  13.0 1.1 collective-permute-done.1
  14.1 3.8 %collective-permute-start.2 = (f32[4,128,128]{2,1,0:T(8,128)S(1)}, f32[4,128,128]{2,1,0:T(8,128)S(1)}, u32[]{:S(2)}, u32[]{:S(2)}) collective-permute-start(f32[4,128,128]{2,1,0:T(8,128)S(1)} %select_add_fusion.1), channel_id=1, source_target_pairs={{0,16},{8,24},{16,32},{24,40},{32,48},{40,56},{48,64},{56,72},{64,... | collective-permute-start | bytes 786440 | tf_op jit(solution)/shard_map/ppermute | solution.py:24
  17.9 8.2 %collective-permute-done.2 = f32[4,128,128]{2,1,0:T(8,128)S(1)} collective-permute-done((f32[4,128,128]{2,1,0:T(8,128)S(1)}, f32[4,128,128]{2,1,0:T(8,128)S(1)}, u32[]{:S(2)}, u32[]{:S(2)}) %collective-permute-start.2) | collective-permute-done | bytes 262176 | tf_op jit(solution)/shard_map/ppermute | solution.py:24
  26.1 4.7 %collective-permute-start.4 = (f32[4,128,128]{2,1,0:T(8,128)S(1)}, f32[4,128,128]{2,1,0:T(8,128)S(1)}, u32[]{:S(2)}, u32[]{:S(2)}) collective-permute-start(f32[4,128,128]{2,1,0:T(8,128)S(1)} %collective-permute-done.2), channel_id=1, source_target_pairs={{0,16},{8,24},{16,32},{24,40},{32,48},{40,56},{48,64},{56,72},{64,... | collective-permute-start | bytes 786440 | tf_op jit(solution)/shard_map/ppermute | solution.py:24
  30.8 4.0 %collective-permute-start.3 = (f32[4]{0:T(128)S(1)}, f32[4]{0:T(128)S(1)}, u32[]{:S(2)}, u32[]{:S(2)}) collective-permute-start(f32[4]{0:T(128)S(1)} %get-tuple-element.36), channel_id=1, source_target_pairs={{0,16},{8,24},{16,32},{24,40},{32,48},{40,56},{48,64},{56,72},{64,... | collective-permute-start | bytes 56 | tf_op jit(solution)/shard_map/ppermute | solution.py:24
  34.8 2.9 %collective-permute-done.3 = f32[4]{0:T(128)S(1)} collective-permute-done((f32[4]{0:T(128)S(1)}, f32[4]{0:T(128)S(1)}, u32[]{:S(2)}, u32[]{:S(2)}) %collective-permute-start.3) | collective-permute-done | bytes 48 | tf_op jit(solution)/shard_map/ppermute | solution.py:24
  37.7 6.2 %collective-permute-start.5 = (f32[4]{0:T(128)S(1)}, f32[4]{0:T(128)S(1)}, u32[]{:S(2)}, u32[]{:S(2)}) collective-permute-start(f32[4]{0:T(128)S(1)} %collective-permute-done.3), channel_id=1, source_target_pairs={{0,16},{8,24},{16,32},{24,40},{32,48},{40,56},{48,64},{56,72},{64,... | collective-permute-start | bytes 56 | tf_op jit(solution)/shard_map/ppermute | solution.py:24
  43.9 1.3 collective-permute-done.5
  45.3 7.6 %collective-permute-start.6 = (f32[4,128,128]{2,1,0:T(8,128)S(1)}, f32[4,128,128]{2,1,0:T(8,128)S(1)}, u32[]{:S(2)}, u32[]{:S(2)}) collective-permute-start(f32[4,128,128]{2,1,0:T(8,128)S(1)} %multiply_add_fusion.9), channel_id=1, source_target_pairs={{0,32},{8,40},{16,48},{24,56},{32,64},{40,72},{48,80},{56,88},{64,... | collective-permute-start | bytes 786440 | tf_op jit(solution)/shard_map/ppermute | solution.py:24
  53.0 3.7 %collective-permute-done.6 = f32[4,128,128]{2,1,0:T(8,128)S(1)} collective-permute-done((f32[4,128,128]{2,1,0:T(8,128)S(1)}, f32[4,128,128]{2,1,0:T(8,128)S(1)}, u32[]{:S(2)}, u32[]{:S(2)}) %collective-permute-start.6) | collective-permute-done | bytes 262176 | tf_op jit(solution)/shard_map/ppermute | solution.py:24
  56.8 5.8 %collective-permute-start.8 = (f32[4,128,128]{2,1,0:T(8,128)S(1)}, f32[4,128,128]{2,1,0:T(8,128)S(1)}, u32[]{:S(2)}, u32[]{:S(2)}) collective-permute-start(f32[4,128,128]{2,1,0:T(8,128)S(1)} %multiply_add_fusion.8), channel_id=1, source_target_pairs={{0,64},{8,72},{16,80},{24,88},{32,96},{40,104},{48,112},{56,120},{... | collective-permute-start | bytes 786440 | tf_op jit(solution)/shard_map/ppermute | solution.py:24
  62.8 1.9 collective-permute-start.7
  64.7 8.0 %collective-permute-done.7 = f32[4]{0:T(128)S(1)} collective-permute-done((f32[4]{0:T(128)S(1)}, f32[4]{0:T(128)S(1)}, u32[]{:S(2)}, u32[]{:S(2)}) %collective-permute-start.7) | collective-permute-done | bytes 48 | tf_op jit(solution)/shard_map/ppermute | solution.py:24
  72.8 4.6 %collective-permute-start.10 = (f32[4,128,128]{2,1,0:T(8,128)S(1)}, f32[4,128,128]{2,1,0:T(8,128)S(1)}, u32[]{:S(2)}, u32[]{:S(2)}) collective-permute-start(f32[4,128,128]{2,1,0:T(8,128)S(1)} %multiply_add_fusion.7), channel_id=1, source_target_pairs={{0,128},{8,136},{16,144},{24,152},{32,160},{40,168},{48,176},{56,1... | collective-permute-start | bytes 786440 | tf_op jit(solution)/shard_map/ppermute | solution.py:24
  78.1 0.8 reshape.77.query_ref
  79.0 3.1 %collective-permute-start.9 = (f32[4]{0:T(128)S(1)}, f32[4]{0:T(128)S(1)}, u32[]{:S(2)}, u32[]{:S(2)}) collective-permute-start(f32[4]{0:T(128)S(1)} %get-tuple-element.14), channel_id=1, source_target_pairs={{0,64},{8,72},{16,80},{24,88},{32,96},{40,104},{48,112},{56,120},{... | collective-permute-start | bytes 56 | tf_op jit(solution)/shard_map/ppermute | solution.py:24
  82.1 7.3 %collective-permute-done.9 = f32[4]{0:T(128)S(1)} collective-permute-done((f32[4]{0:T(128)S(1)}, f32[4]{0:T(128)S(1)}, u32[]{:S(2)}, u32[]{:S(2)}) %collective-permute-start.9) | collective-permute-done | bytes 48 | tf_op jit(solution)/shard_map/ppermute | solution.py:24
  89.6 7.7 %all-gather.2.cloned.1.call-done.key_ref.upper_ref.lower_ref = bf16[4096,384]{1,0:T(8,128)(2,1)} async-done(((bf16[128,384]{1,0:T(8,128)(2,1)}), bf16[4096,384]{1,0:T(8,128)(2,1)}) %all-gather.2.cloned.1.call-update) | async-done | bytes 3145744 | tf_op jit(solution)/shard_map/all_gather | solution.py:168
  97.3 10.9 %shard_map.94 = f32[1024,128]{1,0:T(8,128)} custom-call(s32[1]{0:T(128)} %bitcast.6.first_ref, bf16[1024,128]{1,0:T(8,128)(2,1)} %reshape.77.query_ref, bf16[4096,384]{1,0:T(8,128)(2,1)} %all-gather.2.cloned.1.call-done.key_ref.upper_ref.lower_ref, bf16[4096,384]{1,0:T(8,128)(2,1)} %all-gather.2.cloned.1.call-done.key_ref.upper_ref.lower_ref, ...), custom_call_target="tpu_custom_call" | custom-call | flops 4294967296 | bytes 3932160 | tf_op jit(solution)/shard_map/pallas_call | solution.py:131
  108.3 1.7 fusion.3
  110.0 1.1 fusion.12
  111.6 1.2 collective-permute-done.12
  112.9 8.0 %collective-permute-start.13 = (f32[4,128,128]{2,1,0:T(8,128)S(1)}, f32[4,128,128]{2,1,0:T(8,128)S(1)}, u32[]{:S(2)}, u32[]{:S(2)}) collective-permute-start(f32[4,128,128]{2,1,0:T(8,128)S(1)} %select_add_fusion), channel_id=1, source_target_pairs={{16,0},{24,8},{32,16},{40,24},{48,32},{56,40},{64,48},{72,56},{80,... | collective-permute-start | bytes 786440 | tf_op jit(solution)/shard_map/ppermute | solution.py:24
  120.9 8.6 %collective-permute-done.13 = f32[4,128,128]{2,1,0:T(8,128)S(1)} collective-permute-done((f32[4,128,128]{2,1,0:T(8,128)S(1)}, f32[4,128,128]{2,1,0:T(8,128)S(1)}, u32[]{:S(2)}, u32[]{:S(2)}) %collective-permute-start.13) | collective-permute-done | bytes 262176 | tf_op jit(solution)/shard_map/ppermute | solution.py:24
  129.6 3.2 %collective-permute-start.15 = (f32[4,128,128]{2,1,0:T(8,128)S(1)}, f32[4,128,128]{2,1,0:T(8,128)S(1)}, u32[]{:S(2)}, u32[]{:S(2)}) collective-permute-start(f32[4,128,128]{2,1,0:T(8,128)S(1)} %collective-permute-done.13), channel_id=1, source_target_pairs={{16,0},{24,8},{32,16},{40,24},{48,32},{56,40},{64,48},{72,56},{80,... | collective-permute-start | bytes 786440 | tf_op jit(solution)/shard_map/ppermute | solution.py:24
  132.8 3.1 %collective-permute-start.14 = (f32[4]{0:T(128)S(1)}, f32[4]{0:T(128)S(1)}, u32[]{:S(2)}, u32[]{:S(2)}) collective-permute-start(f32[4]{0:T(128)S(1)} %get-tuple-element.32), channel_id=1, source_target_pairs={{16,0},{24,8},{32,16},{40,24},{48,32},{56,40},{64,48},{72,56},{80,... | collective-permute-start | bytes 56 | tf_op jit(solution)/shard_map/ppermute | solution.py:24
  135.9 6.0 %collective-permute-done.14 = f32[4]{0:T(128)S(1)} collective-permute-done((f32[4]{0:T(128)S(1)}, f32[4]{0:T(128)S(1)}, u32[]{:S(2)}, u32[]{:S(2)}) %collective-permute-start.14) | collective-permute-done | bytes 48 | tf_op jit(solution)/shard_map/ppermute | solution.py:24
  141.9 2.0 collective-permute-start.16
  143.9 5.8 %collective-permute-done.16 = f32[4]{0:T(128)S(1)} collective-permute-done((f32[4]{0:T(128)S(1)}, f32[4]{0:T(128)S(1)}, u32[]{:S(2)}, u32[]{:S(2)}) %collective-permute-start.16) | collective-permute-done | bytes 48 | tf_op jit(solution)/shard_map/ppermute | solution.py:24
  149.8 1.9 collective-permute-start.17
  151.7 1.9 collective-permute-start.18
  153.7 8.6 %collective-permute-done.18 = f32[4]{0:T(128)S(1)} collective-permute-done((f32[4]{0:T(128)S(1)}, f32[4]{0:T(128)S(1)}, u32[]{:S(2)}, u32[]{:S(2)}) %collective-permute-start.18) | collective-permute-done | bytes 48 | tf_op jit(solution)/shard_map/ppermute | solution.py:24
  162.3 1.9 collective-permute-start.20
  164.3 1.9 collective-permute-start.19
  166.2 3.7 %collective-permute-done.20 = f32[4]{0:T(128)S(1)} collective-permute-done((f32[4]{0:T(128)S(1)}, f32[4]{0:T(128)S(1)}, u32[]{:S(2)}, u32[]{:S(2)}) %collective-permute-start.20) | collective-permute-done | bytes 48 | tf_op jit(solution)/shard_map/ppermute | solution.py:24
  170.4 9.8 %collective-permute-done.19 = f32[4,128,128]{2,1,0:T(8,128)S(1)} collective-permute-done((f32[4,128,128]{2,1,0:T(8,128)S(1)}, f32[4,128,128]{2,1,0:T(8,128)S(1)}, u32[]{:S(2)}, u32[]{:S(2)}) %collective-permute-start.19) | collective-permute-done | bytes 262176 | tf_op jit(solution)/shard_map/ppermute | solution.py:24
  180.3 1.3 collective-permute-start.21
  181.9 1.2 fusion.6
  183.0 9.5 %collective-permute-done.21 = f32[4,128,128]{2,1,0:T(8,128)S(1)} collective-permute-done((f32[4,128,128]{2,1,0:T(8,128)S(1)}, f32[4,128,128]{2,1,0:T(8,128)S(1)}, u32[]{:S(2)}, u32[]{:S(2)}) %collective-permute-start.21) | collective-permute-done | bytes 262176 | tf_op jit(solution)/shard_map/ppermute | solution.py:24
  193.2 1.2 convolution_bitcast_fusion.2
  194.4 1.0 fusion.5
  196.2 4.5 %all-to-all-start = ((f32[8,16,256]{2,1,0:T(8,128)}), f32[8,16,256]{2,1,0:T(8,128)S(1)}, u32[]{:S(2)}, u32[]{:S(2)}) async-start(f32[8,16,256]{2,1,0:T(8,128)} %bitcast.13), calls=%async_computation | async-start | bytes 262144 | tf_op jit(solution)/shard_map/all_to_all | solution.py:81
  201.1 1.0 copy.40
  202.1 5.2 %all-to-all-done = f32[8,16,256]{2,1,0:T(8,128)S(1)} async-done(((f32[8,16,256]{2,1,0:T(8,128)}), f32[8,16,256]{2,1,0:T(8,128)S(1)}, u32[]{:S(2)}, u32[]{:S(2)}) %all-to-all-start) | async-done | bytes 131104 | tf_op jit(solution)/shard_map/all_to_all | solution.py:81
  (60 shorter events, 7.0 us)
Async XLA Ops:
  7.2 4.7 %copy-start = (bf16[128,128]{1,0:T(8,128)(2,1)S(1)}, bf16[128,128]{1,0:T(8,128)(2,1)}, u32[]{:S(2)}) copy-start(bf16[128,128]{1,0:T(8,128)(2,1)} %param.11) | copy-start | bytes 98308
  7.2 45.7 %copy-start.1 = (bf16[128,128]{1,0:T(8,128)(2,1)S(1)}, bf16[128,128]{1,0:T(8,128)(2,1)}, u32[]{:S(2)}) copy-start(bf16[128,128]{1,0:T(8,128)(2,1)} %param.12) | copy-start | bytes 98308
  7.2 90.1 %all-gather.2.cloned.1.call-start = ((), (), s32[]{:S(2)}) async-start(), calls=%async_computation.1 | async-start | bytes 3244032 | tf_op jit(solution)/shard_map/all_gather | solution.py:168
  10.5 2.4 %collective-permute-start = (f32[8]{0:T(128)S(1)}, f32[8]{0:T(128)S(1)}, u32[]{:S(2)}, u32[]{:S(2)}) collective-permute-start(f32[8]{0:T(128)S(1)} %slice_bitcast_fusion), channel_id=1, source_target_pairs={{0,8},{8,0},{16,24},{24,16},{32,40},{40,32},{48,56},{56,48},{64,72... | collective-permute-start | bytes 104 | tf_op jit(solution)/shard_map/ppermute | solution.py:39
  10.7 67.4 %copy-start.2 = (bf16[128,1024]{1,0:T(8,128)(2,1)S(1)}, bf16[128,1024]{1,0:T(8,128)(2,1)}, u32[]{:S(2)}) copy-start(bf16[128,1024]{1,0:T(8,128)(2,1)} %param.7) | copy-start | bytes 786436
  12.3 1.7 collective-permute-start.1
  14.1 12.0 %collective-permute-start.2 = (f32[4,128,128]{2,1,0:T(8,128)S(1)}, f32[4,128,128]{2,1,0:T(8,128)S(1)}, u32[]{:S(2)}, u32[]{:S(2)}) collective-permute-start(f32[4,128,128]{2,1,0:T(8,128)S(1)} %select_add_fusion.1), channel_id=1, source_target_pairs={{0,16},{8,24},{16,32},{24,40},{32,48},{40,56},{48,64},{56,72},{64,... | collective-permute-start | bytes 786440 | tf_op jit(solution)/shard_map/ppermute | solution.py:24
  26.1 19.1 %collective-permute-start.4 = (f32[4,128,128]{2,1,0:T(8,128)S(1)}, f32[4,128,128]{2,1,0:T(8,128)S(1)}, u32[]{:S(2)}, u32[]{:S(2)}) collective-permute-start(f32[4,128,128]{2,1,0:T(8,128)S(1)} %collective-permute-done.2), channel_id=1, source_target_pairs={{0,16},{8,24},{16,32},{24,40},{32,48},{40,56},{48,64},{56,72},{64,... | collective-permute-start | bytes 786440 | tf_op jit(solution)/shard_map/ppermute | solution.py:24
  30.8 6.9 %collective-permute-start.3 = (f32[4]{0:T(128)S(1)}, f32[4]{0:T(128)S(1)}, u32[]{:S(2)}, u32[]{:S(2)}) collective-permute-start(f32[4]{0:T(128)S(1)} %get-tuple-element.36), channel_id=1, source_target_pairs={{0,16},{8,24},{16,32},{24,40},{32,48},{40,56},{48,64},{56,72},{64,... | collective-permute-start | bytes 56 | tf_op jit(solution)/shard_map/ppermute | solution.py:24
  37.7 7.4 %collective-permute-start.5 = (f32[4]{0:T(128)S(1)}, f32[4]{0:T(128)S(1)}, u32[]{:S(2)}, u32[]{:S(2)}) collective-permute-start(f32[4]{0:T(128)S(1)} %collective-permute-done.3), channel_id=1, source_target_pairs={{0,16},{8,24},{16,32},{24,40},{32,48},{40,56},{48,64},{56,72},{64,... | collective-permute-start | bytes 56 | tf_op jit(solution)/shard_map/ppermute | solution.py:24
  45.3 11.5 %collective-permute-start.6 = (f32[4,128,128]{2,1,0:T(8,128)S(1)}, f32[4,128,128]{2,1,0:T(8,128)S(1)}, u32[]{:S(2)}, u32[]{:S(2)}) collective-permute-start(f32[4,128,128]{2,1,0:T(8,128)S(1)} %multiply_add_fusion.9), channel_id=1, source_target_pairs={{0,32},{8,40},{16,48},{24,56},{32,64},{40,72},{48,80},{56,88},{64,... | collective-permute-start | bytes 786440 | tf_op jit(solution)/shard_map/ppermute | solution.py:24
  56.8 15.8 %collective-permute-start.8 = (f32[4,128,128]{2,1,0:T(8,128)S(1)}, f32[4,128,128]{2,1,0:T(8,128)S(1)}, u32[]{:S(2)}, u32[]{:S(2)}) collective-permute-start(f32[4,128,128]{2,1,0:T(8,128)S(1)} %multiply_add_fusion.8), channel_id=1, source_target_pairs={{0,64},{8,72},{16,80},{24,88},{32,96},{40,104},{48,112},{56,120},{... | collective-permute-start | bytes 786440 | tf_op jit(solution)/shard_map/ppermute | solution.py:24
  62.8 9.9 %collective-permute-start.7 = (f32[4]{0:T(128)S(1)}, f32[4]{0:T(128)S(1)}, u32[]{:S(2)}, u32[]{:S(2)}) collective-permute-start(f32[4]{0:T(128)S(1)} %get-tuple-element.16), channel_id=1, source_target_pairs={{0,32},{8,40},{16,48},{24,56},{32,64},{40,72},{48,80},{56,88},{64,... | collective-permute-start | bytes 56 | tf_op jit(solution)/shard_map/ppermute | solution.py:24
  72.8 16.6 %collective-permute-start.10 = (f32[4,128,128]{2,1,0:T(8,128)S(1)}, f32[4,128,128]{2,1,0:T(8,128)S(1)}, u32[]{:S(2)}, u32[]{:S(2)}) collective-permute-start(f32[4,128,128]{2,1,0:T(8,128)S(1)} %multiply_add_fusion.7), channel_id=1, source_target_pairs={{0,128},{8,136},{16,144},{24,152},{32,160},{40,168},{48,176},{56,1... | collective-permute-start | bytes 786440 | tf_op jit(solution)/shard_map/ppermute | solution.py:24
  79.0 10.4 %collective-permute-start.9 = (f32[4]{0:T(128)S(1)}, f32[4]{0:T(128)S(1)}, u32[]{:S(2)}, u32[]{:S(2)}) collective-permute-start(f32[4]{0:T(128)S(1)} %get-tuple-element.14), channel_id=1, source_target_pairs={{0,64},{8,72},{16,80},{24,88},{32,96},{40,104},{48,112},{56,120},{... | collective-permute-start | bytes 56 | tf_op jit(solution)/shard_map/ppermute | solution.py:24
  89.5 18.8 %collective-permute-start.11 = (f32[4,128,128]{2,1,0:T(8,128)S(1)}, f32[4,128,128]{2,1,0:T(8,128)S(1)}, u32[]{:S(2)}, u32[]{:S(2)}) collective-permute-start(f32[4,128,128]{2,1,0:T(8,128)S(1)} %get-tuple-element.20), channel_id=1, source_target_pairs={{0,8},{8,0},{16,24},{24,16},{32,40},{40,32},{48,56},{56,48},{64,72... | collective-permute-start | bytes 786440 | tf_op jit(solution)/shard_map/ppermute | solution.py:67
  111.2 1.6 collective-permute-start.12
  112.9 16.6 %collective-permute-start.13 = (f32[4,128,128]{2,1,0:T(8,128)S(1)}, f32[4,128,128]{2,1,0:T(8,128)S(1)}, u32[]{:S(2)}, u32[]{:S(2)}) collective-permute-start(f32[4,128,128]{2,1,0:T(8,128)S(1)} %select_add_fusion), channel_id=1, source_target_pairs={{16,0},{24,8},{32,16},{40,24},{48,32},{56,40},{64,48},{72,56},{80,... | collective-permute-start | bytes 786440 | tf_op jit(solution)/shard_map/ppermute | solution.py:24
  129.6 20.2 %collective-permute-start.15 = (f32[4,128,128]{2,1,0:T(8,128)S(1)}, f32[4,128,128]{2,1,0:T(8,128)S(1)}, u32[]{:S(2)}, u32[]{:S(2)}) collective-permute-start(f32[4,128,128]{2,1,0:T(8,128)S(1)} %collective-permute-done.13), channel_id=1, source_target_pairs={{16,0},{24,8},{32,16},{40,24},{48,32},{56,40},{64,48},{72,56},{80,... | collective-permute-start | bytes 786440 | tf_op jit(solution)/shard_map/ppermute | solution.py:24
  132.8 9.1 %collective-permute-start.14 = (f32[4]{0:T(128)S(1)}, f32[4]{0:T(128)S(1)}, u32[]{:S(2)}, u32[]{:S(2)}) collective-permute-start(f32[4]{0:T(128)S(1)} %get-tuple-element.32), channel_id=1, source_target_pairs={{16,0},{24,8},{32,16},{40,24},{48,32},{56,40},{64,48},{72,56},{80,... | collective-permute-start | bytes 56 | tf_op jit(solution)/shard_map/ppermute | solution.py:24
  141.9 7.8 %collective-permute-start.16 = (f32[4]{0:T(128)S(1)}, f32[4]{0:T(128)S(1)}, u32[]{:S(2)}, u32[]{:S(2)}) collective-permute-start(f32[4]{0:T(128)S(1)} %collective-permute-done.14), channel_id=1, source_target_pairs={{16,0},{24,8},{32,16},{40,24},{48,32},{56,40},{64,48},{72,56},{80,... | collective-permute-start | bytes 56 | tf_op jit(solution)/shard_map/ppermute | solution.py:24
  149.8 14.4 %collective-permute-start.17 = (f32[4,128,128]{2,1,0:T(8,128)S(1)}, f32[4,128,128]{2,1,0:T(8,128)S(1)}, u32[]{:S(2)}, u32[]{:S(2)}) collective-permute-start(f32[4,128,128]{2,1,0:T(8,128)S(1)} %multiply_add_fusion.4), channel_id=1, source_target_pairs={{32,0},{40,8},{48,16},{56,24},{64,32},{72,40},{80,48},{88,56},{96,... | collective-permute-start | bytes 786440 | tf_op jit(solution)/shard_map/ppermute | solution.py:24
  151.7 10.5 %collective-permute-start.18 = (f32[4]{0:T(128)S(1)}, f32[4]{0:T(128)S(1)}, u32[]{:S(2)}, u32[]{:S(2)}) collective-permute-start(f32[4]{0:T(128)S(1)} %get-tuple-element.12), channel_id=1, source_target_pairs={{32,0},{40,8},{48,16},{56,24},{64,32},{72,40},{80,48},{88,56},{96,... | collective-permute-start | bytes 56 | tf_op jit(solution)/shard_map/ppermute | solution.py:24
  162.3 7.7 %collective-permute-start.20 = (f32[4]{0:T(128)S(1)}, f32[4]{0:T(128)S(1)}, u32[]{:S(2)}, u32[]{:S(2)}) collective-permute-start(f32[4]{0:T(128)S(1)} %get-tuple-element.10), channel_id=1, source_target_pairs={{64,0},{72,8},{80,16},{88,24},{96,32},{104,40},{112,48},{120,56},{... | collective-permute-start | bytes 56 | tf_op jit(solution)/shard_map/ppermute | solution.py:24
  164.3 15.9 %collective-permute-start.19 = (f32[4,128,128]{2,1,0:T(8,128)S(1)}, f32[4,128,128]{2,1,0:T(8,128)S(1)}, u32[]{:S(2)}, u32[]{:S(2)}) collective-permute-start(f32[4,128,128]{2,1,0:T(8,128)S(1)} %multiply_add_fusion.3), channel_id=1, source_target_pairs={{64,0},{72,8},{80,16},{88,24},{96,32},{104,40},{112,48},{120,56},{... | collective-permute-start | bytes 786440 | tf_op jit(solution)/shard_map/ppermute | solution.py:24
  180.3 12.2 %collective-permute-start.21 = (f32[4,128,128]{2,1,0:T(8,128)S(1)}, f32[4,128,128]{2,1,0:T(8,128)S(1)}, u32[]{:S(2)}, u32[]{:S(2)}) collective-permute-start(f32[4,128,128]{2,1,0:T(8,128)S(1)} %multiply_add_fusion.2), channel_id=1, source_target_pairs={{128,0},{136,8},{144,16},{152,24},{160,32},{168,40},{176,48},{184,... | collective-permute-start | bytes 786440 | tf_op jit(solution)/shard_map/ppermute | solution.py:24
  192.6 1.8 collective-permute-start.22
  196.2 11.1 %all-to-all-start = ((f32[8,16,256]{2,1,0:T(8,128)}), f32[8,16,256]{2,1,0:T(8,128)S(1)}, u32[]{:S(2)}, u32[]{:S(2)}) async-start(f32[8,16,256]{2,1,0:T(8,128)} %bitcast.13), calls=%async_computation | async-start | bytes 262144 | tf_op jit(solution)/shard_map/all_to_all | solution.py:81
Sparse Core Ops, SparseCore 0:
  11.4 85.9 all-gather.1

commit v5 on v4

--- a/solution.py
+++ b/solution.py
@@ -22,6 +22,21 @@
     else:
         perm = [(j + distance, j) for j in range(count - distance)]
     return lax.ppermute(value, axis, perm)
+
+
+def send_with_logs(state, logs, axis, perm):
+    heads, rows, width = state.shape
+    count = logs.shape[0]
+    log_rows = jnp.pad(jnp.broadcast_to(logs[:, None], (count, width)), ((0, -count % 8), (0, 0)))
+    payload = jnp.concatenate([state.reshape(heads * rows, width), log_rows], axis=0)
+    got = lax.ppermute(payload, axis, perm)
+    return got[: heads * rows].reshape(heads, rows, width), got[heads * rows : heads * rows + count, 0]
+
+
+def shift_perm(count, distance, forward):
+    if forward:
+        return [(j, j + distance) for j in range(count - distance)]
+    return [(j + distance, j) for j in range(count - distance)]
 
 
 def exclusive_scan(state, logs, axis, forward):
@@ -36,8 +51,8 @@
     swap = [(j, j ^ 1) for j in range(count)]
 
     own_half = lax.dynamic_slice_in_dim(state, mine, half, axis=0)
-    got_half, got_logs = lax.ppermute(
-        (lax.dynamic_slice_in_dim(state, partner, half, axis=0), logs), axis, swap
+    got_half, got_logs = send_with_logs(
+        lax.dynamic_slice_in_dim(state, partner, half, axis=0), logs, axis, swap
     )
     first_half = jnp.where(first, own_half, got_half)
     second_half = jnp.where(first, got_half, own_half)
@@ -48,11 +63,13 @@
     chip_state = jnp.exp(second_logs_half)[:, None, None] * first_half + second_half
     chip_logs = first_logs_half + second_logs_half
 
-    window_state, window_log = shift((chip_state, chip_logs), axis, 2, forward)
+    window_state, window_log = send_with_logs(chip_state, chip_logs, axis, shift_perm(count, 2, forward))
     width = 1
     while width < chips:
         if width * 2 < chips:
-            got_state, got_log = shift((window_state, window_log), axis, 2 * width, forward)
+            got_state, got_log = send_with_logs(
+                window_state, window_log, axis, shift_perm(count, 2 * width, forward)
+            )
             window_log_next = window_log + got_log
         else:
             got_state = shift(window_state, axis, 2 * width, forward)

time: 219 us -> 224 us (1.023); the launches traced: 215 us -> 223 us
  starting transfers between devices: 72.8 us -> 42.1 us
  waiting for transfers between devices: 98.7 us -> 124 us
  other arithmetic: 4.31 us -> 9.87 us
  local copies, waits for them, and re-layouts: 4.77 us -> 9.05 us
  matrix products: 8.75 us -> 12.2 us
    ppermute x3 -> x10, waiting for transfers between devices: 2.28 us -> 89.2 us  [send_with_logs(): got = lax.ppermute(payload, axis, perm)]
    ppermute x18 -> x2, waiting for transfers between devices: 83.4 us -> 15.2 us  [shift(): return lax.ppermute(value, axis, perm)]
    ppermute x18 -> x2, starting transfers between devices: 67 us -> 2.78 us  [shift(): return lax.ppermute(value, axis, perm)]
    ppermute x3 -> x10, starting transfers between devices: 0.98 us -> 35.5 us  [send_with_logs(): got = lax.ppermute(payload, axis, perm)]
    all_gather x1, waiting for transfers between devices: 7.7 us -> 14.3 us  [local(): every = lax.all_gather(packed, 'seq', axis=0, tiled=True)]
    slice x0 -> x16, local copies, waits for them, and re-layouts: none -> 3.23 us  [the longest x14 3.01 us: send_with_logs(): got[:heads * rows].reshape(heads, rows, width)]
  transfers between devices with their start and end apart: 25 -> 16, of which waited for: 17 -> 13; matrix products, arithmetic and copies ran while one was open for 5% -> 8% of each run, Pallas kernels for 5% -> 5%
where the time goes in v5:
time: 224 us; the launch traced here: 223 us
  waiting for transfers between devices  124 us (55%)
  starting transfers between devices  42.1 us (19%)
  between operations  14.8 us (7%)
  matrix products  12.2 us (5%)
  Pallas kernels  11 us (5%)
  other arithmetic  9.87 us (4%)
  local copies, waits for them, and re-layouts  9.05 us (4%)
    ppermute x10, waiting for transfers between devices, send_with_logs(): got = lax.ppermute(payload, axis, perm)  89.2 us
    ppermute x10, starting transfers between devices, send_with_logs(): got = lax.ppermute(payload, axis, perm)  35.5 us
    ppermute x2, waiting for transfers between devices, shift(): return lax.ppermute(value, axis, perm)  15.2 us
    all_gather x1, waiting for transfers between devices, local(): every = lax.all_gather(packed, 'seq', axis=0, tiled=True)  14.3 us
    pallas_call x1, Pallas kernels, attend(): pl.pallas_call(functools.partial(attend_kernel, heads=heads), out_shape=j...  11 us
    all_to_all x1, waiting for transfers between devices, mp_sum_scatter(): return jnp.sum(lax.all_to_all(blocks, axis, 0, 0), axis=0)  5.19 us
  transfers between devices with their start and end apart: 16, of which 13 were waited for; matrix products, arithmetic and copies ran while one was open for 8% of the time, Pallas kernels for 5%

profile of v5, /device:TPU:68, one launch (start us, length us, event | category | flops | bytes accessed | tf_op | source)
XLA Modules:
  0.0 222.9 jit_solution(7329366813344705105)
XLA Ops:
  7.2 0.8 copy.63
  8.3 1.1 copy.66
  10.1 0.9 reduce-precision_convert_fusion
  11.0 1.4 pad_maximum_fusion.11
  13.5 3.8 %collective-permute-start.1 = (f32[520,128]{0,1:T(8,128)S(1)}, f32[520,128]{0,1:T(8,128)S(1)}, u32[]{:S(2)}, u32[]{:S(2)}) collective-permute-start(f32[520,128]{0,1:T(8,128)S(1)} %pad_maximum_fusion), channel_id=1, source_target_pairs={{0,16},{8,24},{16,32},{24,40},{32,48},{40,56},{48,64},{56,72},{64,... | collective-permute-start | bytes 798728 | tf_op jit(solution)/shard_map/ppermute | solution.py:32
  17.3 9.7 %collective-permute-done.1 = f32[520,128]{0,1:T(8,128)S(1)} collective-permute-done((f32[520,128]{0,1:T(8,128)S(1)}, f32[520,128]{0,1:T(8,128)S(1)}, u32[]{:S(2)}, u32[]{:S(2)}) %collective-permute-start.1) | collective-permute-done | bytes 266272 | tf_op jit(solution)/shard_map/ppermute | solution.py:32
  27.1 4.7 %collective-permute-start.2 = (f32[520,128]{0,1:T(8,128)S(1)}, f32[520,128]{0,1:T(8,128)S(1)}, u32[]{:S(2)}, u32[]{:S(2)}) collective-permute-start(f32[520,128]{0,1:T(8,128)S(1)} %pad_maximum_fusion.1), channel_id=1, source_target_pairs={{0,16},{8,24},{16,32},{24,40},{32,48},{40,56},{48,64},{56,72},{64,... | collective-permute-start | bytes 798728 | tf_op jit(solution)/shard_map/ppermute | solution.py:32
  31.8 8.2 %collective-permute-done.2 = f32[520,128]{0,1:T(8,128)S(1)} collective-permute-done((f32[520,128]{0,1:T(8,128)S(1)}, f32[520,128]{0,1:T(8,128)S(1)}, u32[]{:S(2)}, u32[]{:S(2)}) %collective-permute-start.2) | collective-permute-done | bytes 266272 | tf_op jit(solution)/shard_map/ppermute | solution.py:32
  40.2 6.3 %collective-permute-start.3 = (f32[520,128]{0,1:T(8,128)S(1)}, f32[520,128]{0,1:T(8,128)S(1)}, u32[]{:S(2)}, u32[]{:S(2)}) collective-permute-start(f32[520,128]{0,1:T(8,128)S(1)} %pad_maximum_fusion.2), channel_id=1, source_target_pairs={{0,32},{8,40},{16,48},{24,56},{32,64},{40,72},{48,80},{56,88},{64,... | collective-permute-start | bytes 798728 | tf_op jit(solution)/shard_map/ppermute | solution.py:32
  46.6 6.4 %collective-permute-done.3 = f32[520,128]{0,1:T(8,128)S(1)} collective-permute-done((f32[520,128]{0,1:T(8,128)S(1)}, f32[520,128]{0,1:T(8,128)S(1)}, u32[]{:S(2)}, u32[]{:S(2)}) %collective-permute-start.3) | collective-permute-done | bytes 266272 | tf_op jit(solution)/shard_map/ppermute | solution.py:32
  53.1 5.7 %collective-permute-start.4 = (f32[520,128]{0,1:T(8,128)S(1)}, f32[520,128]{0,1:T(8,128)}, u32[]{:S(2)}, u32[]{:S(2)}) collective-permute-start(f32[520,128]{0,1:T(8,128)S(1)} %pad_maximum_fusion.3), channel_id=1, source_target_pairs={{0,64},{8,72},{16,80},{24,88},{32,96},{40,104},{48,112},{56,120},{... | collective-permute-start | bytes 798728 | tf_op jit(solution)/shard_map/ppermute | solution.py:32
  59.4 17.4 %collective-permute-done.4 = f32[520,128]{0,1:T(8,128)} collective-permute-done((f32[520,128]{0,1:T(8,128)S(1)}, f32[520,128]{0,1:T(8,128)}, u32[]{:S(2)}, u32[]{:S(2)}) %collective-permute-start.4) | collective-permute-done | bytes 266272 | tf_op jit(solution)/shard_map/ppermute | solution.py:32
  76.8 1.0 slice.101
  77.9 0.7 fusion.49
  78.8 1.3 collective-permute-start.5
  80.3 0.8 reshape.215.query_ref
  81.1 0.7 convolution_bitcast_fusion.1
  81.8 3.6 %collective-permute-done.5 = f32[4,128,128]{2,1,0:T(8,128)S(1)} collective-permute-done((f32[4,128,128]{2,1,0:T(8,128)S(1)}, f32[4,128,128]{2,1,0:T(8,128)S(1)}, u32[]{:S(2)}, u32[]{:S(2)}) %collective-permute-start.5) | collective-permute-done | bytes 262176 | tf_op jit(solution)/shard_map/ppermute | solution.py:24
  85.4 0.7 fusion.19
  86.3 14.3 %all-gather.2.cloned.1.call-done.key_ref.upper_ref.lower_ref = bf16[4096,384]{1,0:T(8,128)(2,1)} async-done(((bf16[128,384]{1,0:T(8,128)(2,1)}), bf16[4096,384]{1,0:T(8,128)(2,1)}) %all-gather.2.cloned.1.call-update) | async-done | bytes 3145744 | tf_op jit(solution)/shard_map/all_gather | solution.py:185
  100.6 11.0 %shard_map.94 = f32[1024,128]{1,0:T(8,128)} custom-call(s32[1]{0:T(128)} %bitcast.21.first_ref, bf16[1024,128]{1,0:T(8,128)(2,1)} %reshape.215.query_ref, bf16[4096,384]{1,0:T(8,128)(2,1)} %all-gather.2.cloned.1.call-done.key_ref.upper_ref.lower_ref, bf16[4096,384]{1,0:T(8,128)(2,1)} %all-gather.2.cloned.1.call-done.key_ref.upper_ref.lower_ref, ...), custom_call_target="tpu_custom_call" | custom-call | flops 4294967296 | bytes 3932160 | tf_op jit(solution)/shard_map/pallas_call | solution.py:148
  111.5 1.9 fusion.3
  113.4 1.1 fusion.12
  115.1 1.3 collective-permute-done.7
  117.4 6.7 %collective-permute-start.8 = (f32[520,128]{0,1:T(8,128)S(1)}, f32[520,128]{0,1:T(8,128)S(1)}, u32[]{:S(2)}, u32[]{:S(2)}) collective-permute-start(f32[520,128]{0,1:T(8,128)S(1)} %pad_maximum_fusion.4), channel_id=1, source_target_pairs={{16,0},{24,8},{32,16},{40,24},{48,32},{56,40},{64,48},{72,56},{80,... | collective-permute-start | bytes 798728 | tf_op jit(solution)/shard_map/ppermute | solution.py:32
  124.2 9.4 %collective-permute-done.8 = f32[520,128]{0,1:T(8,128)S(1)} collective-permute-done((f32[520,128]{0,1:T(8,128)S(1)}, f32[520,128]{0,1:T(8,128)S(1)}, u32[]{:S(2)}, u32[]{:S(2)}) %collective-permute-start.8) | collective-permute-done | bytes 266272 | tf_op jit(solution)/shard_map/ppermute | solution.py:32
  133.6 3.9 %collective-permute-start.9 = (f32[520,128]{0,1:T(8,128)S(1)}, f32[520,128]{0,1:T(8,128)S(1)}, u32[]{:S(2)}, u32[]{:S(2)}) collective-permute-start(f32[520,128]{0,1:T(8,128)S(1)} %pad_maximum_fusion.5), channel_id=1, source_target_pairs={{16,0},{24,8},{32,16},{40,24},{48,32},{56,40},{64,48},{72,56},{80,... | collective-permute-start | bytes 798728 | tf_op jit(solution)/shard_map/ppermute | solution.py:32
  137.5 9.8 %collective-permute-done.9 = f32[520,128]{0,1:T(8,128)S(1)} collective-permute-done((f32[520,128]{0,1:T(8,128)S(1)}, f32[520,128]{0,1:T(8,128)S(1)}, u32[]{:S(2)}, u32[]{:S(2)}) %collective-permute-start.9) | collective-permute-done | bytes 266272 | tf_op jit(solution)/shard_map/ppermute | solution.py:32
  148.0 2.1 collective-permute-start.10
  150.1 11.9 %collective-permute-done.10 = f32[520,128]{0,1:T(8,128)S(1)} collective-permute-done((f32[520,128]{0,1:T(8,128)S(1)}, f32[520,128]{0,1:T(8,128)S(1)}, u32[]{:S(2)}, u32[]{:S(2)}) %collective-permute-start.10) | collective-permute-done | bytes 266272 | tf_op jit(solution)/shard_map/ppermute | solution.py:32
  162.1 0.8 pad_maximum_fusion.7
  162.9 1.9 collective-permute-start.11
  164.8 1.8 fusion.4
  167.0 15.1 %collective-permute-done.11 = f32[520,128]{0,1:T(8,128)} collective-permute-done((f32[520,128]{0,1:T(8,128)}, f32[520,128]{0,1:T(8,128)}, u32[]{:S(2)}, u32[]{:S(2)}) %collective-permute-start.11) | collective-permute-done | bytes 266272 | tf_op jit(solution)/shard_map/ppermute | solution.py:32
  182.1 1.0 slice.111
  183.2 0.7 fusion.47
  184.0 0.8 multiply_add_fusion.2
  184.7 1.5 collective-permute-start.12
  186.2 1.1 fusion.70
  187.3 2.2 fusion.6
  189.5 11.6 %collective-permute-done.12 = f32[4,128,128]{2,1,0:T(8,128)S(1)} collective-permute-done((f32[4,128,128]{2,1,0:T(8,128)S(1)}, f32[4,128,128]{2,1,0:T(8,128)S(1)}, u32[]{:S(2)}, u32[]{:S(2)}) %collective-permute-start.12) | collective-permute-done | bytes 262176 | tf_op jit(solution)/shard_map/ppermute | solution.py:24
  201.0 0.8 fusion.15
  202.3 1.2 convolution_bitcast_fusion.2
  203.5 1.0 fusion.5
  204.5 0.7 copy.87
  205.2 3.7 %all-to-all-start = ((f32[8,16,256]{2,1,0:T(8,128)}), f32[8,16,256]{2,1,0:T(8,128)S(1)}, u32[]{:S(2)}, u32[]{:S(2)}) async-start(f32[8,16,256]{2,1,0:T(8,128)} %bitcast.43), calls=%async_computation | async-start | bytes 262144 | tf_op jit(solution)/shard_map/all_to_all | solution.py:98
  209.3 1.0 copy.88
  210.3 5.2 %all-to-all-done = f32[8,16,256]{2,1,0:T(8,128)S(1)} async-done(((f32[8,16,256]{2,1,0:T(8,128)}), f32[8,16,256]{2,1,0:T(8,128)S(1)}, u32[]{:S(2)}, u32[]{:S(2)}) %all-to-all-start) | async-done | bytes 131104 | tf_op jit(solution)/shard_map/all_to_all | solution.py:98
  (124 shorter events, 7.6 us)
Async XLA Ops:
  7.2 2.3 %copy-start = (bf16[128,128]{1,0:T(8,128)(2,1)S(1)}, bf16[128,128]{1,0:T(8,128)(2,1)}, u32[]{:S(2)}) copy-start(bf16[128,128]{1,0:T(8,128)(2,1)} %param.11) | copy-start | bytes 98308
  7.2 93.4 %all-gather.2.cloned.1.call-start = ((), (), s32[]{:S(2)}) async-start(), calls=%async_computation.1 | async-start | bytes 3244032 | tf_op jit(solution)/shard_map/all_gather | solution.py:185
  8.3 18.8 %copy-start.13 = (f32[520]{0:T(1024)}, f32[520]{0:T(1024)S(1)}, u32[]{:S(2)}) copy-start(f32[520]{0:T(1024)S(1)} %pad.89.clone) | copy-start | bytes 6244
  8.3 18.8 %copy-start.10 = (f32[128,8]{0,1:T(8,128)}, f32[128,8]{0,1:T(8,128)S(1)}, u32[]{:S(2)}) copy-start(f32[128,8]{0,1:T(8,128)S(1)} %copy.68) | copy-start | bytes 12292
  10.0 2.4 %collective-permute-start = (f32[520,128]{1,0:T(8,128)S(1)}, f32[520,128]{1,0:T(8,128)S(1)}, u32[]{:S(2)}, u32[]{:S(2)}) collective-permute-start(f32[520,128]{1,0:T(8,128)S(1)} %pad_maximum_fusion.8), channel_id=1, source_target_pairs={{0,8},{8,0},{16,24},{24,16},{32,40},{40,32},{48,56},{56,48},{64,72... | collective-permute-start | bytes 798728 | tf_op jit(solution)/shard_map/ppermute | solution.py:32
  13.2 45.6 %copy-start.1 = (bf16[128,128]{1,0:T(8,128)(2,1)S(1)}, bf16[128,128]{1,0:T(8,128)(2,1)}, u32[]{:S(2)}) copy-start(bf16[128,128]{1,0:T(8,128)(2,1)} %param.12) | copy-start | bytes 98308
  13.5 13.5 %collective-permute-start.1 = (f32[520,128]{0,1:T(8,128)S(1)}, f32[520,128]{0,1:T(8,128)S(1)}, u32[]{:S(2)}, u32[]{:S(2)}) collective-permute-start(f32[520,128]{0,1:T(8,128)S(1)} %pad_maximum_fusion), channel_id=1, source_target_pairs={{0,16},{8,24},{16,32},{24,40},{32,48},{40,56},{48,64},{56,72},{64,... | collective-permute-start | bytes 798728 | tf_op jit(solution)/shard_map/ppermute | solution.py:32
  27.1 12.9 %collective-permute-start.2 = (f32[520,128]{0,1:T(8,128)S(1)}, f32[520,128]{0,1:T(8,128)S(1)}, u32[]{:S(2)}, u32[]{:S(2)}) collective-permute-start(f32[520,128]{0,1:T(8,128)S(1)} %pad_maximum_fusion.1), channel_id=1, source_target_pairs={{0,16},{8,24},{16,32},{24,40},{32,48},{40,56},{48,64},{56,72},{64,... | collective-permute-start | bytes 798728 | tf_op jit(solution)/shard_map/ppermute | solution.py:32
  40.0 13.0 %copy-start.6 = (f32[520,128]{0,1:T(8,128)}, f32[520,128]{0,1:T(8,128)S(1)}, u32[]{:S(2)}) copy-start(f32[520,128]{0,1:T(8,128)S(1)} %collective-permute-done.2) | copy-start | bytes 798724
  40.2 40.1 %copy-start.4 = (bf16[128,1024]{1,0:T(8,128)(2,1)S(1)}, bf16[128,1024]{1,0:T(8,128)(2,1)}, u32[]{:S(2)}) copy-start(bf16[128,1024]{1,0:T(8,128)(2,1)} %param.7) | copy-start | bytes 786436
  40.2 12.8 %collective-permute-start.3 = (f32[520,128]{0,1:T(8,128)S(1)}, f32[520,128]{0,1:T(8,128)S(1)}, u32[]{:S(2)}, u32[]{:S(2)}) collective-permute-start(f32[520,128]{0,1:T(8,128)S(1)} %pad_maximum_fusion.2), channel_id=1, source_target_pairs={{0,32},{8,40},{16,48},{24,56},{32,64},{40,72},{48,80},{56,88},{64,... | collective-permute-start | bytes 798728 | tf_op jit(solution)/shard_map/ppermute | solution.py:32
  53.0 5.8 %copy-start.8 = (f32[520,128]{0,1:T(8,128)}, f32[520,128]{0,1:T(8,128)S(1)}, u32[]{:S(2)}) copy-start(f32[520,128]{0,1:T(8,128)S(1)} %collective-permute-done.3) | copy-start | bytes 798724
  53.1 23.7 %collective-permute-start.4 = (f32[520,128]{0,1:T(8,128)S(1)}, f32[520,128]{0,1:T(8,128)}, u32[]{:S(2)}, u32[]{:S(2)}) collective-permute-start(f32[520,128]{0,1:T(8,128)S(1)} %pad_maximum_fusion.3), channel_id=1, source_target_pairs={{0,64},{8,72},{16,80},{24,88},{32,96},{40,104},{48,112},{56,120},{... | collective-permute-start | bytes 798728 | tf_op jit(solution)/shard_map/ppermute | solution.py:32
  59.0 27.2 %copy-start.2 = (f32[128,128]{1,0:T(8,128)}, f32[128,128]{1,0:T(8,128)S(1)}, u32[]{:S(2)}) copy-start(f32[128,128]{1,0:T(8,128)S(1)} %convolution_multiply_fusion.2) | copy-start | bytes 196612
  78.8 6.6 %collective-permute-start.5 = (f32[4,128,128]{2,1,0:T(8,128)S(1)}, f32[4,128,128]{2,1,0:T(8,128)S(1)}, u32[]{:S(2)}, u32[]{:S(2)}) collective-permute-start(f32[4,128,128]{2,1,0:T(8,128)S(1)} %multiply_add_fusion.7), channel_id=1, source_target_pairs={{0,128},{8,136},{16,144},{24,152},{32,160},{40,168},{48,176},{56,1... | collective-permute-start | bytes 786440 | tf_op jit(solution)/shard_map/ppermute | solution.py:24
  80.2 31.3 %copy-start.15 = (f32[8,128]{1,0:T(8,128)}, f32[8,128]{1,0:T(8,128)S(1)}, u32[]{:S(2)}) copy-start(f32[8,128]{1,0:T(8,128)S(1)} %copy.64) | copy-start | bytes 12292
  80.2 33.2 %copy-start.17 = (f32[128,8]{0,1:T(8,128)}, f32[128,8]{0,1:T(8,128)S(1)}, u32[]{:S(2)}) copy-start(f32[128,8]{0,1:T(8,128)S(1)} %copy.74) | copy-start | bytes 12292
  86.2 25.4 %collective-permute-start.6 = (f32[4,128,128]{2,1,0:T(8,128)S(1)}, f32[4,128,128]{2,1,0:T(8,128)}, u32[]{:S(2)}, u32[]{:S(2)}) collective-permute-start(f32[4,128,128]{2,1,0:T(8,128)S(1)} %get-tuple-element.19), channel_id=1, source_target_pairs={{0,8},{8,0},{16,24},{24,16},{32,40},{40,32},{48,56},{56,48},{64,72... | collective-permute-start | bytes 786440 | tf_op jit(solution)/shard_map/ppermute | solution.py:84
  111.5 3.1 %copy-start.14 = (f32[520]{0:T(1024)S(1)}, f32[520]{0:T(1024)}, u32[]{:S(2)}) copy-start(f32[520]{0:T(1024)} %copy-done.13) | copy-start | bytes 6244
  114.8 1.6 collective-permute-start.7
  117.4 16.1 %collective-permute-start.8 = (f32[520,128]{0,1:T(8,128)S(1)}, f32[520,128]{0,1:T(8,128)S(1)}, u32[]{:S(2)}, u32[]{:S(2)}) collective-permute-start(f32[520,128]{0,1:T(8,128)S(1)} %pad_maximum_fusion.4), channel_id=1, source_target_pairs={{16,0},{24,8},{32,16},{40,24},{48,32},{56,40},{64,48},{72,56},{80,... | collective-permute-start | bytes 798728 | tf_op jit(solution)/shard_map/ppermute | solution.py:32
  133.6 13.7 %collective-permute-start.9 = (f32[520,128]{0,1:T(8,128)S(1)}, f32[520,128]{0,1:T(8,128)S(1)}, u32[]{:S(2)}, u32[]{:S(2)}) collective-permute-start(f32[520,128]{0,1:T(8,128)S(1)} %pad_maximum_fusion.5), channel_id=1, source_target_pairs={{16,0},{24,8},{32,16},{40,24},{48,32},{56,40},{64,48},{72,56},{80,... | collective-permute-start | bytes 798728 | tf_op jit(solution)/shard_map/ppermute | solution.py:32
  147.3 14.7 %copy-start.7 = (f32[520,128]{0,1:T(8,128)}, f32[520,128]{0,1:T(8,128)S(1)}, u32[]{:S(2)}) copy-start(f32[520,128]{0,1:T(8,128)S(1)} %collective-permute-done.9) | copy-start | bytes 798724
  147.3 0.5 copy-start.19
  147.3 14.7 %copy-start.18 = (f32[4]{0:T(128)}, f32[4]{0:T(128)S(1)}, u32[]{:S(2)}) copy-start(f32[4]{0:T(128)S(1)} %get-tuple-element.24) | copy-start | bytes 52
  148.0 14.0 %collective-permute-start.10 = (f32[520,128]{0,1:T(8,128)S(1)}, f32[520,128]{0,1:T(8,128)S(1)}, u32[]{:S(2)}, u32[]{:S(2)}) collective-permute-start(f32[520,128]{0,1:T(8,128)S(1)} %pad_maximum_fusion.6), channel_id=1, source_target_pairs={{32,0},{40,8},{48,16},{56,24},{64,32},{72,40},{80,48},{88,56},{96,... | collective-permute-start | bytes 798728 | tf_op jit(solution)/shard_map/ppermute | solution.py:32
  162.0 0.9 copy-start.9
  162.9 19.2 %collective-permute-start.11 = (f32[520,128]{0,1:T(8,128)}, f32[520,128]{0,1:T(8,128)}, u32[]{:S(2)}, u32[]{:S(2)}) collective-permute-start(f32[520,128]{0,1:T(8,128)} %pad_maximum_fusion.7), channel_id=1, source_target_pairs={{64,0},{72,8},{80,16},{88,24},{96,32},{104,40},{112,48},{120,56},{... | collective-permute-start | bytes 798728 | tf_op jit(solution)/shard_map/ppermute | solution.py:32
  183.2 18.8 %copy-start.5 = (f32[128,128]{1,0:T(8,128)S(1)}, f32[128,128]{1,0:T(8,128)}, u32[]{:S(2)}) copy-start(f32[128,128]{1,0:T(8,128)} %fusion.4) | copy-start | bytes 196612
  183.2 19.1 %copy-start.3 = (f32[128,128]{1,0:T(8,128)S(1)}, f32[128,128]{1,0:T(8,128)}, u32[]{:S(2)}) copy-start(f32[128,128]{1,0:T(8,128)} %copy-done.2) | copy-start | bytes 196612
  183.2 19.1 %copy-start.16 = (f32[8,128]{1,0:T(8,128)S(1)}, f32[8,128]{1,0:T(8,128)}, u32[]{:S(2)}) copy-start(f32[8,128]{1,0:T(8,128)} %copy-done.15) | copy-start | bytes 12292
  183.2 20.3 %copy-start.11 = (f32[128,8]{0,1:T(8,128)S(1)}, f32[128,8]{0,1:T(8,128)}, u32[]{:S(2)}) copy-start(f32[128,8]{0,1:T(8,128)} %copy-done.10) | copy-start | bytes 12292
  184.7 16.3 %collective-permute-start.12 = (f32[4,128,128]{2,1,0:T(8,128)S(1)}, f32[4,128,128]{2,1,0:T(8,128)S(1)}, u32[]{:S(2)}, u32[]{:S(2)}) collective-permute-start(f32[4,128,128]{2,1,0:T(8,128)S(1)} %multiply_add_fusion.2), channel_id=1, source_target_pairs={{128,0},{136,8},{144,16},{152,24},{160,32},{168,40},{176,48},{184,... | collective-permute-start | bytes 786440 | tf_op jit(solution)/shard_map/ppermute | solution.py:24
  187.3 21.6 %copy-start.12 = (f32[128,8]{0,1:T(8,128)S(1)}, f32[128,8]{0,1:T(8,128)}, u32[]{:S(2)}) copy-start(f32[128,8]{0,1:T(8,128)} %copy-done.10) | copy-start | bytes 12292
  201.8 1.6 collective-permute-start.13
  205.2 10.2 %all-to-all-start = ((f32[8,16,256]{2,1,0:T(8,128)}), f32[8,16,256]{2,1,0:T(8,128)S(1)}, u32[]{:S(2)}, u32[]{:S(2)}) async-start(f32[8,16,256]{2,1,0:T(8,128)} %bitcast.43), calls=%async_computation | async-start | bytes 262144 | tf_op jit(solution)/shard_map/all_to_all | solution.py:98
Sparse Core Ops, SparseCore 0:
  12.6 87.9 all-gather.1

commit v6 on v5

--- a/solution.py
+++ b/solution.py
@@ -39,52 +39,67 @@
     return [(j + distance, j) for j in range(count - distance)]
 
 
+def pair_down(state, logs, axis, bit, forward):
+    count = lax.axis_size(axis)
+    upper = (lax.axis_index(axis) // bit) % 2 == 1
+    first = jnp.logical_not(upper) if forward else upper
+    half = state.shape[0] // 2
+    mine = jnp.where(upper, half, 0)
+    other = half - mine
+    own_state = lax.dynamic_slice_in_dim(state, mine, half, axis=0)
+    own_logs = lax.dynamic_slice_in_dim(logs, mine, half)
+    got_state, got_logs = send_with_logs(
+        lax.dynamic_slice_in_dim(state, other, half, axis=0),
+        lax.dynamic_slice_in_dim(logs, other, half),
+        axis,
+        [(j, j ^ bit) for j in range(count)],
+    )
+    first_state = jnp.where(first, own_state, got_state)
+    second_state = jnp.where(first, got_state, own_state)
+    first_logs = jnp.where(first, own_logs, got_logs)
+    second_logs = jnp.where(first, got_logs, own_logs)
+    pair_state = jnp.exp(second_logs)[:, None, None] * first_state + second_state
+    return pair_state, first_logs + second_logs, (first_state, first_logs)
+
+
+def pair_up(window, saved, axis, bit, forward):
+    count = lax.axis_size(axis)
+    upper = (lax.axis_index(axis) // bit) % 2 == 1
+    first = jnp.logical_not(upper) if forward else upper
+    first_state, first_logs = saved
+    second_window = jnp.exp(first_logs)[:, None, None] * window + first_state
+    keep = jnp.where(first, window, second_window)
+    send = jnp.where(first, second_window, window)
+    got = lax.ppermute(send, axis, [(j, j ^ bit) for j in range(count)])
+    return jnp.where(
+        upper, jnp.concatenate([got, keep], axis=0), jnp.concatenate([keep, got], axis=0)
+    )
+
+
 def exclusive_scan(state, logs, axis, forward):
     count = lax.axis_size(axis)
-    chips = count // 2
-    core = lax.axis_index(axis) % 2
-    first = core == 0 if forward else core == 1
-    heads = state.shape[0]
-    half = heads // 2
-    mine = core * half
-    partner = (1 - core) * half
-    swap = [(j, j ^ 1) for j in range(count)]
-
-    own_half = lax.dynamic_slice_in_dim(state, mine, half, axis=0)
-    got_half, got_logs = send_with_logs(
-        lax.dynamic_slice_in_dim(state, partner, half, axis=0), logs, axis, swap
-    )
-    first_half = jnp.where(first, own_half, got_half)
-    second_half = jnp.where(first, got_half, own_half)
-    first_logs = jnp.where(first, logs, got_logs)
-    second_logs = jnp.where(first, got_logs, logs)
-    first_logs_half = lax.dynamic_slice_in_dim(first_logs, mine, half)
-    second_logs_half = lax.dynamic_slice_in_dim(second_logs, mine, half)
-    chip_state = jnp.exp(second_logs_half)[:, None, None] * first_half + second_half
-    chip_logs = first_logs_half + second_logs_half
-
-    window_state, window_log = send_with_logs(chip_state, chip_logs, axis, shift_perm(count, 2, forward))
+    levels = []
+    for bit in (1, 2):
+        state, logs, saved = pair_down(state, logs, axis, bit, forward)
+        levels.append((bit, saved))
+    stride = 4
+    groups = count // stride
+    window_state, window_log = send_with_logs(state, logs, axis, shift_perm(count, stride, forward))
     width = 1
-    while width < chips:
-        if width * 2 < chips:
-            got_state, got_log = send_with_logs(
-                window_state, window_log, axis, shift_perm(count, 2 * width, forward)
-            )
+    while width < groups:
+        perm = shift_perm(count, stride * width, forward)
+        if width * 2 < groups:
+            got_state, got_log = send_with_logs(window_state, window_log, axis, perm)
             window_log_next = window_log + got_log
         else:
-            got_state = shift(window_state, axis, 2 * width, forward)
+            got_state = lax.ppermute(window_state, axis, perm)
             window_log_next = window_log
         window_state = window_state + jnp.exp(window_log)[:, None, None] * got_state
         window_log = window_log_next
         width *= 2
-
-    second_state = jnp.exp(first_logs_half)[:, None, None] * window_state + first_half
-    keep = jnp.where(first, window_state, second_state)
-    send = jnp.where(first, second_state, window_state)
-    got = lax.ppermute(send, axis, swap)
-    return jnp.where(
-        core == 0, jnp.concatenate([keep, got], axis=0), jnp.concatenate([got, keep], axis=0)
-    )
+    for bit, saved in reversed(levels):
+        window_state = pair_up(window_state, saved, axis, bit, forward)
+    return window_state
 
 
 def split_bf16(value):

time: 224 us -> 203 us (0.906)
  waiting for transfers between devices: 124 us -> 111 us
  matrix products: 12.2 us -> 8.74 us
  other arithmetic: 9.87 us -> 6.44 us
    ppermute x10, waiting for transfers between devices: 89.2 us -> 55.7 us  [send_with_logs(): got = lax.ppermute(payload, axis, perm)]
    all_gather x1, waiting for transfers between devices: 14.3 us -> 24.9 us  [local(): every = lax.all_gather(packed, 'seq', axis=0, tiled=True)]
    ppermute x4 -> x6, waiting for transfers between devices: 15.2 us -> 24.8 us  [the longest x2 13.2 us: exclusive_scan(): got_state = lax.ppermute(window_state, axis, perm)]
    ppermute x10, starting transfers between devices: 35.5 us -> 26.6 us  [send_with_logs(): got = lax.ppermute(payload, axis, perm)]
    ppermute x4 -> x6, starting transfers between devices: 2.98 us -> 9.92 us  [the longest x2 7.3 us: exclusive_scan(): got_state = lax.ppermute(window_state, axis, perm)]
    all_to_all x1, starting transfers between devices: 3.66 us -> 6.1 us  [mp_sum_scatter(): return jnp.sum(lax.all_to_all(blocks, axis, 0, 0), axis=0)]
  transfers between devices with their start and end apart: 16 -> 18, of which waited for: 13 -> 15; matrix products, arithmetic and copies ran while one was open for 8% -> 5% of each run, Pallas kernels for 5% -> 5%
where the time goes in v6:
time: 203 us; the launch traced here: 201 us
  waiting for transfers between devices  111 us (55%)
  starting transfers between devices  42.6 us (21%)
  between operations  14.7 us (7%)
  Pallas kernels  11 us (5%)
  matrix products  8.74 us (4%)
  local copies, waits for them, and re-layouts  7.39 us (4%)
  other arithmetic  6.44 us (3%)
    ppermute x10, waiting for transfers between devices, send_with_logs(): got = lax.ppermute(payload, axis, perm)  55.7 us
    ppermute x10, starting transfers between devices, send_with_logs(): got = lax.ppermute(payload, axis, perm)  26.6 us
    all_gather x1, waiting for transfers between devices, local(): every = lax.all_gather(packed, 'seq', axis=0, tiled=True)  24.9 us
    ppermute x2, waiting for transfers between devices, exclusive_scan(): got_state = lax.ppermute(window_state, axis, perm)  13.2 us
    ppermute x4, waiting for transfers between devices, pair_up(): got = lax.ppermute(send, axis, [(j, j ^ bit) for j in range(count)])  11.6 us
    pallas_call x1, Pallas kernels, attend(): pl.pallas_call(functools.partial(attend_kernel, heads=heads), out_shape=j...  11 us
    ppermute x2, starting transfers between devices, exclusive_scan(): got_state = lax.ppermute(window_state, axis, perm)  7.3 us
    all_to_all x1, starting transfers between devices, mp_sum_scatter(): return jnp.sum(lax.all_to_all(blocks, axis, 0, 0), axis=0)  6.1 us
  transfers between devices with their start and end apart: 18, of which 15 were waited for; matrix products, arithmetic and copies ran while one was open for 5% of the time, Pallas kernels for 5%

profile of v6, /device:TPU:68, one launch (start us, length us, event | category | flops | bytes accessed | tf_op | source)
XLA Modules:
  0.0 201.3 jit_solution(17687304233611332326)
XLA Ops:
  7.2 0.8 copy.61
  8.4 1.1 copy.64
  9.5 0.4 fusion.7
  10.2 0.9 reduce-precision_convert_fusion
  11.1 1.4 pad_maximum_fusion.11
  13.1 0.6 collective-permute-start.1
  13.7 7.0 %collective-permute-done.1 = f32[264,128]{1,0:T(8,128)S(1)} collective-permute-done((f32[264,128]{1,0:T(8,128)S(1)}, f32[264,128]{1,0:T(8,128)S(1)}, u32[]{:S(2)}, u32[]{:S(2)}) %collective-permute-start.1) | collective-permute-done | bytes 135200 | tf_op jit(solution)/shard_map/ppermute | solution.py:32
  21.1 3.8 %collective-permute-start.2 = (f32[264,128]{0,1:T(8,128)S(1)}, f32[264,128]{0,1:T(8,128)S(1)}, u32[]{:S(2)}, u32[]{:S(2)}) collective-permute-start(f32[264,128]{0,1:T(8,128)S(1)} %pad_maximum_fusion.2), channel_id=1, source_target_pairs={{0,32},{8,40},{16,48},{24,56},{32,64},{40,72},{48,80},{56,88},{64,... | collective-permute-start | bytes 405512 | tf_op jit(solution)/shard_map/ppermute | solution.py:32
  25.0 5.1 %collective-permute-done.2 = f32[264,128]{0,1:T(8,128)S(1)} collective-permute-done((f32[264,128]{0,1:T(8,128)S(1)}, f32[264,128]{0,1:T(8,128)S(1)}, u32[]{:S(2)}, u32[]{:S(2)}) %collective-permute-start.2) | collective-permute-done | bytes 135200 | tf_op jit(solution)/shard_map/ppermute | solution.py:32
  30.1 4.5 %collective-permute-start.3 = (f32[264,128]{0,1:T(8,128)S(1)}, f32[264,128]{0,1:T(8,128)S(1)}, u32[]{:S(2)}, u32[]{:S(2)}) collective-permute-start(f32[264,128]{0,1:T(8,128)S(1)} %pad_maximum_fusion.3), channel_id=1, source_target_pairs={{0,32},{8,40},{16,48},{24,56},{32,64},{40,72},{48,80},{56,88},{64,... | collective-permute-start | bytes 405512 | tf_op jit(solution)/shard_map/ppermute | solution.py:32
  34.8 3.6 %collective-permute-done.3 = f32[264,128]{0,1:T(8,128)S(1)} collective-permute-done((f32[264,128]{0,1:T(8,128)S(1)}, f32[264,128]{0,1:T(8,128)S(1)}, u32[]{:S(2)}, u32[]{:S(2)}) %collective-permute-start.3) | collective-permute-done | bytes 135200 | tf_op jit(solution)/shard_map/ppermute | solution.py:32
  38.5 8.9 %collective-permute-start.4 = (f32[264,128]{0,1:T(8,128)S(1)}, f32[264,128]{0,1:T(8,128)S(1)}, u32[]{:S(2)}, u32[]{:S(2)}) collective-permute-start(f32[264,128]{0,1:T(8,128)S(1)} %pad_maximum_fusion.4), channel_id=1, source_target_pairs={{0,64},{8,72},{16,80},{24,88},{32,96},{40,104},{48,112},{56,120},{... | collective-permute-start | bytes 405512 | tf_op jit(solution)/shard_map/ppermute | solution.py:32
  47.6 6.5 %collective-permute-done.4 = f32[264,128]{0,1:T(8,128)S(1)} collective-permute-done((f32[264,128]{0,1:T(8,128)S(1)}, f32[264,128]{0,1:T(8,128)S(1)}, u32[]{:S(2)}, u32[]{:S(2)}) %collective-permute-start.4) | collective-permute-done | bytes 135200 | tf_op jit(solution)/shard_map/ppermute | solution.py:32
  54.3 5.8 %collective-permute-start.5 = (f32[2,128,128]{2,1,0:T(8,128)S(1)}, f32[2,128,128]{2,1,0:T(8,128)S(1)}, u32[]{:S(2)}, u32[]{:S(2)}) collective-permute-start(f32[2,128,128]{2,1,0:T(8,128)S(1)} %multiply_add_fusion.8), channel_id=1, source_target_pairs={{0,128},{8,136},{16,144},{24,152},{32,160},{40,168},{48,176},{56,1... | collective-permute-start | bytes 393224 | tf_op jit(solution)/shard_map/ppermute | solution.py:95
  60.4 0.8 reshape.231.query_ref
  61.3 4.2 %collective-permute-done.5 = f32[2,128,128]{2,1,0:T(8,128)S(1)} collective-permute-done((f32[2,128,128]{2,1,0:T(8,128)S(1)}, f32[2,128,128]{2,1,0:T(8,128)S(1)}, u32[]{:S(2)}, u32[]{:S(2)}) %collective-permute-start.5) | collective-permute-done | bytes 131104 | tf_op jit(solution)/shard_map/ppermute | solution.py:95
  65.7 0.7 convolution_bitcast_fusion.1
  66.3 8.5 %collective-permute-done.6 = f32[2,128,128]{2,1,0:T(8,128)S(1)} collective-permute-done((f32[2,128,128]{2,1,0:T(8,128)S(1)}, f32[2,128,128]{2,1,0:T(8,128)S(1)}, u32[]{:S(2)}, u32[]{:S(2)}) %collective-permute-start.6) | collective-permute-done | bytes 131104 | tf_op jit(solution)/shard_map/ppermute | solution.py:73
  75.0 24.9 %all-gather.2.cloned.1.call-done.key_ref.upper_ref.lower_ref = bf16[4096,384]{1,0:T(8,128)(2,1)} async-done(((bf16[128,384]{1,0:T(8,128)(2,1)}), bf16[4096,384]{1,0:T(8,128)(2,1)}) %all-gather.2.cloned.1.call-update) | async-done | bytes 3145744 | tf_op jit(solution)/shard_map/all_gather | solution.py:200
  99.9 11.0 %shard_map.94 = f32[1024,128]{1,0:T(8,128)} custom-call(s32[1]{0:T(128)} %bitcast.21.first_ref, bf16[1024,128]{1,0:T(8,128)(2,1)} %reshape.231.query_ref, bf16[4096,384]{1,0:T(8,128)(2,1)} %all-gather.2.cloned.1.call-done.key_ref.upper_ref.lower_ref, bf16[4096,384]{1,0:T(8,128)(2,1)} %all-gather.2.cloned.1.call-done.key_ref.upper_ref.lower_ref, ...), custom_call_target="tpu_custom_call" | custom-call | flops 4294967296 | bytes 3932160 | tf_op jit(solution)/shard_map/pallas_call | solution.py:163
  110.9 1.7 fusion.3
  112.6 1.1 fusion.12
  114.3 1.3 collective-permute-done.8
  116.0 2.1 %collective-permute-start.9 = (f32[264,128]{1,0:T(8,128)S(1)}, f32[264,128]{1,0:T(8,128)S(1)}, u32[]{:S(2)}, u32[]{:S(2)}) collective-permute-start(f32[264,128]{1,0:T(8,128)S(1)} %pad_maximum_fusion.9), channel_id=1, source_target_pairs={{0,16},{8,24},{16,0},{24,8},{32,48},{40,56},{48,32},{56,40},{64,80... | collective-permute-start | bytes 405512 | tf_op jit(solution)/shard_map/ppermute | solution.py:32
  118.1 5.2 %collective-permute-done.9 = f32[264,128]{1,0:T(8,128)S(1)} collective-permute-done((f32[264,128]{1,0:T(8,128)S(1)}, f32[264,128]{1,0:T(8,128)S(1)}, u32[]{:S(2)}, u32[]{:S(2)}) %collective-permute-start.9) | collective-permute-done | bytes 135200 | tf_op jit(solution)/shard_map/ppermute | solution.py:32
  123.8 2.4 %collective-permute-start.10 = (f32[264,128]{0,1:T(8,128)S(1)}, f32[264,128]{0,1:T(8,128)S(1)}, u32[]{:S(2)}, u32[]{:S(2)}) collective-permute-start(f32[264,128]{0,1:T(8,128)S(1)} %pad_maximum_fusion.5), channel_id=1, source_target_pairs={{32,0},{40,8},{48,16},{56,24},{64,32},{72,40},{80,48},{88,56},{96,... | collective-permute-start | bytes 405512 | tf_op jit(solution)/shard_map/ppermute | solution.py:32
  126.2 8.8 %collective-permute-done.10 = f32[264,128]{0,1:T(8,128)S(1)} collective-permute-done((f32[264,128]{0,1:T(8,128)S(1)}, f32[264,128]{0,1:T(8,128)S(1)}, u32[]{:S(2)}, u32[]{:S(2)}) %collective-permute-start.10) | collective-permute-done | bytes 135200 | tf_op jit(solution)/shard_map/ppermute | solution.py:32
  135.1 1.9 collective-permute-start.11
  137.1 6.5 %collective-permute-done.11 = f32[264,128]{0,1:T(8,128)S(1)} collective-permute-done((f32[264,128]{0,1:T(8,128)S(1)}, f32[264,128]{0,1:T(8,128)S(1)}, u32[]{:S(2)}, u32[]{:S(2)}) %collective-permute-start.11) | collective-permute-done | bytes 135200 | tf_op jit(solution)/shard_map/ppermute | solution.py:32
  143.6 0.7 pad_maximum_fusion.7
  144.3 1.9 collective-permute-start.12
  146.2 0.4 fusion.4
  146.8 11.6 %collective-permute-done.12 = f32[264,128]{0,1:T(8,128)} collective-permute-done((f32[264,128]{0,1:T(8,128)}, f32[264,128]{0,1:T(8,128)}, u32[]{:S(2)}, u32[]{:S(2)}) %collective-permute-start.12) | collective-permute-done | bytes 135200 | tf_op jit(solution)/shard_map/ppermute | solution.py:32
  158.4 0.9 slice.111
  159.4 0.7 fusion.53
  160.2 1.5 collective-permute-start.13
  162.0 9.0 %collective-permute-done.13 = f32[2,128,128]{2,1,0:T(8,128)S(1)} collective-permute-done((f32[2,128,128]{2,1,0:T(8,128)S(1)}, f32[2,128,128]{2,1,0:T(8,128)S(1)}, u32[]{:S(2)}, u32[]{:S(2)}) %collective-permute-start.13) | collective-permute-done | bytes 131104 | tf_op jit(solution)/shard_map/ppermute | solution.py:95
  171.1 2.3 %collective-permute-start.14 = (f32[2,128,128]{2,1,0:T(8,128)S(1)}, f32[2,128,128]{2,1,0:T(8,128)S(1)}, u32[]{:S(2)}, u32[]{:S(2)}) collective-permute-start(f32[2,128,128]{2,1,0:T(8,128)S(1)} %get-tuple-element.25), channel_id=1, source_target_pairs={{0,16},{8,24},{16,0},{24,8},{32,48},{40,56},{48,32},{56,40},{64,80... | collective-permute-start | bytes 393224 | tf_op jit(solution)/shard_map/ppermute | solution.py:73
  173.5 1.2 fusion.6
  174.6 3.1 %collective-permute-done.14 = f32[2,128,128]{2,1,0:T(8,128)S(1)} collective-permute-done((f32[2,128,128]{2,1,0:T(8,128)S(1)}, f32[2,128,128]{2,1,0:T(8,128)S(1)}, u32[]{:S(2)}, u32[]{:S(2)}) %collective-permute-start.14) | collective-permute-done | bytes 131104 | tf_op jit(solution)/shard_map/ppermute | solution.py:73
  178.2 1.2 convolution_bitcast_fusion.2
  179.4 1.0 fusion.5
  180.4 0.7 copy.83
  181.2 6.1 %all-to-all-start = ((f32[8,16,256]{2,1,0:T(8,128)}), f32[8,16,256]{2,1,0:T(8,128)S(1)}, u32[]{:S(2)}, u32[]{:S(2)}) async-start(f32[8,16,256]{2,1,0:T(8,128)} %bitcast.41), calls=%async_computation | async-start | bytes 262144 | tf_op jit(solution)/shard_map/all_to_all | solution.py:113
  187.3 0.4 fusion.1
  187.7 1.0 copy.84
  188.7 5.2 %all-to-all-done = f32[8,16,256]{2,1,0:T(8,128)S(1)} async-done(((f32[8,16,256]{2,1,0:T(8,128)}), f32[8,16,256]{2,1,0:T(8,128)S(1)}, u32[]{:S(2)}, u32[]{:S(2)}) %all-to-all-start) | async-done | bytes 131104 | tf_op jit(solution)/shard_map/all_to_all | solution.py:113
  193.9 0.6 slice_multiply_fusion
  (104 shorter events, 5.6 us)
Async XLA Ops:
  7.2 2.4 %copy-start = (bf16[128,128]{1,0:T(8,128)(2,1)S(1)}, bf16[128,128]{1,0:T(8,128)(2,1)}, u32[]{:S(2)}) copy-start(bf16[128,128]{1,0:T(8,128)(2,1)} %param.11) | copy-start | bytes 98308
  7.2 92.7 %all-gather.2.cloned.1.call-start = ((), (), s32[]{:S(2)}) async-start(), calls=%async_computation.1 | async-start | bytes 3244032 | tf_op jit(solution)/shard_map/all_gather | solution.py:200
  10.1 2.4 %collective-permute-start = (f32[520,128]{1,0:T(8,128)S(1)}, f32[520,128]{1,0:T(8,128)S(1)}, u32[]{:S(2)}, u32[]{:S(2)}) collective-permute-start(f32[520,128]{1,0:T(8,128)S(1)} %pad_maximum_fusion), channel_id=1, source_target_pairs={{0,8},{8,0},{16,24},{24,16},{32,40},{40,32},{48,56},{56,48},{64,72... | collective-permute-start | bytes 798728 | tf_op jit(solution)/shard_map/ppermute | solution.py:32
  12.5 47.7 %copy-start.1 = (bf16[128,128]{1,0:T(8,128)(2,1)S(1)}, bf16[128,128]{1,0:T(8,128)(2,1)}, u32[]{:S(2)}) copy-start(bf16[128,128]{1,0:T(8,128)(2,1)} %param.12) | copy-start | bytes 98308
  12.8 47.6 %copy-start.2 = (bf16[128,1024]{1,0:T(8,128)(2,1)S(1)}, bf16[128,1024]{1,0:T(8,128)(2,1)}, u32[]{:S(2)}) copy-start(bf16[128,1024]{1,0:T(8,128)(2,1)} %param.7) | copy-start | bytes 786436
  13.1 7.6 %collective-permute-start.1 = (f32[264,128]{1,0:T(8,128)S(1)}, f32[264,128]{1,0:T(8,128)S(1)}, u32[]{:S(2)}, u32[]{:S(2)}) collective-permute-start(f32[264,128]{1,0:T(8,128)S(1)} %pad_maximum_fusion.8), channel_id=1, source_target_pairs={{0,16},{8,24},{16,0},{24,8},{32,48},{40,56},{48,32},{56,40},{64,80... | collective-permute-start | bytes 405512 | tf_op jit(solution)/shard_map/ppermute | solution.py:32
  21.1 8.9 %collective-permute-start.2 = (f32[264,128]{0,1:T(8,128)S(1)}, f32[264,128]{0,1:T(8,128)S(1)}, u32[]{:S(2)}, u32[]{:S(2)}) collective-permute-start(f32[264,128]{0,1:T(8,128)S(1)} %pad_maximum_fusion.2), channel_id=1, source_target_pairs={{0,32},{8,40},{16,48},{24,56},{32,64},{40,72},{48,80},{56,88},{64,... | collective-permute-start | bytes 405512 | tf_op jit(solution)/shard_map/ppermute | solution.py:32
  30.1 8.3 %collective-permute-start.3 = (f32[264,128]{0,1:T(8,128)S(1)}, f32[264,128]{0,1:T(8,128)S(1)}, u32[]{:S(2)}, u32[]{:S(2)}) collective-permute-start(f32[264,128]{0,1:T(8,128)S(1)} %pad_maximum_fusion.3), channel_id=1, source_target_pairs={{0,32},{8,40},{16,48},{24,56},{32,64},{40,72},{48,80},{56,88},{64,... | collective-permute-start | bytes 405512 | tf_op jit(solution)/shard_map/ppermute | solution.py:32
  38.5 15.6 %collective-permute-start.4 = (f32[264,128]{0,1:T(8,128)S(1)}, f32[264,128]{0,1:T(8,128)S(1)}, u32[]{:S(2)}, u32[]{:S(2)}) collective-permute-start(f32[264,128]{0,1:T(8,128)S(1)} %pad_maximum_fusion.4), channel_id=1, source_target_pairs={{0,64},{8,72},{16,80},{24,88},{32,96},{40,104},{48,112},{56,120},{... | collective-permute-start | bytes 405512 | tf_op jit(solution)/shard_map/ppermute | solution.py:32
  54.3 11.1 %collective-permute-start.5 = (f32[2,128,128]{2,1,0:T(8,128)S(1)}, f32[2,128,128]{2,1,0:T(8,128)S(1)}, u32[]{:S(2)}, u32[]{:S(2)}) collective-permute-start(f32[2,128,128]{2,1,0:T(8,128)S(1)} %multiply_add_fusion.8), channel_id=1, source_target_pairs={{0,128},{8,136},{16,144},{24,152},{32,160},{40,168},{48,176},{56,1... | collective-permute-start | bytes 393224 | tf_op jit(solution)/shard_map/ppermute | solution.py:95
  65.6 9.3 %collective-permute-start.6 = (f32[2,128,128]{2,1,0:T(8,128)S(1)}, f32[2,128,128]{2,1,0:T(8,128)S(1)}, u32[]{:S(2)}, u32[]{:S(2)}) collective-permute-start(f32[2,128,128]{2,1,0:T(8,128)S(1)} %get-tuple-element.27), channel_id=1, source_target_pairs={{0,16},{8,24},{16,0},{24,8},{32,48},{40,56},{48,32},{56,40},{64,80... | collective-permute-start | bytes 393224 | tf_op jit(solution)/shard_map/ppermute | solution.py:73
  74.9 35.9 %collective-permute-start.7 = (f32[4,128,128]{2,1,0:T(8,128)S(1)}, f32[4,128,128]{2,1,0:T(8,128)S(1)}, u32[]{:S(2)}, u32[]{:S(2)}) collective-permute-start(f32[4,128,128]{2,1,0:T(8,128)S(1)} %get-tuple-element.22), channel_id=1, source_target_pairs={{0,8},{8,0},{16,24},{24,16},{32,40},{40,32},{48,56},{56,48},{64,72... | collective-permute-start | bytes 786440 | tf_op jit(solution)/shard_map/ppermute | solution.py:73
  113.9 1.6 collective-permute-start.8
  116.0 7.3 %collective-permute-start.9 = (f32[264,128]{1,0:T(8,128)S(1)}, f32[264,128]{1,0:T(8,128)S(1)}, u32[]{:S(2)}, u32[]{:S(2)}) collective-permute-start(f32[264,128]{1,0:T(8,128)S(1)} %pad_maximum_fusion.9), channel_id=1, source_target_pairs={{0,16},{8,24},{16,0},{24,8},{32,48},{40,56},{48,32},{56,40},{64,80... | collective-permute-start | bytes 405512 | tf_op jit(solution)/shard_map/ppermute | solution.py:32
  123.8 11.2 %collective-permute-start.10 = (f32[264,128]{0,1:T(8,128)S(1)}, f32[264,128]{0,1:T(8,128)S(1)}, u32[]{:S(2)}, u32[]{:S(2)}) collective-permute-start(f32[264,128]{0,1:T(8,128)S(1)} %pad_maximum_fusion.5), channel_id=1, source_target_pairs={{32,0},{40,8},{48,16},{56,24},{64,32},{72,40},{80,48},{88,56},{96,... | collective-permute-start | bytes 405512 | tf_op jit(solution)/shard_map/ppermute | solution.py:32
  135.1 8.5 %collective-permute-start.11 = (f32[264,128]{0,1:T(8,128)S(1)}, f32[264,128]{0,1:T(8,128)S(1)}, u32[]{:S(2)}, u32[]{:S(2)}) collective-permute-start(f32[264,128]{0,1:T(8,128)S(1)} %pad_maximum_fusion.6), channel_id=1, source_target_pairs={{32,0},{40,8},{48,16},{56,24},{64,32},{72,40},{80,48},{88,56},{96,... | collective-permute-start | bytes 405512 | tf_op jit(solution)/shard_map/ppermute | solution.py:32
  143.5 0.7 copy-start.3
  144.3 14.1 %collective-permute-start.12 = (f32[264,128]{0,1:T(8,128)}, f32[264,128]{0,1:T(8,128)}, u32[]{:S(2)}, u32[]{:S(2)}) collective-permute-start(f32[264,128]{0,1:T(8,128)} %pad_maximum_fusion.7), channel_id=1, source_target_pairs={{64,0},{72,8},{80,16},{88,24},{96,32},{104,40},{112,48},{120,56},{... | collective-permute-start | bytes 405512 | tf_op jit(solution)/shard_map/ppermute | solution.py:32
  160.2 10.8 %collective-permute-start.13 = (f32[2,128,128]{2,1,0:T(8,128)S(1)}, f32[2,128,128]{2,1,0:T(8,128)S(1)}, u32[]{:S(2)}, u32[]{:S(2)}) collective-permute-start(f32[2,128,128]{2,1,0:T(8,128)S(1)} %multiply_add_fusion.4), channel_id=1, source_target_pairs={{128,0},{136,8},{144,16},{152,24},{160,32},{168,40},{176,48},{184,... | collective-permute-start | bytes 393224 | tf_op jit(solution)/shard_map/ppermute | solution.py:95
  171.1 6.6 %collective-permute-start.14 = (f32[2,128,128]{2,1,0:T(8,128)S(1)}, f32[2,128,128]{2,1,0:T(8,128)S(1)}, u32[]{:S(2)}, u32[]{:S(2)}) collective-permute-start(f32[2,128,128]{2,1,0:T(8,128)S(1)} %get-tuple-element.25), channel_id=1, source_target_pairs={{0,16},{8,24},{16,0},{24,8},{32,48},{40,56},{48,32},{56,40},{64,80... | collective-permute-start | bytes 393224 | tf_op jit(solution)/shard_map/ppermute | solution.py:73
  177.8 1.6 collective-permute-start.15
  181.2 12.7 %all-to-all-start = ((f32[8,16,256]{2,1,0:T(8,128)}), f32[8,16,256]{2,1,0:T(8,128)S(1)}, u32[]{:S(2)}, u32[]{:S(2)}) async-start(f32[8,16,256]{2,1,0:T(8,128)} %bitcast.41), calls=%async_computation | async-start | bytes 262144 | tf_op jit(solution)/shard_map/all_to_all | solution.py:113
Sparse Core Ops, SparseCore 0:
  12.6 87.2 all-gather.1

commit v7 on v6

--- a/solution.py
+++ b/solution.py
@@ -100,6 +100,20 @@
     for bit, saved in reversed(levels):
         window_state = pair_up(window_state, saved, axis, bit, forward)
     return window_state
+
+
+def gather_blocks(block, axis):
+    count = lax.axis_size(axis)
+    index = lax.axis_index(axis)
+    pieces = block
+    for bit in (1, 2):
+        got = lax.ppermute(pieces, axis, [(j, j ^ bit) for j in range(count)])
+        upper = (index // bit) % 2 == 1
+        pieces = jnp.where(
+            upper, jnp.concatenate([got, pieces], axis=0), jnp.concatenate([pieces, got], axis=0)
+        )
+    groups = [[z * 4 + r for z in range(count // 4)] for r in range(4)]
+    return lax.all_gather(pieces, axis, axis=0, tiled=True, axis_index_groups=groups)
 
 
 def split_bf16(value):
@@ -197,7 +211,7 @@
 
     values_hi, values_lo = split_bf16(values)
     packed = jnp.concatenate([keys, values_hi, values_lo], axis=1)
-    every = lax.all_gather(packed, "seq", axis=0, tiled=True)
+    every = gather_blocks(packed, "seq")
 
     c_scale = 0.5 / math.sqrt(N * row_count * seq_count)
     student_x = inputs_x.astype(jnp.float32).reshape(row_count, heads, HEAD_WIDTH)

time: 203 us -> 196 us (0.966)
  waiting for transfers between devices: 111 us -> 104 us
    all_gather x1, waiting for transfers between devices: 24.9 us -> 0.02 us  [gather_blocks(): lax.all_gather(pieces, axis, axis=0, tiled=True, axis_index_groups=groups)]
    ppermute x10, waiting for transfers between devices: 55.7 us -> 68 us  [send_with_logs(): got = lax.ppermute(payload, axis, perm)]
    ppermute x0 -> x2, waiting for transfers between devices: none -> 8.89 us  [gather_blocks(): got = lax.ppermute(pieces, axis, [(j, j ^ bit) for j in range(count)])]
    ppermute x10, starting transfers between devices: 26.6 us -> 30.1 us  [send_with_logs(): got = lax.ppermute(payload, axis, perm)]
    ppermute x2, starting transfers between devices: 7.3 us -> 4.34 us  [exclusive_scan(): got_state = lax.ppermute(window_state, axis, perm)]
  transfers between devices with their start and end apart: 18 -> 20, of which waited for: 15 -> 16; matrix products, arithmetic and copies ran while one was open for 5% -> 5% of each run, Pallas kernels for 5% -> 6%
where the time goes in v7:
time: 196 us; the launch traced here: 195 us
  waiting for transfers between devices  104 us (53%)
  starting transfers between devices  42.1 us (21%)
  between operations  14.6 us (7%)
  Pallas kernels  11 us (6%)
  matrix products  8.74 us (4%)
  local copies, waits for them, and re-layouts  7.42 us (4%)
  other arithmetic  6.69 us (3%)
    ppermute x10, waiting for transfers between devices, send_with_logs(): got = lax.ppermute(payload, axis, perm)  68 us
    ppermute x10, starting transfers between devices, send_with_logs(): got = lax.ppermute(payload, axis, perm)  30.1 us
    ppermute x2, waiting for transfers between devices, exclusive_scan(): got_state = lax.ppermute(window_state, axis, perm)  12.2 us
    pallas_call x1, Pallas kernels, attend(): pl.pallas_call(functools.partial(attend_kernel, heads=heads), out_shape=j...  11 us
    ppermute x4, waiting for transfers between devices, pair_up(): got = lax.ppermute(send, axis, [(j, j ^ bit) for j in range(count)])  10.1 us
    ppermute x2, waiting for transfers between devices, gather_blocks(): got = lax.ppermute(pieces, axis, [(j, j ^ bit) for j in range(count)])  8.89 us
    all_to_all x1, waiting for transfers between devices, mp_sum_scatter(): return jnp.sum(lax.all_to_all(blocks, axis, 0, 0), axis=0)  5.19 us
    all_to_all x1, starting transfers between devices, mp_sum_scatter(): return jnp.sum(lax.all_to_all(blocks, axis, 0, 0), axis=0)  5.08 us
  transfers between devices with their start and end apart: 20, of which 16 were waited for; matrix products, arithmetic and copies ran while one was open for 5% of the time, Pallas kernels for 6%

profile of v7, /device:TPU:68, one launch (start us, length us, event | category | flops | bytes accessed | tf_op | source)
XLA Modules:
  0.0 195.0 jit_solution(2195823606183405469)
XLA Ops:
  7.3 0.8 copy.61
  8.4 1.1 copy.64
  10.2 0.9 reduce-precision_convert_fusion
  11.1 0.8 pad_maximum_fusion.11
  12.4 0.9 collective-permute-done.8
  13.4 0.6 collective-permute-start.9
  14.2 8.0 %collective-permute-done.9 = bf16[256,384]{1,0:T(8,128)(2,1)S(1)} collective-permute-done((bf16[256,384]{1,0:T(8,128)(2,1)S(1)}, bf16[256,384]{1,0:T(8,128)(2,1)S(1)}, u32[]{:S(2)}, u32[]{:S(2)}) %collective-permute-start.9) | collective-permute-done | bytes 196640 | tf_op jit(solution)/shard_map/ppermute | solution.py:110
  22.2 0.9 maximum_select_fusion.2
  24.1 6.0 %collective-permute-done.1 = f32[264,128]{1,0:T(8,128)S(1)} collective-permute-done((f32[264,128]{1,0:T(8,128)S(1)}, f32[264,128]{1,0:T(8,128)S(1)}, u32[]{:S(2)}, u32[]{:S(2)}) %collective-permute-start.1) | collective-permute-done | bytes 135200 | tf_op jit(solution)/shard_map/ppermute | solution.py:32
  30.5 3.8 %collective-permute-start.2 = (f32[264,128]{0,1:T(8,128)S(1)}, f32[264,128]{0,1:T(8,128)S(1)}, u32[]{:S(2)}, u32[]{:S(2)}) collective-permute-start(f32[264,128]{0,1:T(8,128)S(1)} %pad_maximum_fusion.2), channel_id=1, source_target_pairs={{0,32},{8,40},{16,48},{24,56},{32,64},{40,72},{48,80},{56,88},{64,... | collective-permute-start | bytes 405512 | tf_op jit(solution)/shard_map/ppermute | solution.py:32
  34.4 5.1 %collective-permute-done.2 = f32[264,128]{0,1:T(8,128)S(1)} collective-permute-done((f32[264,128]{0,1:T(8,128)S(1)}, f32[264,128]{0,1:T(8,128)S(1)}, u32[]{:S(2)}, u32[]{:S(2)}) %collective-permute-start.2) | collective-permute-done | bytes 135200 | tf_op jit(solution)/shard_map/ppermute | solution.py:32
  39.5 7.4 %collective-permute-start.3 = (f32[264,128]{0,1:T(8,128)S(1)}, f32[264,128]{0,1:T(8,128)S(1)}, u32[]{:S(2)}, u32[]{:S(2)}) collective-permute-start(f32[264,128]{0,1:T(8,128)S(1)} %pad_maximum_fusion.3), channel_id=1, source_target_pairs={{0,32},{8,40},{16,48},{24,56},{32,64},{40,72},{48,80},{56,88},{64,... | collective-permute-start | bytes 405512 | tf_op jit(solution)/shard_map/ppermute | solution.py:32
  47.0 7.1 %collective-permute-done.3 = f32[264,128]{0,1:T(8,128)S(1)} collective-permute-done((f32[264,128]{0,1:T(8,128)S(1)}, f32[264,128]{0,1:T(8,128)S(1)}, u32[]{:S(2)}, u32[]{:S(2)}) %collective-permute-start.3) | collective-permute-done | bytes 135200 | tf_op jit(solution)/shard_map/ppermute | solution.py:32
  54.2 10.8 %collective-permute-start.4 = (f32[264,128]{0,1:T(8,128)S(1)}, f32[264,128]{0,1:T(8,128)S(1)}, u32[]{:S(2)}, u32[]{:S(2)}) collective-permute-start(f32[264,128]{0,1:T(8,128)S(1)} %pad_maximum_fusion.4), channel_id=1, source_target_pairs={{0,64},{8,72},{16,80},{24,88},{32,96},{40,104},{48,112},{56,120},{... | collective-permute-start | bytes 405512 | tf_op jit(solution)/shard_map/ppermute | solution.py:32
  65.2 11.3 %collective-permute-done.4 = f32[264,128]{0,1:T(8,128)S(1)} collective-permute-done((f32[264,128]{0,1:T(8,128)S(1)}, f32[264,128]{0,1:T(8,128)S(1)}, u32[]{:S(2)}, u32[]{:S(2)}) %collective-permute-start.4) | collective-permute-done | bytes 135200 | tf_op jit(solution)/shard_map/ppermute | solution.py:32
  76.7 3.0 %collective-permute-start.5 = (f32[2,128,128]{2,1,0:T(8,128)S(1)}, f32[2,128,128]{2,1,0:T(8,128)S(1)}, u32[]{:S(2)}, u32[]{:S(2)}) collective-permute-start(f32[2,128,128]{2,1,0:T(8,128)S(1)} %multiply_add_fusion.8), channel_id=1, source_target_pairs={{0,128},{8,136},{16,144},{24,152},{32,160},{40,168},{48,176},{56,1... | collective-permute-start | bytes 393224 | tf_op jit(solution)/shard_map/ppermute | solution.py:95
  80.0 0.8 reshape.231.query_ref
  80.9 3.0 %collective-permute-done.5 = f32[2,128,128]{2,1,0:T(8,128)S(1)} collective-permute-done((f32[2,128,128]{2,1,0:T(8,128)S(1)}, f32[2,128,128]{2,1,0:T(8,128)S(1)}, u32[]{:S(2)}, u32[]{:S(2)}) %collective-permute-start.5) | collective-permute-done | bytes 131104 | tf_op jit(solution)/shard_map/ppermute | solution.py:95
  84.0 0.6 collective-permute-start.6
  84.6 0.7 convolution_bitcast_fusion.1
  85.3 5.3 %collective-permute-done.6 = f32[2,128,128]{2,1,0:T(8,128)S(1)} collective-permute-done((f32[2,128,128]{2,1,0:T(8,128)S(1)}, f32[2,128,128]{2,1,0:T(8,128)S(1)}, u32[]{:S(2)}, u32[]{:S(2)}) %collective-permute-start.6) | collective-permute-done | bytes 131104 | tf_op jit(solution)/shard_map/ppermute | solution.py:73
  90.8 11.0 %shard_map.94 = f32[1024,128]{1,0:T(8,128)} custom-call(s32[1]{0:T(128)} %bitcast.21.first_ref, bf16[1024,128]{1,0:T(8,128)(2,1)} %reshape.231.query_ref, bf16[4096,384]{1,0:T(8,128)(2,1)} %all-gather.2.cloned.1.call-done.key_ref.upper_ref.lower_ref, bf16[4096,384]{1,0:T(8,128)(2,1)} %all-gather.2.cloned.1.call-done.key_ref.upper_ref.lower_ref, ...), custom_call_target="tpu_custom_call" | custom-call | flops 4294967296 | bytes 3932160 | tf_op jit(solution)/shard_map/pallas_call | solution.py:177
  101.8 1.7 fusion.3
  103.5 1.1 fusion.12
  105.4 1.2 collective-permute-done.10
  107.0 0.8 collective-permute-start.11
  107.8 6.8 %collective-permute-done.11 = f32[264,128]{1,0:T(8,128)S(1)} collective-permute-done((f32[264,128]{1,0:T(8,128)S(1)}, f32[264,128]{1,0:T(8,128)S(1)}, u32[]{:S(2)}, u32[]{:S(2)}) %collective-permute-start.11) | collective-permute-done | bytes 135200 | tf_op jit(solution)/shard_map/ppermute | solution.py:32
  115.1 1.9 collective-permute-start.12
  117.0 6.3 %collective-permute-done.12 = f32[264,128]{0,1:T(8,128)S(1)} collective-permute-done((f32[264,128]{0,1:T(8,128)S(1)}, f32[264,128]{0,1:T(8,128)S(1)}, u32[]{:S(2)}, u32[]{:S(2)}) %collective-permute-start.12) | collective-permute-done | bytes 135200 | tf_op jit(solution)/shard_map/ppermute | solution.py:32
  123.4 2.2 %collective-permute-start.13 = (f32[264,128]{0,1:T(8,128)S(1)}, f32[264,128]{0,1:T(8,128)S(1)}, u32[]{:S(2)}, u32[]{:S(2)}) collective-permute-start(f32[264,128]{0,1:T(8,128)S(1)} %pad_maximum_fusion.6), channel_id=1, source_target_pairs={{32,0},{40,8},{48,16},{56,24},{64,32},{72,40},{80,48},{88,56},{96,... | collective-permute-start | bytes 405512 | tf_op jit(solution)/shard_map/ppermute | solution.py:32
  125.7 13.9 %collective-permute-done.13 = f32[264,128]{0,1:T(8,128)S(1)} collective-permute-done((f32[264,128]{0,1:T(8,128)S(1)}, f32[264,128]{0,1:T(8,128)S(1)}, u32[]{:S(2)}, u32[]{:S(2)}) %collective-permute-start.13) | collective-permute-done | bytes 135200 | tf_op jit(solution)/shard_map/ppermute | solution.py:32
  139.6 0.7 pad_maximum_fusion.7
  140.3 1.9 collective-permute-start.14
  142.9 10.2 %collective-permute-done.14 = f32[264,128]{0,1:T(8,128)} collective-permute-done((f32[264,128]{0,1:T(8,128)}, f32[264,128]{0,1:T(8,128)}, u32[]{:S(2)}, u32[]{:S(2)}) %collective-permute-start.14) | collective-permute-done | bytes 135200 | tf_op jit(solution)/shard_map/ppermute | solution.py:32
  153.1 0.9 slice.111
  154.1 0.7 fusion.53
  154.9 1.3 collective-permute-start.15
  156.5 9.2 %collective-permute-done.15 = f32[2,128,128]{2,1,0:T(8,128)S(1)} collective-permute-done((f32[2,128,128]{2,1,0:T(8,128)S(1)}, f32[2,128,128]{2,1,0:T(8,128)S(1)}, u32[]{:S(2)}, u32[]{:S(2)}) %collective-permute-start.15) | collective-permute-done | bytes 131104 | tf_op jit(solution)/shard_map/ppermute | solution.py:95
  165.8 0.6 collective-permute-start.16
  166.4 1.1 fusion.6
  167.5 4.8 %collective-permute-done.16 = f32[2,128,128]{2,1,0:T(8,128)S(1)} collective-permute-done((f32[2,128,128]{2,1,0:T(8,128)S(1)}, f32[2,128,128]{2,1,0:T(8,128)S(1)}, u32[]{:S(2)}, u32[]{:S(2)}) %collective-permute-start.16) | collective-permute-done | bytes 131104 | tf_op jit(solution)/shard_map/ppermute | solution.py:73
  172.8 1.2 convolution_bitcast_fusion.2
  174.1 1.0 fusion.5
  175.1 0.7 copy.83
  175.8 5.1 %all-to-all-start = ((f32[8,16,256]{2,1,0:T(8,128)}), f32[8,16,256]{2,1,0:T(8,128)S(1)}, u32[]{:S(2)}, u32[]{:S(2)}) async-start(f32[8,16,256]{2,1,0:T(8,128)} %bitcast.41), calls=%async_computation | async-start | bytes 262144 | tf_op jit(solution)/shard_map/all_to_all | solution.py:127
  181.3 1.0 copy.84
  182.3 5.2 %all-to-all-done = f32[8,16,256]{2,1,0:T(8,128)S(1)} async-done(((f32[8,16,256]{2,1,0:T(8,128)}), f32[8,16,256]{2,1,0:T(8,128)S(1)}, u32[]{:S(2)}, u32[]{:S(2)}) %all-to-all-start) | async-done | bytes 131104 | tf_op jit(solution)/shard_map/all_to_all | solution.py:127
  187.5 0.6 slice_multiply_fusion
  (112 shorter events, 8.1 us)
Async XLA Ops:
  7.2 2.4 %copy-start = (bf16[128,128]{1,0:T(8,128)(2,1)S(1)}, bf16[128,128]{1,0:T(8,128)(2,1)}, u32[]{:S(2)}) copy-start(bf16[128,128]{1,0:T(8,128)(2,1)} %param.11) | copy-start | bytes 98308
  7.2 6.2 %copy-start.3 = (bf16[128,128]{1,0:T(8,128)(2,1)S(1)}, bf16[128,128]{1,0:T(8,128)(2,1)}, u32[]{:S(2)}) copy-start(bf16[128,128]{1,0:T(8,128)(2,1)} %param.8) | copy-start | bytes 98308
  7.2 83.6 %all-gather.2.cloned.1.call-start = ((), (), s32[]{:S(2)}) async-start(), calls=%async_computation.1 | async-start | bytes 3538944 | tf_op jit(solution)/shard_map/all_gather | solution.py:116
  10.1 3.9 %collective-permute-start = (f32[520,128]{1,0:T(8,128)S(1)}, f32[520,128]{1,0:T(8,128)S(1)}, u32[]{:S(2)}, u32[]{:S(2)}) collective-permute-start(f32[520,128]{1,0:T(8,128)S(1)} %pad_maximum_fusion), channel_id=1, source_target_pairs={{0,8},{8,0},{16,24},{24,16},{32,40},{40,32},{48,56},{56,48},{64,72... | collective-permute-start | bytes 798728 | tf_op jit(solution)/shard_map/ppermute | solution.py:32
  11.8 1.5 collective-permute-start.8
  13.4 8.8 %collective-permute-start.9 = (bf16[256,384]{1,0:T(8,128)(2,1)S(1)}, bf16[256,384]{1,0:T(8,128)(2,1)S(1)}, u32[]{:S(2)}, u32[]{:S(2)}) collective-permute-start(bf16[256,384]{1,0:T(8,128)(2,1)S(1)} %maximum_select_fusion.9), channel_id=1, source_target_pairs={{0,16},{8,24},{16,0},{24,8},{32,48},{40,56},{48,32},{56,40},{64,80... | collective-permute-start | bytes 589832 | tf_op jit(solution)/shard_map/ppermute | solution.py:110
  23.1 56.7 %copy-start.1 = (bf16[128,128]{1,0:T(8,128)(2,1)S(1)}, bf16[128,128]{1,0:T(8,128)(2,1)}, u32[]{:S(2)}) copy-start(bf16[128,128]{1,0:T(8,128)(2,1)} %param.12) | copy-start | bytes 98308
  23.2 56.9 %copy-start.2 = (bf16[128,1024]{1,0:T(8,128)(2,1)S(1)}, bf16[128,1024]{1,0:T(8,128)(2,1)}, u32[]{:S(2)}) copy-start(bf16[128,1024]{1,0:T(8,128)(2,1)} %param.7) | copy-start | bytes 786436
  23.5 6.6 %collective-permute-start.1 = (f32[264,128]{1,0:T(8,128)S(1)}, f32[264,128]{1,0:T(8,128)S(1)}, u32[]{:S(2)}, u32[]{:S(2)}) collective-permute-start(f32[264,128]{1,0:T(8,128)S(1)} %pad_maximum_fusion.8), channel_id=1, source_target_pairs={{0,16},{8,24},{16,0},{24,8},{32,48},{40,56},{48,32},{56,40},{64,80... | collective-permute-start | bytes 405512 | tf_op jit(solution)/shard_map/ppermute | solution.py:32
  30.5 8.9 %collective-permute-start.2 = (f32[264,128]{0,1:T(8,128)S(1)}, f32[264,128]{0,1:T(8,128)S(1)}, u32[]{:S(2)}, u32[]{:S(2)}) collective-permute-start(f32[264,128]{0,1:T(8,128)S(1)} %pad_maximum_fusion.2), channel_id=1, source_target_pairs={{0,32},{8,40},{16,48},{24,56},{32,64},{40,72},{48,80},{56,88},{64,... | collective-permute-start | bytes 405512 | tf_op jit(solution)/shard_map/ppermute | solution.py:32
  39.5 14.6 %collective-permute-start.3 = (f32[264,128]{0,1:T(8,128)S(1)}, f32[264,128]{0,1:T(8,128)S(1)}, u32[]{:S(2)}, u32[]{:S(2)}) collective-permute-start(f32[264,128]{0,1:T(8,128)S(1)} %pad_maximum_fusion.3), channel_id=1, source_target_pairs={{0,32},{8,40},{16,48},{24,56},{32,64},{40,72},{48,80},{56,88},{64,... | collective-permute-start | bytes 405512 | tf_op jit(solution)/shard_map/ppermute | solution.py:32
  54.2 22.3 %collective-permute-start.4 = (f32[264,128]{0,1:T(8,128)S(1)}, f32[264,128]{0,1:T(8,128)S(1)}, u32[]{:S(2)}, u32[]{:S(2)}) collective-permute-start(f32[264,128]{0,1:T(8,128)S(1)} %pad_maximum_fusion.4), channel_id=1, source_target_pairs={{0,64},{8,72},{16,80},{24,88},{32,96},{40,104},{48,112},{56,120},{... | collective-permute-start | bytes 405512 | tf_op jit(solution)/shard_map/ppermute | solution.py:32
  76.7 7.2 %collective-permute-start.5 = (f32[2,128,128]{2,1,0:T(8,128)S(1)}, f32[2,128,128]{2,1,0:T(8,128)S(1)}, u32[]{:S(2)}, u32[]{:S(2)}) collective-permute-start(f32[2,128,128]{2,1,0:T(8,128)S(1)} %multiply_add_fusion.8), channel_id=1, source_target_pairs={{0,128},{8,136},{16,144},{24,152},{32,160},{40,168},{48,176},{56,1... | collective-permute-start | bytes 393224 | tf_op jit(solution)/shard_map/ppermute | solution.py:95
  84.0 6.6 %collective-permute-start.6 = (f32[2,128,128]{2,1,0:T(8,128)S(1)}, f32[2,128,128]{2,1,0:T(8,128)S(1)}, u32[]{:S(2)}, u32[]{:S(2)}) collective-permute-start(f32[2,128,128]{2,1,0:T(8,128)S(1)} %get-tuple-element.27), channel_id=1, source_target_pairs={{0,16},{8,24},{16,0},{24,8},{32,48},{40,56},{48,32},{56,40},{64,80... | collective-permute-start | bytes 393224 | tf_op jit(solution)/shard_map/ppermute | solution.py:73
  90.7 11.1 %collective-permute-start.7 = (f32[4,128,128]{2,1,0:T(8,128)S(1)}, f32[4,128,128]{2,1,0:T(8,128)S(1)}, u32[]{:S(2)}, u32[]{:S(2)}) collective-permute-start(f32[4,128,128]{2,1,0:T(8,128)S(1)} %get-tuple-element.22), channel_id=1, source_target_pairs={{0,8},{8,0},{16,24},{24,16},{32,40},{40,32},{48,56},{56,48},{64,72... | collective-permute-start | bytes 786440 | tf_op jit(solution)/shard_map/ppermute | solution.py:73
  104.8 1.7 collective-permute-start.10
  107.0 7.6 %collective-permute-start.11 = (f32[264,128]{1,0:T(8,128)S(1)}, f32[264,128]{1,0:T(8,128)S(1)}, u32[]{:S(2)}, u32[]{:S(2)}) collective-permute-start(f32[264,128]{1,0:T(8,128)S(1)} %pad_maximum_fusion.9), channel_id=1, source_target_pairs={{0,16},{8,24},{16,0},{24,8},{32,48},{40,56},{48,32},{56,40},{64,80... | collective-permute-start | bytes 405512 | tf_op jit(solution)/shard_map/ppermute | solution.py:32
  115.1 8.3 %collective-permute-start.12 = (f32[264,128]{0,1:T(8,128)S(1)}, f32[264,128]{0,1:T(8,128)S(1)}, u32[]{:S(2)}, u32[]{:S(2)}) collective-permute-start(f32[264,128]{0,1:T(8,128)S(1)} %pad_maximum_fusion.5), channel_id=1, source_target_pairs={{32,0},{40,8},{48,16},{56,24},{64,32},{72,40},{80,48},{88,56},{96,... | collective-permute-start | bytes 405512 | tf_op jit(solution)/shard_map/ppermute | solution.py:32
  123.4 16.2 %collective-permute-start.13 = (f32[264,128]{0,1:T(8,128)S(1)}, f32[264,128]{0,1:T(8,128)S(1)}, u32[]{:S(2)}, u32[]{:S(2)}) collective-permute-start(f32[264,128]{0,1:T(8,128)S(1)} %pad_maximum_fusion.6), channel_id=1, source_target_pairs={{32,0},{40,8},{48,16},{56,24},{64,32},{72,40},{80,48},{88,56},{96,... | collective-permute-start | bytes 405512 | tf_op jit(solution)/shard_map/ppermute | solution.py:32
  139.6 0.7 copy-start.4
  140.3 12.8 %collective-permute-start.14 = (f32[264,128]{0,1:T(8,128)}, f32[264,128]{0,1:T(8,128)}, u32[]{:S(2)}, u32[]{:S(2)}) collective-permute-start(f32[264,128]{0,1:T(8,128)} %pad_maximum_fusion.7), channel_id=1, source_target_pairs={{64,0},{72,8},{80,16},{88,24},{96,32},{104,40},{112,48},{120,56},{... | collective-permute-start | bytes 405512 | tf_op jit(solution)/shard_map/ppermute | solution.py:32
  154.9 10.8 %collective-permute-start.15 = (f32[2,128,128]{2,1,0:T(8,128)S(1)}, f32[2,128,128]{2,1,0:T(8,128)S(1)}, u32[]{:S(2)}, u32[]{:S(2)}) collective-permute-start(f32[2,128,128]{2,1,0:T(8,128)S(1)} %multiply_add_fusion.4), channel_id=1, source_target_pairs={{128,0},{136,8},{144,16},{152,24},{160,32},{168,40},{176,48},{184,... | collective-permute-start | bytes 393224 | tf_op jit(solution)/shard_map/ppermute | solution.py:95
  165.8 6.6 %collective-permute-start.16 = (f32[2,128,128]{2,1,0:T(8,128)S(1)}, f32[2,128,128]{2,1,0:T(8,128)S(1)}, u32[]{:S(2)}, u32[]{:S(2)}) collective-permute-start(f32[2,128,128]{2,1,0:T(8,128)S(1)} %get-tuple-element.25), channel_id=1, source_target_pairs={{0,16},{8,24},{16,0},{24,8},{32,48},{40,56},{48,32},{56,40},{64,80... | collective-permute-start | bytes 393224 | tf_op jit(solution)/shard_map/ppermute | solution.py:73
  172.5 1.6 collective-permute-start.17
  175.8 11.7 %all-to-all-start = ((f32[8,16,256]{2,1,0:T(8,128)}), f32[8,16,256]{2,1,0:T(8,128)S(1)}, u32[]{:S(2)}, u32[]{:S(2)}) async-start(f32[8,16,256]{2,1,0:T(8,128)} %bitcast.41), calls=%async_computation | async-start | bytes 262144 | tf_op jit(solution)/shard_map/all_to_all | solution.py:127
Sparse Core Ops, SparseCore 0:
  23.2 60.6 all-gather.1

commit v8 on v7

--- a/solution.py
+++ b/solution.py
@@ -140,19 +140,21 @@
         total_ref[...] = jnp.zeros(total_ref.shape, jnp.float32)
         mix_ref[...] = jnp.zeros(mix_ref.shape, jnp.float32)
 
-    @pl.when(block * keys_per_block <= first + rows // heads - 1)
-    def _():
+    def accumulate(masked):
         scores = lax.dot_general(
             query_ref[...], key_ref[...], (((1,), (1,)), ((), ())), preferred_element_type=jnp.float32
-        ) / math.sqrt(width)
-        row = lax.broadcasted_iota(jnp.int32, scores.shape, 0)
-        col = lax.broadcasted_iota(jnp.int32, scores.shape, 1)
-        allowed = block * keys_per_block + col <= first + row // heads
-        scores = jnp.where(allowed, scores, very_negative)
+        ) * (1.0 / math.sqrt(width))
+        if masked:
+            row = lax.broadcasted_iota(jnp.int32, scores.shape, 0)
+            col = lax.broadcasted_iota(jnp.int32, scores.shape, 1)
+            allowed = block * keys_per_block + col <= first + row // heads
+            scores = jnp.where(allowed, scores, very_negative)
         top_old = top_ref[...]
         top_new = jnp.maximum(top_old, jnp.max(scores, axis=1, keepdims=True))
         rescale = jnp.exp(top_old - top_new)
-        weights = jnp.where(allowed, jnp.exp(scores - top_new), 0.0)
+        weights = jnp.exp(scores - top_new)
+        if masked:
+            weights = jnp.where(allowed, weights, 0.0)
         total_ref[...] = rescale * total_ref[...] + jnp.sum(weights, axis=1, keepdims=True)
         weights_hi = weights.astype(jnp.bfloat16)
         weights_lo = (weights - weights_hi.astype(jnp.float32)).astype(jnp.bfloat16)
@@ -164,6 +166,16 @@
         )
         mix_ref[...] = rescale * mix_ref[...] + mixed
         top_ref[...] = top_new
+
+    block_end = (block + 1) * keys_per_block - 1
+
+    @pl.when(block_end <= first)
+    def _():
+        accumulate(False)
+
+    @pl.when(jnp.logical_and(block_end > first, block * keys_per_block <= first + rows // heads - 1))
+    def _():
+        accumulate(True)
 
     @pl.when(block == pl.num_programs(0) - 1)
     def _():

time: 196 us -> 195 us (level)
  transfers between devices with their start and end apart: 20 -> 20, of which waited for: 16 -> 16; matrix products, arithmetic and copies ran while one was open for 5% -> 5% of each run, Pallas kernels for 6% -> 5%
where the time goes in v8:
time: 195 us; the launch traced here: 194 us
  waiting for transfers between devices  103 us (53%)
  starting transfers between devices  42.3 us (22%)
  between operations  14.6 us (7%)
  Pallas kernels  10.4 us (5%)
  matrix products  8.74 us (4%)
  local copies, waits for them, and re-layouts  7.42 us (4%)
  other arithmetic  6.69 us (3%)
    ppermute x10, waiting for transfers between devices, send_with_logs(): got = lax.ppermute(payload, axis, perm)  66.9 us
    ppermute x10, starting transfers between devices, send_with_logs(): got = lax.ppermute(payload, axis, perm)  29.9 us
    ppermute x2, waiting for transfers between devices, exclusive_scan(): got_state = lax.ppermute(window_state, axis, perm)  12.2 us
    pallas_call x1, Pallas kernels, attend(): pl.pallas_call(functools.partial(attend_kernel, heads=heads), out_shape=j...  10.4 us
    ppermute x4, waiting for transfers between devices, pair_up(): got = lax.ppermute(send, axis, [(j, j ^ bit) for j in range(count)])  10.1 us
    ppermute x2, waiting for transfers between devices, gather_blocks(): got = lax.ppermute(pieces, axis, [(j, j ^ bit) for j in range(count)])  8.89 us
    all_to_all x1, waiting for transfers between devices, mp_sum_scatter(): return jnp.sum(lax.all_to_all(blocks, axis, 0, 0), axis=0)  5.19 us
    all_to_all x1, starting transfers between devices, mp_sum_scatter(): return jnp.sum(lax.all_to_all(blocks, axis, 0, 0), axis=0)  5.06 us
  transfers between devices with their start and end apart: 20, of which 16 were waited for; matrix products, arithmetic and copies ran while one was open for 5% of the time, Pallas kernels for 5%

profile of v8, /device:TPU:68, one launch (start us, length us, event | category | flops | bytes accessed | tf_op | source)
XLA Modules:
  0.0 193.5 jit_solution(3012270586644569735)
XLA Ops:
  7.3 0.8 copy.61
  8.4 1.1 copy.64
  10.2 0.9 reduce-precision_convert_fusion
  11.1 0.8 pad_maximum_fusion.11
  12.4 0.9 collective-permute-done.8
  13.4 0.6 collective-permute-start.9
  14.2 8.0 %collective-permute-done.9 = bf16[256,384]{1,0:T(8,128)(2,1)S(1)} collective-permute-done((bf16[256,384]{1,0:T(8,128)(2,1)S(1)}, bf16[256,384]{1,0:T(8,128)(2,1)S(1)}, u32[]{:S(2)}, u32[]{:S(2)}) %collective-permute-start.9) | collective-permute-done | bytes 196640 | tf_op jit(solution)/shard_map/ppermute | solution.py:110
  22.2 0.9 maximum_select_fusion.2
  23.5 0.6 collective-permute-start.1
  24.1 6.0 %collective-permute-done.1 = f32[264,128]{1,0:T(8,128)S(1)} collective-permute-done((f32[264,128]{1,0:T(8,128)S(1)}, f32[264,128]{1,0:T(8,128)S(1)}, u32[]{:S(2)}, u32[]{:S(2)}) %collective-permute-start.1) | collective-permute-done | bytes 135200 | tf_op jit(solution)/shard_map/ppermute | solution.py:32
  30.5 3.8 %collective-permute-start.2 = (f32[264,128]{0,1:T(8,128)S(1)}, f32[264,128]{0,1:T(8,128)S(1)}, u32[]{:S(2)}, u32[]{:S(2)}) collective-permute-start(f32[264,128]{0,1:T(8,128)S(1)} %pad_maximum_fusion.2), channel_id=1, source_target_pairs={{0,32},{8,40},{16,48},{24,56},{32,64},{40,72},{48,80},{56,88},{64,... | collective-permute-start | bytes 405512 | tf_op jit(solution)/shard_map/ppermute | solution.py:32
  34.4 5.1 %collective-permute-done.2 = f32[264,128]{0,1:T(8,128)S(1)} collective-permute-done((f32[264,128]{0,1:T(8,128)S(1)}, f32[264,128]{0,1:T(8,128)S(1)}, u32[]{:S(2)}, u32[]{:S(2)}) %collective-permute-start.2) | collective-permute-done | bytes 135200 | tf_op jit(solution)/shard_map/ppermute | solution.py:32
  39.5 7.4 %collective-permute-start.3 = (f32[264,128]{0,1:T(8,128)S(1)}, f32[264,128]{0,1:T(8,128)S(1)}, u32[]{:S(2)}, u32[]{:S(2)}) collective-permute-start(f32[264,128]{0,1:T(8,128)S(1)} %pad_maximum_fusion.3), channel_id=1, source_target_pairs={{0,32},{8,40},{16,48},{24,56},{32,64},{40,72},{48,80},{56,88},{64,... | collective-permute-start | bytes 405512 | tf_op jit(solution)/shard_map/ppermute | solution.py:32
  47.0 7.1 %collective-permute-done.3 = f32[264,128]{0,1:T(8,128)S(1)} collective-permute-done((f32[264,128]{0,1:T(8,128)S(1)}, f32[264,128]{0,1:T(8,128)S(1)}, u32[]{:S(2)}, u32[]{:S(2)}) %collective-permute-start.3) | collective-permute-done | bytes 135200 | tf_op jit(solution)/shard_map/ppermute | solution.py:32
  54.2 10.8 %collective-permute-start.4 = (f32[264,128]{0,1:T(8,128)S(1)}, f32[264,128]{0,1:T(8,128)S(1)}, u32[]{:S(2)}, u32[]{:S(2)}) collective-permute-start(f32[264,128]{0,1:T(8,128)S(1)} %pad_maximum_fusion.4), channel_id=1, source_target_pairs={{0,64},{8,72},{16,80},{24,88},{32,96},{40,104},{48,112},{56,120},{... | collective-permute-start | bytes 405512 | tf_op jit(solution)/shard_map/ppermute | solution.py:32
  65.2 11.3 %collective-permute-done.4 = f32[264,128]{0,1:T(8,128)S(1)} collective-permute-done((f32[264,128]{0,1:T(8,128)S(1)}, f32[264,128]{0,1:T(8,128)S(1)}, u32[]{:S(2)}, u32[]{:S(2)}) %collective-permute-start.4) | collective-permute-done | bytes 135200 | tf_op jit(solution)/shard_map/ppermute | solution.py:32
  76.7 3.0 %collective-permute-start.5 = (f32[2,128,128]{2,1,0:T(8,128)S(1)}, f32[2,128,128]{2,1,0:T(8,128)S(1)}, u32[]{:S(2)}, u32[]{:S(2)}) collective-permute-start(f32[2,128,128]{2,1,0:T(8,128)S(1)} %multiply_add_fusion.8), channel_id=1, source_target_pairs={{0,128},{8,136},{16,144},{24,152},{32,160},{40,168},{48,176},{56,1... | collective-permute-start | bytes 393224 | tf_op jit(solution)/shard_map/ppermute | solution.py:95
  80.0 0.8 reshape.231.query_ref
  80.9 3.0 %collective-permute-done.5 = f32[2,128,128]{2,1,0:T(8,128)S(1)} collective-permute-done((f32[2,128,128]{2,1,0:T(8,128)S(1)}, f32[2,128,128]{2,1,0:T(8,128)S(1)}, u32[]{:S(2)}, u32[]{:S(2)}) %collective-permute-start.5) | collective-permute-done | bytes 131104 | tf_op jit(solution)/shard_map/ppermute | solution.py:95
  84.0 0.6 collective-permute-start.6
  84.6 0.7 convolution_bitcast_fusion.1
  85.3 5.3 %collective-permute-done.6 = f32[2,128,128]{2,1,0:T(8,128)S(1)} collective-permute-done((f32[2,128,128]{2,1,0:T(8,128)S(1)}, f32[2,128,128]{2,1,0:T(8,128)S(1)}, u32[]{:S(2)}, u32[]{:S(2)}) %collective-permute-start.6) | collective-permute-done | bytes 131104 | tf_op jit(solution)/shard_map/ppermute | solution.py:73
  91.0 10.4 %shard_map.94 = f32[1024,128]{1,0:T(8,128)} custom-call(s32[1]{0:T(128)} %bitcast.21.first_ref, bf16[1024,128]{1,0:T(8,128)(2,1)} %reshape.231.query_ref, bf16[4096,384]{1,0:T(8,128)(2,1)} %all-gather.2.cloned.1.call-done.key_ref.upper_ref.lower_ref, bf16[4096,384]{1,0:T(8,128)(2,1)} %all-gather.2.cloned.1.call-done.key_ref.upper_ref.lower_ref, ...), custom_call_target="tpu_custom_call" | custom-call | flops 4294967296 | bytes 3932160 | tf_op jit(solution)/shard_map/pallas_call | solution.py:189
  101.4 1.7 fusion.3
  103.1 1.1 fusion.12
  105.0 1.2 collective-permute-done.10
  106.6 0.6 collective-permute-start.11
  107.2 6.8 %collective-permute-done.11 = f32[264,128]{1,0:T(8,128)S(1)} collective-permute-done((f32[264,128]{1,0:T(8,128)S(1)}, f32[264,128]{1,0:T(8,128)S(1)}, u32[]{:S(2)}, u32[]{:S(2)}) %collective-permute-start.11) | collective-permute-done | bytes 135200 | tf_op jit(solution)/shard_map/ppermute | solution.py:32
  114.5 1.9 collective-permute-start.12
  116.4 6.3 %collective-permute-done.12 = f32[264,128]{0,1:T(8,128)S(1)} collective-permute-done((f32[264,128]{0,1:T(8,128)S(1)}, f32[264,128]{0,1:T(8,128)S(1)}, u32[]{:S(2)}, u32[]{:S(2)}) %collective-permute-start.12) | collective-permute-done | bytes 135200 | tf_op jit(solution)/shard_map/ppermute | solution.py:32
  122.8 2.2 %collective-permute-start.13 = (f32[264,128]{0,1:T(8,128)S(1)}, f32[264,128]{0,1:T(8,128)S(1)}, u32[]{:S(2)}, u32[]{:S(2)}) collective-permute-start(f32[264,128]{0,1:T(8,128)S(1)} %pad_maximum_fusion.6), channel_id=1, source_target_pairs={{32,0},{40,8},{48,16},{56,24},{64,32},{72,40},{80,48},{88,56},{96,... | collective-permute-start | bytes 405512 | tf_op jit(solution)/shard_map/ppermute | solution.py:32
  125.1 13.3 %collective-permute-done.13 = f32[264,128]{0,1:T(8,128)S(1)} collective-permute-done((f32[264,128]{0,1:T(8,128)S(1)}, f32[264,128]{0,1:T(8,128)S(1)}, u32[]{:S(2)}, u32[]{:S(2)}) %collective-permute-start.13) | collective-permute-done | bytes 135200 | tf_op jit(solution)/shard_map/ppermute | solution.py:32
  138.5 0.7 pad_maximum_fusion.7
  139.2 1.9 collective-permute-start.14
  141.7 9.7 %collective-permute-done.14 = f32[264,128]{0,1:T(8,128)} collective-permute-done((f32[264,128]{0,1:T(8,128)}, f32[264,128]{0,1:T(8,128)}, u32[]{:S(2)}, u32[]{:S(2)}) %collective-permute-start.14) | collective-permute-done | bytes 135200 | tf_op jit(solution)/shard_map/ppermute | solution.py:32
  151.4 0.9 slice.111
  152.4 0.7 fusion.53
  153.2 1.3 collective-permute-start.15
  154.8 9.2 %collective-permute-done.15 = f32[2,128,128]{2,1,0:T(8,128)S(1)} collective-permute-done((f32[2,128,128]{2,1,0:T(8,128)S(1)}, f32[2,128,128]{2,1,0:T(8,128)S(1)}, u32[]{:S(2)}, u32[]{:S(2)}) %collective-permute-start.15) | collective-permute-done | bytes 131104 | tf_op jit(solution)/shard_map/ppermute | solution.py:95
  164.7 1.2 fusion.6
  165.9 4.8 %collective-permute-done.16 = f32[2,128,128]{2,1,0:T(8,128)S(1)} collective-permute-done((f32[2,128,128]{2,1,0:T(8,128)S(1)}, f32[2,128,128]{2,1,0:T(8,128)S(1)}, u32[]{:S(2)}, u32[]{:S(2)}) %collective-permute-start.16) | collective-permute-done | bytes 131104 | tf_op jit(solution)/shard_map/ppermute | solution.py:73
  171.4 1.2 convolution_bitcast_fusion.2
  172.6 1.0 fusion.5
  173.7 0.7 copy.83
  174.4 5.1 %all-to-all-start = ((f32[8,16,256]{2,1,0:T(8,128)}), f32[8,16,256]{2,1,0:T(8,128)S(1)}, u32[]{:S(2)}, u32[]{:S(2)}) async-start(f32[8,16,256]{2,1,0:T(8,128)} %bitcast.41), calls=%async_computation | async-start | bytes 262144 | tf_op jit(solution)/shard_map/all_to_all | solution.py:127
  179.8 1.0 copy.84
  180.8 5.2 %all-to-all-done = f32[8,16,256]{2,1,0:T(8,128)S(1)} async-done(((f32[8,16,256]{2,1,0:T(8,128)}), f32[8,16,256]{2,1,0:T(8,128)S(1)}, u32[]{:S(2)}, u32[]{:S(2)}) %all-to-all-start) | async-done | bytes 131104 | tf_op jit(solution)/shard_map/all_to_all | solution.py:127
  186.1 0.6 slice_multiply_fusion
  (112 shorter events, 8.5 us)
Async XLA Ops:
  7.2 2.4 %copy-start = (bf16[128,128]{1,0:T(8,128)(2,1)S(1)}, bf16[128,128]{1,0:T(8,128)(2,1)}, u32[]{:S(2)}) copy-start(bf16[128,128]{1,0:T(8,128)(2,1)} %param.11) | copy-start | bytes 98308
  7.2 6.2 %copy-start.3 = (bf16[128,128]{1,0:T(8,128)(2,1)S(1)}, bf16[128,128]{1,0:T(8,128)(2,1)}, u32[]{:S(2)}) copy-start(bf16[128,128]{1,0:T(8,128)(2,1)} %param.8) | copy-start | bytes 98308
  7.2 83.8 %all-gather.2.cloned.1.call-start = ((), (), s32[]{:S(2)}) async-start(), calls=%async_computation.1 | async-start | bytes 3538944 | tf_op jit(solution)/shard_map/all_gather | solution.py:116
  10.1 3.9 %collective-permute-start = (f32[520,128]{1,0:T(8,128)S(1)}, f32[520,128]{1,0:T(8,128)S(1)}, u32[]{:S(2)}, u32[]{:S(2)}) collective-permute-start(f32[520,128]{1,0:T(8,128)S(1)} %pad_maximum_fusion), channel_id=1, source_target_pairs={{0,8},{8,0},{16,24},{24,16},{32,40},{40,32},{48,56},{56,48},{64,72... | collective-permute-start | bytes 798728 | tf_op jit(solution)/shard_map/ppermute | solution.py:32
  11.8 1.5 collective-permute-start.8
  13.4 8.8 %collective-permute-start.9 = (bf16[256,384]{1,0:T(8,128)(2,1)S(1)}, bf16[256,384]{1,0:T(8,128)(2,1)S(1)}, u32[]{:S(2)}, u32[]{:S(2)}) collective-permute-start(bf16[256,384]{1,0:T(8,128)(2,1)S(1)} %maximum_select_fusion.9), channel_id=1, source_target_pairs={{0,16},{8,24},{16,0},{24,8},{32,48},{40,56},{48,32},{56,40},{64,80... | collective-permute-start | bytes 589832 | tf_op jit(solution)/shard_map/ppermute | solution.py:110
  23.1 56.7 %copy-start.1 = (bf16[128,128]{1,0:T(8,128)(2,1)S(1)}, bf16[128,128]{1,0:T(8,128)(2,1)}, u32[]{:S(2)}) copy-start(bf16[128,128]{1,0:T(8,128)(2,1)} %param.12) | copy-start | bytes 98308
  23.2 56.9 %copy-start.2 = (bf16[128,1024]{1,0:T(8,128)(2,1)S(1)}, bf16[128,1024]{1,0:T(8,128)(2,1)}, u32[]{:S(2)}) copy-start(bf16[128,1024]{1,0:T(8,128)(2,1)} %param.7) | copy-start | bytes 786436
  23.5 6.6 %collective-permute-start.1 = (f32[264,128]{1,0:T(8,128)S(1)}, f32[264,128]{1,0:T(8,128)S(1)}, u32[]{:S(2)}, u32[]{:S(2)}) collective-permute-start(f32[264,128]{1,0:T(8,128)S(1)} %pad_maximum_fusion.8), channel_id=1, source_target_pairs={{0,16},{8,24},{16,0},{24,8},{32,48},{40,56},{48,32},{56,40},{64,80... | collective-permute-start | bytes 405512 | tf_op jit(solution)/shard_map/ppermute | solution.py:32
  30.5 8.9 %collective-permute-start.2 = (f32[264,128]{0,1:T(8,128)S(1)}, f32[264,128]{0,1:T(8,128)S(1)}, u32[]{:S(2)}, u32[]{:S(2)}) collective-permute-start(f32[264,128]{0,1:T(8,128)S(1)} %pad_maximum_fusion.2), channel_id=1, source_target_pairs={{0,32},{8,40},{16,48},{24,56},{32,64},{40,72},{48,80},{56,88},{64,... | collective-permute-start | bytes 405512 | tf_op jit(solution)/shard_map/ppermute | solution.py:32
  39.5 14.6 %collective-permute-start.3 = (f32[264,128]{0,1:T(8,128)S(1)}, f32[264,128]{0,1:T(8,128)S(1)}, u32[]{:S(2)}, u32[]{:S(2)}) collective-permute-start(f32[264,128]{0,1:T(8,128)S(1)} %pad_maximum_fusion.3), channel_id=1, source_target_pairs={{0,32},{8,40},{16,48},{24,56},{32,64},{40,72},{48,80},{56,88},{64,... | collective-permute-start | bytes 405512 | tf_op jit(solution)/shard_map/ppermute | solution.py:32
  54.2 22.3 %collective-permute-start.4 = (f32[264,128]{0,1:T(8,128)S(1)}, f32[264,128]{0,1:T(8,128)S(1)}, u32[]{:S(2)}, u32[]{:S(2)}) collective-permute-start(f32[264,128]{0,1:T(8,128)S(1)} %pad_maximum_fusion.4), channel_id=1, source_target_pairs={{0,64},{8,72},{16,80},{24,88},{32,96},{40,104},{48,112},{56,120},{... | collective-permute-start | bytes 405512 | tf_op jit(solution)/shard_map/ppermute | solution.py:32
  76.7 7.2 %collective-permute-start.5 = (f32[2,128,128]{2,1,0:T(8,128)S(1)}, f32[2,128,128]{2,1,0:T(8,128)S(1)}, u32[]{:S(2)}, u32[]{:S(2)}) collective-permute-start(f32[2,128,128]{2,1,0:T(8,128)S(1)} %multiply_add_fusion.8), channel_id=1, source_target_pairs={{0,128},{8,136},{16,144},{24,152},{32,160},{40,168},{48,176},{56,1... | collective-permute-start | bytes 393224 | tf_op jit(solution)/shard_map/ppermute | solution.py:95
  84.0 6.6 %collective-permute-start.6 = (f32[2,128,128]{2,1,0:T(8,128)S(1)}, f32[2,128,128]{2,1,0:T(8,128)S(1)}, u32[]{:S(2)}, u32[]{:S(2)}) collective-permute-start(f32[2,128,128]{2,1,0:T(8,128)S(1)} %get-tuple-element.27), channel_id=1, source_target_pairs={{0,16},{8,24},{16,0},{24,8},{32,48},{40,56},{48,32},{56,40},{64,80... | collective-permute-start | bytes 393224 | tf_op jit(solution)/shard_map/ppermute | solution.py:73
  90.7 10.7 %collective-permute-start.7 = (f32[4,128,128]{2,1,0:T(8,128)S(1)}, f32[4,128,128]{2,1,0:T(8,128)S(1)}, u32[]{:S(2)}, u32[]{:S(2)}) collective-permute-start(f32[4,128,128]{2,1,0:T(8,128)S(1)} %get-tuple-element.22), channel_id=1, source_target_pairs={{0,8},{8,0},{16,24},{24,16},{32,40},{40,32},{48,56},{56,48},{64,72... | collective-permute-start | bytes 786440 | tf_op jit(solution)/shard_map/ppermute | solution.py:73
  104.4 1.7 collective-permute-start.10
  106.6 7.5 %collective-permute-start.11 = (f32[264,128]{1,0:T(8,128)S(1)}, f32[264,128]{1,0:T(8,128)S(1)}, u32[]{:S(2)}, u32[]{:S(2)}) collective-permute-start(f32[264,128]{1,0:T(8,128)S(1)} %pad_maximum_fusion.9), channel_id=1, source_target_pairs={{0,16},{8,24},{16,0},{24,8},{32,48},{40,56},{48,32},{56,40},{64,80... | collective-permute-start | bytes 405512 | tf_op jit(solution)/shard_map/ppermute | solution.py:32
  114.5 8.3 %collective-permute-start.12 = (f32[264,128]{0,1:T(8,128)S(1)}, f32[264,128]{0,1:T(8,128)S(1)}, u32[]{:S(2)}, u32[]{:S(2)}) collective-permute-start(f32[264,128]{0,1:T(8,128)S(1)} %pad_maximum_fusion.5), channel_id=1, source_target_pairs={{32,0},{40,8},{48,16},{56,24},{64,32},{72,40},{80,48},{88,56},{96,... | collective-permute-start | bytes 405512 | tf_op jit(solution)/shard_map/ppermute | solution.py:32
  122.8 15.6 %collective-permute-start.13 = (f32[264,128]{0,1:T(8,128)S(1)}, f32[264,128]{0,1:T(8,128)S(1)}, u32[]{:S(2)}, u32[]{:S(2)}) collective-permute-start(f32[264,128]{0,1:T(8,128)S(1)} %pad_maximum_fusion.6), channel_id=1, source_target_pairs={{32,0},{40,8},{48,16},{56,24},{64,32},{72,40},{80,48},{88,56},{96,... | collective-permute-start | bytes 405512 | tf_op jit(solution)/shard_map/ppermute | solution.py:32
  138.5 0.7 copy-start.4
  139.2 12.2 %collective-permute-start.14 = (f32[264,128]{0,1:T(8,128)}, f32[264,128]{0,1:T(8,128)}, u32[]{:S(2)}, u32[]{:S(2)}) collective-permute-start(f32[264,128]{0,1:T(8,128)} %pad_maximum_fusion.7), channel_id=1, source_target_pairs={{64,0},{72,8},{80,16},{88,24},{96,32},{104,40},{112,48},{120,56},{... | collective-permute-start | bytes 405512 | tf_op jit(solution)/shard_map/ppermute | solution.py:32
  153.2 10.8 %collective-permute-start.15 = (f32[2,128,128]{2,1,0:T(8,128)S(1)}, f32[2,128,128]{2,1,0:T(8,128)S(1)}, u32[]{:S(2)}, u32[]{:S(2)}) collective-permute-start(f32[2,128,128]{2,1,0:T(8,128)S(1)} %multiply_add_fusion.4), channel_id=1, source_target_pairs={{128,0},{136,8},{144,16},{152,24},{160,32},{168,40},{176,48},{184,... | collective-permute-start | bytes 393224 | tf_op jit(solution)/shard_map/ppermute | solution.py:95
  164.1 6.6 %collective-permute-start.16 = (f32[2,128,128]{2,1,0:T(8,128)S(1)}, f32[2,128,128]{2,1,0:T(8,128)S(1)}, u32[]{:S(2)}, u32[]{:S(2)}) collective-permute-start(f32[2,128,128]{2,1,0:T(8,128)S(1)} %get-tuple-element.25), channel_id=1, source_target_pairs={{0,16},{8,24},{16,0},{24,8},{32,48},{40,56},{48,32},{56,40},{64,80... | collective-permute-start | bytes 393224 | tf_op jit(solution)/shard_map/ppermute | solution.py:73
  170.8 1.8 collective-permute-start.17
  174.4 11.6 %all-to-all-start = ((f32[8,16,256]{2,1,0:T(8,128)}), f32[8,16,256]{2,1,0:T(8,128)S(1)}, u32[]{:S(2)}, u32[]{:S(2)}) async-start(f32[8,16,256]{2,1,0:T(8,128)} %bitcast.41), calls=%async_computation | async-start | bytes 262144 | tf_op jit(solution)/shard_map/all_to_all | solution.py:127
Sparse Core Ops, SparseCore 0:
  23.2 60.6 all-gather.1

commit v9 on v8

--- a/solution.py
+++ b/solution.py
@@ -24,13 +24,21 @@
     return lax.ppermute(value, axis, perm)
 
 
-def send_with_logs(state, logs, axis, perm):
+def send_with_logs(state, logs, axis, perm, extra=None):
     heads, rows, width = state.shape
     count = logs.shape[0]
     log_rows = jnp.pad(jnp.broadcast_to(logs[:, None], (count, width)), ((0, -count % 8), (0, 0)))
     payload = jnp.concatenate([state.reshape(heads * rows, width), log_rows], axis=0)
-    got = lax.ppermute(payload, axis, perm)
-    return got[: heads * rows].reshape(heads, rows, width), got[heads * rows : heads * rows + count, 0]
+    if extra is None:
+        got = lax.ppermute(payload, axis, perm)
+        got_extra = None
+    else:
+        got, got_extra = lax.ppermute((payload, extra), axis, perm)
+    got_state = got[: heads * rows].reshape(heads, rows, width)
+    got_logs = got[heads * rows : heads * rows + count, 0]
+    if extra is None:
+        return got_state, got_logs
+    return got_state, got_logs, got_extra
 
 
 def shift_perm(count, distance, forward):
@@ -39,7 +47,7 @@
     return [(j + distance, j) for j in range(count - distance)]
 
 
-def pair_down(state, logs, axis, bit, forward):
+def pair_down(state, logs, axis, bit, forward, extra=None):
     count = lax.axis_size(axis)
     upper = (lax.axis_index(axis) // bit) % 2 == 1
     first = jnp.logical_not(upper) if forward else upper
@@ -48,18 +56,26 @@
     other = half - mine
     own_state = lax.dynamic_slice_in_dim(state, mine, half, axis=0)
     own_logs = lax.dynamic_slice_in_dim(logs, mine, half)
-    got_state, got_logs = send_with_logs(
+    sent = send_with_logs(
         lax.dynamic_slice_in_dim(state, other, half, axis=0),
         lax.dynamic_slice_in_dim(logs, other, half),
         axis,
         [(j, j ^ bit) for j in range(count)],
-    )
+        extra,
+    )
+    got_state, got_logs = sent[:2]
+    joined = None
+    if extra is not None:
+        joined = sent[2]
+        joined = jnp.where(
+            upper, jnp.concatenate([joined, extra], axis=0), jnp.concatenate([extra, joined], axis=0)
+        )
     first_state = jnp.where(first, own_state, got_state)
     second_state = jnp.where(first, got_state, own_state)
     first_logs = jnp.where(first, own_logs, got_logs)
     second_logs = jnp.where(first, got_logs, own_logs)
     pair_state = jnp.exp(second_logs)[:, None, None] * first_state + second_state
-    return pair_state, first_logs + second_logs, (first_state, first_logs)
+    return pair_state, first_logs + second_logs, (first_state, first_logs), joined
 
 
 def pair_up(window, saved, axis, bit, forward):
@@ -76,11 +92,11 @@
     )
 
 
-def exclusive_scan(state, logs, axis, forward):
+def exclusive_scan(state, logs, axis, forward, extra=None):
     count = lax.axis_size(axis)
     levels = []
     for bit in (1, 2):
-        state, logs, saved = pair_down(state, logs, axis, bit, forward)
+        state, logs, saved, extra = pair_down(state, logs, axis, bit, forward, extra)
         levels.append((bit, saved))
     stride = 4
     groups = count // stride
@@ -99,19 +115,11 @@
         width *= 2
     for bit, saved in reversed(levels):
         window_state = pair_up(window_state, saved, axis, bit, forward)
-    return window_state
-
-
-def gather_blocks(block, axis):
-    count = lax.axis_size(axis)
-    index = lax.axis_index(axis)
-    pieces = block
-    for bit in (1, 2):
-        got = lax.ppermute(pieces, axis, [(j, j ^ bit) for j in range(count)])
-        upper = (index // bit) % 2 == 1
-        pieces = jnp.where(
-            upper, jnp.concatenate([got, pieces], axis=0), jnp.concatenate([pieces, got], axis=0)
-        )
+    return window_state, extra
+
+
+def gather_groups(pieces, axis):
+    count = lax.axis_size(axis)
     groups = [[z * 4 + r for z in range(count // 4)] for r in range(4)]
     return lax.all_gather(pieces, axis, axis=0, tiled=True, axis_index_groups=groups)
 
@@ -223,7 +231,6 @@
 
     values_hi, values_lo = split_bf16(values)
     packed = jnp.concatenate([keys, values_hi, values_lo], axis=1)
-    every = gather_blocks(packed, "seq")
 
     c_scale = 0.5 / math.sqrt(N * row_count * seq_count)
     student_x = inputs_x.astype(jnp.float32).reshape(row_count, heads, HEAD_WIDTH)
@@ -243,7 +250,8 @@
     local_state = jnp.einsum(
         "shp,sn->hpn", student_x * ending[:, :, None], b_rows, precision=highest
     )
-    state_in = exclusive_scan(local_state, totals, "seq", True)
+    state_in, plane_blocks = exclusive_scan(local_state, totals, "seq", True, packed)
+    every = gather_groups(plane_blocks, "seq")
 
     query_rows = queries.reshape(row_count * heads, HEAD_WIDTH)
     teacher_out = attend(
@@ -255,7 +263,7 @@
     mismatch = y_intra + y_inter - teacher_out
     scaled_mismatch = mismatch * rising[:, :, None]
     local_grad = jnp.einsum("thp,tn->hpn", scaled_mismatch, c_rows, precision=highest)
-    later_grad = exclusive_scan(local_grad, totals, "seq", False)
+    later_grad, _ = exclusive_scan(local_grad, totals, "seq", False)
     grad_x = jnp.einsum("hts,thp->shp", mixing, mismatch, precision=highest)
     grad_x = (
         grad_x

time: 195 us -> 195 us (level)
    ppermute x10 -> x8, waiting for transfers between devices: 66.9 us -> 60.9 us  [send_with_logs(): got = lax.ppermute(payload, axis, perm)]
    ppermute x2 -> x4, waiting for transfers between devices: 8.89 us -> 14.9 us  [send_with_logs(): got, got_extra = lax.ppermute((payload, extra), axis, perm)]
    ppermute x10 -> x8, starting transfers between devices: 29.9 us -> 29.2 us  [send_with_logs(): got = lax.ppermute(payload, axis, perm)]
where the time goes in v9:
time: 195 us; the launch traced here: 194 us
  waiting for transfers between devices  103 us (53%)
  starting transfers between devices  42.3 us (22%)
  between operations  14.6 us (7%)
  Pallas kernels  10.4 us (5%)
  matrix products  8.74 us (4%)
  local copies, waits for them, and re-layouts  7.42 us (4%)
  other arithmetic  6.69 us (3%)
    ppermute x8, waiting for transfers between devices, send_with_logs(): got = lax.ppermute(payload, axis, perm)  60.9 us
    ppermute x8, starting transfers between devices, send_with_logs(): got = lax.ppermute(payload, axis, perm)  29.2 us
    ppermute x4, waiting for transfers between devices, send_with_logs(): got, got_extra = lax.ppermute((payload, extra), axis, perm)  14.9 us
    ppermute x2, waiting for transfers between devices, exclusive_scan(): got_state = lax.ppermute(window_state, axis, perm)  12.2 us
    pallas_call x1, Pallas kernels, attend(): pl.pallas_call(functools.partial(attend_kernel, heads=heads), out_shape=j...  10.4 us
    ppermute x4, waiting for transfers between devices, pair_up(): got = lax.ppermute(send, axis, [(j, j ^ bit) for j in range(count)])  10.1 us
    all_to_all x1, waiting for transfers between devices, mp_sum_scatter(): return jnp.sum(lax.all_to_all(blocks, axis, 0, 0), axis=0)  5.19 us
    all_to_all x1, starting transfers between devices, mp_sum_scatter(): return jnp.sum(lax.all_to_all(blocks, axis, 0, 0), axis=0)  5.06 us
  transfers between devices with their start and end apart: 20, of which 16 were waited for; matrix products, arithmetic and copies ran while one was open for 5% of the time, Pallas kernels for 5%

profile of v9, /device:TPU:68, one launch (start us, length us, event | category | flops | bytes accessed | tf_op | source)
XLA Modules:
  0.0 193.5 jit_solution(3012270586644569735)
XLA Ops:
  7.3 0.8 copy.61
  8.4 1.1 copy.64
  10.2 0.9 reduce-precision_convert_fusion
  11.1 0.8 pad_maximum_fusion.11
  12.4 0.9 collective-permute-done.8
  13.4 0.6 collective-permute-start.9
  14.2 8.0 %collective-permute-done.9 = bf16[256,384]{1,0:T(8,128)(2,1)S(1)} collective-permute-done((bf16[256,384]{1,0:T(8,128)(2,1)S(1)}, bf16[256,384]{1,0:T(8,128)(2,1)S(1)}, u32[]{:S(2)}, u32[]{:S(2)}) %collective-permute-start.9) | collective-permute-done | bytes 196640 | tf_op jit(solution)/shard_map/ppermute | solution.py:36
  22.2 0.9 maximum_select_fusion.2
  23.5 0.6 collective-permute-start.1
  24.1 6.0 %collective-permute-done.1 = f32[264,128]{1,0:T(8,128)S(1)} collective-permute-done((f32[264,128]{1,0:T(8,128)S(1)}, f32[264,128]{1,0:T(8,128)S(1)}, u32[]{:S(2)}, u32[]{:S(2)}) %collective-permute-start.1) | collective-permute-done | bytes 135200 | tf_op jit(solution)/shard_map/ppermute | solution.py:36
  30.5 3.8 %collective-permute-start.2 = (f32[264,128]{0,1:T(8,128)S(1)}, f32[264,128]{0,1:T(8,128)S(1)}, u32[]{:S(2)}, u32[]{:S(2)}) collective-permute-start(f32[264,128]{0,1:T(8,128)S(1)} %pad_maximum_fusion.2), channel_id=1, source_target_pairs={{0,32},{8,40},{16,48},{24,56},{32,64},{40,72},{48,80},{56,88},{64,... | collective-permute-start | bytes 405512 | tf_op jit(solution)/shard_map/ppermute | solution.py:33
  34.4 5.1 %collective-permute-done.2 = f32[264,128]{0,1:T(8,128)S(1)} collective-permute-done((f32[264,128]{0,1:T(8,128)S(1)}, f32[264,128]{0,1:T(8,128)S(1)}, u32[]{:S(2)}, u32[]{:S(2)}) %collective-permute-start.2) | collective-permute-done | bytes 135200 | tf_op jit(solution)/shard_map/ppermute | solution.py:33
  39.5 7.4 %collective-permute-start.3 = (f32[264,128]{0,1:T(8,128)S(1)}, f32[264,128]{0,1:T(8,128)S(1)}, u32[]{:S(2)}, u32[]{:S(2)}) collective-permute-start(f32[264,128]{0,1:T(8,128)S(1)} %pad_maximum_fusion.3), channel_id=1, source_target_pairs={{0,32},{8,40},{16,48},{24,56},{32,64},{40,72},{48,80},{56,88},{64,... | collective-permute-start | bytes 405512 | tf_op jit(solution)/shard_map/ppermute | solution.py:33
  47.0 7.1 %collective-permute-done.3 = f32[264,128]{0,1:T(8,128)S(1)} collective-permute-done((f32[264,128]{0,1:T(8,128)S(1)}, f32[264,128]{0,1:T(8,128)S(1)}, u32[]{:S(2)}, u32[]{:S(2)}) %collective-permute-start.3) | collective-permute-done | bytes 135200 | tf_op jit(solution)/shard_map/ppermute | solution.py:33
  54.2 10.8 %collective-permute-start.4 = (f32[264,128]{0,1:T(8,128)S(1)}, f32[264,128]{0,1:T(8,128)S(1)}, u32[]{:S(2)}, u32[]{:S(2)}) collective-permute-start(f32[264,128]{0,1:T(8,128)S(1)} %pad_maximum_fusion.4), channel_id=1, source_target_pairs={{0,64},{8,72},{16,80},{24,88},{32,96},{40,104},{48,112},{56,120},{... | collective-permute-start | bytes 405512 | tf_op jit(solution)/shard_map/ppermute | solution.py:33
  65.2 11.3 %collective-permute-done.4 = f32[264,128]{0,1:T(8,128)S(1)} collective-permute-done((f32[264,128]{0,1:T(8,128)S(1)}, f32[264,128]{0,1:T(8,128)S(1)}, u32[]{:S(2)}, u32[]{:S(2)}) %collective-permute-start.4) | collective-permute-done | bytes 135200 | tf_op jit(solution)/shard_map/ppermute | solution.py:33
  76.7 3.0 %collective-permute-start.5 = (f32[2,128,128]{2,1,0:T(8,128)S(1)}, f32[2,128,128]{2,1,0:T(8,128)S(1)}, u32[]{:S(2)}, u32[]{:S(2)}) collective-permute-start(f32[2,128,128]{2,1,0:T(8,128)S(1)} %multiply_add_fusion.8), channel_id=1, source_target_pairs={{0,128},{8,136},{16,144},{24,152},{32,160},{40,168},{48,176},{56,1... | collective-permute-start | bytes 393224 | tf_op jit(solution)/shard_map/ppermute | solution.py:111
  80.0 0.8 reshape.231.query_ref
  80.9 3.0 %collective-permute-done.5 = f32[2,128,128]{2,1,0:T(8,128)S(1)} collective-permute-done((f32[2,128,128]{2,1,0:T(8,128)S(1)}, f32[2,128,128]{2,1,0:T(8,128)S(1)}, u32[]{:S(2)}, u32[]{:S(2)}) %collective-permute-start.5) | collective-permute-done | bytes 131104 | tf_op jit(solution)/shard_map/ppermute | solution.py:111
  84.0 0.6 collective-permute-start.6
  84.6 0.7 convolution_bitcast_fusion.1
  85.3 5.3 %collective-permute-done.6 = f32[2,128,128]{2,1,0:T(8,128)S(1)} collective-permute-done((f32[2,128,128]{2,1,0:T(8,128)S(1)}, f32[2,128,128]{2,1,0:T(8,128)S(1)}, u32[]{:S(2)}, u32[]{:S(2)}) %collective-permute-start.6) | collective-permute-done | bytes 131104 | tf_op jit(solution)/shard_map/ppermute | solution.py:89
  91.0 10.4 %shard_map.94 = f32[1024,128]{1,0:T(8,128)} custom-call(s32[1]{0:T(128)} %bitcast.21.first_ref, bf16[1024,128]{1,0:T(8,128)(2,1)} %reshape.231.query_ref, bf16[4096,384]{1,0:T(8,128)(2,1)} %all-gather.2.cloned.1.call-done.key_ref.upper_ref.lower_ref, bf16[4096,384]{1,0:T(8,128)(2,1)} %all-gather.2.cloned.1.call-done.key_ref.upper_ref.lower_ref, ...), custom_call_target="tpu_custom_call" | custom-call | flops 4294967296 | bytes 3932160 | tf_op jit(solution)/shard_map/pallas_call | solution.py:197
  101.4 1.7 fusion.3
  103.1 1.1 fusion.12
  105.0 1.2 collective-permute-done.10
  106.6 0.6 collective-permute-start.11
  107.2 6.8 %collective-permute-done.11 = f32[264,128]{1,0:T(8,128)S(1)} collective-permute-done((f32[264,128]{1,0:T(8,128)S(1)}, f32[264,128]{1,0:T(8,128)S(1)}, u32[]{:S(2)}, u32[]{:S(2)}) %collective-permute-start.11) | collective-permute-done | bytes 135200 | tf_op jit(solution)/shard_map/ppermute | solution.py:33
  114.5 1.9 collective-permute-start.12
  116.4 6.3 %collective-permute-done.12 = f32[264,128]{0,1:T(8,128)S(1)} collective-permute-done((f32[264,128]{0,1:T(8,128)S(1)}, f32[264,128]{0,1:T(8,128)S(1)}, u32[]{:S(2)}, u32[]{:S(2)}) %collective-permute-start.12) | collective-permute-done | bytes 135200 | tf_op jit(solution)/shard_map/ppermute | solution.py:33
  122.8 2.2 %collective-permute-start.13 = (f32[264,128]{0,1:T(8,128)S(1)}, f32[264,128]{0,1:T(8,128)S(1)}, u32[]{:S(2)}, u32[]{:S(2)}) collective-permute-start(f32[264,128]{0,1:T(8,128)S(1)} %pad_maximum_fusion.6), channel_id=1, source_target_pairs={{32,0},{40,8},{48,16},{56,24},{64,32},{72,40},{80,48},{88,56},{96,... | collective-permute-start | bytes 405512 | tf_op jit(solution)/shard_map/ppermute | solution.py:33
  125.1 13.3 %collective-permute-done.13 = f32[264,128]{0,1:T(8,128)S(1)} collective-permute-done((f32[264,128]{0,1:T(8,128)S(1)}, f32[264,128]{0,1:T(8,128)S(1)}, u32[]{:S(2)}, u32[]{:S(2)}) %collective-permute-start.13) | collective-permute-done | bytes 135200 | tf_op jit(solution)/shard_map/ppermute | solution.py:33
  138.5 0.7 pad_maximum_fusion.7
  139.2 1.9 collective-permute-start.14
  141.7 9.7 %collective-permute-done.14 = f32[264,128]{0,1:T(8,128)} collective-permute-done((f32[264,128]{0,1:T(8,128)}, f32[264,128]{0,1:T(8,128)}, u32[]{:S(2)}, u32[]{:S(2)}) %collective-permute-start.14) | collective-permute-done | bytes 135200 | tf_op jit(solution)/shard_map/ppermute | solution.py:33
  151.4 0.9 slice.111
  152.4 0.7 fusion.53
  153.2 1.3 collective-permute-start.15
  154.8 9.2 %collective-permute-done.15 = f32[2,128,128]{2,1,0:T(8,128)S(1)} collective-permute-done((f32[2,128,128]{2,1,0:T(8,128)S(1)}, f32[2,128,128]{2,1,0:T(8,128)S(1)}, u32[]{:S(2)}, u32[]{:S(2)}) %collective-permute-start.15) | collective-permute-done | bytes 131104 | tf_op jit(solution)/shard_map/ppermute | solution.py:111
  164.7 1.2 fusion.6
  165.9 4.8 %collective-permute-done.16 = f32[2,128,128]{2,1,0:T(8,128)S(1)} collective-permute-done((f32[2,128,128]{2,1,0:T(8,128)S(1)}, f32[2,128,128]{2,1,0:T(8,128)S(1)}, u32[]{:S(2)}, u32[]{:S(2)}) %collective-permute-start.16) | collective-permute-done | bytes 131104 | tf_op jit(solution)/shard_map/ppermute | solution.py:89
  171.4 1.2 convolution_bitcast_fusion.2
  172.6 1.0 fusion.5
  173.7 0.7 copy.83
  174.4 5.1 %all-to-all-start = ((f32[8,16,256]{2,1,0:T(8,128)}), f32[8,16,256]{2,1,0:T(8,128)S(1)}, u32[]{:S(2)}, u32[]{:S(2)}) async-start(f32[8,16,256]{2,1,0:T(8,128)} %bitcast.41), calls=%async_computation | async-start | bytes 262144 | tf_op jit(solution)/shard_map/all_to_all | solution.py:135
  179.8 1.0 copy.84
  180.8 5.2 %all-to-all-done = f32[8,16,256]{2,1,0:T(8,128)S(1)} async-done(((f32[8,16,256]{2,1,0:T(8,128)}), f32[8,16,256]{2,1,0:T(8,128)S(1)}, u32[]{:S(2)}, u32[]{:S(2)}) %all-to-all-start) | async-done | bytes 131104 | tf_op jit(solution)/shard_map/all_to_all | solution.py:135
  186.1 0.6 slice_multiply_fusion
  (112 shorter events, 8.5 us)
Async XLA Ops:
  7.2 2.4 %copy-start = (bf16[128,128]{1,0:T(8,128)(2,1)S(1)}, bf16[128,128]{1,0:T(8,128)(2,1)}, u32[]{:S(2)}) copy-start(bf16[128,128]{1,0:T(8,128)(2,1)} %param.11) | copy-start | bytes 98308
  7.2 6.2 %copy-start.3 = (bf16[128,128]{1,0:T(8,128)(2,1)S(1)}, bf16[128,128]{1,0:T(8,128)(2,1)}, u32[]{:S(2)}) copy-start(bf16[128,128]{1,0:T(8,128)(2,1)} %param.8) | copy-start | bytes 98308
  7.2 83.8 %all-gather.2.cloned.1.call-start = ((), (), s32[]{:S(2)}) async-start(), calls=%async_computation.1 | async-start | bytes 3538944 | tf_op jit(solution)/shard_map/all_gather | solution.py:124
  10.1 3.9 %collective-permute-start = (f32[520,128]{1,0:T(8,128)S(1)}, f32[520,128]{1,0:T(8,128)S(1)}, u32[]{:S(2)}, u32[]{:S(2)}) collective-permute-start(f32[520,128]{1,0:T(8,128)S(1)} %pad_maximum_fusion), channel_id=1, source_target_pairs={{0,8},{8,0},{16,24},{24,16},{32,40},{40,32},{48,56},{56,48},{64,72... | collective-permute-start | bytes 798728 | tf_op jit(solution)/shard_map/ppermute | solution.py:36
  11.8 1.5 collective-permute-start.8
  13.4 8.8 %collective-permute-start.9 = (bf16[256,384]{1,0:T(8,128)(2,1)S(1)}, bf16[256,384]{1,0:T(8,128)(2,1)S(1)}, u32[]{:S(2)}, u32[]{:S(2)}) collective-permute-start(bf16[256,384]{1,0:T(8,128)(2,1)S(1)} %maximum_select_fusion.9), channel_id=1, source_target_pairs={{0,16},{8,24},{16,0},{24,8},{32,48},{40,56},{48,32},{56,40},{64,80... | collective-permute-start | bytes 589832 | tf_op jit(solution)/shard_map/ppermute | solution.py:36
  23.1 56.7 %copy-start.1 = (bf16[128,128]{1,0:T(8,128)(2,1)S(1)}, bf16[128,128]{1,0:T(8,128)(2,1)}, u32[]{:S(2)}) copy-start(bf16[128,128]{1,0:T(8,128)(2,1)} %param.12) | copy-start | bytes 98308
  23.2 56.9 %copy-start.2 = (bf16[128,1024]{1,0:T(8,128)(2,1)S(1)}, bf16[128,1024]{1,0:T(8,128)(2,1)}, u32[]{:S(2)}) copy-start(bf16[128,1024]{1,0:T(8,128)(2,1)} %param.7) | copy-start | bytes 786436
  23.5 6.6 %collective-permute-start.1 = (f32[264,128]{1,0:T(8,128)S(1)}, f32[264,128]{1,0:T(8,128)S(1)}, u32[]{:S(2)}, u32[]{:S(2)}) collective-permute-start(f32[264,128]{1,0:T(8,128)S(1)} %pad_maximum_fusion.8), channel_id=1, source_target_pairs={{0,16},{8,24},{16,0},{24,8},{32,48},{40,56},{48,32},{56,40},{64,80... | collective-permute-start | bytes 405512 | tf_op jit(solution)/shard_map/ppermute | solution.py:36
  30.5 8.9 %collective-permute-start.2 = (f32[264,128]{0,1:T(8,128)S(1)}, f32[264,128]{0,1:T(8,128)S(1)}, u32[]{:S(2)}, u32[]{:S(2)}) collective-permute-start(f32[264,128]{0,1:T(8,128)S(1)} %pad_maximum_fusion.2), channel_id=1, source_target_pairs={{0,32},{8,40},{16,48},{24,56},{32,64},{40,72},{48,80},{56,88},{64,... | collective-permute-start | bytes 405512 | tf_op jit(solution)/shard_map/ppermute | solution.py:33
  39.5 14.6 %collective-permute-start.3 = (f32[264,128]{0,1:T(8,128)S(1)}, f32[264,128]{0,1:T(8,128)S(1)}, u32[]{:S(2)}, u32[]{:S(2)}) collective-permute-start(f32[264,128]{0,1:T(8,128)S(1)} %pad_maximum_fusion.3), channel_id=1, source_target_pairs={{0,32},{8,40},{16,48},{24,56},{32,64},{40,72},{48,80},{56,88},{64,... | collective-permute-start | bytes 405512 | tf_op jit(solution)/shard_map/ppermute | solution.py:33
  54.2 22.3 %collective-permute-start.4 = (f32[264,128]{0,1:T(8,128)S(1)}, f32[264,128]{0,1:T(8,128)S(1)}, u32[]{:S(2)}, u32[]{:S(2)}) collective-permute-start(f32[264,128]{0,1:T(8,128)S(1)} %pad_maximum_fusion.4), channel_id=1, source_target_pairs={{0,64},{8,72},{16,80},{24,88},{32,96},{40,104},{48,112},{56,120},{... | collective-permute-start | bytes 405512 | tf_op jit(solution)/shard_map/ppermute | solution.py:33
  76.7 7.2 %collective-permute-start.5 = (f32[2,128,128]{2,1,0:T(8,128)S(1)}, f32[2,128,128]{2,1,0:T(8,128)S(1)}, u32[]{:S(2)}, u32[]{:S(2)}) collective-permute-start(f32[2,128,128]{2,1,0:T(8,128)S(1)} %multiply_add_fusion.8), channel_id=1, source_target_pairs={{0,128},{8,136},{16,144},{24,152},{32,160},{40,168},{48,176},{56,1... | collective-permute-start | bytes 393224 | tf_op jit(solution)/shard_map/ppermute | solution.py:111
  84.0 6.6 %collective-permute-start.6 = (f32[2,128,128]{2,1,0:T(8,128)S(1)}, f32[2,128,128]{2,1,0:T(8,128)S(1)}, u32[]{:S(2)}, u32[]{:S(2)}) collective-permute-start(f32[2,128,128]{2,1,0:T(8,128)S(1)} %get-tuple-element.27), channel_id=1, source_target_pairs={{0,16},{8,24},{16,0},{24,8},{32,48},{40,56},{48,32},{56,40},{64,80... | collective-permute-start | bytes 393224 | tf_op jit(solution)/shard_map/ppermute | solution.py:89
  90.7 10.7 %collective-permute-start.7 = (f32[4,128,128]{2,1,0:T(8,128)S(1)}, f32[4,128,128]{2,1,0:T(8,128)S(1)}, u32[]{:S(2)}, u32[]{:S(2)}) collective-permute-start(f32[4,128,128]{2,1,0:T(8,128)S(1)} %get-tuple-element.22), channel_id=1, source_target_pairs={{0,8},{8,0},{16,24},{24,16},{32,40},{40,32},{48,56},{56,48},{64,72... | collective-permute-start | bytes 786440 | tf_op jit(solution)/shard_map/ppermute | solution.py:89
  104.4 1.7 collective-permute-start.10
  106.6 7.5 %collective-permute-start.11 = (f32[264,128]{1,0:T(8,128)S(1)}, f32[264,128]{1,0:T(8,128)S(1)}, u32[]{:S(2)}, u32[]{:S(2)}) collective-permute-start(f32[264,128]{1,0:T(8,128)S(1)} %pad_maximum_fusion.9), channel_id=1, source_target_pairs={{0,16},{8,24},{16,0},{24,8},{32,48},{40,56},{48,32},{56,40},{64,80... | collective-permute-start | bytes 405512 | tf_op jit(solution)/shard_map/ppermute | solution.py:33
  114.5 8.3 %collective-permute-start.12 = (f32[264,128]{0,1:T(8,128)S(1)}, f32[264,128]{0,1:T(8,128)S(1)}, u32[]{:S(2)}, u32[]{:S(2)}) collective-permute-start(f32[264,128]{0,1:T(8,128)S(1)} %pad_maximum_fusion.5), channel_id=1, source_target_pairs={{32,0},{40,8},{48,16},{56,24},{64,32},{72,40},{80,48},{88,56},{96,... | collective-permute-start | bytes 405512 | tf_op jit(solution)/shard_map/ppermute | solution.py:33
  122.8 15.6 %collective-permute-start.13 = (f32[264,128]{0,1:T(8,128)S(1)}, f32[264,128]{0,1:T(8,128)S(1)}, u32[]{:S(2)}, u32[]{:S(2)}) collective-permute-start(f32[264,128]{0,1:T(8,128)S(1)} %pad_maximum_fusion.6), channel_id=1, source_target_pairs={{32,0},{40,8},{48,16},{56,24},{64,32},{72,40},{80,48},{88,56},{96,... | collective-permute-start | bytes 405512 | tf_op jit(solution)/shard_map/ppermute | solution.py:33
  138.5 0.7 copy-start.4
  139.2 12.2 %collective-permute-start.14 = (f32[264,128]{0,1:T(8,128)}, f32[264,128]{0,1:T(8,128)}, u32[]{:S(2)}, u32[]{:S(2)}) collective-permute-start(f32[264,128]{0,1:T(8,128)} %pad_maximum_fusion.7), channel_id=1, source_target_pairs={{64,0},{72,8},{80,16},{88,24},{96,32},{104,40},{112,48},{120,56},{... | collective-permute-start | bytes 405512 | tf_op jit(solution)/shard_map/ppermute | solution.py:33
  153.2 10.8 %collective-permute-start.15 = (f32[2,128,128]{2,1,0:T(8,128)S(1)}, f32[2,128,128]{2,1,0:T(8,128)S(1)}, u32[]{:S(2)}, u32[]{:S(2)}) collective-permute-start(f32[2,128,128]{2,1,0:T(8,128)S(1)} %multiply_add_fusion.4), channel_id=1, source_target_pairs={{128,0},{136,8},{144,16},{152,24},{160,32},{168,40},{176,48},{184,... | collective-permute-start | bytes 393224 | tf_op jit(solution)/shard_map/ppermute | solution.py:111
  164.1 6.6 %collective-permute-start.16 = (f32[2,128,128]{2,1,0:T(8,128)S(1)}, f32[2,128,128]{2,1,0:T(8,128)S(1)}, u32[]{:S(2)}, u32[]{:S(2)}) collective-permute-start(f32[2,128,128]{2,1,0:T(8,128)S(1)} %get-tuple-element.25), channel_id=1, source_target_pairs={{0,16},{8,24},{16,0},{24,8},{32,48},{40,56},{48,32},{56,40},{64,80... | collective-permute-start | bytes 393224 | tf_op jit(solution)/shard_map/ppermute | solution.py:89
  170.8 1.8 collective-permute-start.17
  174.4 11.6 %all-to-all-start = ((f32[8,16,256]{2,1,0:T(8,128)}), f32[8,16,256]{2,1,0:T(8,128)S(1)}, u32[]{:S(2)}, u32[]{:S(2)}) async-start(f32[8,16,256]{2,1,0:T(8,128)} %bitcast.41), calls=%async_computation | async-start | bytes 262144 | tf_op jit(solution)/shard_map/all_to_all | solution.py:135
Sparse Core Ops, SparseCore 0:
  23.2 60.6 all-gather.1

commit v10 on v9

--- a/solution.py
+++ b/solution.py
@@ -190,7 +190,7 @@
         out_ref[...] = mix_ref[...] / total_ref[...]
 
 
-def attend(first_query, query_rows, every, heads, keys_per_block=512):
+def attend(first_query, query_rows, every, heads, keys_per_block=1024):
     rows, width = query_rows.shape
     blocks = every.shape[0] // keys_per_block
     flops = 2 * rows * every.shape[0] * width * 4

time: 195 us -> 196 us (level)
  transfers between devices with their start and end apart: 20 -> 20, of which waited for: 16 -> 16; matrix products, arithmetic and copies ran while one was open for 5% -> 5% of each run, Pallas kernels for 5% -> 6%
where the time goes in v10:
time: 196 us; the launch traced here: 195 us
  waiting for transfers between devices  104 us (53%)
  starting transfers between devices  42.2 us (22%)
  between operations  14.6 us (7%)
  Pallas kernels  11.4 us (6%)
  matrix products  8.74 us (4%)
  local copies, waits for them, and re-layouts  7.42 us (4%)
  other arithmetic  6.69 us (3%)
    ppermute x8, waiting for transfers between devices, send_with_logs(): got = lax.ppermute(payload, axis, perm)  61.7 us
    ppermute x8, starting transfers between devices, send_with_logs(): got = lax.ppermute(payload, axis, perm)  29.4 us
    ppermute x4, waiting for transfers between devices, send_with_logs(): got, got_extra = lax.ppermute((payload, extra), axis, perm)  14.9 us
    ppermute x2, waiting for transfers between devices, exclusive_scan(): got_state = lax.ppermute(window_state, axis, perm)  12.2 us
    pallas_call x1, Pallas kernels, attend(): pl.pallas_call(functools.partial(attend_kernel, heads=heads), out_shape=j...  11.4 us
    ppermute x4, waiting for transfers between devices, pair_up(): got = lax.ppermute(send, axis, [(j, j ^ bit) for j in range(count)])  10.1 us
    all_to_all x1, waiting for transfers between devices, mp_sum_scatter(): return jnp.sum(lax.all_to_all(blocks, axis, 0, 0), axis=0)  5.19 us
    all_to_all x1, starting transfers between devices, mp_sum_scatter(): return jnp.sum(lax.all_to_all(blocks, axis, 0, 0), axis=0)  4.96 us
  transfers between devices with their start and end apart: 20, of which 16 were waited for; matrix products, arithmetic and copies ran while one was open for 5% of the time, Pallas kernels for 6%

profile of v10, /device:TPU:68, one launch (start us, length us, event | category | flops | bytes accessed | tf_op | source)
XLA Modules:
  0.0 195.2 jit_solution(13961818242049127350)
XLA Ops:
  7.3 0.8 copy.61
  8.4 1.1 copy.64
  10.2 0.9 reduce-precision_convert_fusion
  11.1 0.8 pad_maximum_fusion.11
  12.4 0.9 collective-permute-done.8
  13.4 0.6 collective-permute-start.9
  14.2 8.0 %collective-permute-done.9 = bf16[256,384]{1,0:T(8,128)(2,1)S(1)} collective-permute-done((bf16[256,384]{1,0:T(8,128)(2,1)S(1)}, bf16[256,384]{1,0:T(8,128)(2,1)S(1)}, u32[]{:S(2)}, u32[]{:S(2)}) %collective-permute-start.9) | collective-permute-done | bytes 196640 | tf_op jit(solution)/shard_map/ppermute | solution.py:36
  22.2 0.9 maximum_select_fusion.2
  24.1 6.0 %collective-permute-done.1 = f32[264,128]{1,0:T(8,128)S(1)} collective-permute-done((f32[264,128]{1,0:T(8,128)S(1)}, f32[264,128]{1,0:T(8,128)S(1)}, u32[]{:S(2)}, u32[]{:S(2)}) %collective-permute-start.1) | collective-permute-done | bytes 135200 | tf_op jit(solution)/shard_map/ppermute | solution.py:36
  30.5 3.8 %collective-permute-start.2 = (f32[264,128]{0,1:T(8,128)S(1)}, f32[264,128]{0,1:T(8,128)S(1)}, u32[]{:S(2)}, u32[]{:S(2)}) collective-permute-start(f32[264,128]{0,1:T(8,128)S(1)} %pad_maximum_fusion.2), channel_id=1, source_target_pairs={{0,32},{8,40},{16,48},{24,56},{32,64},{40,72},{48,80},{56,88},{64,... | collective-permute-start | bytes 405512 | tf_op jit(solution)/shard_map/ppermute | solution.py:33
  34.4 5.1 %collective-permute-done.2 = f32[264,128]{0,1:T(8,128)S(1)} collective-permute-done((f32[264,128]{0,1:T(8,128)S(1)}, f32[264,128]{0,1:T(8,128)S(1)}, u32[]{:S(2)}, u32[]{:S(2)}) %collective-permute-start.2) | collective-permute-done | bytes 135200 | tf_op jit(solution)/shard_map/ppermute | solution.py:33
  39.5 7.4 %collective-permute-start.3 = (f32[264,128]{0,1:T(8,128)S(1)}, f32[264,128]{0,1:T(8,128)S(1)}, u32[]{:S(2)}, u32[]{:S(2)}) collective-permute-start(f32[264,128]{0,1:T(8,128)S(1)} %pad_maximum_fusion.3), channel_id=1, source_target_pairs={{0,32},{8,40},{16,48},{24,56},{32,64},{40,72},{48,80},{56,88},{64,... | collective-permute-start | bytes 405512 | tf_op jit(solution)/shard_map/ppermute | solution.py:33
  47.0 7.1 %collective-permute-done.3 = f32[264,128]{0,1:T(8,128)S(1)} collective-permute-done((f32[264,128]{0,1:T(8,128)S(1)}, f32[264,128]{0,1:T(8,128)S(1)}, u32[]{:S(2)}, u32[]{:S(2)}) %collective-permute-start.3) | collective-permute-done | bytes 135200 | tf_op jit(solution)/shard_map/ppermute | solution.py:33
  54.2 10.8 %collective-permute-start.4 = (f32[264,128]{0,1:T(8,128)S(1)}, f32[264,128]{0,1:T(8,128)S(1)}, u32[]{:S(2)}, u32[]{:S(2)}) collective-permute-start(f32[264,128]{0,1:T(8,128)S(1)} %pad_maximum_fusion.4), channel_id=1, source_target_pairs={{0,64},{8,72},{16,80},{24,88},{32,96},{40,104},{48,112},{56,120},{... | collective-permute-start | bytes 405512 | tf_op jit(solution)/shard_map/ppermute | solution.py:33
  65.2 11.3 %collective-permute-done.4 = f32[264,128]{0,1:T(8,128)S(1)} collective-permute-done((f32[264,128]{0,1:T(8,128)S(1)}, f32[264,128]{0,1:T(8,128)S(1)}, u32[]{:S(2)}, u32[]{:S(2)}) %collective-permute-start.4) | collective-permute-done | bytes 135200 | tf_op jit(solution)/shard_map/ppermute | solution.py:33
  76.7 3.0 %collective-permute-start.5 = (f32[2,128,128]{2,1,0:T(8,128)S(1)}, f32[2,128,128]{2,1,0:T(8,128)S(1)}, u32[]{:S(2)}, u32[]{:S(2)}) collective-permute-start(f32[2,128,128]{2,1,0:T(8,128)S(1)} %multiply_add_fusion.8), channel_id=1, source_target_pairs={{0,128},{8,136},{16,144},{24,152},{32,160},{40,168},{48,176},{56,1... | collective-permute-start | bytes 393224 | tf_op jit(solution)/shard_map/ppermute | solution.py:111
  80.0 0.8 reshape.231.query_ref
  80.9 3.0 %collective-permute-done.5 = f32[2,128,128]{2,1,0:T(8,128)S(1)} collective-permute-done((f32[2,128,128]{2,1,0:T(8,128)S(1)}, f32[2,128,128]{2,1,0:T(8,128)S(1)}, u32[]{:S(2)}, u32[]{:S(2)}) %collective-permute-start.5) | collective-permute-done | bytes 131104 | tf_op jit(solution)/shard_map/ppermute | solution.py:111
  84.0 0.6 collective-permute-start.6
  84.6 0.7 convolution_bitcast_fusion.1
  85.3 5.3 %collective-permute-done.6 = f32[2,128,128]{2,1,0:T(8,128)S(1)} collective-permute-done((f32[2,128,128]{2,1,0:T(8,128)S(1)}, f32[2,128,128]{2,1,0:T(8,128)S(1)}, u32[]{:S(2)}, u32[]{:S(2)}) %collective-permute-start.6) | collective-permute-done | bytes 131104 | tf_op jit(solution)/shard_map/ppermute | solution.py:89
  91.0 11.4 %shard_map.94 = f32[1024,128]{1,0:T(8,128)} custom-call(s32[1]{0:T(128)} %bitcast.21.first_ref, bf16[1024,128]{1,0:T(8,128)(2,1)} %reshape.231.query_ref, bf16[4096,384]{1,0:T(8,128)(2,1)} %all-gather.2.cloned.1.call-done.key_ref.upper_ref.lower_ref, bf16[4096,384]{1,0:T(8,128)(2,1)} %all-gather.2.cloned.1.call-done.key_ref.upper_ref.lower_ref, ...), custom_call_target="tpu_custom_call" | custom-call | flops 4294967296 | bytes 3932160 | tf_op jit(solution)/shard_map/pallas_call | solution.py:197
  102.3 1.7 fusion.3
  104.1 1.1 fusion.12
  105.9 1.2 collective-permute-done.10
  107.6 0.6 collective-permute-start.11
  108.2 6.8 %collective-permute-done.11 = f32[264,128]{1,0:T(8,128)S(1)} collective-permute-done((f32[264,128]{1,0:T(8,128)S(1)}, f32[264,128]{1,0:T(8,128)S(1)}, u32[]{:S(2)}, u32[]{:S(2)}) %collective-permute-start.11) | collective-permute-done | bytes 135200 | tf_op jit(solution)/shard_map/ppermute | solution.py:33
  115.5 1.9 collective-permute-start.12
  117.4 6.3 %collective-permute-done.12 = f32[264,128]{0,1:T(8,128)S(1)} collective-permute-done((f32[264,128]{0,1:T(8,128)S(1)}, f32[264,128]{0,1:T(8,128)S(1)}, u32[]{:S(2)}, u32[]{:S(2)}) %collective-permute-start.12) | collective-permute-done | bytes 135200 | tf_op jit(solution)/shard_map/ppermute | solution.py:33
  123.8 2.2 %collective-permute-start.13 = (f32[264,128]{0,1:T(8,128)S(1)}, f32[264,128]{0,1:T(8,128)S(1)}, u32[]{:S(2)}, u32[]{:S(2)}) collective-permute-start(f32[264,128]{0,1:T(8,128)S(1)} %pad_maximum_fusion.6), channel_id=1, source_target_pairs={{32,0},{40,8},{48,16},{56,24},{64,32},{72,40},{80,48},{88,56},{96,... | collective-permute-start | bytes 405512 | tf_op jit(solution)/shard_map/ppermute | solution.py:33
  126.1 13.3 %collective-permute-done.13 = f32[264,128]{0,1:T(8,128)S(1)} collective-permute-done((f32[264,128]{0,1:T(8,128)S(1)}, f32[264,128]{0,1:T(8,128)S(1)}, u32[]{:S(2)}, u32[]{:S(2)}) %collective-permute-start.13) | collective-permute-done | bytes 135200 | tf_op jit(solution)/shard_map/ppermute | solution.py:33
  139.4 0.7 pad_maximum_fusion.7
  140.1 2.1 %collective-permute-start.14 = (f32[264,128]{0,1:T(8,128)}, f32[264,128]{0,1:T(8,128)}, u32[]{:S(2)}, u32[]{:S(2)}) collective-permute-start(f32[264,128]{0,1:T(8,128)} %pad_maximum_fusion.7), channel_id=1, source_target_pairs={{64,0},{72,8},{80,16},{88,24},{96,32},{104,40},{112,48},{120,56},{... | collective-permute-start | bytes 405512 | tf_op jit(solution)/shard_map/ppermute | solution.py:33
  142.9 10.6 %collective-permute-done.14 = f32[264,128]{0,1:T(8,128)} collective-permute-done((f32[264,128]{0,1:T(8,128)}, f32[264,128]{0,1:T(8,128)}, u32[]{:S(2)}, u32[]{:S(2)}) %collective-permute-start.14) | collective-permute-done | bytes 135200 | tf_op jit(solution)/shard_map/ppermute | solution.py:33
  153.5 0.9 slice.111
  154.5 0.7 fusion.53
  155.3 1.3 collective-permute-start.15
  156.8 9.2 %collective-permute-done.15 = f32[2,128,128]{2,1,0:T(8,128)S(1)} collective-permute-done((f32[2,128,128]{2,1,0:T(8,128)S(1)}, f32[2,128,128]{2,1,0:T(8,128)S(1)}, u32[]{:S(2)}, u32[]{:S(2)}) %collective-permute-start.15) | collective-permute-done | bytes 131104 | tf_op jit(solution)/shard_map/ppermute | solution.py:111
  166.1 0.6 collective-permute-start.16
  166.7 1.1 fusion.6
  167.9 4.8 %collective-permute-done.16 = f32[2,128,128]{2,1,0:T(8,128)S(1)} collective-permute-done((f32[2,128,128]{2,1,0:T(8,128)S(1)}, f32[2,128,128]{2,1,0:T(8,128)S(1)}, u32[]{:S(2)}, u32[]{:S(2)}) %collective-permute-start.16) | collective-permute-done | bytes 131104 | tf_op jit(solution)/shard_map/ppermute | solution.py:89
  173.2 1.2 convolution_bitcast_fusion.2
  174.4 1.0 fusion.5
  175.5 0.7 copy.83
  176.2 5.0 %all-to-all-start = ((f32[8,16,256]{2,1,0:T(8,128)}), f32[8,16,256]{2,1,0:T(8,128)S(1)}, u32[]{:S(2)}, u32[]{:S(2)}) async-start(f32[8,16,256]{2,1,0:T(8,128)} %bitcast.41), calls=%async_computation | async-start | bytes 262144 | tf_op jit(solution)/shard_map/all_to_all | solution.py:135
  181.6 1.0 copy.84
  182.6 5.2 %all-to-all-done = f32[8,16,256]{2,1,0:T(8,128)S(1)} async-done(((f32[8,16,256]{2,1,0:T(8,128)}), f32[8,16,256]{2,1,0:T(8,128)S(1)}, u32[]{:S(2)}, u32[]{:S(2)}) %all-to-all-start) | async-done | bytes 131104 | tf_op jit(solution)/shard_map/all_to_all | solution.py:135
  187.8 0.6 slice_multiply_fusion
  (112 shorter events, 8.3 us)
Async XLA Ops:
  7.2 2.4 %copy-start = (bf16[128,128]{1,0:T(8,128)(2,1)S(1)}, bf16[128,128]{1,0:T(8,128)(2,1)}, u32[]{:S(2)}) copy-start(bf16[128,128]{1,0:T(8,128)(2,1)} %param.11) | copy-start | bytes 98308
  7.2 6.2 %copy-start.3 = (bf16[128,128]{1,0:T(8,128)(2,1)S(1)}, bf16[128,128]{1,0:T(8,128)(2,1)}, u32[]{:S(2)}) copy-start(bf16[128,128]{1,0:T(8,128)(2,1)} %param.8) | copy-start | bytes 98308
  7.2 83.8 %all-gather.2.cloned.1.call-start = ((), (), s32[]{:S(2)}) async-start(), calls=%async_computation.1 | async-start | bytes 3538944 | tf_op jit(solution)/shard_map/all_gather | solution.py:124
  10.1 3.9 %collective-permute-start = (f32[520,128]{1,0:T(8,128)S(1)}, f32[520,128]{1,0:T(8,128)S(1)}, u32[]{:S(2)}, u32[]{:S(2)}) collective-permute-start(f32[520,128]{1,0:T(8,128)S(1)} %pad_maximum_fusion), channel_id=1, source_target_pairs={{0,8},{8,0},{16,24},{24,16},{32,40},{40,32},{48,56},{56,48},{64,72... | collective-permute-start | bytes 798728 | tf_op jit(solution)/shard_map/ppermute | solution.py:36
  11.8 1.5 collective-permute-start.8
  13.4 8.8 %collective-permute-start.9 = (bf16[256,384]{1,0:T(8,128)(2,1)S(1)}, bf16[256,384]{1,0:T(8,128)(2,1)S(1)}, u32[]{:S(2)}, u32[]{:S(2)}) collective-permute-start(bf16[256,384]{1,0:T(8,128)(2,1)S(1)} %maximum_select_fusion.9), channel_id=1, source_target_pairs={{0,16},{8,24},{16,0},{24,8},{32,48},{40,56},{48,32},{56,40},{64,80... | collective-permute-start | bytes 589832 | tf_op jit(solution)/shard_map/ppermute | solution.py:36
  23.1 56.7 %copy-start.1 = (bf16[128,128]{1,0:T(8,128)(2,1)S(1)}, bf16[128,128]{1,0:T(8,128)(2,1)}, u32[]{:S(2)}) copy-start(bf16[128,128]{1,0:T(8,128)(2,1)} %param.12) | copy-start | bytes 98308
  23.2 56.9 %copy-start.2 = (bf16[128,1024]{1,0:T(8,128)(2,1)S(1)}, bf16[128,1024]{1,0:T(8,128)(2,1)}, u32[]{:S(2)}) copy-start(bf16[128,1024]{1,0:T(8,128)(2,1)} %param.7) | copy-start | bytes 786436
  23.5 6.6 %collective-permute-start.1 = (f32[264,128]{1,0:T(8,128)S(1)}, f32[264,128]{1,0:T(8,128)S(1)}, u32[]{:S(2)}, u32[]{:S(2)}) collective-permute-start(f32[264,128]{1,0:T(8,128)S(1)} %pad_maximum_fusion.8), channel_id=1, source_target_pairs={{0,16},{8,24},{16,0},{24,8},{32,48},{40,56},{48,32},{56,40},{64,80... | collective-permute-start | bytes 405512 | tf_op jit(solution)/shard_map/ppermute | solution.py:36
  30.5 8.9 %collective-permute-start.2 = (f32[264,128]{0,1:T(8,128)S(1)}, f32[264,128]{0,1:T(8,128)S(1)}, u32[]{:S(2)}, u32[]{:S(2)}) collective-permute-start(f32[264,128]{0,1:T(8,128)S(1)} %pad_maximum_fusion.2), channel_id=1, source_target_pairs={{0,32},{8,40},{16,48},{24,56},{32,64},{40,72},{48,80},{56,88},{64,... | collective-permute-start | bytes 405512 | tf_op jit(solution)/shard_map/ppermute | solution.py:33
  39.5 14.6 %collective-permute-start.3 = (f32[264,128]{0,1:T(8,128)S(1)}, f32[264,128]{0,1:T(8,128)S(1)}, u32[]{:S(2)}, u32[]{:S(2)}) collective-permute-start(f32[264,128]{0,1:T(8,128)S(1)} %pad_maximum_fusion.3), channel_id=1, source_target_pairs={{0,32},{8,40},{16,48},{24,56},{32,64},{40,72},{48,80},{56,88},{64,... | collective-permute-start | bytes 405512 | tf_op jit(solution)/shard_map/ppermute | solution.py:33
  54.2 22.3 %collective-permute-start.4 = (f32[264,128]{0,1:T(8,128)S(1)}, f32[264,128]{0,1:T(8,128)S(1)}, u32[]{:S(2)}, u32[]{:S(2)}) collective-permute-start(f32[264,128]{0,1:T(8,128)S(1)} %pad_maximum_fusion.4), channel_id=1, source_target_pairs={{0,64},{8,72},{16,80},{24,88},{32,96},{40,104},{48,112},{56,120},{... | collective-permute-start | bytes 405512 | tf_op jit(solution)/shard_map/ppermute | solution.py:33
  76.7 7.2 %collective-permute-start.5 = (f32[2,128,128]{2,1,0:T(8,128)S(1)}, f32[2,128,128]{2,1,0:T(8,128)S(1)}, u32[]{:S(2)}, u32[]{:S(2)}) collective-permute-start(f32[2,128,128]{2,1,0:T(8,128)S(1)} %multiply_add_fusion.8), channel_id=1, source_target_pairs={{0,128},{8,136},{16,144},{24,152},{32,160},{40,168},{48,176},{56,1... | collective-permute-start | bytes 393224 | tf_op jit(solution)/shard_map/ppermute | solution.py:111
  84.0 6.6 %collective-permute-start.6 = (f32[2,128,128]{2,1,0:T(8,128)S(1)}, f32[2,128,128]{2,1,0:T(8,128)S(1)}, u32[]{:S(2)}, u32[]{:S(2)}) collective-permute-start(f32[2,128,128]{2,1,0:T(8,128)S(1)} %get-tuple-element.27), channel_id=1, source_target_pairs={{0,16},{8,24},{16,0},{24,8},{32,48},{40,56},{48,32},{56,40},{64,80... | collective-permute-start | bytes 393224 | tf_op jit(solution)/shard_map/ppermute | solution.py:89
  90.7 11.7 %collective-permute-start.7 = (f32[4,128,128]{2,1,0:T(8,128)S(1)}, f32[4,128,128]{2,1,0:T(8,128)S(1)}, u32[]{:S(2)}, u32[]{:S(2)}) collective-permute-start(f32[4,128,128]{2,1,0:T(8,128)S(1)} %get-tuple-element.22), channel_id=1, source_target_pairs={{0,8},{8,0},{16,24},{24,16},{32,40},{40,32},{48,56},{56,48},{64,72... | collective-permute-start | bytes 786440 | tf_op jit(solution)/shard_map/ppermute | solution.py:89
  105.4 1.7 collective-permute-start.10
  107.6 7.5 %collective-permute-start.11 = (f32[264,128]{1,0:T(8,128)S(1)}, f32[264,128]{1,0:T(8,128)S(1)}, u32[]{:S(2)}, u32[]{:S(2)}) collective-permute-start(f32[264,128]{1,0:T(8,128)S(1)} %pad_maximum_fusion.9), channel_id=1, source_target_pairs={{0,16},{8,24},{16,0},{24,8},{32,48},{40,56},{48,32},{56,40},{64,80... | collective-permute-start | bytes 405512 | tf_op jit(solution)/shard_map/ppermute | solution.py:33
  115.5 8.3 %collective-permute-start.12 = (f32[264,128]{0,1:T(8,128)S(1)}, f32[264,128]{0,1:T(8,128)S(1)}, u32[]{:S(2)}, u32[]{:S(2)}) collective-permute-start(f32[264,128]{0,1:T(8,128)S(1)} %pad_maximum_fusion.5), channel_id=1, source_target_pairs={{32,0},{40,8},{48,16},{56,24},{64,32},{72,40},{80,48},{88,56},{96,... | collective-permute-start | bytes 405512 | tf_op jit(solution)/shard_map/ppermute | solution.py:33
  123.8 15.6 %collective-permute-start.13 = (f32[264,128]{0,1:T(8,128)S(1)}, f32[264,128]{0,1:T(8,128)S(1)}, u32[]{:S(2)}, u32[]{:S(2)}) collective-permute-start(f32[264,128]{0,1:T(8,128)S(1)} %pad_maximum_fusion.6), channel_id=1, source_target_pairs={{32,0},{40,8},{48,16},{56,24},{64,32},{72,40},{80,48},{88,56},{96,... | collective-permute-start | bytes 405512 | tf_op jit(solution)/shard_map/ppermute | solution.py:33
  139.4 0.7 copy-start.4
  140.1 13.3 %collective-permute-start.14 = (f32[264,128]{0,1:T(8,128)}, f32[264,128]{0,1:T(8,128)}, u32[]{:S(2)}, u32[]{:S(2)}) collective-permute-start(f32[264,128]{0,1:T(8,128)} %pad_maximum_fusion.7), channel_id=1, source_target_pairs={{64,0},{72,8},{80,16},{88,24},{96,32},{104,40},{112,48},{120,56},{... | collective-permute-start | bytes 405512 | tf_op jit(solution)/shard_map/ppermute | solution.py:33
  155.3 10.8 %collective-permute-start.15 = (f32[2,128,128]{2,1,0:T(8,128)S(1)}, f32[2,128,128]{2,1,0:T(8,128)S(1)}, u32[]{:S(2)}, u32[]{:S(2)}) collective-permute-start(f32[2,128,128]{2,1,0:T(8,128)S(1)} %multiply_add_fusion.4), channel_id=1, source_target_pairs={{128,0},{136,8},{144,16},{152,24},{160,32},{168,40},{176,48},{184,... | collective-permute-start | bytes 393224 | tf_op jit(solution)/shard_map/ppermute | solution.py:111
  166.1 6.6 %collective-permute-start.16 = (f32[2,128,128]{2,1,0:T(8,128)S(1)}, f32[2,128,128]{2,1,0:T(8,128)S(1)}, u32[]{:S(2)}, u32[]{:S(2)}) collective-permute-start(f32[2,128,128]{2,1,0:T(8,128)S(1)} %get-tuple-element.25), channel_id=1, source_target_pairs={{0,16},{8,24},{16,0},{24,8},{32,48},{40,56},{48,32},{56,40},{64,80... | collective-permute-start | bytes 393224 | tf_op jit(solution)/shard_map/ppermute | solution.py:89
  172.8 1.6 collective-permute-start.17
  176.2 11.5 %all-to-all-start = ((f32[8,16,256]{2,1,0:T(8,128)}), f32[8,16,256]{2,1,0:T(8,128)S(1)}, u32[]{:S(2)}, u32[]{:S(2)}) async-start(f32[8,16,256]{2,1,0:T(8,128)} %bitcast.41), calls=%async_computation | async-start | bytes 262144 | tf_op jit(solution)/shard_map/all_to_all | solution.py:135
Sparse Core Ops, SparseCore 0:
  23.2 60.6 all-gather.1

commit v11 on v9

--- a/solution.py
+++ b/solution.py
@@ -164,13 +164,9 @@
         if masked:
             weights = jnp.where(allowed, weights, 0.0)
         total_ref[...] = rescale * total_ref[...] + jnp.sum(weights, axis=1, keepdims=True)
-        weights_hi = weights.astype(jnp.bfloat16)
-        weights_lo = (weights - weights_hi.astype(jnp.float32)).astype(jnp.bfloat16)
-        upper = upper_ref[...]
-        mixed = (
-            jnp.dot(weights_hi, upper, preferred_element_type=jnp.float32)
-            + jnp.dot(weights_hi, lower_ref[...], preferred_element_type=jnp.float32)
-            + jnp.dot(weights_lo, upper, preferred_element_type=jnp.float32)
+        value_rows = upper_ref[...].astype(jnp.float32) + lower_ref[...].astype(jnp.float32)
+        mixed = jnp.dot(
+            weights, value_rows, precision=lax.Precision.HIGHEST, preferred_element_type=jnp.float32
         )
         mix_ref[...] = rescale * mix_ref[...] + mixed
         top_ref[...] = top_new

time: 195 us -> 199 us (1.021)
  waiting for transfers between devices: 103 us -> 106 us
    ppermute x8, waiting for transfers between devices: 60.9 us -> 63.5 us  [send_with_logs(): got = lax.ppermute(payload, axis, perm)]
  transfers between devices with their start and end apart: 20 -> 20, of which waited for: 16 -> 16; matrix products, arithmetic and copies ran while one was open for 5% -> 5% of each run, Pallas kernels for 5% -> 6%
where the time goes in v11:
time: 199 us; the launch traced here: 198 us
  waiting for transfers between devices  106 us (53%)
  starting transfers between devices  42.2 us (21%)
  between operations  14.6 us (7%)
  Pallas kernels  12.3 us (6%)
  matrix products  8.74 us (4%)
  local copies, waits for them, and re-layouts  7.42 us (4%)
  other arithmetic  6.69 us (3%)
    ppermute x8, waiting for transfers between devices, send_with_logs(): got = lax.ppermute(payload, axis, perm)  63.5 us
    ppermute x8, starting transfers between devices, send_with_logs(): got = lax.ppermute(payload, axis, perm)  29.2 us
    ppermute x4, waiting for transfers between devices, send_with_logs(): got, got_extra = lax.ppermute((payload, extra), axis, perm)  14.9 us
    pallas_call x1, Pallas kernels, attend(): pl.pallas_call(functools.partial(attend_kernel, heads=heads), out_shape=j...  12.3 us
    ppermute x2, waiting for transfers between devices, exclusive_scan(): got_state = lax.ppermute(window_state, axis, perm)  12.2 us
    ppermute x4, waiting for transfers between devices, pair_up(): got = lax.ppermute(send, axis, [(j, j ^ bit) for j in range(count)])  10.1 us
    all_to_all x1, waiting for transfers between devices, mp_sum_scatter(): return jnp.sum(lax.all_to_all(blocks, axis, 0, 0), axis=0)  5.19 us
    all_to_all x1, starting transfers between devices, mp_sum_scatter(): return jnp.sum(lax.all_to_all(blocks, axis, 0, 0), axis=0)  4.97 us
  transfers between devices with their start and end apart: 20, of which 16 were waited for; matrix products, arithmetic and copies ran while one was open for 5% of the time, Pallas kernels for 6%

profile of v11, /device:TPU:68, one launch (start us, length us, event | category | flops | bytes accessed | tf_op | source)
XLA Modules:
  0.0 197.9 jit_solution(3592401868982575869)
XLA Ops:
  7.3 0.8 copy.61
  8.4 1.1 copy.64
  10.2 0.9 reduce-precision_convert_fusion
  11.1 0.8 pad_maximum_fusion.11
  12.4 0.9 collective-permute-done.8
  13.4 0.6 collective-permute-start.9
  14.2 8.0 %collective-permute-done.9 = bf16[256,384]{1,0:T(8,128)(2,1)S(1)} collective-permute-done((bf16[256,384]{1,0:T(8,128)(2,1)S(1)}, bf16[256,384]{1,0:T(8,128)(2,1)S(1)}, u32[]{:S(2)}, u32[]{:S(2)}) %collective-permute-start.9) | collective-permute-done | bytes 196640 | tf_op jit(solution)/shard_map/ppermute | solution.py:36
  22.2 0.9 maximum_select_fusion.2
  24.1 6.0 %collective-permute-done.1 = f32[264,128]{1,0:T(8,128)S(1)} collective-permute-done((f32[264,128]{1,0:T(8,128)S(1)}, f32[264,128]{1,0:T(8,128)S(1)}, u32[]{:S(2)}, u32[]{:S(2)}) %collective-permute-start.1) | collective-permute-done | bytes 135200 | tf_op jit(solution)/shard_map/ppermute | solution.py:36
  30.5 3.8 %collective-permute-start.2 = (f32[264,128]{0,1:T(8,128)S(1)}, f32[264,128]{0,1:T(8,128)S(1)}, u32[]{:S(2)}, u32[]{:S(2)}) collective-permute-start(f32[264,128]{0,1:T(8,128)S(1)} %pad_maximum_fusion.2), channel_id=1, source_target_pairs={{0,32},{8,40},{16,48},{24,56},{32,64},{40,72},{48,80},{56,88},{64,... | collective-permute-start | bytes 405512 | tf_op jit(solution)/shard_map/ppermute | solution.py:33
  34.4 5.1 %collective-permute-done.2 = f32[264,128]{0,1:T(8,128)S(1)} collective-permute-done((f32[264,128]{0,1:T(8,128)S(1)}, f32[264,128]{0,1:T(8,128)S(1)}, u32[]{:S(2)}, u32[]{:S(2)}) %collective-permute-start.2) | collective-permute-done | bytes 135200 | tf_op jit(solution)/shard_map/ppermute | solution.py:33
  39.5 7.4 %collective-permute-start.3 = (f32[264,128]{0,1:T(8,128)S(1)}, f32[264,128]{0,1:T(8,128)S(1)}, u32[]{:S(2)}, u32[]{:S(2)}) collective-permute-start(f32[264,128]{0,1:T(8,128)S(1)} %pad_maximum_fusion.3), channel_id=1, source_target_pairs={{0,32},{8,40},{16,48},{24,56},{32,64},{40,72},{48,80},{56,88},{64,... | collective-permute-start | bytes 405512 | tf_op jit(solution)/shard_map/ppermute | solution.py:33
  47.0 7.1 %collective-permute-done.3 = f32[264,128]{0,1:T(8,128)S(1)} collective-permute-done((f32[264,128]{0,1:T(8,128)S(1)}, f32[264,128]{0,1:T(8,128)S(1)}, u32[]{:S(2)}, u32[]{:S(2)}) %collective-permute-start.3) | collective-permute-done | bytes 135200 | tf_op jit(solution)/shard_map/ppermute | solution.py:33
  54.2 10.8 %collective-permute-start.4 = (f32[264,128]{0,1:T(8,128)S(1)}, f32[264,128]{0,1:T(8,128)S(1)}, u32[]{:S(2)}, u32[]{:S(2)}) collective-permute-start(f32[264,128]{0,1:T(8,128)S(1)} %pad_maximum_fusion.4), channel_id=1, source_target_pairs={{0,64},{8,72},{16,80},{24,88},{32,96},{40,104},{48,112},{56,120},{... | collective-permute-start | bytes 405512 | tf_op jit(solution)/shard_map/ppermute | solution.py:33
  65.2 11.3 %collective-permute-done.4 = f32[264,128]{0,1:T(8,128)S(1)} collective-permute-done((f32[264,128]{0,1:T(8,128)S(1)}, f32[264,128]{0,1:T(8,128)S(1)}, u32[]{:S(2)}, u32[]{:S(2)}) %collective-permute-start.4) | collective-permute-done | bytes 135200 | tf_op jit(solution)/shard_map/ppermute | solution.py:33
  76.7 3.0 %collective-permute-start.5 = (f32[2,128,128]{2,1,0:T(8,128)S(1)}, f32[2,128,128]{2,1,0:T(8,128)S(1)}, u32[]{:S(2)}, u32[]{:S(2)}) collective-permute-start(f32[2,128,128]{2,1,0:T(8,128)S(1)} %multiply_add_fusion.8), channel_id=1, source_target_pairs={{0,128},{8,136},{16,144},{24,152},{32,160},{40,168},{48,176},{56,1... | collective-permute-start | bytes 393224 | tf_op jit(solution)/shard_map/ppermute | solution.py:111
  80.0 0.8 reshape.231.query_ref
  80.9 3.0 %collective-permute-done.5 = f32[2,128,128]{2,1,0:T(8,128)S(1)} collective-permute-done((f32[2,128,128]{2,1,0:T(8,128)S(1)}, f32[2,128,128]{2,1,0:T(8,128)S(1)}, u32[]{:S(2)}, u32[]{:S(2)}) %collective-permute-start.5) | collective-permute-done | bytes 131104 | tf_op jit(solution)/shard_map/ppermute | solution.py:111
  84.0 0.6 collective-permute-start.6
  84.6 0.7 convolution_bitcast_fusion.1
  85.3 5.3 %collective-permute-done.6 = f32[2,128,128]{2,1,0:T(8,128)S(1)} collective-permute-done((f32[2,128,128]{2,1,0:T(8,128)S(1)}, f32[2,128,128]{2,1,0:T(8,128)S(1)}, u32[]{:S(2)}, u32[]{:S(2)}) %collective-permute-start.6) | collective-permute-done | bytes 131104 | tf_op jit(solution)/shard_map/ppermute | solution.py:89
  91.0 12.3 %shard_map.94 = f32[1024,128]{1,0:T(8,128)} custom-call(s32[1]{0:T(128)} %bitcast.21.first_ref, bf16[1024,128]{1,0:T(8,128)(2,1)} %reshape.231.query_ref, bf16[4096,384]{1,0:T(8,128)(2,1)} %all-gather.2.cloned.1.call-done.key_ref.upper_ref.lower_ref, bf16[4096,384]{1,0:T(8,128)(2,1)} %all-gather.2.cloned.1.call-done.key_ref.upper_ref.lower_ref, ...), custom_call_target="tpu_custom_call" | custom-call | flops 4294967296 | bytes 3932160 | tf_op jit(solution)/shard_map/pallas_call | solution.py:193
  103.2 1.7 fusion.3
  105.0 1.1 fusion.12
  106.8 1.2 collective-permute-done.10
  108.5 0.6 collective-permute-start.11
  109.1 6.9 %collective-permute-done.11 = f32[264,128]{1,0:T(8,128)S(1)} collective-permute-done((f32[264,128]{1,0:T(8,128)S(1)}, f32[264,128]{1,0:T(8,128)S(1)}, u32[]{:S(2)}, u32[]{:S(2)}) %collective-permute-start.11) | collective-permute-done | bytes 135200 | tf_op jit(solution)/shard_map/ppermute | solution.py:33
  116.4 1.9 collective-permute-start.12
  118.3 6.3 %collective-permute-done.12 = f32[264,128]{0,1:T(8,128)S(1)} collective-permute-done((f32[264,128]{0,1:T(8,128)S(1)}, f32[264,128]{0,1:T(8,128)S(1)}, u32[]{:S(2)}, u32[]{:S(2)}) %collective-permute-start.12) | collective-permute-done | bytes 135200 | tf_op jit(solution)/shard_map/ppermute | solution.py:33
  124.7 2.2 %collective-permute-start.13 = (f32[264,128]{0,1:T(8,128)S(1)}, f32[264,128]{0,1:T(8,128)S(1)}, u32[]{:S(2)}, u32[]{:S(2)}) collective-permute-start(f32[264,128]{0,1:T(8,128)S(1)} %pad_maximum_fusion.6), channel_id=1, source_target_pairs={{32,0},{40,8},{48,16},{56,24},{64,32},{72,40},{80,48},{88,56},{96,... | collective-permute-start | bytes 405512 | tf_op jit(solution)/shard_map/ppermute | solution.py:33
  127.0 14.7 %collective-permute-done.13 = f32[264,128]{0,1:T(8,128)S(1)} collective-permute-done((f32[264,128]{0,1:T(8,128)S(1)}, f32[264,128]{0,1:T(8,128)S(1)}, u32[]{:S(2)}, u32[]{:S(2)}) %collective-permute-start.13) | collective-permute-done | bytes 135200 | tf_op jit(solution)/shard_map/ppermute | solution.py:33
  141.7 0.7 pad_maximum_fusion.7
  142.4 1.9 collective-permute-start.14
  144.9 11.0 %collective-permute-done.14 = f32[264,128]{0,1:T(8,128)} collective-permute-done((f32[264,128]{0,1:T(8,128)}, f32[264,128]{0,1:T(8,128)}, u32[]{:S(2)}, u32[]{:S(2)}) %collective-permute-start.14) | collective-permute-done | bytes 135200 | tf_op jit(solution)/shard_map/ppermute | solution.py:33
  155.9 0.9 slice.111
  156.9 0.7 fusion.53
  157.7 1.3 collective-permute-start.15
  159.3 9.2 %collective-permute-done.15 = f32[2,128,128]{2,1,0:T(8,128)S(1)} collective-permute-done((f32[2,128,128]{2,1,0:T(8,128)S(1)}, f32[2,128,128]{2,1,0:T(8,128)S(1)}, u32[]{:S(2)}, u32[]{:S(2)}) %collective-permute-start.15) | collective-permute-done | bytes 131104 | tf_op jit(solution)/shard_map/ppermute | solution.py:111
  168.6 0.6 collective-permute-start.16
  169.2 1.2 fusion.6
  170.4 4.8 %collective-permute-done.16 = f32[2,128,128]{2,1,0:T(8,128)S(1)} collective-permute-done((f32[2,128,128]{2,1,0:T(8,128)S(1)}, f32[2,128,128]{2,1,0:T(8,128)S(1)}, u32[]{:S(2)}, u32[]{:S(2)}) %collective-permute-start.16) | collective-permute-done | bytes 131104 | tf_op jit(solution)/shard_map/ppermute | solution.py:89
  175.9 1.2 convolution_bitcast_fusion.2
  177.1 1.0 fusion.5
  178.2 0.7 copy.83
  178.9 5.0 %all-to-all-start = ((f32[8,16,256]{2,1,0:T(8,128)}), f32[8,16,256]{2,1,0:T(8,128)S(1)}, u32[]{:S(2)}, u32[]{:S(2)}) async-start(f32[8,16,256]{2,1,0:T(8,128)} %bitcast.41), calls=%async_computation | async-start | bytes 262144 | tf_op jit(solution)/shard_map/all_to_all | solution.py:135
  184.3 1.0 copy.84
  185.2 5.2 %all-to-all-done = f32[8,16,256]{2,1,0:T(8,128)S(1)} async-done(((f32[8,16,256]{2,1,0:T(8,128)}), f32[8,16,256]{2,1,0:T(8,128)S(1)}, u32[]{:S(2)}, u32[]{:S(2)}) %all-to-all-start) | async-done | bytes 131104 | tf_op jit(solution)/shard_map/all_to_all | solution.py:135
  190.5 0.6 slice_multiply_fusion
  (112 shorter events, 8.5 us)
Async XLA Ops:
  7.2 2.4 %copy-start = (bf16[128,128]{1,0:T(8,128)(2,1)S(1)}, bf16[128,128]{1,0:T(8,128)(2,1)}, u32[]{:S(2)}) copy-start(bf16[128,128]{1,0:T(8,128)(2,1)} %param.11) | copy-start | bytes 98308
  7.2 6.2 %copy-start.3 = (bf16[128,128]{1,0:T(8,128)(2,1)S(1)}, bf16[128,128]{1,0:T(8,128)(2,1)}, u32[]{:S(2)}) copy-start(bf16[128,128]{1,0:T(8,128)(2,1)} %param.8) | copy-start | bytes 98308
  7.2 83.8 %all-gather.2.cloned.1.call-start = ((), (), s32[]{:S(2)}) async-start(), calls=%async_computation.1 | async-start | bytes 3538944 | tf_op jit(solution)/shard_map/all_gather | solution.py:124
  10.1 3.9 %collective-permute-start = (f32[520,128]{1,0:T(8,128)S(1)}, f32[520,128]{1,0:T(8,128)S(1)}, u32[]{:S(2)}, u32[]{:S(2)}) collective-permute-start(f32[520,128]{1,0:T(8,128)S(1)} %pad_maximum_fusion), channel_id=1, source_target_pairs={{0,8},{8,0},{16,24},{24,16},{32,40},{40,32},{48,56},{56,48},{64,72... | collective-permute-start | bytes 798728 | tf_op jit(solution)/shard_map/ppermute | solution.py:36
  11.8 1.5 collective-permute-start.8
  13.4 8.8 %collective-permute-start.9 = (bf16[256,384]{1,0:T(8,128)(2,1)S(1)}, bf16[256,384]{1,0:T(8,128)(2,1)S(1)}, u32[]{:S(2)}, u32[]{:S(2)}) collective-permute-start(bf16[256,384]{1,0:T(8,128)(2,1)S(1)} %maximum_select_fusion.9), channel_id=1, source_target_pairs={{0,16},{8,24},{16,0},{24,8},{32,48},{40,56},{48,32},{56,40},{64,80... | collective-permute-start | bytes 589832 | tf_op jit(solution)/shard_map/ppermute | solution.py:36
  23.1 56.7 %copy-start.1 = (bf16[128,128]{1,0:T(8,128)(2,1)S(1)}, bf16[128,128]{1,0:T(8,128)(2,1)}, u32[]{:S(2)}) copy-start(bf16[128,128]{1,0:T(8,128)(2,1)} %param.12) | copy-start | bytes 98308
  23.2 56.9 %copy-start.2 = (bf16[128,1024]{1,0:T(8,128)(2,1)S(1)}, bf16[128,1024]{1,0:T(8,128)(2,1)}, u32[]{:S(2)}) copy-start(bf16[128,1024]{1,0:T(8,128)(2,1)} %param.7) | copy-start | bytes 786436
  23.5 6.6 %collective-permute-start.1 = (f32[264,128]{1,0:T(8,128)S(1)}, f32[264,128]{1,0:T(8,128)S(1)}, u32[]{:S(2)}, u32[]{:S(2)}) collective-permute-start(f32[264,128]{1,0:T(8,128)S(1)} %pad_maximum_fusion.8), channel_id=1, source_target_pairs={{0,16},{8,24},{16,0},{24,8},{32,48},{40,56},{48,32},{56,40},{64,80... | collective-permute-start | bytes 405512 | tf_op jit(solution)/shard_map/ppermute | solution.py:36
  30.5 8.9 %collective-permute-start.2 = (f32[264,128]{0,1:T(8,128)S(1)}, f32[264,128]{0,1:T(8,128)S(1)}, u32[]{:S(2)}, u32[]{:S(2)}) collective-permute-start(f32[264,128]{0,1:T(8,128)S(1)} %pad_maximum_fusion.2), channel_id=1, source_target_pairs={{0,32},{8,40},{16,48},{24,56},{32,64},{40,72},{48,80},{56,88},{64,... | collective-permute-start | bytes 405512 | tf_op jit(solution)/shard_map/ppermute | solution.py:33
  39.5 14.6 %collective-permute-start.3 = (f32[264,128]{0,1:T(8,128)S(1)}, f32[264,128]{0,1:T(8,128)S(1)}, u32[]{:S(2)}, u32[]{:S(2)}) collective-permute-start(f32[264,128]{0,1:T(8,128)S(1)} %pad_maximum_fusion.3), channel_id=1, source_target_pairs={{0,32},{8,40},{16,48},{24,56},{32,64},{40,72},{48,80},{56,88},{64,... | collective-permute-start | bytes 405512 | tf_op jit(solution)/shard_map/ppermute | solution.py:33
  54.2 22.3 %collective-permute-start.4 = (f32[264,128]{0,1:T(8,128)S(1)}, f32[264,128]{0,1:T(8,128)S(1)}, u32[]{:S(2)}, u32[]{:S(2)}) collective-permute-start(f32[264,128]{0,1:T(8,128)S(1)} %pad_maximum_fusion.4), channel_id=1, source_target_pairs={{0,64},{8,72},{16,80},{24,88},{32,96},{40,104},{48,112},{56,120},{... | collective-permute-start | bytes 405512 | tf_op jit(solution)/shard_map/ppermute | solution.py:33
  76.7 7.2 %collective-permute-start.5 = (f32[2,128,128]{2,1,0:T(8,128)S(1)}, f32[2,128,128]{2,1,0:T(8,128)S(1)}, u32[]{:S(2)}, u32[]{:S(2)}) collective-permute-start(f32[2,128,128]{2,1,0:T(8,128)S(1)} %multiply_add_fusion.8), channel_id=1, source_target_pairs={{0,128},{8,136},{16,144},{24,152},{32,160},{40,168},{48,176},{56,1... | collective-permute-start | bytes 393224 | tf_op jit(solution)/shard_map/ppermute | solution.py:111
  84.0 6.6 %collective-permute-start.6 = (f32[2,128,128]{2,1,0:T(8,128)S(1)}, f32[2,128,128]{2,1,0:T(8,128)S(1)}, u32[]{:S(2)}, u32[]{:S(2)}) collective-permute-start(f32[2,128,128]{2,1,0:T(8,128)S(1)} %get-tuple-element.27), channel_id=1, source_target_pairs={{0,16},{8,24},{16,0},{24,8},{32,48},{40,56},{48,32},{56,40},{64,80... | collective-permute-start | bytes 393224 | tf_op jit(solution)/shard_map/ppermute | solution.py:89
  90.7 12.6 %collective-permute-start.7 = (f32[4,128,128]{2,1,0:T(8,128)S(1)}, f32[4,128,128]{2,1,0:T(8,128)S(1)}, u32[]{:S(2)}, u32[]{:S(2)}) collective-permute-start(f32[4,128,128]{2,1,0:T(8,128)S(1)} %get-tuple-element.22), channel_id=1, source_target_pairs={{0,8},{8,0},{16,24},{24,16},{32,40},{40,32},{48,56},{56,48},{64,72... | collective-permute-start | bytes 786440 | tf_op jit(solution)/shard_map/ppermute | solution.py:89
  106.3 1.7 collective-permute-start.10
  108.5 7.5 %collective-permute-start.11 = (f32[264,128]{1,0:T(8,128)S(1)}, f32[264,128]{1,0:T(8,128)S(1)}, u32[]{:S(2)}, u32[]{:S(2)}) collective-permute-start(f32[264,128]{1,0:T(8,128)S(1)} %pad_maximum_fusion.9), channel_id=1, source_target_pairs={{0,16},{8,24},{16,0},{24,8},{32,48},{40,56},{48,32},{56,40},{64,80... | collective-permute-start | bytes 405512 | tf_op jit(solution)/shard_map/ppermute | solution.py:33
  116.4 8.3 %collective-permute-start.12 = (f32[264,128]{0,1:T(8,128)S(1)}, f32[264,128]{0,1:T(8,128)S(1)}, u32[]{:S(2)}, u32[]{:S(2)}) collective-permute-start(f32[264,128]{0,1:T(8,128)S(1)} %pad_maximum_fusion.5), channel_id=1, source_target_pairs={{32,0},{40,8},{48,16},{56,24},{64,32},{72,40},{80,48},{88,56},{96,... | collective-permute-start | bytes 405512 | tf_op jit(solution)/shard_map/ppermute | solution.py:33
  124.7 17.0 %collective-permute-start.13 = (f32[264,128]{0,1:T(8,128)S(1)}, f32[264,128]{0,1:T(8,128)S(1)}, u32[]{:S(2)}, u32[]{:S(2)}) collective-permute-start(f32[264,128]{0,1:T(8,128)S(1)} %pad_maximum_fusion.6), channel_id=1, source_target_pairs={{32,0},{40,8},{48,16},{56,24},{64,32},{72,40},{80,48},{88,56},{96,... | collective-permute-start | bytes 405512 | tf_op jit(solution)/shard_map/ppermute | solution.py:33
  141.6 0.7 copy-start.4
  142.4 13.5 %collective-permute-start.14 = (f32[264,128]{0,1:T(8,128)}, f32[264,128]{0,1:T(8,128)}, u32[]{:S(2)}, u32[]{:S(2)}) collective-permute-start(f32[264,128]{0,1:T(8,128)} %pad_maximum_fusion.7), channel_id=1, source_target_pairs={{64,0},{72,8},{80,16},{88,24},{96,32},{104,40},{112,48},{120,56},{... | collective-permute-start | bytes 405512 | tf_op jit(solution)/shard_map/ppermute | solution.py:33
  157.7 10.8 %collective-permute-start.15 = (f32[2,128,128]{2,1,0:T(8,128)S(1)}, f32[2,128,128]{2,1,0:T(8,128)S(1)}, u32[]{:S(2)}, u32[]{:S(2)}) collective-permute-start(f32[2,128,128]{2,1,0:T(8,128)S(1)} %multiply_add_fusion.4), channel_id=1, source_target_pairs={{128,0},{136,8},{144,16},{152,24},{160,32},{168,40},{176,48},{184,... | collective-permute-start | bytes 393224 | tf_op jit(solution)/shard_map/ppermute | solution.py:111
  168.6 6.6 %collective-permute-start.16 = (f32[2,128,128]{2,1,0:T(8,128)S(1)}, f32[2,128,128]{2,1,0:T(8,128)S(1)}, u32[]{:S(2)}, u32[]{:S(2)}) collective-permute-start(f32[2,128,128]{2,1,0:T(8,128)S(1)} %get-tuple-element.25), channel_id=1, source_target_pairs={{0,16},{8,24},{16,0},{24,8},{32,48},{40,56},{48,32},{56,40},{64,80... | collective-permute-start | bytes 393224 | tf_op jit(solution)/shard_map/ppermute | solution.py:89
  175.3 1.8 collective-permute-start.17
  178.9 11.5 %all-to-all-start = ((f32[8,16,256]{2,1,0:T(8,128)}), f32[8,16,256]{2,1,0:T(8,128)S(1)}, u32[]{:S(2)}, u32[]{:S(2)}) async-start(f32[8,16,256]{2,1,0:T(8,128)} %bitcast.41), calls=%async_computation | async-start | bytes 262144 | tf_op jit(solution)/shard_map/all_to_all | solution.py:135
Sparse Core Ops, SparseCore 0:
  23.2 60.6 all-gather.1

commit v12 on v9

--- a/solution.py
+++ b/solution.py
@@ -151,7 +151,8 @@
     def accumulate(masked):
         scores = lax.dot_general(
             query_ref[...], key_ref[...], (((1,), (1,)), ((), ())), preferred_element_type=jnp.float32
-        ) * (1.0 / math.sqrt(width))
+        )
+        factor = math.log2(math.e) / math.sqrt(width)
         if masked:
             row = lax.broadcasted_iota(jnp.int32, scores.shape, 0)
             col = lax.broadcasted_iota(jnp.int32, scores.shape, 1)
@@ -159,8 +160,8 @@
             scores = jnp.where(allowed, scores, very_negative)
         top_old = top_ref[...]
         top_new = jnp.maximum(top_old, jnp.max(scores, axis=1, keepdims=True))
-        rescale = jnp.exp(top_old - top_new)
-        weights = jnp.exp(scores - top_new)
+        rescale = jnp.exp2((top_old - top_new) * factor)
+        weights = jnp.exp2((scores - top_new) * factor)
         if masked:
             weights = jnp.where(allowed, weights, 0.0)
         total_ref[...] = rescale * total_ref[...] + jnp.sum(weights, axis=1, keepdims=True)

time: 195 us -> 195 us (level)
  no operation moved by 1% of the time
where the time goes in v12:
time: 195 us; the launch traced here: 193 us
  waiting for transfers between devices  103 us (53%)
  starting transfers between devices  42.4 us (22%)
  between operations  14.6 us (7%)
  Pallas kernels  10.3 us (5%)
  matrix products  8.74 us (4%)
  local copies, waits for them, and re-layouts  7.42 us (4%)
  other arithmetic  6.69 us (3%)
    ppermute x8, waiting for transfers between devices, send_with_logs(): got = lax.ppermute(payload, axis, perm)  60.7 us
    ppermute x8, starting transfers between devices, send_with_logs(): got = lax.ppermute(payload, axis, perm)  29.2 us
    ppermute x4, waiting for transfers between devices, send_with_logs(): got, got_extra = lax.ppermute((payload, extra), axis, perm)  14.9 us
    ppermute x2, waiting for transfers between devices, exclusive_scan(): got_state = lax.ppermute(window_state, axis, perm)  12.2 us
    pallas_call x1, Pallas kernels, attend(): pl.pallas_call(functools.partial(attend_kernel, heads=heads), out_shape=j...  10.3 us
    ppermute x4, waiting for transfers between devices, pair_up(): got = lax.ppermute(send, axis, [(j, j ^ bit) for j in range(count)])  10.1 us
    all_to_all x1, waiting for transfers between devices, mp_sum_scatter(): return jnp.sum(lax.all_to_all(blocks, axis, 0, 0), axis=0)  5.19 us
    all_to_all x1, starting transfers between devices, mp_sum_scatter(): return jnp.sum(lax.all_to_all(blocks, axis, 0, 0), axis=0)  5.06 us
  transfers between devices with their start and end apart: 20, of which 16 were waited for; matrix products, arithmetic and copies ran while one was open for 5% of the time, Pallas kernels for 5%

profile of v12, /device:TPU:68, one launch (start us, length us, event | category | flops | bytes accessed | tf_op | source)
XLA Modules:
  0.0 193.2 jit_solution(9647687217304322397)
XLA Ops:
  7.3 0.8 copy.61
  8.4 1.1 copy.64
  10.2 0.9 reduce-precision_convert_fusion
  11.1 0.8 pad_maximum_fusion.11
  12.4 0.9 collective-permute-done.8
  13.4 0.6 collective-permute-start.9
  14.2 8.0 %collective-permute-done.9 = bf16[256,384]{1,0:T(8,128)(2,1)S(1)} collective-permute-done((bf16[256,384]{1,0:T(8,128)(2,1)S(1)}, bf16[256,384]{1,0:T(8,128)(2,1)S(1)}, u32[]{:S(2)}, u32[]{:S(2)}) %collective-permute-start.9) | collective-permute-done | bytes 196640 | tf_op jit(solution)/shard_map/ppermute | solution.py:36
  22.2 0.9 maximum_select_fusion.2
  24.1 6.0 %collective-permute-done.1 = f32[264,128]{1,0:T(8,128)S(1)} collective-permute-done((f32[264,128]{1,0:T(8,128)S(1)}, f32[264,128]{1,0:T(8,128)S(1)}, u32[]{:S(2)}, u32[]{:S(2)}) %collective-permute-start.1) | collective-permute-done | bytes 135200 | tf_op jit(solution)/shard_map/ppermute | solution.py:36
  30.5 3.8 %collective-permute-start.2 = (f32[264,128]{0,1:T(8,128)S(1)}, f32[264,128]{0,1:T(8,128)S(1)}, u32[]{:S(2)}, u32[]{:S(2)}) collective-permute-start(f32[264,128]{0,1:T(8,128)S(1)} %pad_maximum_fusion.2), channel_id=1, source_target_pairs={{0,32},{8,40},{16,48},{24,56},{32,64},{40,72},{48,80},{56,88},{64,... | collective-permute-start | bytes 405512 | tf_op jit(solution)/shard_map/ppermute | solution.py:33
  34.4 5.1 %collective-permute-done.2 = f32[264,128]{0,1:T(8,128)S(1)} collective-permute-done((f32[264,128]{0,1:T(8,128)S(1)}, f32[264,128]{0,1:T(8,128)S(1)}, u32[]{:S(2)}, u32[]{:S(2)}) %collective-permute-start.2) | collective-permute-done | bytes 135200 | tf_op jit(solution)/shard_map/ppermute | solution.py:33
  39.5 7.4 %collective-permute-start.3 = (f32[264,128]{0,1:T(8,128)S(1)}, f32[264,128]{0,1:T(8,128)S(1)}, u32[]{:S(2)}, u32[]{:S(2)}) collective-permute-start(f32[264,128]{0,1:T(8,128)S(1)} %pad_maximum_fusion.3), channel_id=1, source_target_pairs={{0,32},{8,40},{16,48},{24,56},{32,64},{40,72},{48,80},{56,88},{64,... | collective-permute-start | bytes 405512 | tf_op jit(solution)/shard_map/ppermute | solution.py:33
  47.0 7.1 %collective-permute-done.3 = f32[264,128]{0,1:T(8,128)S(1)} collective-permute-done((f32[264,128]{0,1:T(8,128)S(1)}, f32[264,128]{0,1:T(8,128)S(1)}, u32[]{:S(2)}, u32[]{:S(2)}) %collective-permute-start.3) | collective-permute-done | bytes 135200 | tf_op jit(solution)/shard_map/ppermute | solution.py:33
  54.2 10.8 %collective-permute-start.4 = (f32[264,128]{0,1:T(8,128)S(1)}, f32[264,128]{0,1:T(8,128)S(1)}, u32[]{:S(2)}, u32[]{:S(2)}) collective-permute-start(f32[264,128]{0,1:T(8,128)S(1)} %pad_maximum_fusion.4), channel_id=1, source_target_pairs={{0,64},{8,72},{16,80},{24,88},{32,96},{40,104},{48,112},{56,120},{... | collective-permute-start | bytes 405512 | tf_op jit(solution)/shard_map/ppermute | solution.py:33
  65.2 11.3 %collective-permute-done.4 = f32[264,128]{0,1:T(8,128)S(1)} collective-permute-done((f32[264,128]{0,1:T(8,128)S(1)}, f32[264,128]{0,1:T(8,128)S(1)}, u32[]{:S(2)}, u32[]{:S(2)}) %collective-permute-start.4) | collective-permute-done | bytes 135200 | tf_op jit(solution)/shard_map/ppermute | solution.py:33
  76.7 3.0 %collective-permute-start.5 = (f32[2,128,128]{2,1,0:T(8,128)S(1)}, f32[2,128,128]{2,1,0:T(8,128)S(1)}, u32[]{:S(2)}, u32[]{:S(2)}) collective-permute-start(f32[2,128,128]{2,1,0:T(8,128)S(1)} %multiply_add_fusion.8), channel_id=1, source_target_pairs={{0,128},{8,136},{16,144},{24,152},{32,160},{40,168},{48,176},{56,1... | collective-permute-start | bytes 393224 | tf_op jit(solution)/shard_map/ppermute | solution.py:111
  80.0 0.8 reshape.231.query_ref
  80.9 3.0 %collective-permute-done.5 = f32[2,128,128]{2,1,0:T(8,128)S(1)} collective-permute-done((f32[2,128,128]{2,1,0:T(8,128)S(1)}, f32[2,128,128]{2,1,0:T(8,128)S(1)}, u32[]{:S(2)}, u32[]{:S(2)}) %collective-permute-start.5) | collective-permute-done | bytes 131104 | tf_op jit(solution)/shard_map/ppermute | solution.py:111
  84.0 0.6 collective-permute-start.6
  84.6 0.7 convolution_bitcast_fusion.1
  85.3 5.3 %collective-permute-done.6 = f32[2,128,128]{2,1,0:T(8,128)S(1)} collective-permute-done((f32[2,128,128]{2,1,0:T(8,128)S(1)}, f32[2,128,128]{2,1,0:T(8,128)S(1)}, u32[]{:S(2)}, u32[]{:S(2)}) %collective-permute-start.6) | collective-permute-done | bytes 131104 | tf_op jit(solution)/shard_map/ppermute | solution.py:89
  91.0 10.3 %shard_map.94 = f32[1024,128]{1,0:T(8,128)} custom-call(s32[1]{0:T(128)} %bitcast.21.first_ref, bf16[1024,128]{1,0:T(8,128)(2,1)} %reshape.231.query_ref, bf16[4096,384]{1,0:T(8,128)(2,1)} %all-gather.2.cloned.1.call-done.key_ref.upper_ref.lower_ref, bf16[4096,384]{1,0:T(8,128)(2,1)} %all-gather.2.cloned.1.call-done.key_ref.upper_ref.lower_ref, ...), custom_call_target="tpu_custom_call" | custom-call | flops 4294967296 | bytes 3932160 | tf_op jit(solution)/shard_map/pallas_call | solution.py:198
  101.2 1.7 fusion.3
  103.0 1.1 fusion.12
  104.8 1.2 collective-permute-done.10
  106.5 0.6 collective-permute-start.11
  107.1 6.9 %collective-permute-done.11 = f32[264,128]{1,0:T(8,128)S(1)} collective-permute-done((f32[264,128]{1,0:T(8,128)S(1)}, f32[264,128]{1,0:T(8,128)S(1)}, u32[]{:S(2)}, u32[]{:S(2)}) %collective-permute-start.11) | collective-permute-done | bytes 135200 | tf_op jit(solution)/shard_map/ppermute | solution.py:33
  114.4 1.9 collective-permute-start.12
  116.3 6.3 %collective-permute-done.12 = f32[264,128]{0,1:T(8,128)S(1)} collective-permute-done((f32[264,128]{0,1:T(8,128)S(1)}, f32[264,128]{0,1:T(8,128)S(1)}, u32[]{:S(2)}, u32[]{:S(2)}) %collective-permute-start.12) | collective-permute-done | bytes 135200 | tf_op jit(solution)/shard_map/ppermute | solution.py:33
  122.7 2.2 %collective-permute-start.13 = (f32[264,128]{0,1:T(8,128)S(1)}, f32[264,128]{0,1:T(8,128)S(1)}, u32[]{:S(2)}, u32[]{:S(2)}) collective-permute-start(f32[264,128]{0,1:T(8,128)S(1)} %pad_maximum_fusion.6), channel_id=1, source_target_pairs={{32,0},{40,8},{48,16},{56,24},{64,32},{72,40},{80,48},{88,56},{96,... | collective-permute-start | bytes 405512 | tf_op jit(solution)/shard_map/ppermute | solution.py:33
  125.0 13.2 %collective-permute-done.13 = f32[264,128]{0,1:T(8,128)S(1)} collective-permute-done((f32[264,128]{0,1:T(8,128)S(1)}, f32[264,128]{0,1:T(8,128)S(1)}, u32[]{:S(2)}, u32[]{:S(2)}) %collective-permute-start.13) | collective-permute-done | bytes 135200 | tf_op jit(solution)/shard_map/ppermute | solution.py:33
  138.2 0.7 pad_maximum_fusion.7
  138.9 1.9 collective-permute-start.14
  141.4 9.6 %collective-permute-done.14 = f32[264,128]{0,1:T(8,128)} collective-permute-done((f32[264,128]{0,1:T(8,128)}, f32[264,128]{0,1:T(8,128)}, u32[]{:S(2)}, u32[]{:S(2)}) %collective-permute-start.14) | collective-permute-done | bytes 135200 | tf_op jit(solution)/shard_map/ppermute | solution.py:33
  151.1 0.9 slice.111
  152.1 0.7 fusion.53
  152.9 1.3 collective-permute-start.15
  154.4 9.2 %collective-permute-done.15 = f32[2,128,128]{2,1,0:T(8,128)S(1)} collective-permute-done((f32[2,128,128]{2,1,0:T(8,128)S(1)}, f32[2,128,128]{2,1,0:T(8,128)S(1)}, u32[]{:S(2)}, u32[]{:S(2)}) %collective-permute-start.15) | collective-permute-done | bytes 131104 | tf_op jit(solution)/shard_map/ppermute | solution.py:111
  163.7 0.7 collective-permute-start.16
  164.4 1.1 fusion.6
  165.6 4.7 %collective-permute-done.16 = f32[2,128,128]{2,1,0:T(8,128)S(1)} collective-permute-done((f32[2,128,128]{2,1,0:T(8,128)S(1)}, f32[2,128,128]{2,1,0:T(8,128)S(1)}, u32[]{:S(2)}, u32[]{:S(2)}) %collective-permute-start.16) | collective-permute-done | bytes 131104 | tf_op jit(solution)/shard_map/ppermute | solution.py:89
  171.0 1.2 convolution_bitcast_fusion.2
  172.3 1.0 fusion.5
  173.3 0.7 copy.83
  174.0 5.1 %all-to-all-start = ((f32[8,16,256]{2,1,0:T(8,128)}), f32[8,16,256]{2,1,0:T(8,128)S(1)}, u32[]{:S(2)}, u32[]{:S(2)}) async-start(f32[8,16,256]{2,1,0:T(8,128)} %bitcast.41), calls=%async_computation | async-start | bytes 262144 | tf_op jit(solution)/shard_map/all_to_all | solution.py:135
  179.5 1.0 copy.84
  180.5 5.2 %all-to-all-done = f32[8,16,256]{2,1,0:T(8,128)S(1)} async-done(((f32[8,16,256]{2,1,0:T(8,128)}), f32[8,16,256]{2,1,0:T(8,128)S(1)}, u32[]{:S(2)}, u32[]{:S(2)}) %all-to-all-start) | async-done | bytes 131104 | tf_op jit(solution)/shard_map/all_to_all | solution.py:135
  185.7 0.6 slice_multiply_fusion
  (112 shorter events, 8.5 us)
Async XLA Ops:
  7.2 2.4 %copy-start = (bf16[128,128]{1,0:T(8,128)(2,1)S(1)}, bf16[128,128]{1,0:T(8,128)(2,1)}, u32[]{:S(2)}) copy-start(bf16[128,128]{1,0:T(8,128)(2,1)} %param.11) | copy-start | bytes 98308
  7.2 6.2 %copy-start.3 = (bf16[128,128]{1,0:T(8,128)(2,1)S(1)}, bf16[128,128]{1,0:T(8,128)(2,1)}, u32[]{:S(2)}) copy-start(bf16[128,128]{1,0:T(8,128)(2,1)} %param.8) | copy-start | bytes 98308
  7.2 83.8 %all-gather.2.cloned.1.call-start = ((), (), s32[]{:S(2)}) async-start(), calls=%async_computation.1 | async-start | bytes 3538944 | tf_op jit(solution)/shard_map/all_gather | solution.py:124
  10.1 3.9 %collective-permute-start = (f32[520,128]{1,0:T(8,128)S(1)}, f32[520,128]{1,0:T(8,128)S(1)}, u32[]{:S(2)}, u32[]{:S(2)}) collective-permute-start(f32[520,128]{1,0:T(8,128)S(1)} %pad_maximum_fusion), channel_id=1, source_target_pairs={{0,8},{8,0},{16,24},{24,16},{32,40},{40,32},{48,56},{56,48},{64,72... | collective-permute-start | bytes 798728 | tf_op jit(solution)/shard_map/ppermute | solution.py:36
  11.8 1.5 collective-permute-start.8
  13.4 8.8 %collective-permute-start.9 = (bf16[256,384]{1,0:T(8,128)(2,1)S(1)}, bf16[256,384]{1,0:T(8,128)(2,1)S(1)}, u32[]{:S(2)}, u32[]{:S(2)}) collective-permute-start(bf16[256,384]{1,0:T(8,128)(2,1)S(1)} %maximum_select_fusion.9), channel_id=1, source_target_pairs={{0,16},{8,24},{16,0},{24,8},{32,48},{40,56},{48,32},{56,40},{64,80... | collective-permute-start | bytes 589832 | tf_op jit(solution)/shard_map/ppermute | solution.py:36
  23.1 56.7 %copy-start.1 = (bf16[128,128]{1,0:T(8,128)(2,1)S(1)}, bf16[128,128]{1,0:T(8,128)(2,1)}, u32[]{:S(2)}) copy-start(bf16[128,128]{1,0:T(8,128)(2,1)} %param.12) | copy-start | bytes 98308
  23.2 56.9 %copy-start.2 = (bf16[128,1024]{1,0:T(8,128)(2,1)S(1)}, bf16[128,1024]{1,0:T(8,128)(2,1)}, u32[]{:S(2)}) copy-start(bf16[128,1024]{1,0:T(8,128)(2,1)} %param.7) | copy-start | bytes 786436
  23.5 6.6 %collective-permute-start.1 = (f32[264,128]{1,0:T(8,128)S(1)}, f32[264,128]{1,0:T(8,128)S(1)}, u32[]{:S(2)}, u32[]{:S(2)}) collective-permute-start(f32[264,128]{1,0:T(8,128)S(1)} %pad_maximum_fusion.8), channel_id=1, source_target_pairs={{0,16},{8,24},{16,0},{24,8},{32,48},{40,56},{48,32},{56,40},{64,80... | collective-permute-start | bytes 405512 | tf_op jit(solution)/shard_map/ppermute | solution.py:36
  30.5 8.9 %collective-permute-start.2 = (f32[264,128]{0,1:T(8,128)S(1)}, f32[264,128]{0,1:T(8,128)S(1)}, u32[]{:S(2)}, u32[]{:S(2)}) collective-permute-start(f32[264,128]{0,1:T(8,128)S(1)} %pad_maximum_fusion.2), channel_id=1, source_target_pairs={{0,32},{8,40},{16,48},{24,56},{32,64},{40,72},{48,80},{56,88},{64,... | collective-permute-start | bytes 405512 | tf_op jit(solution)/shard_map/ppermute | solution.py:33
  39.5 14.6 %collective-permute-start.3 = (f32[264,128]{0,1:T(8,128)S(1)}, f32[264,128]{0,1:T(8,128)S(1)}, u32[]{:S(2)}, u32[]{:S(2)}) collective-permute-start(f32[264,128]{0,1:T(8,128)S(1)} %pad_maximum_fusion.3), channel_id=1, source_target_pairs={{0,32},{8,40},{16,48},{24,56},{32,64},{40,72},{48,80},{56,88},{64,... | collective-permute-start | bytes 405512 | tf_op jit(solution)/shard_map/ppermute | solution.py:33
  54.2 22.3 %collective-permute-start.4 = (f32[264,128]{0,1:T(8,128)S(1)}, f32[264,128]{0,1:T(8,128)S(1)}, u32[]{:S(2)}, u32[]{:S(2)}) collective-permute-start(f32[264,128]{0,1:T(8,128)S(1)} %pad_maximum_fusion.4), channel_id=1, source_target_pairs={{0,64},{8,72},{16,80},{24,88},{32,96},{40,104},{48,112},{56,120},{... | collective-permute-start | bytes 405512 | tf_op jit(solution)/shard_map/ppermute | solution.py:33
  76.7 7.2 %collective-permute-start.5 = (f32[2,128,128]{2,1,0:T(8,128)S(1)}, f32[2,128,128]{2,1,0:T(8,128)S(1)}, u32[]{:S(2)}, u32[]{:S(2)}) collective-permute-start(f32[2,128,128]{2,1,0:T(8,128)S(1)} %multiply_add_fusion.8), channel_id=1, source_target_pairs={{0,128},{8,136},{16,144},{24,152},{32,160},{40,168},{48,176},{56,1... | collective-permute-start | bytes 393224 | tf_op jit(solution)/shard_map/ppermute | solution.py:111
  84.0 6.6 %collective-permute-start.6 = (f32[2,128,128]{2,1,0:T(8,128)S(1)}, f32[2,128,128]{2,1,0:T(8,128)S(1)}, u32[]{:S(2)}, u32[]{:S(2)}) collective-permute-start(f32[2,128,128]{2,1,0:T(8,128)S(1)} %get-tuple-element.27), channel_id=1, source_target_pairs={{0,16},{8,24},{16,0},{24,8},{32,48},{40,56},{48,32},{56,40},{64,80... | collective-permute-start | bytes 393224 | tf_op jit(solution)/shard_map/ppermute | solution.py:89
  90.7 10.6 %collective-permute-start.7 = (f32[4,128,128]{2,1,0:T(8,128)S(1)}, f32[4,128,128]{2,1,0:T(8,128)S(1)}, u32[]{:S(2)}, u32[]{:S(2)}) collective-permute-start(f32[4,128,128]{2,1,0:T(8,128)S(1)} %get-tuple-element.22), channel_id=1, source_target_pairs={{0,8},{8,0},{16,24},{24,16},{32,40},{40,32},{48,56},{56,48},{64,72... | collective-permute-start | bytes 786440 | tf_op jit(solution)/shard_map/ppermute | solution.py:89
  104.3 1.7 collective-permute-start.10
  106.5 7.5 %collective-permute-start.11 = (f32[264,128]{1,0:T(8,128)S(1)}, f32[264,128]{1,0:T(8,128)S(1)}, u32[]{:S(2)}, u32[]{:S(2)}) collective-permute-start(f32[264,128]{1,0:T(8,128)S(1)} %pad_maximum_fusion.9), channel_id=1, source_target_pairs={{0,16},{8,24},{16,0},{24,8},{32,48},{40,56},{48,32},{56,40},{64,80... | collective-permute-start | bytes 405512 | tf_op jit(solution)/shard_map/ppermute | solution.py:33
  114.4 8.3 %collective-permute-start.12 = (f32[264,128]{0,1:T(8,128)S(1)}, f32[264,128]{0,1:T(8,128)S(1)}, u32[]{:S(2)}, u32[]{:S(2)}) collective-permute-start(f32[264,128]{0,1:T(8,128)S(1)} %pad_maximum_fusion.5), channel_id=1, source_target_pairs={{32,0},{40,8},{48,16},{56,24},{64,32},{72,40},{80,48},{88,56},{96,... | collective-permute-start | bytes 405512 | tf_op jit(solution)/shard_map/ppermute | solution.py:33
  122.7 15.5 %collective-permute-start.13 = (f32[264,128]{0,1:T(8,128)S(1)}, f32[264,128]{0,1:T(8,128)S(1)}, u32[]{:S(2)}, u32[]{:S(2)}) collective-permute-start(f32[264,128]{0,1:T(8,128)S(1)} %pad_maximum_fusion.6), channel_id=1, source_target_pairs={{32,0},{40,8},{48,16},{56,24},{64,32},{72,40},{80,48},{88,56},{96,... | collective-permute-start | bytes 405512 | tf_op jit(solution)/shard_map/ppermute | solution.py:33
  138.2 0.7 copy-start.4
  138.9 12.2 %collective-permute-start.14 = (f32[264,128]{0,1:T(8,128)}, f32[264,128]{0,1:T(8,128)}, u32[]{:S(2)}, u32[]{:S(2)}) collective-permute-start(f32[264,128]{0,1:T(8,128)} %pad_maximum_fusion.7), channel_id=1, source_target_pairs={{64,0},{72,8},{80,16},{88,24},{96,32},{104,40},{112,48},{120,56},{... | collective-permute-start | bytes 405512 | tf_op jit(solution)/shard_map/ppermute | solution.py:33
  152.9 10.8 %collective-permute-start.15 = (f32[2,128,128]{2,1,0:T(8,128)S(1)}, f32[2,128,128]{2,1,0:T(8,128)S(1)}, u32[]{:S(2)}, u32[]{:S(2)}) collective-permute-start(f32[2,128,128]{2,1,0:T(8,128)S(1)} %multiply_add_fusion.4), channel_id=1, source_target_pairs={{128,0},{136,8},{144,16},{152,24},{160,32},{168,40},{176,48},{184,... | collective-permute-start | bytes 393224 | tf_op jit(solution)/shard_map/ppermute | solution.py:111
  163.7 6.6 %collective-permute-start.16 = (f32[2,128,128]{2,1,0:T(8,128)S(1)}, f32[2,128,128]{2,1,0:T(8,128)S(1)}, u32[]{:S(2)}, u32[]{:S(2)}) collective-permute-start(f32[2,128,128]{2,1,0:T(8,128)S(1)} %get-tuple-element.25), channel_id=1, source_target_pairs={{0,16},{8,24},{16,0},{24,8},{32,48},{40,56},{48,32},{56,40},{64,80... | collective-permute-start | bytes 393224 | tf_op jit(solution)/shard_map/ppermute | solution.py:89
  170.4 1.8 collective-permute-start.17
  174.0 11.6 %all-to-all-start = ((f32[8,16,256]{2,1,0:T(8,128)}), f32[8,16,256]{2,1,0:T(8,128)S(1)}, u32[]{:S(2)}, u32[]{:S(2)}) async-start(f32[8,16,256]{2,1,0:T(8,128)} %bitcast.41), calls=%async_computation | async-start | bytes 262144 | tf_op jit(solution)/shard_map/all_to_all | solution.py:135
Sparse Core Ops, SparseCore 0:
  23.2 60.6 all-gather.1

commit v13 on v12

--- a/solution.py
+++ b/solution.py
@@ -92,7 +92,7 @@
     )
 
 
-def exclusive_scan(state, logs, axis, forward, extra=None):
+def exclusive_scan(state, logs, axis, forward, extra=None, before_up=None):
     count = lax.axis_size(axis)
     levels = []
     for bit in (1, 2):
@@ -113,8 +113,12 @@
         window_state = window_state + jnp.exp(window_log)[:, None, None] * got_state
         window_log = window_log_next
         width *= 2
+    if before_up is not None:
+        window_state, done = lax.optimization_barrier((window_state, before_up(extra)))
     for bit, saved in reversed(levels):
         window_state = pair_up(window_state, saved, axis, bit, forward)
+    if before_up is not None:
+        return window_state, done
     return window_state, extra
 
 
@@ -251,13 +255,15 @@
     local_state = jnp.einsum(
         "shp,sn->hpn", student_x * ending[:, :, None], b_rows, precision=highest
     )
-    state_in, plane_blocks = exclusive_scan(local_state, totals, "seq", True, packed)
-    every = gather_groups(plane_blocks, "seq")
-
     query_rows = queries.reshape(row_count * heads, HEAD_WIDTH)
-    teacher_out = attend(
-        jnp.reshape(first_query, (1,)).astype(jnp.int32), query_rows, every, heads
-    ).reshape(row_count, heads, HEAD_WIDTH)
+
+    def teacher(plane_blocks):
+        every = gather_groups(plane_blocks, "seq")
+        return attend(jnp.reshape(first_query, (1,)).astype(jnp.int32), query_rows, every, heads)
+
+    state_in, teacher_rows = exclusive_scan(local_state, totals, "seq", True, packed, teacher)
+
+    teacher_out = teacher_rows.reshape(row_count, heads, HEAD_WIDTH)
 
     y_intra = jnp.einsum("hts,shp->thp", mixing, student_x, precision=highest)
     y_inter = jnp.einsum("tn,hpn->thp", c_rows, state_in, precision=highest) * rising[:, :, None]

time: 195 us -> 196 us (level)
  starting transfers between devices: 42.4 us -> 40.1 us
  waiting for transfers between devices: 103 us -> 105 us
    ppermute x8, starting transfers between devices: 29.2 us -> 25.8 us  [send_with_logs(): got = lax.ppermute(payload, axis, perm)]
    ppermute x2, starting transfers between devices: 4.34 us -> 6.67 us  [exclusive_scan(): got_state = lax.ppermute(window_state, axis, perm)]
    ppermute x2, waiting for transfers between devices: 12.2 us -> 14.2 us  [exclusive_scan(): got_state = lax.ppermute(window_state, axis, perm)]
  transfers between devices with their start and end apart: 20 -> 20, of which waited for: 16 -> 16; matrix products, arithmetic and copies ran while one was open for 5% -> 6% of each run, Pallas kernels for 5% -> 0%
where the time goes in v13:
time: 196 us; the launch traced here: 193 us
  waiting for transfers between devices  105 us (54%)
  starting transfers between devices  40.1 us (20%)
  between operations  14.7 us (8%)
  Pallas kernels  10.3 us (5%)
  matrix products  7.74 us (4%)
  other arithmetic  7.68 us (4%)
  local copies, waits for them, and re-layouts  7.35 us (4%)
    ppermute x8, waiting for transfers between devices, send_with_logs(): got = lax.ppermute(payload, axis, perm)  60.2 us
    ppermute x8, starting transfers between devices, send_with_logs(): got = lax.ppermute(payload, axis, perm)  25.8 us
    ppermute x2, waiting for transfers between devices, exclusive_scan(): got_state = lax.ppermute(window_state, axis, perm)  14.2 us
    ppermute x4, waiting for transfers between devices, send_with_logs(): got, got_extra = lax.ppermute((payload, extra), axis, perm)  14 us
    ppermute x4, waiting for transfers between devices, pair_up(): got = lax.ppermute(send, axis, [(j, j ^ bit) for j in range(count)])  11.4 us
    pallas_call x1, Pallas kernels, attend(): pl.pallas_call(functools.partial(attend_kernel, heads=heads), out_shape=j...  10.3 us
    ppermute x2, starting transfers between devices, exclusive_scan(): got_state = lax.ppermute(window_state, axis, perm)  6.67 us
    all_to_all x1, waiting for transfers between devices, mp_sum_scatter(): return jnp.sum(lax.all_to_all(blocks, axis, 0, 0), axis=0)  5.19 us
  transfers between devices with their start and end apart: 20, of which 16 were waited for; matrix products, arithmetic and copies ran while one was open for 6% of the time, Pallas kernels for 0%

profile of v13, /device:TPU:68, one launch (start us, length us, event | category | flops | bytes accessed | tf_op | source)
XLA Modules:
  0.0 192.9 jit_solution(14708172883371406735)
XLA Ops:
  7.2 0.9 reduce-precision_convert_fusion
  8.1 0.8 pad_maximum_fusion.11
  9.0 0.8 copy.61
  10.0 1.1 copy.64
  11.7 0.9 maximum_select_fusion.9
  12.6 0.6 collective-permute-start.7
  13.6 7.9 %collective-permute-done.7 = bf16[256,384]{1,0:T(8,128)(2,1)S(1)} collective-permute-done((bf16[256,384]{1,0:T(8,128)(2,1)S(1)}, bf16[256,384]{1,0:T(8,128)(2,1)S(1)}, u32[]{:S(2)}, u32[]{:S(2)}) %collective-permute-start.7) | collective-permute-done | bytes 196640 | tf_op jit(solution)/shard_map/ppermute | solution.py:36
  21.5 0.9 maximum_select_fusion.2
  23.0 0.6 collective-permute-start.1
  23.6 6.2 %collective-permute-done.1 = f32[264,128]{1,0:T(8,128)S(1)} collective-permute-done((f32[264,128]{1,0:T(8,128)S(1)}, f32[264,128]{1,0:T(8,128)S(1)}, u32[]{:S(2)}, u32[]{:S(2)}) %collective-permute-start.1) | collective-permute-done | bytes 135200 | tf_op jit(solution)/shard_map/ppermute | solution.py:36
  30.3 3.8 %collective-permute-start.2 = (f32[264,128]{0,1:T(8,128)S(1)}, f32[264,128]{0,1:T(8,128)S(1)}, u32[]{:S(2)}, u32[]{:S(2)}) collective-permute-start(f32[264,128]{0,1:T(8,128)S(1)} %pad_maximum_fusion.2), channel_id=1, source_target_pairs={{0,32},{8,40},{16,48},{24,56},{32,64},{40,72},{48,80},{56,88},{64,... | collective-permute-start | bytes 405512 | tf_op jit(solution)/shard_map/ppermute | solution.py:33
  34.1 6.1 %collective-permute-done.2 = f32[264,128]{0,1:T(8,128)S(1)} collective-permute-done((f32[264,128]{0,1:T(8,128)S(1)}, f32[264,128]{0,1:T(8,128)S(1)}, u32[]{:S(2)}, u32[]{:S(2)}) %collective-permute-start.2) | collective-permute-done | bytes 135200 | tf_op jit(solution)/shard_map/ppermute | solution.py:33
  40.2 6.5 %collective-permute-start.3 = (f32[264,128]{0,1:T(8,128)S(1)}, f32[264,128]{0,1:T(8,128)S(1)}, u32[]{:S(2)}, u32[]{:S(2)}) collective-permute-start(f32[264,128]{0,1:T(8,128)S(1)} %pad_maximum_fusion.3), channel_id=1, source_target_pairs={{0,32},{8,40},{16,48},{24,56},{32,64},{40,72},{48,80},{56,88},{64,... | collective-permute-start | bytes 405512 | tf_op jit(solution)/shard_map/ppermute | solution.py:33
  46.8 7.6 %collective-permute-done.3 = f32[264,128]{0,1:T(8,128)S(1)} collective-permute-done((f32[264,128]{0,1:T(8,128)S(1)}, f32[264,128]{0,1:T(8,128)S(1)}, u32[]{:S(2)}, u32[]{:S(2)}) %collective-permute-start.3) | collective-permute-done | bytes 135200 | tf_op jit(solution)/shard_map/ppermute | solution.py:33
  54.6 8.9 %collective-permute-start.4 = (f32[264,128]{0,1:T(8,128)S(1)}, f32[264,128]{0,1:T(8,128)S(1)}, u32[]{:S(2)}, u32[]{:S(2)}) collective-permute-start(f32[264,128]{0,1:T(8,128)S(1)} %pad_maximum_fusion.4), channel_id=1, source_target_pairs={{0,64},{8,72},{16,80},{24,88},{32,96},{40,104},{48,112},{56,120},{... | collective-permute-start | bytes 405512 | tf_op jit(solution)/shard_map/ppermute | solution.py:33
  63.7 9.9 %collective-permute-done.4 = f32[264,128]{0,1:T(8,128)S(1)} collective-permute-done((f32[264,128]{0,1:T(8,128)S(1)}, f32[264,128]{0,1:T(8,128)S(1)}, u32[]{:S(2)}, u32[]{:S(2)}) %collective-permute-start.4) | collective-permute-done | bytes 135200 | tf_op jit(solution)/shard_map/ppermute | solution.py:33
  73.8 5.4 %collective-permute-start.5 = (f32[2,128,128]{2,1,0:T(8,128)S(1)}, f32[2,128,128]{2,1,0:T(8,128)S(1)}, u32[]{:S(2)}, u32[]{:S(2)}) collective-permute-start(f32[2,128,128]{2,1,0:T(8,128)S(1)} %multiply_add_fusion.8), channel_id=1, source_target_pairs={{0,128},{8,136},{16,144},{24,152},{32,160},{40,168},{48,176},{56,1... | collective-permute-start | bytes 393224 | tf_op jit(solution)/shard_map/ppermute | solution.py:111
  79.2 0.8 reshape.231.query_ref
  80.0 5.0 %collective-permute-done.5 = f32[2,128,128]{2,1,0:T(8,128)S(1)} collective-permute-done((f32[2,128,128]{2,1,0:T(8,128)S(1)}, f32[2,128,128]{2,1,0:T(8,128)S(1)}, u32[]{:S(2)}, u32[]{:S(2)}) %collective-permute-start.5) | collective-permute-done | bytes 131104 | tf_op jit(solution)/shard_map/ppermute | solution.py:111
  85.2 10.3 %shard_map.94 = f32[1024,128]{1,0:T(8,128)} custom-call(s32[1]{0:T(128)} %bitcast.21.first_ref, bf16[1024,128]{1,0:T(8,128)(2,1)} %reshape.231.query_ref, bf16[4096,384]{1,0:T(8,128)(2,1)} %all-gather.2.cloned.1.call-done.key_ref.upper_ref.lower_ref, bf16[4096,384]{1,0:T(8,128)(2,1)} %all-gather.2.cloned.1.call-done.key_ref.upper_ref.lower_ref, ...), custom_call_target="tpu_custom_call" | custom-call | flops 4294967296 | bytes 3932160 | tf_op jit(solution)/shard_map/pallas_call | solution.py:202
  96.2 5.8 %collective-permute-done.8 = f32[2,128,128]{2,1,0:T(8,128)S(1)} collective-permute-done((f32[2,128,128]{2,1,0:T(8,128)S(1)}, f32[2,128,128]{2,1,0:T(8,128)S(1)}, u32[]{:S(2)}, u32[]{:S(2)}) %collective-permute-start.8) | collective-permute-done | bytes 131104 | tf_op jit(solution)/shard_map/ppermute | solution.py:89
  102.6 0.7 convolution_bitcast_fusion.1
  103.3 0.7 collective-permute-done.9
  104.0 0.7 fusion.3
  104.7 1.1 fusion.12
  106.3 1.4 collective-permute-done.10
  108.7 6.6 %collective-permute-done.11 = f32[264,128]{1,0:T(8,128)S(1)} collective-permute-done((f32[264,128]{1,0:T(8,128)S(1)}, f32[264,128]{1,0:T(8,128)S(1)}, u32[]{:S(2)}, u32[]{:S(2)}) %collective-permute-start.11) | collective-permute-done | bytes 135200 | tf_op jit(solution)/shard_map/ppermute | solution.py:33
  115.8 1.9 collective-permute-start.12
  117.7 9.5 %collective-permute-done.12 = f32[264,128]{0,1:T(8,128)S(1)} collective-permute-done((f32[264,128]{0,1:T(8,128)S(1)}, f32[264,128]{0,1:T(8,128)S(1)}, u32[]{:S(2)}, u32[]{:S(2)}) %collective-permute-start.12) | collective-permute-done | bytes 135200 | tf_op jit(solution)/shard_map/ppermute | solution.py:33
  127.3 1.9 collective-permute-start.13
  129.3 8.7 %collective-permute-done.13 = f32[264,128]{0,1:T(8,128)S(1)} collective-permute-done((f32[264,128]{0,1:T(8,128)S(1)}, f32[264,128]{0,1:T(8,128)S(1)}, u32[]{:S(2)}, u32[]{:S(2)}) %collective-permute-start.13) | collective-permute-done | bytes 135200 | tf_op jit(solution)/shard_map/ppermute | solution.py:33
  138.1 0.7 pad_maximum_fusion.7
  138.8 1.9 collective-permute-start.14
  141.4 10.2 %collective-permute-done.14 = f32[264,128]{0,1:T(8,128)} collective-permute-done((f32[264,128]{0,1:T(8,128)}, f32[264,128]{0,1:T(8,128)}, u32[]{:S(2)}, u32[]{:S(2)}) %collective-permute-start.14) | collective-permute-done | bytes 135200 | tf_op jit(solution)/shard_map/ppermute | solution.py:33
  151.6 0.9 slice.111
  152.6 0.7 fusion.53
  153.4 1.3 collective-permute-start.15
  155.0 9.2 %collective-permute-done.15 = f32[2,128,128]{2,1,0:T(8,128)S(1)} collective-permute-done((f32[2,128,128]{2,1,0:T(8,128)S(1)}, f32[2,128,128]{2,1,0:T(8,128)S(1)}, u32[]{:S(2)}, u32[]{:S(2)}) %collective-permute-start.15) | collective-permute-done | bytes 131104 | tf_op jit(solution)/shard_map/ppermute | solution.py:111
  164.3 0.6 collective-permute-start.16
  164.9 1.1 fusion.6
  166.0 4.8 %collective-permute-done.16 = f32[2,128,128]{2,1,0:T(8,128)S(1)} collective-permute-done((f32[2,128,128]{2,1,0:T(8,128)S(1)}, f32[2,128,128]{2,1,0:T(8,128)S(1)}, u32[]{:S(2)}, u32[]{:S(2)}) %collective-permute-start.16) | collective-permute-done | bytes 131104 | tf_op jit(solution)/shard_map/ppermute | solution.py:89
  171.3 1.2 convolution_bitcast_fusion.2
  172.6 1.0 fusion.5
  173.6 0.7 copy.83
  174.3 4.5 %all-to-all-start = ((f32[8,16,256]{2,1,0:T(8,128)}), f32[8,16,256]{2,1,0:T(8,128)S(1)}, u32[]{:S(2)}, u32[]{:S(2)}) async-start(f32[8,16,256]{2,1,0:T(8,128)} %bitcast.41), calls=%async_computation | async-start | bytes 262144 | tf_op jit(solution)/shard_map/all_to_all | solution.py:139
  179.2 1.0 copy.84
  180.2 5.2 %all-to-all-done = f32[8,16,256]{2,1,0:T(8,128)S(1)} async-done(((f32[8,16,256]{2,1,0:T(8,128)}), f32[8,16,256]{2,1,0:T(8,128)S(1)}, u32[]{:S(2)}, u32[]{:S(2)}) %all-to-all-start) | async-done | bytes 131104 | tf_op jit(solution)/shard_map/all_to_all | solution.py:139
  185.4 0.6 slice_multiply_fusion
  (113 shorter events, 8.3 us)
Async XLA Ops:
  7.2 4.1 %copy-start = (bf16[128,128]{1,0:T(8,128)(2,1)S(1)}, bf16[128,128]{1,0:T(8,128)(2,1)}, u32[]{:S(2)}) copy-start(bf16[128,128]{1,0:T(8,128)(2,1)} %param.11) | copy-start | bytes 98308
  7.2 78.0 %all-gather.2.cloned.1.call-start = ((), (), s32[]{:S(2)}) async-start(), calls=%async_computation.1 | async-start | bytes 3538944 | tf_op jit(solution)/shard_map/all_gather | solution.py:128
  8.9 2.8 %collective-permute-start.6 = (bf16[128,384]{1,0:T(8,128)(2,1)S(1)}, bf16[128,384]{1,0:T(8,128)(2,1)S(1)}, u32[]{:S(2)}, u32[]{:S(2)}) collective-permute-start(bf16[128,384]{1,0:T(8,128)(2,1)S(1)} %pad_maximum_fusion.11), channel_id=1, source_target_pairs={{0,8},{8,0},{16,24},{24,16},{32,40},{40,32},{48,56},{56,48},{64,72... | collective-permute-start | bytes 294920 | tf_op jit(solution)/shard_map/ppermute | solution.py:36
  12.6 8.9 %collective-permute-start.7 = (bf16[256,384]{1,0:T(8,128)(2,1)S(1)}, bf16[256,384]{1,0:T(8,128)(2,1)S(1)}, u32[]{:S(2)}, u32[]{:S(2)}) collective-permute-start(bf16[256,384]{1,0:T(8,128)(2,1)S(1)} %maximum_select_fusion.9), channel_id=1, source_target_pairs={{0,16},{8,24},{16,0},{24,8},{32,48},{40,56},{48,32},{56,40},{64,80... | collective-permute-start | bytes 589832 | tf_op jit(solution)/shard_map/ppermute | solution.py:36
  13.3 9.1 %collective-permute-start = (f32[520,128]{1,0:T(8,128)S(1)}, f32[520,128]{1,0:T(8,128)S(1)}, u32[]{:S(2)}, u32[]{:S(2)}) collective-permute-start(f32[520,128]{1,0:T(8,128)S(1)} %pad_maximum_fusion), channel_id=1, source_target_pairs={{0,8},{8,0},{16,24},{24,16},{32,40},{40,32},{48,56},{56,48},{64,72... | collective-permute-start | bytes 798728 | tf_op jit(solution)/shard_map/ppermute | solution.py:36
  22.4 56.8 %copy-start.3 = (bf16[128,1024]{1,0:T(8,128)(2,1)S(1)}, bf16[128,1024]{1,0:T(8,128)(2,1)}, u32[]{:S(2)}) copy-start(bf16[128,1024]{1,0:T(8,128)(2,1)} %param.7) | copy-start | bytes 786436
  23.0 6.8 %collective-permute-start.1 = (f32[264,128]{1,0:T(8,128)S(1)}, f32[264,128]{1,0:T(8,128)S(1)}, u32[]{:S(2)}, u32[]{:S(2)}) collective-permute-start(f32[264,128]{1,0:T(8,128)S(1)} %pad_maximum_fusion.8), channel_id=1, source_target_pairs={{0,16},{8,24},{16,0},{24,8},{32,48},{40,56},{48,32},{56,40},{64,80... | collective-permute-start | bytes 405512 | tf_op jit(solution)/shard_map/ppermute | solution.py:36
  30.3 9.9 %collective-permute-start.2 = (f32[264,128]{0,1:T(8,128)S(1)}, f32[264,128]{0,1:T(8,128)S(1)}, u32[]{:S(2)}, u32[]{:S(2)}) collective-permute-start(f32[264,128]{0,1:T(8,128)S(1)} %pad_maximum_fusion.2), channel_id=1, source_target_pairs={{0,32},{8,40},{16,48},{24,56},{32,64},{40,72},{48,80},{56,88},{64,... | collective-permute-start | bytes 405512 | tf_op jit(solution)/shard_map/ppermute | solution.py:33
  40.2 14.2 %collective-permute-start.3 = (f32[264,128]{0,1:T(8,128)S(1)}, f32[264,128]{0,1:T(8,128)S(1)}, u32[]{:S(2)}, u32[]{:S(2)}) collective-permute-start(f32[264,128]{0,1:T(8,128)S(1)} %pad_maximum_fusion.3), channel_id=1, source_target_pairs={{0,32},{8,40},{16,48},{24,56},{32,64},{40,72},{48,80},{56,88},{64,... | collective-permute-start | bytes 405512 | tf_op jit(solution)/shard_map/ppermute | solution.py:33
  54.6 19.1 %collective-permute-start.4 = (f32[264,128]{0,1:T(8,128)S(1)}, f32[264,128]{0,1:T(8,128)S(1)}, u32[]{:S(2)}, u32[]{:S(2)}) collective-permute-start(f32[264,128]{0,1:T(8,128)S(1)} %pad_maximum_fusion.4), channel_id=1, source_target_pairs={{0,64},{8,72},{16,80},{24,88},{32,96},{40,104},{48,112},{56,120},{... | collective-permute-start | bytes 405512 | tf_op jit(solution)/shard_map/ppermute | solution.py:33
  73.8 11.2 %collective-permute-start.5 = (f32[2,128,128]{2,1,0:T(8,128)S(1)}, f32[2,128,128]{2,1,0:T(8,128)S(1)}, u32[]{:S(2)}, u32[]{:S(2)}) collective-permute-start(f32[2,128,128]{2,1,0:T(8,128)S(1)} %multiply_add_fusion.8), channel_id=1, source_target_pairs={{0,128},{8,136},{16,144},{24,152},{32,160},{40,168},{48,176},{56,1... | collective-permute-start | bytes 393224 | tf_op jit(solution)/shard_map/ppermute | solution.py:111
  85.2 11.0 %copy-start.1 = (bf16[128,128]{1,0:T(8,128)(2,1)S(1)}, bf16[128,128]{1,0:T(8,128)(2,1)}, u32[]{:S(2)}) copy-start(bf16[128,128]{1,0:T(8,128)(2,1)} %param.12) | copy-start | bytes 98308
  95.4 8.6 %copy-start.2 = (f32[1024,128]{1,0:T(8,128)S(1)}, f32[1024,128]{1,0:T(8,128)}, u32[]{:S(2)}) copy-start(f32[1024,128]{1,0:T(8,128)} %shard_map.94) | copy-start | bytes 1572868
  95.5 6.6 %collective-permute-start.8 = (f32[2,128,128]{2,1,0:T(8,128)S(1)}, f32[2,128,128]{2,1,0:T(8,128)S(1)}, u32[]{:S(2)}, u32[]{:S(2)}) collective-permute-start(f32[2,128,128]{2,1,0:T(8,128)S(1)} %get-tuple-element.32), channel_id=1, source_target_pairs={{0,16},{8,24},{16,0},{24,8},{32,48},{40,56},{48,32},{56,40},{64,80... | collective-permute-start | bytes 393224 | tf_op jit(solution)/shard_map/ppermute | solution.py:89
  102.2 1.8 collective-permute-start.9
  106.0 1.6 collective-permute-start.10
  108.1 7.2 %collective-permute-start.11 = (f32[264,128]{1,0:T(8,128)S(1)}, f32[264,128]{1,0:T(8,128)S(1)}, u32[]{:S(2)}, u32[]{:S(2)}) collective-permute-start(f32[264,128]{1,0:T(8,128)S(1)} %pad_maximum_fusion.9), channel_id=1, source_target_pairs={{0,16},{8,24},{16,0},{24,8},{32,48},{40,56},{48,32},{56,40},{64,80... | collective-permute-start | bytes 405512 | tf_op jit(solution)/shard_map/ppermute | solution.py:33
  115.8 11.5 %collective-permute-start.12 = (f32[264,128]{0,1:T(8,128)S(1)}, f32[264,128]{0,1:T(8,128)S(1)}, u32[]{:S(2)}, u32[]{:S(2)}) collective-permute-start(f32[264,128]{0,1:T(8,128)S(1)} %pad_maximum_fusion.5), channel_id=1, source_target_pairs={{32,0},{40,8},{48,16},{56,24},{64,32},{72,40},{80,48},{88,56},{96,... | collective-permute-start | bytes 405512 | tf_op jit(solution)/shard_map/ppermute | solution.py:33
  127.3 10.8 %collective-permute-start.13 = (f32[264,128]{0,1:T(8,128)S(1)}, f32[264,128]{0,1:T(8,128)S(1)}, u32[]{:S(2)}, u32[]{:S(2)}) collective-permute-start(f32[264,128]{0,1:T(8,128)S(1)} %pad_maximum_fusion.6), channel_id=1, source_target_pairs={{32,0},{40,8},{48,16},{56,24},{64,32},{72,40},{80,48},{88,56},{96,... | collective-permute-start | bytes 405512 | tf_op jit(solution)/shard_map/ppermute | solution.py:33
  138.1 0.7 copy-start.4
  138.8 12.8 %collective-permute-start.14 = (f32[264,128]{0,1:T(8,128)}, f32[264,128]{0,1:T(8,128)}, u32[]{:S(2)}, u32[]{:S(2)}) collective-permute-start(f32[264,128]{0,1:T(8,128)} %pad_maximum_fusion.7), channel_id=1, source_target_pairs={{64,0},{72,8},{80,16},{88,24},{96,32},{104,40},{112,48},{120,56},{... | collective-permute-start | bytes 405512 | tf_op jit(solution)/shard_map/ppermute | solution.py:33
  153.4 10.8 %collective-permute-start.15 = (f32[2,128,128]{2,1,0:T(8,128)S(1)}, f32[2,128,128]{2,1,0:T(8,128)S(1)}, u32[]{:S(2)}, u32[]{:S(2)}) collective-permute-start(f32[2,128,128]{2,1,0:T(8,128)S(1)} %multiply_add_fusion.4), channel_id=1, source_target_pairs={{128,0},{136,8},{144,16},{152,24},{160,32},{168,40},{176,48},{184,... | collective-permute-start | bytes 393224 | tf_op jit(solution)/shard_map/ppermute | solution.py:111
  164.3 6.6 %collective-permute-start.16 = (f32[2,128,128]{2,1,0:T(8,128)S(1)}, f32[2,128,128]{2,1,0:T(8,128)S(1)}, u32[]{:S(2)}, u32[]{:S(2)}) collective-permute-start(f32[2,128,128]{2,1,0:T(8,128)S(1)} %get-tuple-element.30), channel_id=1, source_target_pairs={{0,16},{8,24},{16,0},{24,8},{32,48},{40,56},{48,32},{56,40},{64,80... | collective-permute-start | bytes 393224 | tf_op jit(solution)/shard_map/ppermute | solution.py:89
  170.9 1.6 collective-permute-start.17
  174.3 11.0 %all-to-all-start = ((f32[8,16,256]{2,1,0:T(8,128)}), f32[8,16,256]{2,1,0:T(8,128)S(1)}, u32[]{:S(2)}, u32[]{:S(2)}) async-start(f32[8,16,256]{2,1,0:T(8,128)} %bitcast.41), calls=%async_computation | async-start | bytes 262144 | tf_op jit(solution)/shard_map/all_to_all | solution.py:139
Sparse Core Ops, SparseCore 0:
  22.5 60.8 all-gather.1

commit v14 on v11

--- a/solution.py
+++ b/solution.py
@@ -149,27 +149,41 @@
         mix_ref[...] = jnp.zeros(mix_ref.shape, jnp.float32)
 
     def accumulate(masked):
-        scores = lax.dot_general(
-            query_ref[...], key_ref[...], (((1,), (1,)), ((), ())), preferred_element_type=jnp.float32
-        ) * (1.0 / math.sqrt(width))
-        if masked:
-            row = lax.broadcasted_iota(jnp.int32, scores.shape, 0)
-            col = lax.broadcasted_iota(jnp.int32, scores.shape, 1)
-            allowed = block * keys_per_block + col <= first + row // heads
-            scores = jnp.where(allowed, scores, very_negative)
-        top_old = top_ref[...]
-        top_new = jnp.maximum(top_old, jnp.max(scores, axis=1, keepdims=True))
-        rescale = jnp.exp(top_old - top_new)
-        weights = jnp.exp(scores - top_new)
-        if masked:
-            weights = jnp.where(allowed, weights, 0.0)
-        total_ref[...] = rescale * total_ref[...] + jnp.sum(weights, axis=1, keepdims=True)
-        value_rows = upper_ref[...].astype(jnp.float32) + lower_ref[...].astype(jnp.float32)
-        mixed = jnp.dot(
-            weights, value_rows, precision=lax.Precision.HIGHEST, preferred_element_type=jnp.float32
-        )
-        mix_ref[...] = rescale * mix_ref[...] + mixed
-        top_ref[...] = top_new
+        chunk = 128
+        factor = math.log2(math.e) / math.sqrt(width)
+
+        def body(step, carry):
+            start = pl.multiple_of(step * chunk, chunk)
+            rows_now = pl.ds(start, chunk)
+            scores = lax.dot_general(
+                query_ref[rows_now, :], key_ref[...], (((1,), (1,)), ((), ())),
+                preferred_element_type=jnp.float32,
+            )
+            if masked:
+                row = start + lax.broadcasted_iota(jnp.int32, scores.shape, 0)
+                col = lax.broadcasted_iota(jnp.int32, scores.shape, 1)
+                allowed = block * keys_per_block + col <= first + row // heads
+                scores = jnp.where(allowed, scores, very_negative)
+            top_old = top_ref[rows_now, :]
+            top_new = jnp.maximum(top_old, jnp.max(scores, axis=1, keepdims=True))
+            rescale = jnp.exp2((top_old - top_new) * factor)
+            weights = jnp.exp2((scores - top_new) * factor)
+            if masked:
+                weights = jnp.where(allowed, weights, 0.0)
+            total_ref[rows_now, :] = rescale * total_ref[rows_now, :] + jnp.sum(weights, axis=1, keepdims=True)
+            weights_hi = weights.astype(jnp.bfloat16)
+            weights_lo = (weights - weights_hi.astype(jnp.float32)).astype(jnp.bfloat16)
+            upper = upper_ref[...]
+            mixed = (
+                jnp.dot(weights_hi, upper, preferred_element_type=jnp.float32)
+                + jnp.dot(weights_hi, lower_ref[...], preferred_element_type=jnp.float32)
+                + jnp.dot(weights_lo, upper, preferred_element_type=jnp.float32)
+            )
+            mix_ref[rows_now, :] = rescale * mix_ref[rows_now, :] + mixed
+            top_ref[rows_now, :] = top_new
+            return carry
+
+        lax.fori_loop(0, rows // chunk, body, 0)
 
     block_end = (block + 1) * keys_per_block - 1
 

time: 199 us -> 213 us (1.070)
  waiting for transfers between devices: 106 us -> 114 us
  Pallas kernels: 12.3 us -> 18.3 us
    ppermute x8, waiting for transfers between devices: 63.5 us -> 70.4 us  [send_with_logs(): got = lax.ppermute(payload, axis, perm)]
    pallas_call x1, Pallas kernels: 12.3 us -> 18.3 us  [attend(): pl.pallas_call(functools.partial(attend_kernel, heads=heads), out_shape=j...]
  transfers between devices with their start and end apart: 20 -> 20, of which waited for: 16 -> 16; matrix products, arithmetic and copies ran while one was open for 5% -> 5% of each run, Pallas kernels for 6% -> 9%
where the time goes in v14:
time: 213 us; the launch traced here: 212 us
  waiting for transfers between devices  114 us (54%)
  starting transfers between devices  42.1 us (20%)
  Pallas kernels  18.3 us (9%)
  between operations  14.6 us (7%)
  matrix products  8.74 us (4%)
  local copies, waits for them, and re-layouts  7.42 us (3%)
  other arithmetic  6.69 us (3%)
    ppermute x8, waiting for transfers between devices, send_with_logs(): got = lax.ppermute(payload, axis, perm)  70.4 us
    ppermute x8, starting transfers between devices, send_with_logs(): got = lax.ppermute(payload, axis, perm)  29.4 us
    pallas_call x1, Pallas kernels, attend(): pl.pallas_call(functools.partial(attend_kernel, heads=heads), out_shape=j...  18.3 us
    ppermute x4, waiting for transfers between devices, send_with_logs(): got, got_extra = lax.ppermute((payload, extra), axis, perm)  14.9 us
    ppermute x2, waiting for transfers between devices, exclusive_scan(): got_state = lax.ppermute(window_state, axis, perm)  12.9 us
    ppermute x4, waiting for transfers between devices, pair_up(): got = lax.ppermute(send, axis, [(j, j ^ bit) for j in range(count)])  10.1 us
    all_to_all x1, waiting for transfers between devices, mp_sum_scatter(): return jnp.sum(lax.all_to_all(blocks, axis, 0, 0), axis=0)  5.19 us
    all_to_all x1, starting transfers between devices, mp_sum_scatter(): return jnp.sum(lax.all_to_all(blocks, axis, 0, 0), axis=0)  5.07 us
  transfers between devices with their start and end apart: 20, of which 16 were waited for; matrix products, arithmetic and copies ran while one was open for 5% of the time, Pallas kernels for 9%

profile of v14, /device:TPU:68, one launch (start us, length us, event | category | flops | bytes accessed | tf_op | source)
XLA Modules:
  0.0 211.5 jit_solution(12673166676045738799)
XLA Ops:
  7.3 0.8 copy.61
  8.4 1.1 copy.64
  10.2 0.9 reduce-precision_convert_fusion
  11.1 0.8 pad_maximum_fusion.11
  12.4 0.9 collective-permute-done.8
  13.4 0.6 collective-permute-start.9
  14.2 8.0 %collective-permute-done.9 = bf16[256,384]{1,0:T(8,128)(2,1)S(1)} collective-permute-done((bf16[256,384]{1,0:T(8,128)(2,1)S(1)}, bf16[256,384]{1,0:T(8,128)(2,1)S(1)}, u32[]{:S(2)}, u32[]{:S(2)}) %collective-permute-start.9) | collective-permute-done | bytes 196640 | tf_op jit(solution)/shard_map/ppermute | solution.py:36
  22.2 0.9 maximum_select_fusion.2
  24.1 6.0 %collective-permute-done.1 = f32[264,128]{1,0:T(8,128)S(1)} collective-permute-done((f32[264,128]{1,0:T(8,128)S(1)}, f32[264,128]{1,0:T(8,128)S(1)}, u32[]{:S(2)}, u32[]{:S(2)}) %collective-permute-start.1) | collective-permute-done | bytes 135200 | tf_op jit(solution)/shard_map/ppermute | solution.py:36
  30.5 3.8 %collective-permute-start.2 = (f32[264,128]{0,1:T(8,128)S(1)}, f32[264,128]{0,1:T(8,128)S(1)}, u32[]{:S(2)}, u32[]{:S(2)}) collective-permute-start(f32[264,128]{0,1:T(8,128)S(1)} %pad_maximum_fusion.2), channel_id=1, source_target_pairs={{0,32},{8,40},{16,48},{24,56},{32,64},{40,72},{48,80},{56,88},{64,... | collective-permute-start | bytes 405512 | tf_op jit(solution)/shard_map/ppermute | solution.py:33
  34.4 5.1 %collective-permute-done.2 = f32[264,128]{0,1:T(8,128)S(1)} collective-permute-done((f32[264,128]{0,1:T(8,128)S(1)}, f32[264,128]{0,1:T(8,128)S(1)}, u32[]{:S(2)}, u32[]{:S(2)}) %collective-permute-start.2) | collective-permute-done | bytes 135200 | tf_op jit(solution)/shard_map/ppermute | solution.py:33
  39.5 7.4 %collective-permute-start.3 = (f32[264,128]{0,1:T(8,128)S(1)}, f32[264,128]{0,1:T(8,128)S(1)}, u32[]{:S(2)}, u32[]{:S(2)}) collective-permute-start(f32[264,128]{0,1:T(8,128)S(1)} %pad_maximum_fusion.3), channel_id=1, source_target_pairs={{0,32},{8,40},{16,48},{24,56},{32,64},{40,72},{48,80},{56,88},{64,... | collective-permute-start | bytes 405512 | tf_op jit(solution)/shard_map/ppermute | solution.py:33
  47.0 7.1 %collective-permute-done.3 = f32[264,128]{0,1:T(8,128)S(1)} collective-permute-done((f32[264,128]{0,1:T(8,128)S(1)}, f32[264,128]{0,1:T(8,128)S(1)}, u32[]{:S(2)}, u32[]{:S(2)}) %collective-permute-start.3) | collective-permute-done | bytes 135200 | tf_op jit(solution)/shard_map/ppermute | solution.py:33
  54.2 10.8 %collective-permute-start.4 = (f32[264,128]{0,1:T(8,128)S(1)}, f32[264,128]{0,1:T(8,128)S(1)}, u32[]{:S(2)}, u32[]{:S(2)}) collective-permute-start(f32[264,128]{0,1:T(8,128)S(1)} %pad_maximum_fusion.4), channel_id=1, source_target_pairs={{0,64},{8,72},{16,80},{24,88},{32,96},{40,104},{48,112},{56,120},{... | collective-permute-start | bytes 405512 | tf_op jit(solution)/shard_map/ppermute | solution.py:33
  65.2 11.3 %collective-permute-done.4 = f32[264,128]{0,1:T(8,128)S(1)} collective-permute-done((f32[264,128]{0,1:T(8,128)S(1)}, f32[264,128]{0,1:T(8,128)S(1)}, u32[]{:S(2)}, u32[]{:S(2)}) %collective-permute-start.4) | collective-permute-done | bytes 135200 | tf_op jit(solution)/shard_map/ppermute | solution.py:33
  76.7 3.0 %collective-permute-start.5 = (f32[2,128,128]{2,1,0:T(8,128)S(1)}, f32[2,128,128]{2,1,0:T(8,128)S(1)}, u32[]{:S(2)}, u32[]{:S(2)}) collective-permute-start(f32[2,128,128]{2,1,0:T(8,128)S(1)} %multiply_add_fusion.8), channel_id=1, source_target_pairs={{0,128},{8,136},{16,144},{24,152},{32,160},{40,168},{48,176},{56,1... | collective-permute-start | bytes 393224 | tf_op jit(solution)/shard_map/ppermute | solution.py:111
  80.0 0.8 reshape.231.query_ref
  80.9 3.0 %collective-permute-done.5 = f32[2,128,128]{2,1,0:T(8,128)S(1)} collective-permute-done((f32[2,128,128]{2,1,0:T(8,128)S(1)}, f32[2,128,128]{2,1,0:T(8,128)S(1)}, u32[]{:S(2)}, u32[]{:S(2)}) %collective-permute-start.5) | collective-permute-done | bytes 131104 | tf_op jit(solution)/shard_map/ppermute | solution.py:111
  84.0 0.6 collective-permute-start.6
  84.6 0.7 convolution_bitcast_fusion.1
  85.3 5.3 %collective-permute-done.6 = f32[2,128,128]{2,1,0:T(8,128)S(1)} collective-permute-done((f32[2,128,128]{2,1,0:T(8,128)S(1)}, f32[2,128,128]{2,1,0:T(8,128)S(1)}, u32[]{:S(2)}, u32[]{:S(2)}) %collective-permute-start.6) | collective-permute-done | bytes 131104 | tf_op jit(solution)/shard_map/ppermute | solution.py:89
  90.8 18.3 %shard_map.94 = f32[1024,128]{1,0:T(8,128)} custom-call(s32[1]{0:T(128)} %bitcast.21.first_ref, bf16[1024,128]{1,0:T(8,128)(2,1)} %reshape.231.query_ref, bf16[4096,384]{1,0:T(8,128)(2,1)} %all-gather.2.cloned.1.call-done.key_ref.upper_ref.lower_ref, bf16[4096,384]{1,0:T(8,128)(2,1)} %all-gather.2.cloned.1.call-done.key_ref.upper_ref.lower_ref, ...), custom_call_target="tpu_custom_call" | custom-call | flops 4294967296 | bytes 3932160 | tf_op jit(solution)/shard_map/pallas_call | solution.py:207
  109.1 1.7 fusion.3
  110.8 1.1 fusion.12
  112.7 1.2 collective-permute-done.10
  114.3 0.6 collective-permute-start.11
  114.9 6.8 %collective-permute-done.11 = f32[264,128]{1,0:T(8,128)S(1)} collective-permute-done((f32[264,128]{1,0:T(8,128)S(1)}, f32[264,128]{1,0:T(8,128)S(1)}, u32[]{:S(2)}, u32[]{:S(2)}) %collective-permute-start.11) | collective-permute-done | bytes 135200 | tf_op jit(solution)/shard_map/ppermute | solution.py:33
  122.2 1.9 collective-permute-start.12
  124.2 6.3 %collective-permute-done.12 = f32[264,128]{0,1:T(8,128)S(1)} collective-permute-done((f32[264,128]{0,1:T(8,128)S(1)}, f32[264,128]{0,1:T(8,128)S(1)}, u32[]{:S(2)}, u32[]{:S(2)}) %collective-permute-start.12) | collective-permute-done | bytes 135200 | tf_op jit(solution)/shard_map/ppermute | solution.py:33
  130.5 2.2 %collective-permute-start.13 = (f32[264,128]{0,1:T(8,128)S(1)}, f32[264,128]{0,1:T(8,128)S(1)}, u32[]{:S(2)}, u32[]{:S(2)}) collective-permute-start(f32[264,128]{0,1:T(8,128)S(1)} %pad_maximum_fusion.6), channel_id=1, source_target_pairs={{32,0},{40,8},{48,16},{56,24},{64,32},{72,40},{80,48},{88,56},{96,... | collective-permute-start | bytes 405512 | tf_op jit(solution)/shard_map/ppermute | solution.py:33
  132.8 18.7 %collective-permute-done.13 = f32[264,128]{0,1:T(8,128)S(1)} collective-permute-done((f32[264,128]{0,1:T(8,128)S(1)}, f32[264,128]{0,1:T(8,128)S(1)}, u32[]{:S(2)}, u32[]{:S(2)}) %collective-permute-start.13) | collective-permute-done | bytes 135200 | tf_op jit(solution)/shard_map/ppermute | solution.py:33
  151.6 0.7 pad_maximum_fusion.7
  152.3 2.1 collective-permute-start.14
  155.0 13.8 %collective-permute-done.14 = f32[264,128]{0,1:T(8,128)} collective-permute-done((f32[264,128]{0,1:T(8,128)}, f32[264,128]{0,1:T(8,128)}, u32[]{:S(2)}, u32[]{:S(2)}) %collective-permute-start.14) | collective-permute-done | bytes 135200 | tf_op jit(solution)/shard_map/ppermute | solution.py:33
  168.9 0.9 slice.111
  169.9 0.7 fusion.53
  170.7 1.3 collective-permute-start.15
  172.2 10.0 %collective-permute-done.15 = f32[2,128,128]{2,1,0:T(8,128)S(1)} collective-permute-done((f32[2,128,128]{2,1,0:T(8,128)S(1)}, f32[2,128,128]{2,1,0:T(8,128)S(1)}, u32[]{:S(2)}, u32[]{:S(2)}) %collective-permute-start.15) | collective-permute-done | bytes 131104 | tf_op jit(solution)/shard_map/ppermute | solution.py:111
  182.3 0.6 collective-permute-start.16
  182.9 1.1 fusion.6
  184.1 4.8 %collective-permute-done.16 = f32[2,128,128]{2,1,0:T(8,128)S(1)} collective-permute-done((f32[2,128,128]{2,1,0:T(8,128)S(1)}, f32[2,128,128]{2,1,0:T(8,128)S(1)}, u32[]{:S(2)}, u32[]{:S(2)}) %collective-permute-start.16) | collective-permute-done | bytes 131104 | tf_op jit(solution)/shard_map/ppermute | solution.py:89
  189.4 1.2 convolution_bitcast_fusion.2
  190.6 1.0 fusion.5
  191.6 0.7 copy.83
  192.4 5.1 %all-to-all-start = ((f32[8,16,256]{2,1,0:T(8,128)}), f32[8,16,256]{2,1,0:T(8,128)S(1)}, u32[]{:S(2)}, u32[]{:S(2)}) async-start(f32[8,16,256]{2,1,0:T(8,128)} %bitcast.41), calls=%async_computation | async-start | bytes 262144 | tf_op jit(solution)/shard_map/all_to_all | solution.py:135
  197.8 1.0 copy.84
  198.8 5.2 %all-to-all-done = f32[8,16,256]{2,1,0:T(8,128)S(1)} async-done(((f32[8,16,256]{2,1,0:T(8,128)}), f32[8,16,256]{2,1,0:T(8,128)S(1)}, u32[]{:S(2)}, u32[]{:S(2)}) %all-to-all-start) | async-done | bytes 131104 | tf_op jit(solution)/shard_map/all_to_all | solution.py:135
  204.0 0.6 slice_multiply_fusion
  (112 shorter events, 8.1 us)
Async XLA Ops:
  7.2 2.4 %copy-start = (bf16[128,128]{1,0:T(8,128)(2,1)S(1)}, bf16[128,128]{1,0:T(8,128)(2,1)}, u32[]{:S(2)}) copy-start(bf16[128,128]{1,0:T(8,128)(2,1)} %param.11) | copy-start | bytes 98308
  7.2 6.2 %copy-start.3 = (bf16[128,128]{1,0:T(8,128)(2,1)S(1)}, bf16[128,128]{1,0:T(8,128)(2,1)}, u32[]{:S(2)}) copy-start(bf16[128,128]{1,0:T(8,128)(2,1)} %param.8) | copy-start | bytes 98308
  7.2 83.6 %all-gather.2.cloned.1.call-start = ((), (), s32[]{:S(2)}) async-start(), calls=%async_computation.1 | async-start | bytes 3538944 | tf_op jit(solution)/shard_map/all_gather | solution.py:124
  10.1 3.9 %collective-permute-start = (f32[520,128]{1,0:T(8,128)S(1)}, f32[520,128]{1,0:T(8,128)S(1)}, u32[]{:S(2)}, u32[]{:S(2)}) collective-permute-start(f32[520,128]{1,0:T(8,128)S(1)} %pad_maximum_fusion), channel_id=1, source_target_pairs={{0,8},{8,0},{16,24},{24,16},{32,40},{40,32},{48,56},{56,48},{64,72... | collective-permute-start | bytes 798728 | tf_op jit(solution)/shard_map/ppermute | solution.py:36
  11.8 1.5 collective-permute-start.8
  13.4 8.8 %collective-permute-start.9 = (bf16[256,384]{1,0:T(8,128)(2,1)S(1)}, bf16[256,384]{1,0:T(8,128)(2,1)S(1)}, u32[]{:S(2)}, u32[]{:S(2)}) collective-permute-start(bf16[256,384]{1,0:T(8,128)(2,1)S(1)} %maximum_select_fusion.9), channel_id=1, source_target_pairs={{0,16},{8,24},{16,0},{24,8},{32,48},{40,56},{48,32},{56,40},{64,80... | collective-permute-start | bytes 589832 | tf_op jit(solution)/shard_map/ppermute | solution.py:36
  23.1 56.7 %copy-start.1 = (bf16[128,128]{1,0:T(8,128)(2,1)S(1)}, bf16[128,128]{1,0:T(8,128)(2,1)}, u32[]{:S(2)}) copy-start(bf16[128,128]{1,0:T(8,128)(2,1)} %param.12) | copy-start | bytes 98308
  23.2 56.9 %copy-start.2 = (bf16[128,1024]{1,0:T(8,128)(2,1)S(1)}, bf16[128,1024]{1,0:T(8,128)(2,1)}, u32[]{:S(2)}) copy-start(bf16[128,1024]{1,0:T(8,128)(2,1)} %param.7) | copy-start | bytes 786436
  23.5 6.6 %collective-permute-start.1 = (f32[264,128]{1,0:T(8,128)S(1)}, f32[264,128]{1,0:T(8,128)S(1)}, u32[]{:S(2)}, u32[]{:S(2)}) collective-permute-start(f32[264,128]{1,0:T(8,128)S(1)} %pad_maximum_fusion.8), channel_id=1, source_target_pairs={{0,16},{8,24},{16,0},{24,8},{32,48},{40,56},{48,32},{56,40},{64,80... | collective-permute-start | bytes 405512 | tf_op jit(solution)/shard_map/ppermute | solution.py:36
  30.5 8.9 %collective-permute-start.2 = (f32[264,128]{0,1:T(8,128)S(1)}, f32[264,128]{0,1:T(8,128)S(1)}, u32[]{:S(2)}, u32[]{:S(2)}) collective-permute-start(f32[264,128]{0,1:T(8,128)S(1)} %pad_maximum_fusion.2), channel_id=1, source_target_pairs={{0,32},{8,40},{16,48},{24,56},{32,64},{40,72},{48,80},{56,88},{64,... | collective-permute-start | bytes 405512 | tf_op jit(solution)/shard_map/ppermute | solution.py:33
  39.5 14.6 %collective-permute-start.3 = (f32[264,128]{0,1:T(8,128)S(1)}, f32[264,128]{0,1:T(8,128)S(1)}, u32[]{:S(2)}, u32[]{:S(2)}) collective-permute-start(f32[264,128]{0,1:T(8,128)S(1)} %pad_maximum_fusion.3), channel_id=1, source_target_pairs={{0,32},{8,40},{16,48},{24,56},{32,64},{40,72},{48,80},{56,88},{64,... | collective-permute-start | bytes 405512 | tf_op jit(solution)/shard_map/ppermute | solution.py:33
  54.2 22.3 %collective-permute-start.4 = (f32[264,128]{0,1:T(8,128)S(1)}, f32[264,128]{0,1:T(8,128)S(1)}, u32[]{:S(2)}, u32[]{:S(2)}) collective-permute-start(f32[264,128]{0,1:T(8,128)S(1)} %pad_maximum_fusion.4), channel_id=1, source_target_pairs={{0,64},{8,72},{16,80},{24,88},{32,96},{40,104},{48,112},{56,120},{... | collective-permute-start | bytes 405512 | tf_op jit(solution)/shard_map/ppermute | solution.py:33
  76.7 7.2 %collective-permute-start.5 = (f32[2,128,128]{2,1,0:T(8,128)S(1)}, f32[2,128,128]{2,1,0:T(8,128)S(1)}, u32[]{:S(2)}, u32[]{:S(2)}) collective-permute-start(f32[2,128,128]{2,1,0:T(8,128)S(1)} %multiply_add_fusion.8), channel_id=1, source_target_pairs={{0,128},{8,136},{16,144},{24,152},{32,160},{40,168},{48,176},{56,1... | collective-permute-start | bytes 393224 | tf_op jit(solution)/shard_map/ppermute | solution.py:111
  84.0 6.6 %collective-permute-start.6 = (f32[2,128,128]{2,1,0:T(8,128)S(1)}, f32[2,128,128]{2,1,0:T(8,128)S(1)}, u32[]{:S(2)}, u32[]{:S(2)}) collective-permute-start(f32[2,128,128]{2,1,0:T(8,128)S(1)} %get-tuple-element.27), channel_id=1, source_target_pairs={{0,16},{8,24},{16,0},{24,8},{32,48},{40,56},{48,32},{56,40},{64,80... | collective-permute-start | bytes 393224 | tf_op jit(solution)/shard_map/ppermute | solution.py:89
  90.7 18.4 %collective-permute-start.7 = (f32[4,128,128]{2,1,0:T(8,128)S(1)}, f32[4,128,128]{2,1,0:T(8,128)S(1)}, u32[]{:S(2)}, u32[]{:S(2)}) collective-permute-start(f32[4,128,128]{2,1,0:T(8,128)S(1)} %get-tuple-element.22), channel_id=1, source_target_pairs={{0,8},{8,0},{16,24},{24,16},{32,40},{40,32},{48,56},{56,48},{64,72... | collective-permute-start | bytes 786440 | tf_op jit(solution)/shard_map/ppermute | solution.py:89
  112.2 1.7 collective-permute-start.10
  114.3 7.5 %collective-permute-start.11 = (f32[264,128]{1,0:T(8,128)S(1)}, f32[264,128]{1,0:T(8,128)S(1)}, u32[]{:S(2)}, u32[]{:S(2)}) collective-permute-start(f32[264,128]{1,0:T(8,128)S(1)} %pad_maximum_fusion.9), channel_id=1, source_target_pairs={{0,16},{8,24},{16,0},{24,8},{32,48},{40,56},{48,32},{56,40},{64,80... | collective-permute-start | bytes 405512 | tf_op jit(solution)/shard_map/ppermute | solution.py:33
  122.2 8.3 %collective-permute-start.12 = (f32[264,128]{0,1:T(8,128)S(1)}, f32[264,128]{0,1:T(8,128)S(1)}, u32[]{:S(2)}, u32[]{:S(2)}) collective-permute-start(f32[264,128]{0,1:T(8,128)S(1)} %pad_maximum_fusion.5), channel_id=1, source_target_pairs={{32,0},{40,8},{48,16},{56,24},{64,32},{72,40},{80,48},{88,56},{96,... | collective-permute-start | bytes 405512 | tf_op jit(solution)/shard_map/ppermute | solution.py:33
  130.5 21.0 %collective-permute-start.13 = (f32[264,128]{0,1:T(8,128)S(1)}, f32[264,128]{0,1:T(8,128)S(1)}, u32[]{:S(2)}, u32[]{:S(2)}) collective-permute-start(f32[264,128]{0,1:T(8,128)S(1)} %pad_maximum_fusion.6), channel_id=1, source_target_pairs={{32,0},{40,8},{48,16},{56,24},{64,32},{72,40},{80,48},{88,56},{96,... | collective-permute-start | bytes 405512 | tf_op jit(solution)/shard_map/ppermute | solution.py:33
  151.6 0.7 copy-start.4
  152.3 16.6 %collective-permute-start.14 = (f32[264,128]{0,1:T(8,128)}, f32[264,128]{0,1:T(8,128)}, u32[]{:S(2)}, u32[]{:S(2)}) collective-permute-start(f32[264,128]{0,1:T(8,128)} %pad_maximum_fusion.7), channel_id=1, source_target_pairs={{64,0},{72,8},{80,16},{88,24},{96,32},{104,40},{112,48},{120,56},{... | collective-permute-start | bytes 405512 | tf_op jit(solution)/shard_map/ppermute | solution.py:33
  170.7 11.5 %collective-permute-start.15 = (f32[2,128,128]{2,1,0:T(8,128)S(1)}, f32[2,128,128]{2,1,0:T(8,128)S(1)}, u32[]{:S(2)}, u32[]{:S(2)}) collective-permute-start(f32[2,128,128]{2,1,0:T(8,128)S(1)} %multiply_add_fusion.4), channel_id=1, source_target_pairs={{128,0},{136,8},{144,16},{152,24},{160,32},{168,40},{176,48},{184,... | collective-permute-start | bytes 393224 | tf_op jit(solution)/shard_map/ppermute | solution.py:111
  182.3 6.6 %collective-permute-start.16 = (f32[2,128,128]{2,1,0:T(8,128)S(1)}, f32[2,128,128]{2,1,0:T(8,128)S(1)}, u32[]{:S(2)}, u32[]{:S(2)}) collective-permute-start(f32[2,128,128]{2,1,0:T(8,128)S(1)} %get-tuple-element.25), channel_id=1, source_target_pairs={{0,16},{8,24},{16,0},{24,8},{32,48},{40,56},{48,32},{56,40},{64,80... | collective-permute-start | bytes 393224 | tf_op jit(solution)/shard_map/ppermute | solution.py:89
  189.0 1.6 collective-permute-start.17
  192.4 11.7 %all-to-all-start = ((f32[8,16,256]{2,1,0:T(8,128)}), f32[8,16,256]{2,1,0:T(8,128)S(1)}, u32[]{:S(2)}, u32[]{:S(2)}) async-start(f32[8,16,256]{2,1,0:T(8,128)} %bitcast.41), calls=%async_computation | async-start | bytes 262144 | tf_op jit(solution)/shard_map/all_to_all | solution.py:135
Sparse Core Ops, SparseCore 0:
  23.2 60.6 all-gather.1

commit v15 on v12

--- a/solution.py
+++ b/solution.py
@@ -191,7 +191,7 @@
         out_ref[...] = mix_ref[...] / total_ref[...]
 
 
-def attend(first_query, query_rows, every, heads, keys_per_block=512):
+def attend(first_query, query_rows, every, heads, keys_per_block=256):
     rows, width = query_rows.shape
     blocks = every.shape[0] // keys_per_block
     flops = 2 * rows * every.shape[0] * width * 4

time: 195 us -> 221 us (1.13)
  Pallas kernels: 10.3 us -> 23.6 us
  waiting for transfers between devices: 103 us -> 116 us
    pallas_call x1, Pallas kernels: 10.3 us -> 23.6 us  [attend(): pl.pallas_call(functools.partial(attend_kernel, heads=heads), out_shape=j...]
    ppermute x8, waiting for transfers between devices: 60.7 us -> 73.7 us  [send_with_logs(): got = lax.ppermute(payload, axis, perm)]
  transfers between devices with their start and end apart: 20 -> 20, of which waited for: 16 -> 16; matrix products, arithmetic and copies ran while one was open for 5% -> 5% of each run, Pallas kernels for 5% -> 11%
where the time goes in v15:
time: 221 us; the launch traced here: 220 us
  waiting for transfers between devices  116 us (52%)
  starting transfers between devices  42.4 us (19%)
  Pallas kernels  23.6 us (11%)
  between operations  14.6 us (7%)
  matrix products  8.74 us (4%)
  local copies, waits for them, and re-layouts  7.42 us (3%)
  other arithmetic  6.69 us (3%)
    ppermute x8, waiting for transfers between devices, send_with_logs(): got = lax.ppermute(payload, axis, perm)  73.7 us
    ppermute x8, starting transfers between devices, send_with_logs(): got = lax.ppermute(payload, axis, perm)  28.7 us
    pallas_call x1, Pallas kernels, attend(): pl.pallas_call(functools.partial(attend_kernel, heads=heads), out_shape=j...  23.6 us
    ppermute x4, waiting for transfers between devices, send_with_logs(): got, got_extra = lax.ppermute((payload, extra), axis, perm)  14.9 us
    ppermute x2, waiting for transfers between devices, exclusive_scan(): got_state = lax.ppermute(window_state, axis, perm)  12.9 us
    ppermute x4, waiting for transfers between devices, pair_up(): got = lax.ppermute(send, axis, [(j, j ^ bit) for j in range(count)])  9.52 us
    all_to_all x1, waiting for transfers between devices, mp_sum_scatter(): return jnp.sum(lax.all_to_all(blocks, axis, 0, 0), axis=0)  5.19 us
    all_to_all x1, starting transfers between devices, mp_sum_scatter(): return jnp.sum(lax.all_to_all(blocks, axis, 0, 0), axis=0)  5.07 us
  transfers between devices with their start and end apart: 20, of which 16 were waited for; matrix products, arithmetic and copies ran while one was open for 5% of the time, Pallas kernels for 11%

profile of v15, /device:TPU:68, one launch (start us, length us, event | category | flops | bytes accessed | tf_op | source)
XLA Modules:
  0.0 219.8 jit_solution(17787086052176084666)
XLA Ops:
  7.3 0.8 copy.61
  8.4 1.1 copy.64
  10.2 0.9 reduce-precision_convert_fusion
  11.1 0.8 pad_maximum_fusion.11
  12.4 0.9 collective-permute-done.8
  13.4 0.6 collective-permute-start.9
  14.2 8.0 %collective-permute-done.9 = bf16[256,384]{1,0:T(8,128)(2,1)S(1)} collective-permute-done((bf16[256,384]{1,0:T(8,128)(2,1)S(1)}, bf16[256,384]{1,0:T(8,128)(2,1)S(1)}, u32[]{:S(2)}, u32[]{:S(2)}) %collective-permute-start.9) | collective-permute-done | bytes 196640 | tf_op jit(solution)/shard_map/ppermute | solution.py:36
  22.2 0.9 maximum_select_fusion.2
  23.5 0.6 collective-permute-start.1
  24.1 6.0 %collective-permute-done.1 = f32[264,128]{1,0:T(8,128)S(1)} collective-permute-done((f32[264,128]{1,0:T(8,128)S(1)}, f32[264,128]{1,0:T(8,128)S(1)}, u32[]{:S(2)}, u32[]{:S(2)}) %collective-permute-start.1) | collective-permute-done | bytes 135200 | tf_op jit(solution)/shard_map/ppermute | solution.py:36
  30.5 3.8 %collective-permute-start.2 = (f32[264,128]{0,1:T(8,128)S(1)}, f32[264,128]{0,1:T(8,128)S(1)}, u32[]{:S(2)}, u32[]{:S(2)}) collective-permute-start(f32[264,128]{0,1:T(8,128)S(1)} %pad_maximum_fusion.2), channel_id=1, source_target_pairs={{0,32},{8,40},{16,48},{24,56},{32,64},{40,72},{48,80},{56,88},{64,... | collective-permute-start | bytes 405512 | tf_op jit(solution)/shard_map/ppermute | solution.py:33
  34.4 5.1 %collective-permute-done.2 = f32[264,128]{0,1:T(8,128)S(1)} collective-permute-done((f32[264,128]{0,1:T(8,128)S(1)}, f32[264,128]{0,1:T(8,128)S(1)}, u32[]{:S(2)}, u32[]{:S(2)}) %collective-permute-start.2) | collective-permute-done | bytes 135200 | tf_op jit(solution)/shard_map/ppermute | solution.py:33
  39.5 7.4 %collective-permute-start.3 = (f32[264,128]{0,1:T(8,128)S(1)}, f32[264,128]{0,1:T(8,128)S(1)}, u32[]{:S(2)}, u32[]{:S(2)}) collective-permute-start(f32[264,128]{0,1:T(8,128)S(1)} %pad_maximum_fusion.3), channel_id=1, source_target_pairs={{0,32},{8,40},{16,48},{24,56},{32,64},{40,72},{48,80},{56,88},{64,... | collective-permute-start | bytes 405512 | tf_op jit(solution)/shard_map/ppermute | solution.py:33
  47.0 7.1 %collective-permute-done.3 = f32[264,128]{0,1:T(8,128)S(1)} collective-permute-done((f32[264,128]{0,1:T(8,128)S(1)}, f32[264,128]{0,1:T(8,128)S(1)}, u32[]{:S(2)}, u32[]{:S(2)}) %collective-permute-start.3) | collective-permute-done | bytes 135200 | tf_op jit(solution)/shard_map/ppermute | solution.py:33
  54.2 10.8 %collective-permute-start.4 = (f32[264,128]{0,1:T(8,128)S(1)}, f32[264,128]{0,1:T(8,128)S(1)}, u32[]{:S(2)}, u32[]{:S(2)}) collective-permute-start(f32[264,128]{0,1:T(8,128)S(1)} %pad_maximum_fusion.4), channel_id=1, source_target_pairs={{0,64},{8,72},{16,80},{24,88},{32,96},{40,104},{48,112},{56,120},{... | collective-permute-start | bytes 405512 | tf_op jit(solution)/shard_map/ppermute | solution.py:33
  65.2 11.3 %collective-permute-done.4 = f32[264,128]{0,1:T(8,128)S(1)} collective-permute-done((f32[264,128]{0,1:T(8,128)S(1)}, f32[264,128]{0,1:T(8,128)S(1)}, u32[]{:S(2)}, u32[]{:S(2)}) %collective-permute-start.4) | collective-permute-done | bytes 135200 | tf_op jit(solution)/shard_map/ppermute | solution.py:33
  76.7 3.0 %collective-permute-start.5 = (f32[2,128,128]{2,1,0:T(8,128)S(1)}, f32[2,128,128]{2,1,0:T(8,128)S(1)}, u32[]{:S(2)}, u32[]{:S(2)}) collective-permute-start(f32[2,128,128]{2,1,0:T(8,128)S(1)} %multiply_add_fusion.8), channel_id=1, source_target_pairs={{0,128},{8,136},{16,144},{24,152},{32,160},{40,168},{48,176},{56,1... | collective-permute-start | bytes 393224 | tf_op jit(solution)/shard_map/ppermute | solution.py:111
  80.0 0.8 reshape.231.query_ref
  80.9 3.0 %collective-permute-done.5 = f32[2,128,128]{2,1,0:T(8,128)S(1)} collective-permute-done((f32[2,128,128]{2,1,0:T(8,128)S(1)}, f32[2,128,128]{2,1,0:T(8,128)S(1)}, u32[]{:S(2)}, u32[]{:S(2)}) %collective-permute-start.5) | collective-permute-done | bytes 131104 | tf_op jit(solution)/shard_map/ppermute | solution.py:111
  84.0 0.6 collective-permute-start.6
  84.6 0.7 convolution_bitcast_fusion.1
  85.3 5.3 %collective-permute-done.6 = f32[2,128,128]{2,1,0:T(8,128)S(1)} collective-permute-done((f32[2,128,128]{2,1,0:T(8,128)S(1)}, f32[2,128,128]{2,1,0:T(8,128)S(1)}, u32[]{:S(2)}, u32[]{:S(2)}) %collective-permute-start.6) | collective-permute-done | bytes 131104 | tf_op jit(solution)/shard_map/ppermute | solution.py:89
  91.0 23.6 %shard_map.94 = f32[1024,128]{1,0:T(8,128)} custom-call(s32[1]{0:T(128)} %bitcast.21.first_ref, bf16[1024,128]{1,0:T(8,128)(2,1)} %reshape.231.query_ref, bf16[4096,384]{1,0:T(8,128)(2,1)} %all-gather.2.cloned.1.call-done.key_ref.upper_ref.lower_ref, bf16[4096,384]{1,0:T(8,128)(2,1)} %all-gather.2.cloned.1.call-done.key_ref.upper_ref.lower_ref, ...), custom_call_target="tpu_custom_call" | custom-call | flops 4294967296 | bytes 3932160 | tf_op jit(solution)/shard_map/pallas_call | solution.py:198
  114.5 1.7 fusion.3
  116.3 1.1 fusion.12
  118.1 1.2 collective-permute-done.10
  119.9 7.4 %collective-permute-done.11 = f32[264,128]{1,0:T(8,128)S(1)} collective-permute-done((f32[264,128]{1,0:T(8,128)S(1)}, f32[264,128]{1,0:T(8,128)S(1)}, u32[]{:S(2)}, u32[]{:S(2)}) %collective-permute-start.11) | collective-permute-done | bytes 135200 | tf_op jit(solution)/shard_map/ppermute | solution.py:33
  127.7 1.9 collective-permute-start.12
  129.6 6.3 %collective-permute-done.12 = f32[264,128]{0,1:T(8,128)S(1)} collective-permute-done((f32[264,128]{0,1:T(8,128)S(1)}, f32[264,128]{0,1:T(8,128)S(1)}, u32[]{:S(2)}, u32[]{:S(2)}) %collective-permute-start.12) | collective-permute-done | bytes 135200 | tf_op jit(solution)/shard_map/ppermute | solution.py:33
  136.0 2.2 %collective-permute-start.13 = (f32[264,128]{0,1:T(8,128)S(1)}, f32[264,128]{0,1:T(8,128)S(1)}, u32[]{:S(2)}, u32[]{:S(2)}) collective-permute-start(f32[264,128]{0,1:T(8,128)S(1)} %pad_maximum_fusion.6), channel_id=1, source_target_pairs={{32,0},{40,8},{48,16},{56,24},{64,32},{72,40},{80,48},{88,56},{96,... | collective-permute-start | bytes 405512 | tf_op jit(solution)/shard_map/ppermute | solution.py:33
  138.3 20.0 %collective-permute-done.13 = f32[264,128]{0,1:T(8,128)S(1)} collective-permute-done((f32[264,128]{0,1:T(8,128)S(1)}, f32[264,128]{0,1:T(8,128)S(1)}, u32[]{:S(2)}, u32[]{:S(2)}) %collective-permute-start.13) | collective-permute-done | bytes 135200 | tf_op jit(solution)/shard_map/ppermute | solution.py:33
  158.3 0.7 pad_maximum_fusion.7
  159.0 1.9 collective-permute-start.14
  161.5 15.4 %collective-permute-done.14 = f32[264,128]{0,1:T(8,128)} collective-permute-done((f32[264,128]{0,1:T(8,128)}, f32[264,128]{0,1:T(8,128)}, u32[]{:S(2)}, u32[]{:S(2)}) %collective-permute-start.14) | collective-permute-done | bytes 135200 | tf_op jit(solution)/shard_map/ppermute | solution.py:33
  176.9 0.9 slice.111
  177.9 0.7 fusion.53
  178.7 1.3 collective-permute-start.15
  180.3 10.0 %collective-permute-done.15 = f32[2,128,128]{2,1,0:T(8,128)S(1)} collective-permute-done((f32[2,128,128]{2,1,0:T(8,128)S(1)}, f32[2,128,128]{2,1,0:T(8,128)S(1)}, u32[]{:S(2)}, u32[]{:S(2)}) %collective-permute-start.15) | collective-permute-done | bytes 131104 | tf_op jit(solution)/shard_map/ppermute | solution.py:111
  190.3 1.2 collective-permute-start.16
  191.6 1.1 fusion.6
  192.7 4.2 %collective-permute-done.16 = f32[2,128,128]{2,1,0:T(8,128)S(1)} collective-permute-done((f32[2,128,128]{2,1,0:T(8,128)S(1)}, f32[2,128,128]{2,1,0:T(8,128)S(1)}, u32[]{:S(2)}, u32[]{:S(2)}) %collective-permute-start.16) | collective-permute-done | bytes 131104 | tf_op jit(solution)/shard_map/ppermute | solution.py:89
  197.6 1.2 convolution_bitcast_fusion.2
  198.9 1.0 fusion.5
  199.9 0.7 copy.83
  200.6 5.1 %all-to-all-start = ((f32[8,16,256]{2,1,0:T(8,128)}), f32[8,16,256]{2,1,0:T(8,128)S(1)}, u32[]{:S(2)}, u32[]{:S(2)}) async-start(f32[8,16,256]{2,1,0:T(8,128)} %bitcast.41), calls=%async_computation | async-start | bytes 262144 | tf_op jit(solution)/shard_map/all_to_all | solution.py:135
  206.1 1.0 copy.84
  207.1 5.2 %all-to-all-done = f32[8,16,256]{2,1,0:T(8,128)S(1)} async-done(((f32[8,16,256]{2,1,0:T(8,128)}), f32[8,16,256]{2,1,0:T(8,128)S(1)}, u32[]{:S(2)}, u32[]{:S(2)}) %all-to-all-start) | async-done | bytes 131104 | tf_op jit(solution)/shard_map/all_to_all | solution.py:135
  212.3 0.6 slice_multiply_fusion
  (112 shorter events, 8.0 us)
Async XLA Ops:
  7.2 2.4 %copy-start = (bf16[128,128]{1,0:T(8,128)(2,1)S(1)}, bf16[128,128]{1,0:T(8,128)(2,1)}, u32[]{:S(2)}) copy-start(bf16[128,128]{1,0:T(8,128)(2,1)} %param.11) | copy-start | bytes 98308
  7.2 6.2 %copy-start.3 = (bf16[128,128]{1,0:T(8,128)(2,1)S(1)}, bf16[128,128]{1,0:T(8,128)(2,1)}, u32[]{:S(2)}) copy-start(bf16[128,128]{1,0:T(8,128)(2,1)} %param.8) | copy-start | bytes 98308
  7.2 83.8 %all-gather.2.cloned.1.call-start = ((), (), s32[]{:S(2)}) async-start(), calls=%async_computation.1 | async-start | bytes 3538944 | tf_op jit(solution)/shard_map/all_gather | solution.py:124
  10.1 3.9 %collective-permute-start = (f32[520,128]{1,0:T(8,128)S(1)}, f32[520,128]{1,0:T(8,128)S(1)}, u32[]{:S(2)}, u32[]{:S(2)}) collective-permute-start(f32[520,128]{1,0:T(8,128)S(1)} %pad_maximum_fusion), channel_id=1, source_target_pairs={{0,8},{8,0},{16,24},{24,16},{32,40},{40,32},{48,56},{56,48},{64,72... | collective-permute-start | bytes 798728 | tf_op jit(solution)/shard_map/ppermute | solution.py:36
  11.8 1.5 collective-permute-start.8
  13.4 8.8 %collective-permute-start.9 = (bf16[256,384]{1,0:T(8,128)(2,1)S(1)}, bf16[256,384]{1,0:T(8,128)(2,1)S(1)}, u32[]{:S(2)}, u32[]{:S(2)}) collective-permute-start(bf16[256,384]{1,0:T(8,128)(2,1)S(1)} %maximum_select_fusion.9), channel_id=1, source_target_pairs={{0,16},{8,24},{16,0},{24,8},{32,48},{40,56},{48,32},{56,40},{64,80... | collective-permute-start | bytes 589832 | tf_op jit(solution)/shard_map/ppermute | solution.py:36
  23.1 56.7 %copy-start.1 = (bf16[128,128]{1,0:T(8,128)(2,1)S(1)}, bf16[128,128]{1,0:T(8,128)(2,1)}, u32[]{:S(2)}) copy-start(bf16[128,128]{1,0:T(8,128)(2,1)} %param.12) | copy-start | bytes 98308
  23.2 56.9 %copy-start.2 = (bf16[128,1024]{1,0:T(8,128)(2,1)S(1)}, bf16[128,1024]{1,0:T(8,128)(2,1)}, u32[]{:S(2)}) copy-start(bf16[128,1024]{1,0:T(8,128)(2,1)} %param.7) | copy-start | bytes 786436
  23.5 6.6 %collective-permute-start.1 = (f32[264,128]{1,0:T(8,128)S(1)}, f32[264,128]{1,0:T(8,128)S(1)}, u32[]{:S(2)}, u32[]{:S(2)}) collective-permute-start(f32[264,128]{1,0:T(8,128)S(1)} %pad_maximum_fusion.8), channel_id=1, source_target_pairs={{0,16},{8,24},{16,0},{24,8},{32,48},{40,56},{48,32},{56,40},{64,80... | collective-permute-start | bytes 405512 | tf_op jit(solution)/shard_map/ppermute | solution.py:36
  30.5 8.9 %collective-permute-start.2 = (f32[264,128]{0,1:T(8,128)S(1)}, f32[264,128]{0,1:T(8,128)S(1)}, u32[]{:S(2)}, u32[]{:S(2)}) collective-permute-start(f32[264,128]{0,1:T(8,128)S(1)} %pad_maximum_fusion.2), channel_id=1, source_target_pairs={{0,32},{8,40},{16,48},{24,56},{32,64},{40,72},{48,80},{56,88},{64,... | collective-permute-start | bytes 405512 | tf_op jit(solution)/shard_map/ppermute | solution.py:33
  39.5 14.6 %collective-permute-start.3 = (f32[264,128]{0,1:T(8,128)S(1)}, f32[264,128]{0,1:T(8,128)S(1)}, u32[]{:S(2)}, u32[]{:S(2)}) collective-permute-start(f32[264,128]{0,1:T(8,128)S(1)} %pad_maximum_fusion.3), channel_id=1, source_target_pairs={{0,32},{8,40},{16,48},{24,56},{32,64},{40,72},{48,80},{56,88},{64,... | collective-permute-start | bytes 405512 | tf_op jit(solution)/shard_map/ppermute | solution.py:33
  54.2 22.3 %collective-permute-start.4 = (f32[264,128]{0,1:T(8,128)S(1)}, f32[264,128]{0,1:T(8,128)S(1)}, u32[]{:S(2)}, u32[]{:S(2)}) collective-permute-start(f32[264,128]{0,1:T(8,128)S(1)} %pad_maximum_fusion.4), channel_id=1, source_target_pairs={{0,64},{8,72},{16,80},{24,88},{32,96},{40,104},{48,112},{56,120},{... | collective-permute-start | bytes 405512 | tf_op jit(solution)/shard_map/ppermute | solution.py:33
  76.7 7.2 %collective-permute-start.5 = (f32[2,128,128]{2,1,0:T(8,128)S(1)}, f32[2,128,128]{2,1,0:T(8,128)S(1)}, u32[]{:S(2)}, u32[]{:S(2)}) collective-permute-start(f32[2,128,128]{2,1,0:T(8,128)S(1)} %multiply_add_fusion.8), channel_id=1, source_target_pairs={{0,128},{8,136},{16,144},{24,152},{32,160},{40,168},{48,176},{56,1... | collective-permute-start | bytes 393224 | tf_op jit(solution)/shard_map/ppermute | solution.py:111
  84.0 6.6 %collective-permute-start.6 = (f32[2,128,128]{2,1,0:T(8,128)S(1)}, f32[2,128,128]{2,1,0:T(8,128)S(1)}, u32[]{:S(2)}, u32[]{:S(2)}) collective-permute-start(f32[2,128,128]{2,1,0:T(8,128)S(1)} %get-tuple-element.27), channel_id=1, source_target_pairs={{0,16},{8,24},{16,0},{24,8},{32,48},{40,56},{48,32},{56,40},{64,80... | collective-permute-start | bytes 393224 | tf_op jit(solution)/shard_map/ppermute | solution.py:89
  90.7 23.9 %collective-permute-start.7 = (f32[4,128,128]{2,1,0:T(8,128)S(1)}, f32[4,128,128]{2,1,0:T(8,128)S(1)}, u32[]{:S(2)}, u32[]{:S(2)}) collective-permute-start(f32[4,128,128]{2,1,0:T(8,128)S(1)} %get-tuple-element.22), channel_id=1, source_target_pairs={{0,8},{8,0},{16,24},{24,16},{32,40},{40,32},{48,56},{56,48},{64,72... | collective-permute-start | bytes 786440 | tf_op jit(solution)/shard_map/ppermute | solution.py:89
  117.6 1.7 collective-permute-start.10
  119.8 7.5 %collective-permute-start.11 = (f32[264,128]{1,0:T(8,128)S(1)}, f32[264,128]{1,0:T(8,128)S(1)}, u32[]{:S(2)}, u32[]{:S(2)}) collective-permute-start(f32[264,128]{1,0:T(8,128)S(1)} %pad_maximum_fusion.9), channel_id=1, source_target_pairs={{0,16},{8,24},{16,0},{24,8},{32,48},{40,56},{48,32},{56,40},{64,80... | collective-permute-start | bytes 405512 | tf_op jit(solution)/shard_map/ppermute | solution.py:33
  127.7 8.3 %collective-permute-start.12 = (f32[264,128]{0,1:T(8,128)S(1)}, f32[264,128]{0,1:T(8,128)S(1)}, u32[]{:S(2)}, u32[]{:S(2)}) collective-permute-start(f32[264,128]{0,1:T(8,128)S(1)} %pad_maximum_fusion.5), channel_id=1, source_target_pairs={{32,0},{40,8},{48,16},{56,24},{64,32},{72,40},{80,48},{88,56},{96,... | collective-permute-start | bytes 405512 | tf_op jit(solution)/shard_map/ppermute | solution.py:33
  136.0 22.3 %collective-permute-start.13 = (f32[264,128]{0,1:T(8,128)S(1)}, f32[264,128]{0,1:T(8,128)S(1)}, u32[]{:S(2)}, u32[]{:S(2)}) collective-permute-start(f32[264,128]{0,1:T(8,128)S(1)} %pad_maximum_fusion.6), channel_id=1, source_target_pairs={{32,0},{40,8},{48,16},{56,24},{64,32},{72,40},{80,48},{88,56},{96,... | collective-permute-start | bytes 405512 | tf_op jit(solution)/shard_map/ppermute | solution.py:33
  158.2 0.7 copy-start.4
  159.0 17.9 %collective-permute-start.14 = (f32[264,128]{0,1:T(8,128)}, f32[264,128]{0,1:T(8,128)}, u32[]{:S(2)}, u32[]{:S(2)}) collective-permute-start(f32[264,128]{0,1:T(8,128)} %pad_maximum_fusion.7), channel_id=1, source_target_pairs={{64,0},{72,8},{80,16},{88,24},{96,32},{104,40},{112,48},{120,56},{... | collective-permute-start | bytes 405512 | tf_op jit(solution)/shard_map/ppermute | solution.py:33
  178.7 11.5 %collective-permute-start.15 = (f32[2,128,128]{2,1,0:T(8,128)S(1)}, f32[2,128,128]{2,1,0:T(8,128)S(1)}, u32[]{:S(2)}, u32[]{:S(2)}) collective-permute-start(f32[2,128,128]{2,1,0:T(8,128)S(1)} %multiply_add_fusion.4), channel_id=1, source_target_pairs={{128,0},{136,8},{144,16},{152,24},{160,32},{168,40},{176,48},{184,... | collective-permute-start | bytes 393224 | tf_op jit(solution)/shard_map/ppermute | solution.py:111
  190.3 6.6 %collective-permute-start.16 = (f32[2,128,128]{2,1,0:T(8,128)S(1)}, f32[2,128,128]{2,1,0:T(8,128)S(1)}, u32[]{:S(2)}, u32[]{:S(2)}) collective-permute-start(f32[2,128,128]{2,1,0:T(8,128)S(1)} %get-tuple-element.25), channel_id=1, source_target_pairs={{0,16},{8,24},{16,0},{24,8},{32,48},{40,56},{48,32},{56,40},{64,80... | collective-permute-start | bytes 393224 | tf_op jit(solution)/shard_map/ppermute | solution.py:89
  197.0 1.8 collective-permute-start.17
  200.6 11.7 %all-to-all-start = ((f32[8,16,256]{2,1,0:T(8,128)}), f32[8,16,256]{2,1,0:T(8,128)S(1)}, u32[]{:S(2)}, u32[]{:S(2)}) async-start(f32[8,16,256]{2,1,0:T(8,128)} %bitcast.41), calls=%async_computation | async-start | bytes 262144 | tf_op jit(solution)/shard_map/all_to_all | solution.py:135
Sparse Core Ops, SparseCore 0:
  23.2 60.6 all-gather.1

commit v16 on v12

--- a/solution.py
+++ b/solution.py
@@ -278,9 +278,9 @@
     )
     grad_c = jnp.einsum("hts,sn->tn", weighted, b_rows, precision=highest)
     grad_c = grad_c + jnp.einsum("thp,hpn->tn", scaled_mismatch, state_in, precision=highest)
-    summed = mp_sum_scatter(jnp.concatenate([grad_b, grad_c], axis=1), "mp")
+    summed = mp_sum_scatter(jnp.concatenate([grad_b, grad_c * c_scale], axis=1), "mp")
     summed_b, summed_c = summed[:, :N], summed[:, N:]
-    return (grad_x.reshape(row_count, heads * HEAD_WIDTH), summed_b, summed_c * c_scale)
+    return (grad_x.reshape(row_count, heads * HEAD_WIDTH), summed_b, summed_c)
 
 
 def solution(mesh):

time: 195 us -> 195 us (level)
  transfers between devices with their start and end apart: 20 -> 20, of which waited for: 16 -> 17; matrix products, arithmetic and copies ran while one was open for 5% -> 5% of each run, Pallas kernels for 5% -> 5%
where the time goes in v16:
time: 195 us; the launch traced here: 193 us
  waiting for transfers between devices  104 us (53%)
  starting transfers between devices  42.3 us (22%)
  between operations  14.6 us (7%)
  Pallas kernels  10.3 us (5%)
  matrix products  8.22 us (4%)
  local copies, waits for them, and re-layouts  7.28 us (4%)
  other arithmetic  6.72 us (3%)
    ppermute x8, waiting for transfers between devices, send_with_logs(): got = lax.ppermute(payload, axis, perm)  60.7 us
    ppermute x8, starting transfers between devices, send_with_logs(): got = lax.ppermute(payload, axis, perm)  29.2 us
    ppermute x4, waiting for transfers between devices, send_with_logs(): got, got_extra = lax.ppermute((payload, extra), axis, perm)  14.9 us
    ppermute x2, waiting for transfers between devices, exclusive_scan(): got_state = lax.ppermute(window_state, axis, perm)  12.2 us
    ppermute x4, waiting for transfers between devices, pair_up(): got = lax.ppermute(send, axis, [(j, j ^ bit) for j in range(count)])  10.5 us
    pallas_call x1, Pallas kernels, attend(): pl.pallas_call(functools.partial(attend_kernel, heads=heads), out_shape=j...  10.3 us
    all_to_all x1, waiting for transfers between devices, mp_sum_scatter(): return jnp.sum(lax.all_to_all(blocks, axis, 0, 0), axis=0)  5.19 us
    all_to_all x1, starting transfers between devices, mp_sum_scatter(): return jnp.sum(lax.all_to_all(blocks, axis, 0, 0), axis=0)  5.06 us
  transfers between devices with their start and end apart: 20, of which 17 were waited for; matrix products, arithmetic and copies ran while one was open for 5% of the time, Pallas kernels for 5%

profile of v16, /device:TPU:68, one launch (start us, length us, event | category | flops | bytes accessed | tf_op | source)
XLA Modules:
  0.0 193.0 jit_solution(4521183627904160550)
XLA Ops:
  7.3 0.8 copy.68
  8.4 1.1 copy.71
  10.2 0.9 reduce-precision_convert_fusion
  11.1 0.8 pad_maximum_fusion.11
  12.4 0.9 collective-permute-done.8
  13.4 0.6 collective-permute-start.9
  14.2 8.0 %collective-permute-done.9 = bf16[256,384]{1,0:T(8,128)(2,1)S(1)} collective-permute-done((bf16[256,384]{1,0:T(8,128)(2,1)S(1)}, bf16[256,384]{1,0:T(8,128)(2,1)S(1)}, u32[]{:S(2)}, u32[]{:S(2)}) %collective-permute-start.9) | collective-permute-done | bytes 196640 | tf_op jit(solution)/shard_map/ppermute | solution.py:36
  22.2 0.9 maximum_select_fusion.2
  24.1 6.0 %collective-permute-done.1 = f32[264,128]{1,0:T(8,128)S(1)} collective-permute-done((f32[264,128]{1,0:T(8,128)S(1)}, f32[264,128]{1,0:T(8,128)S(1)}, u32[]{:S(2)}, u32[]{:S(2)}) %collective-permute-start.1) | collective-permute-done | bytes 135200 | tf_op jit(solution)/shard_map/ppermute | solution.py:36
  30.5 3.8 %collective-permute-start.2 = (f32[264,128]{0,1:T(8,128)S(1)}, f32[264,128]{0,1:T(8,128)S(1)}, u32[]{:S(2)}, u32[]{:S(2)}) collective-permute-start(f32[264,128]{0,1:T(8,128)S(1)} %pad_maximum_fusion.2), channel_id=1, source_target_pairs={{0,32},{8,40},{16,48},{24,56},{32,64},{40,72},{48,80},{56,88},{64,... | collective-permute-start | bytes 405512 | tf_op jit(solution)/shard_map/ppermute | solution.py:33
  34.4 5.1 %collective-permute-done.2 = f32[264,128]{0,1:T(8,128)S(1)} collective-permute-done((f32[264,128]{0,1:T(8,128)S(1)}, f32[264,128]{0,1:T(8,128)S(1)}, u32[]{:S(2)}, u32[]{:S(2)}) %collective-permute-start.2) | collective-permute-done | bytes 135200 | tf_op jit(solution)/shard_map/ppermute | solution.py:33
  39.5 7.4 %collective-permute-start.3 = (f32[264,128]{0,1:T(8,128)S(1)}, f32[264,128]{0,1:T(8,128)S(1)}, u32[]{:S(2)}, u32[]{:S(2)}) collective-permute-start(f32[264,128]{0,1:T(8,128)S(1)} %pad_maximum_fusion.3), channel_id=1, source_target_pairs={{0,32},{8,40},{16,48},{24,56},{32,64},{40,72},{48,80},{56,88},{64,... | collective-permute-start | bytes 405512 | tf_op jit(solution)/shard_map/ppermute | solution.py:33
  47.0 7.1 %collective-permute-done.3 = f32[264,128]{0,1:T(8,128)S(1)} collective-permute-done((f32[264,128]{0,1:T(8,128)S(1)}, f32[264,128]{0,1:T(8,128)S(1)}, u32[]{:S(2)}, u32[]{:S(2)}) %collective-permute-start.3) | collective-permute-done | bytes 135200 | tf_op jit(solution)/shard_map/ppermute | solution.py:33
  54.2 10.8 %collective-permute-start.4 = (f32[264,128]{0,1:T(8,128)S(1)}, f32[264,128]{0,1:T(8,128)S(1)}, u32[]{:S(2)}, u32[]{:S(2)}) collective-permute-start(f32[264,128]{0,1:T(8,128)S(1)} %pad_maximum_fusion.4), channel_id=1, source_target_pairs={{0,64},{8,72},{16,80},{24,88},{32,96},{40,104},{48,112},{56,120},{... | collective-permute-start | bytes 405512 | tf_op jit(solution)/shard_map/ppermute | solution.py:33
  65.2 11.3 %collective-permute-done.4 = f32[264,128]{0,1:T(8,128)S(1)} collective-permute-done((f32[264,128]{0,1:T(8,128)S(1)}, f32[264,128]{0,1:T(8,128)S(1)}, u32[]{:S(2)}, u32[]{:S(2)}) %collective-permute-start.4) | collective-permute-done | bytes 135200 | tf_op jit(solution)/shard_map/ppermute | solution.py:33
  76.7 3.0 %collective-permute-start.5 = (f32[2,128,128]{2,1,0:T(8,128)S(1)}, f32[2,128,128]{2,1,0:T(8,128)S(1)}, u32[]{:S(2)}, u32[]{:S(2)}) collective-permute-start(f32[2,128,128]{2,1,0:T(8,128)S(1)} %multiply_add_fusion.8), channel_id=1, source_target_pairs={{0,128},{8,136},{16,144},{24,152},{32,160},{40,168},{48,176},{56,1... | collective-permute-start | bytes 393224 | tf_op jit(solution)/shard_map/ppermute | solution.py:111
  80.0 0.8 reshape.231.query_ref
  80.9 3.0 %collective-permute-done.5 = f32[2,128,128]{2,1,0:T(8,128)S(1)} collective-permute-done((f32[2,128,128]{2,1,0:T(8,128)S(1)}, f32[2,128,128]{2,1,0:T(8,128)S(1)}, u32[]{:S(2)}, u32[]{:S(2)}) %collective-permute-start.5) | collective-permute-done | bytes 131104 | tf_op jit(solution)/shard_map/ppermute | solution.py:111
  84.0 0.6 collective-permute-start.6
  84.6 0.7 convolution_bitcast_fusion.1
  85.3 5.3 %collective-permute-done.6 = f32[2,128,128]{2,1,0:T(8,128)S(1)} collective-permute-done((f32[2,128,128]{2,1,0:T(8,128)S(1)}, f32[2,128,128]{2,1,0:T(8,128)S(1)}, u32[]{:S(2)}, u32[]{:S(2)}) %collective-permute-start.6) | collective-permute-done | bytes 131104 | tf_op jit(solution)/shard_map/ppermute | solution.py:89
  91.0 10.3 %shard_map.94 = f32[1024,128]{1,0:T(8,128)} custom-call(s32[1]{0:T(128)} %bitcast.21.first_ref, bf16[1024,128]{1,0:T(8,128)(2,1)} %reshape.231.query_ref, bf16[4096,384]{1,0:T(8,128)(2,1)} %all-gather.2.cloned.1.call-done.key_ref.upper_ref.lower_ref, bf16[4096,384]{1,0:T(8,128)(2,1)} %all-gather.2.cloned.1.call-done.key_ref.upper_ref.lower_ref, ...), custom_call_target="tpu_custom_call" | custom-call | flops 4294967296 | bytes 3932160 | tf_op jit(solution)/shard_map/pallas_call | solution.py:198
  101.2 1.7 fusion.3
  103.0 1.1 fusion.13
  104.8 1.2 collective-permute-done.10
  106.5 0.6 collective-permute-start.11
  107.1 6.9 %collective-permute-done.11 = f32[264,128]{1,0:T(8,128)S(1)} collective-permute-done((f32[264,128]{1,0:T(8,128)S(1)}, f32[264,128]{1,0:T(8,128)S(1)}, u32[]{:S(2)}, u32[]{:S(2)}) %collective-permute-start.11) | collective-permute-done | bytes 135200 | tf_op jit(solution)/shard_map/ppermute | solution.py:33
  114.4 1.9 collective-permute-start.12
  116.3 6.3 %collective-permute-done.12 = f32[264,128]{0,1:T(8,128)S(1)} collective-permute-done((f32[264,128]{0,1:T(8,128)S(1)}, f32[264,128]{0,1:T(8,128)S(1)}, u32[]{:S(2)}, u32[]{:S(2)}) %collective-permute-start.12) | collective-permute-done | bytes 135200 | tf_op jit(solution)/shard_map/ppermute | solution.py:33
  122.7 2.2 %collective-permute-start.13 = (f32[264,128]{0,1:T(8,128)S(1)}, f32[264,128]{0,1:T(8,128)S(1)}, u32[]{:S(2)}, u32[]{:S(2)}) collective-permute-start(f32[264,128]{0,1:T(8,128)S(1)} %pad_maximum_fusion.6), channel_id=1, source_target_pairs={{32,0},{40,8},{48,16},{56,24},{64,32},{72,40},{80,48},{88,56},{96,... | collective-permute-start | bytes 405512 | tf_op jit(solution)/shard_map/ppermute | solution.py:33
  125.0 13.2 %collective-permute-done.13 = f32[264,128]{0,1:T(8,128)S(1)} collective-permute-done((f32[264,128]{0,1:T(8,128)S(1)}, f32[264,128]{0,1:T(8,128)S(1)}, u32[]{:S(2)}, u32[]{:S(2)}) %collective-permute-start.13) | collective-permute-done | bytes 135200 | tf_op jit(solution)/shard_map/ppermute | solution.py:33
  138.2 0.7 pad_maximum_fusion.7
  138.9 1.9 collective-permute-start.14
  141.4 9.6 %collective-permute-done.14 = f32[264,128]{0,1:T(8,128)} collective-permute-done((f32[264,128]{0,1:T(8,128)}, f32[264,128]{0,1:T(8,128)}, u32[]{:S(2)}, u32[]{:S(2)}) %collective-permute-start.14) | collective-permute-done | bytes 135200 | tf_op jit(solution)/shard_map/ppermute | solution.py:33
  151.1 0.9 slice.111
  152.1 0.7 fusion.54
  152.9 1.3 collective-permute-start.15
  154.4 9.3 %collective-permute-done.15 = f32[2,128,128]{2,1,0:T(8,128)S(1)} collective-permute-done((f32[2,128,128]{2,1,0:T(8,128)S(1)}, f32[2,128,128]{2,1,0:T(8,128)S(1)}, u32[]{:S(2)}, u32[]{:S(2)}) %collective-permute-start.15) | collective-permute-done | bytes 131104 | tf_op jit(solution)/shard_map/ppermute | solution.py:111
  163.7 0.7 collective-permute-start.16
  164.4 0.7 fusion.7
  165.1 5.2 %collective-permute-done.16 = f32[2,128,128]{2,1,0:T(8,128)S(1)} collective-permute-done((f32[2,128,128]{2,1,0:T(8,128)S(1)}, f32[2,128,128]{2,1,0:T(8,128)S(1)}, u32[]{:S(2)}, u32[]{:S(2)}) %collective-permute-start.16) | collective-permute-done | bytes 131104 | tf_op jit(solution)/shard_map/ppermute | solution.py:89
  171.0 1.2 convolution_bitcast_fusion.2
  172.3 1.0 fusion.5
  173.3 0.7 pad_maximum_fusion.10
  173.9 5.1 %all-to-all-start = ((f32[8,16,256]{2,1,0:T(8,128)}), f32[8,16,256]{2,1,0:T(8,128)S(1)}, u32[]{:S(2)}, u32[]{:S(2)}) async-start(f32[8,16,256]{2,1,0:T(8,128)} %bitcast.41), calls=%async_computation | async-start | bytes 262144 | tf_op jit(solution)/shard_map/all_to_all | solution.py:135
  179.4 1.0 copy.94
  180.4 5.2 %all-to-all-done = f32[8,16,256]{2,1,0:T(8,128)S(1)} async-done(((f32[8,16,256]{2,1,0:T(8,128)}), f32[8,16,256]{2,1,0:T(8,128)S(1)}, u32[]{:S(2)}, u32[]{:S(2)}) %all-to-all-start) | async-done | bytes 131104 | tf_op jit(solution)/shard_map/all_to_all | solution.py:135
  185.6 0.6 fusion.83
  (111 shorter events, 8.4 us)
Async XLA Ops:
  7.2 2.4 %copy-start = (bf16[128,128]{1,0:T(8,128)(2,1)S(1)}, bf16[128,128]{1,0:T(8,128)(2,1)}, u32[]{:S(2)}) copy-start(bf16[128,128]{1,0:T(8,128)(2,1)} %param.11) | copy-start | bytes 98308
  7.2 6.2 %copy-start.3 = (bf16[128,128]{1,0:T(8,128)(2,1)S(1)}, bf16[128,128]{1,0:T(8,128)(2,1)}, u32[]{:S(2)}) copy-start(bf16[128,128]{1,0:T(8,128)(2,1)} %param.8) | copy-start | bytes 98308
  7.2 83.8 %all-gather.2.cloned.1.call-start = ((), (), s32[]{:S(2)}) async-start(), calls=%async_computation.1 | async-start | bytes 3538944 | tf_op jit(solution)/shard_map/all_gather | solution.py:124
  10.1 3.9 %collective-permute-start = (f32[520,128]{1,0:T(8,128)S(1)}, f32[520,128]{1,0:T(8,128)S(1)}, u32[]{:S(2)}, u32[]{:S(2)}) collective-permute-start(f32[520,128]{1,0:T(8,128)S(1)} %pad_maximum_fusion), channel_id=1, source_target_pairs={{0,8},{8,0},{16,24},{24,16},{32,40},{40,32},{48,56},{56,48},{64,72... | collective-permute-start | bytes 798728 | tf_op jit(solution)/shard_map/ppermute | solution.py:36
  11.8 1.5 collective-permute-start.8
  13.4 8.8 %collective-permute-start.9 = (bf16[256,384]{1,0:T(8,128)(2,1)S(1)}, bf16[256,384]{1,0:T(8,128)(2,1)S(1)}, u32[]{:S(2)}, u32[]{:S(2)}) collective-permute-start(bf16[256,384]{1,0:T(8,128)(2,1)S(1)} %maximum_select_fusion.9), channel_id=1, source_target_pairs={{0,16},{8,24},{16,0},{24,8},{32,48},{40,56},{48,32},{56,40},{64,80... | collective-permute-start | bytes 589832 | tf_op jit(solution)/shard_map/ppermute | solution.py:36
  23.1 56.7 %copy-start.1 = (bf16[128,128]{1,0:T(8,128)(2,1)S(1)}, bf16[128,128]{1,0:T(8,128)(2,1)}, u32[]{:S(2)}) copy-start(bf16[128,128]{1,0:T(8,128)(2,1)} %param.12) | copy-start | bytes 98308
  23.2 56.9 %copy-start.2 = (bf16[128,1024]{1,0:T(8,128)(2,1)S(1)}, bf16[128,1024]{1,0:T(8,128)(2,1)}, u32[]{:S(2)}) copy-start(bf16[128,1024]{1,0:T(8,128)(2,1)} %param.7) | copy-start | bytes 786436
  23.5 6.6 %collective-permute-start.1 = (f32[264,128]{1,0:T(8,128)S(1)}, f32[264,128]{1,0:T(8,128)S(1)}, u32[]{:S(2)}, u32[]{:S(2)}) collective-permute-start(f32[264,128]{1,0:T(8,128)S(1)} %pad_maximum_fusion.8), channel_id=1, source_target_pairs={{0,16},{8,24},{16,0},{24,8},{32,48},{40,56},{48,32},{56,40},{64,80... | collective-permute-start | bytes 405512 | tf_op jit(solution)/shard_map/ppermute | solution.py:36
  30.5 8.9 %collective-permute-start.2 = (f32[264,128]{0,1:T(8,128)S(1)}, f32[264,128]{0,1:T(8,128)S(1)}, u32[]{:S(2)}, u32[]{:S(2)}) collective-permute-start(f32[264,128]{0,1:T(8,128)S(1)} %pad_maximum_fusion.2), channel_id=1, source_target_pairs={{0,32},{8,40},{16,48},{24,56},{32,64},{40,72},{48,80},{56,88},{64,... | collective-permute-start | bytes 405512 | tf_op jit(solution)/shard_map/ppermute | solution.py:33
  39.5 14.6 %collective-permute-start.3 = (f32[264,128]{0,1:T(8,128)S(1)}, f32[264,128]{0,1:T(8,128)S(1)}, u32[]{:S(2)}, u32[]{:S(2)}) collective-permute-start(f32[264,128]{0,1:T(8,128)S(1)} %pad_maximum_fusion.3), channel_id=1, source_target_pairs={{0,32},{8,40},{16,48},{24,56},{32,64},{40,72},{48,80},{56,88},{64,... | collective-permute-start | bytes 405512 | tf_op jit(solution)/shard_map/ppermute | solution.py:33
  54.2 22.3 %collective-permute-start.4 = (f32[264,128]{0,1:T(8,128)S(1)}, f32[264,128]{0,1:T(8,128)S(1)}, u32[]{:S(2)}, u32[]{:S(2)}) collective-permute-start(f32[264,128]{0,1:T(8,128)S(1)} %pad_maximum_fusion.4), channel_id=1, source_target_pairs={{0,64},{8,72},{16,80},{24,88},{32,96},{40,104},{48,112},{56,120},{... | collective-permute-start | bytes 405512 | tf_op jit(solution)/shard_map/ppermute | solution.py:33
  76.7 7.2 %collective-permute-start.5 = (f32[2,128,128]{2,1,0:T(8,128)S(1)}, f32[2,128,128]{2,1,0:T(8,128)S(1)}, u32[]{:S(2)}, u32[]{:S(2)}) collective-permute-start(f32[2,128,128]{2,1,0:T(8,128)S(1)} %multiply_add_fusion.8), channel_id=1, source_target_pairs={{0,128},{8,136},{16,144},{24,152},{32,160},{40,168},{48,176},{56,1... | collective-permute-start | bytes 393224 | tf_op jit(solution)/shard_map/ppermute | solution.py:111
  84.0 6.6 %collective-permute-start.6 = (f32[2,128,128]{2,1,0:T(8,128)S(1)}, f32[2,128,128]{2,1,0:T(8,128)S(1)}, u32[]{:S(2)}, u32[]{:S(2)}) collective-permute-start(f32[2,128,128]{2,1,0:T(8,128)S(1)} %get-tuple-element.27), channel_id=1, source_target_pairs={{0,16},{8,24},{16,0},{24,8},{32,48},{40,56},{48,32},{56,40},{64,80... | collective-permute-start | bytes 393224 | tf_op jit(solution)/shard_map/ppermute | solution.py:89
  90.7 10.6 %collective-permute-start.7 = (f32[4,128,128]{2,1,0:T(8,128)S(1)}, f32[4,128,128]{2,1,0:T(8,128)S(1)}, u32[]{:S(2)}, u32[]{:S(2)}) collective-permute-start(f32[4,128,128]{2,1,0:T(8,128)S(1)} %get-tuple-element.22), channel_id=1, source_target_pairs={{0,8},{8,0},{16,24},{24,16},{32,40},{40,32},{48,56},{56,48},{64,72... | collective-permute-start | bytes 786440 | tf_op jit(solution)/shard_map/ppermute | solution.py:89
  104.3 1.7 collective-permute-start.10
  106.5 7.5 %collective-permute-start.11 = (f32[264,128]{1,0:T(8,128)S(1)}, f32[264,128]{1,0:T(8,128)S(1)}, u32[]{:S(2)}, u32[]{:S(2)}) collective-permute-start(f32[264,128]{1,0:T(8,128)S(1)} %pad_maximum_fusion.9), channel_id=1, source_target_pairs={{0,16},{8,24},{16,0},{24,8},{32,48},{40,56},{48,32},{56,40},{64,80... | collective-permute-start | bytes 405512 | tf_op jit(solution)/shard_map/ppermute | solution.py:33
  114.4 8.3 %collective-permute-start.12 = (f32[264,128]{0,1:T(8,128)S(1)}, f32[264,128]{0,1:T(8,128)S(1)}, u32[]{:S(2)}, u32[]{:S(2)}) collective-permute-start(f32[264,128]{0,1:T(8,128)S(1)} %pad_maximum_fusion.5), channel_id=1, source_target_pairs={{32,0},{40,8},{48,16},{56,24},{64,32},{72,40},{80,48},{88,56},{96,... | collective-permute-start | bytes 405512 | tf_op jit(solution)/shard_map/ppermute | solution.py:33
  122.7 15.5 %collective-permute-start.13 = (f32[264,128]{0,1:T(8,128)S(1)}, f32[264,128]{0,1:T(8,128)S(1)}, u32[]{:S(2)}, u32[]{:S(2)}) collective-permute-start(f32[264,128]{0,1:T(8,128)S(1)} %pad_maximum_fusion.6), channel_id=1, source_target_pairs={{32,0},{40,8},{48,16},{56,24},{64,32},{72,40},{80,48},{88,56},{96,... | collective-permute-start | bytes 405512 | tf_op jit(solution)/shard_map/ppermute | solution.py:33
  138.2 0.7 copy-start.4
  138.9 12.2 %collective-permute-start.14 = (f32[264,128]{0,1:T(8,128)}, f32[264,128]{0,1:T(8,128)}, u32[]{:S(2)}, u32[]{:S(2)}) collective-permute-start(f32[264,128]{0,1:T(8,128)} %pad_maximum_fusion.7), channel_id=1, source_target_pairs={{64,0},{72,8},{80,16},{88,24},{96,32},{104,40},{112,48},{120,56},{... | collective-permute-start | bytes 405512 | tf_op jit(solution)/shard_map/ppermute | solution.py:33
  152.9 10.8 %collective-permute-start.15 = (f32[2,128,128]{2,1,0:T(8,128)S(1)}, f32[2,128,128]{2,1,0:T(8,128)S(1)}, u32[]{:S(2)}, u32[]{:S(2)}) collective-permute-start(f32[2,128,128]{2,1,0:T(8,128)S(1)} %multiply_add_fusion.4), channel_id=1, source_target_pairs={{128,0},{136,8},{144,16},{152,24},{160,32},{168,40},{176,48},{184,... | collective-permute-start | bytes 393224 | tf_op jit(solution)/shard_map/ppermute | solution.py:111
  163.7 6.6 %collective-permute-start.16 = (f32[2,128,128]{2,1,0:T(8,128)S(1)}, f32[2,128,128]{2,1,0:T(8,128)S(1)}, u32[]{:S(2)}, u32[]{:S(2)}) collective-permute-start(f32[2,128,128]{2,1,0:T(8,128)S(1)} %get-tuple-element.25), channel_id=1, source_target_pairs={{0,16},{8,24},{16,0},{24,8},{32,48},{40,56},{48,32},{56,40},{64,80... | collective-permute-start | bytes 393224 | tf_op jit(solution)/shard_map/ppermute | solution.py:89
  170.4 1.8 collective-permute-start.17
  173.9 11.6 %all-to-all-start = ((f32[8,16,256]{2,1,0:T(8,128)}), f32[8,16,256]{2,1,0:T(8,128)S(1)}, u32[]{:S(2)}, u32[]{:S(2)}) async-start(f32[8,16,256]{2,1,0:T(8,128)} %bitcast.41), calls=%async_computation | async-start | bytes 262144 | tf_op jit(solution)/shard_map/all_to_all | solution.py:135
Sparse Core Ops, SparseCore 0:
  23.2 60.6 all-gather.1
